TPU v7x, 256 devices: a whole 4x4x8 slice. The times are simulated.
256 devices in a mesh: dp: 8 (over z), seq: 32 (over y, x, core).
Axes of the slice: x: 4, y: 4, z: 8, core: 2. Of those that a mesh axis runs over, the one named last changes fastest.
Arguments:
- inputs: bfloat16 [8, 4096, 2048], P('dp', 'seq'), may hold values from -6 to 6
- weight_codes: bfloat16 [2048, 1280], P('seq'), may hold values from -4 to 4
- scales: bfloat16 [2048, 10], P('seq'), may hold values from 0.010986328 to 0.043945312
- log_decay: float32 [8, 16, 4096], P('dp', None, 'seq'), may hold values from -0.85 to 0, as said below
- cotangent: bfloat16 [8, 4096, 1024], P('dp', 'seq'), may hold values from -6 to 6
Outputs:
- grad_inputs: float32 [8, 4096, 2048], P('dp', 'seq')
- grad_weight: float32 [2048, 1280], P('seq')
Inputs may be any that keep to these rules, and one draw needn't show every extreme that they name: log_decay is negative everywhere.
All inputs are finite; a program needn't handle non-finite values.
Results may differ from a plain program's by a relative error of at most 0.017.
Values may be sent and summed in bfloat16 or wider, within the bound.
No kernel may reach another device: no remote copies, remote signals or barrier semaphores. Data moves between devices by JAX's collectives and lax.ppermute only.
A program may use at most 128 MiB of HBM per device.

v0:
```python
import math

import jax
import jax.numpy as jnp
from jax import lax
from jax.sharding import PartitionSpec as P


def entering(part, axis, combine, identity, reverse):
    count = lax.axis_size(axis)
    place = lax.axis_index(axis)
    ahead = count - 1 - place if reverse else place
    gathered = jax.tree.map(lambda a: lax.all_gather(a, axis), part)
    state = jax.tree.map(lambda a, e: jnp.zeros_like(a) + jnp.asarray(e, a.dtype), part, identity)

    def one(hop, state):
        source = count - 1 - hop if reverse else hop
        return combine(
            state, jax.tree.map(lambda a: lax.dynamic_index_in_dim(a, source, 0, False), gathered)
        )

    return lax.fori_loop(0, ahead, one, state)


def dequantize(code_rows, scale_rows):
    row_count, col_count = code_rows.shape
    group_count = scale_rows.shape[1]
    spread = code_rows.astype(jnp.float32).reshape(row_count, group_count, col_count // group_count)
    spread = spread * scale_rows.astype(jnp.float32)[:, :, None]
    return spread.reshape(row_count, col_count).astype(jnp.bfloat16)


def block_prep(ld_block):
    cum_log = jnp.cumsum(ld_block, axis=1)
    input_scale = jnp.sqrt(-jnp.expm1(2.0 * ld_block))
    tail_weight = jnp.exp(cum_log[:, -1:] - cum_log) * input_scale
    return (cum_log, input_scale, tail_weight)


def weighted_pair(x_vals, grad_out, tail_weight, cum_log, inv_root):
    head_weight = jnp.exp(cum_log) * inv_root
    weighted_x = (x_vals.astype(jnp.float32) * tail_weight.T[:, :, None]).astype(jnp.bfloat16)
    weighted_g = (grad_out.astype(jnp.float32) * head_weight.T[:, :, None]).astype(jnp.bfloat16)
    return (weighted_x, weighted_g)


def summaries(x_vals, b_mat, c_mat, grad_out, ld_block):
    cum_log, input_scale, tail_weight = block_prep(ld_block)
    inv_root = 1.0 / math.sqrt(b_mat.shape[1])
    weighted_x, weighted_g = weighted_pair(x_vals, grad_out, tail_weight, cum_log, inv_root)
    fwd_state = jnp.einsum("sn,shp->hnp", b_mat, weighted_x, preferred_element_type=jnp.float32)
    back_state = jnp.einsum("tn,thp->hnp", c_mat, weighted_g, preferred_element_type=jnp.float32)
    return (jnp.exp(cum_log[:, -1]), fwd_state, back_state)


def block_grads(x_vals, b_mat, c_mat, grad_out, ld_block, state_in, back_in):
    block_len = ld_block.shape[1]
    cum_log, input_scale, tail_weight = block_prep(ld_block)
    inv_root = 1.0 / math.sqrt(b_mat.shape[1])
    weighted_x, weighted_g = weighted_pair(x_vals, grad_out, tail_weight, cum_log, inv_root)
    row_ids = lax.broadcasted_iota(jnp.int32, (block_len, block_len), 0)
    col_ids = lax.broadcasted_iota(jnp.int32, (block_len, block_len), 1)
    lower_mask = (row_ids >= col_ids)[None]
    log_gap = cum_log[:, :, None] - cum_log[:, None, :]
    decay_mat = jnp.where(lower_mask, jnp.exp(jnp.where(lower_mask, log_gap, 0.0)), 0.0)
    state_low = state_in.astype(jnp.bfloat16)
    back_low = back_in.astype(jnp.bfloat16)
    x_dot_g = jnp.einsum("thp,shp->hts", grad_out, x_vals, preferred_element_type=jnp.float32)
    c_dot_b = jnp.dot(c_mat, b_mat.T, preferred_element_type=jnp.float32)
    mix_weights = (
        jnp.sum(decay_mat * input_scale[:, None, :] * x_dot_g, axis=0) * inv_root
    ).astype(jnp.bfloat16)
    d_c = jnp.einsum("hnp,thp->tn", state_low, weighted_g, preferred_element_type=jnp.float32)
    d_c = d_c + jnp.dot(mix_weights, b_mat, preferred_element_type=jnp.float32)
    d_b = jnp.einsum("hnp,thp->tn", back_low, weighted_x, preferred_element_type=jnp.float32)
    d_b = d_b + jnp.dot(mix_weights.T, c_mat, preferred_element_type=jnp.float32)
    d_x = (
        jnp.einsum("tn,hnp->thp", b_mat, back_low, preferred_element_type=jnp.float32)
        * tail_weight.T[:, :, None]
    )
    inner_weights = (decay_mat * c_dot_b[None] * inv_root).astype(jnp.bfloat16)
    inner = jnp.einsum("hus,uhp->shp", inner_weights, grad_out, preferred_element_type=jnp.float32)
    d_x = d_x + input_scale.T[:, :, None] * inner
    return (d_x, d_b, d_c)


def state_chain(decays, adds, start, backward):

    def step(carry, item):
        return (item[0][:, None, None] * carry + item[1], carry)

    return lax.scan(step, start, (decays, adds), reverse=backward)


def join_summary(earlier, later):
    return (earlier[0] * later[0], later[0][:, None, None] * earlier[1] + later[1])


def local(inputs, weight_codes, scales, log_decay, cotangent):
    tok_count = inputs.shape[1]
    features = inputs[0]
    grad_out = cotangent[0]
    head_count = log_decay.shape[1]
    hp_width = grad_out.shape[1]
    head_dim = hp_width // head_count
    proj_width = weight_codes.shape[1]
    state_width = (proj_width - hp_width) // 2
    full_codes, full_scales = (
        lax.all_gather(weight_codes, "seq", axis=0, tiled=True),
        lax.all_gather(scales, "seq", axis=0, tiled=True),
    )
    weights = dequantize(full_codes, full_scales)
    projected = jnp.dot(features, weights, preferred_element_type=jnp.float32).astype(jnp.bfloat16)
    block_len = min(128, tok_count)
    block_count = tok_count // block_len
    x_blocks = projected[:, :hp_width].reshape(block_count, block_len, head_count, head_dim)
    b_blocks = projected[:, hp_width : hp_width + state_width].reshape(
        block_count, block_len, state_width
    )
    c_blocks = projected[:, hp_width + state_width :].reshape(block_count, block_len, state_width)
    g_blocks = grad_out.reshape(block_count, block_len, head_count, head_dim)
    ld_blocks = log_decay[0].reshape(head_count, block_count, block_len).transpose(1, 0, 2)
    decays, fwd_states, back_states = jax.vmap(summaries)(
        x_blocks, b_blocks, c_blocks, g_blocks, ld_blocks
    )
    zero_state = jnp.zeros((head_count, state_width, head_dim), jnp.float32)
    dev_decay = jnp.prod(decays, axis=0)
    dev_fwd, unused_a = state_chain(decays, fwd_states, zero_state, False)
    dev_back, unused_b = state_chain(decays, back_states, zero_state, True)
    neutral = (jnp.ones((head_count,), jnp.float32), zero_state)
    carried = entering((dev_decay, dev_fwd), "seq", join_summary, neutral, False)
    returned = entering((dev_decay, dev_back), "seq", join_summary, neutral, True)
    unused_c, state_starts = state_chain(decays, fwd_states, carried[1], False)
    unused_d, back_starts = state_chain(decays, back_states, returned[1], True)
    d_x, d_b, d_c = lax.map(
        lambda block_item: block_grads(*block_item),
        (x_blocks, b_blocks, c_blocks, g_blocks, ld_blocks, state_starts, back_starts),
    )
    d_proj = jnp.concatenate(
        [
            d_x.reshape(tok_count, hp_width),
            d_b.reshape(tok_count, state_width),
            d_c.reshape(tok_count, state_width),
        ],
        axis=1,
    ).astype(jnp.bfloat16)
    grad_in = lax.dot_general(
        d_proj, weights, (((1,), (1,)), ((), ())), preferred_element_type=jnp.float32
    )
    seq_count = lax.axis_size("seq")
    group_count = lax.axis_size("dp")
    norm_factor = 1.0 / math.sqrt(group_count * seq_count * tok_count)
    partial_grad = lax.psum_scatter(
        lax.dot_general(
            features, d_proj, (((0,), (0,)), ((), ())), preferred_element_type=jnp.float32
        ),
        "seq",
        scatter_dimension=0,
        tiled=True,
    )
    summed_grad = lax.psum(partial_grad, "dp")
    return (grad_in[None], summed_grad * norm_factor)


def solution(mesh):
    placed = (
        P("dp", "seq", None),
        P("seq", None),
        P("seq", None),
        P("dp", None, "seq"),
        P("dp", "seq", None),
    )
    return jax.shard_map(
        local,
        mesh=mesh,
        in_specs=placed,
        out_specs=(P("dp", "seq", None), P("seq", None)),
        check_vma=False,
    )
```

profile of v0, /device:TPU:8, one launch (start us, length us, event | category | flops | bytes accessed | tf_op | source)
XLA Modules:
  0.0 521.6 jit_solution(17085878530613788069)
XLA Ops:
  8.0 24.5 %all-gather.1 = bf16[32,64,10]{1,2,0:T(8,128)(2,1)S(1)} all-gather(bf16[1,64,10]{1,2,0:T(8,128)(2,1)} %bitcast.145), channel_id=1, replica_groups=mesh['dp'=8,'seq'=32] {'seq'}, dimensions={0}, use_global_device_ids=true | all-gather | bytes 42240 | tf_op jit(solution)/shard_map/all_gather | solution.py:110
  35.7 1.3 fusion.43
  37.0 28.6 %all-gather.6.cloned.1.call-done = bf16[2048,1280]{1,0:T(8,128)(2,1)} async-done(((bf16[64,1280]{1,0:T(8,128)(2,1)}), bf16[2048,1280]{1,0:T(8,128)(2,1)}) %all-gather.6.cloned.1.call-update) | async-done | bytes 5242896 | tf_op jit(solution)/shard_map/all_gather | solution.py:109
  65.6 7.9 %copy.59 = bf16[2048,1280]{0,1:T(8,128)(2,1)} copy(bf16[2048,1280]{1,0:T(8,128)(2,1)} %all-gather.6.cloned.1.call-done) | data formatting | bytes 10485760 | tf_op jit(solution)/shard_map/all_gather | solution.py:109
  73.5 3.9 fusion
  77.5 2.4 copy-done.2
  79.9 1.5 fusion.1
  85.4 21.5 %all-gather = f32[32,16,1]{1,2,0:T(1,128)} all-gather(f32[1,16,1]{1,2,0:T(1,128)S(1)} %exp.58), channel_id=2, replica_groups=mesh['dp'=8,'seq'=32] {'seq'}, dimensions={0}, use_global_device_ids=true | all-gather | bytes 2112 | tf_op jit(solution)/shard_map/all_gather | solution.py:13
  108.7 51.6 %all-gather.10.cloned.1.call-done = f32[32,16,128,64]{2,3,1,0:T(8,128)} async-done(((f32[1,16,128,64]{2,3,1,0:T(8,128)}), f32[32,16,128,64]{2,3,1,0:T(8,128)}) %all-gather.10.cloned.1.call-update) | async-done | bytes 16777232 | tf_op jit(solution)/shard_map/all_gather | solution.py:13
  160.4 19.0 %while.17 = (s32[]{:T(128)}, f32[16,128,64]{2,1,0:T(8,128)S(1)}, s32[]{:T(128)}, f32[32,16]{1,0:T(8,128)}, f32[32,16,128,64]{2,3,1,0:T(8,128)}, /*index=5*/s32[]{:T(128)}, s32[]{:T(128)}, s32[]{:T(128)}) while((s32[]{:T(128)}, f32[16,128,64]{2,1,0:T(8,128)S(1)}, s32[]{:T(128)}, f32[32,16]{1,0:T(8,128)}, f32[32,16,128,64]{2,3,1,0:T(8,128)}, ...), condition=%wide.region_6.7_spmd, body=%wide.region_5.6_spmd.sunk | while | flops 262149 | bytes 3670343 | solution.py:22
  165.2 1.1 constant_dynamic-slice_fusion.5
  167.5 1.1 constant_dynamic-slice_fusion.5
  169.9 1.1 constant_dynamic-slice_fusion.5
  174.6 1.1 constant_dynamic-slice_fusion.5
  177.0 1.1 constant_dynamic-slice_fusion.5
  179.4 60.6 %all-gather.8.cloned.1.call-done = f32[32,16,128,64]{2,3,1,0:T(8,128)} async-done(((f32[1,16,128,64]{2,3,1,0:T(8,128)}), f32[32,16,128,64]{2,3,1,0:T(8,128)}) %all-gather.8.cloned.1.call-update) | async-done | bytes 16777232 | tf_op jit(solution)/shard_map/all_gather | solution.py:13
  240.1 54.5 %while.16 = (s32[]{:T(128)}, f32[16,128,64]{2,1,0:T(8,128)S(1)}, s32[]{:T(128)}, f32[32,16]{1,0:T(8,128)}, f32[32,16,128,64]{2,3,1,0:T(8,128)}, /*index=5*/s32[]{:T(128)}, s32[]{:T(128)}, s32[]{:T(128)}, s32[]{:T(128)}) while((s32[]{:T(128)}, f32[16,128,64]{2,1,0:T(8,128)S(1)}, s32[]{:T(128)}, f32[32,16]{1,0:T(8,128)}, ...), condition=%wide.region_2.3_spmd, body=%wide.region_1.2_spmd.sunk | while | flops 262150 | bytes 3670363 | solution.py:22
  242.5 1.1 constant_dynamic-slice_fusion.4
  244.8 1.1 constant_dynamic-slice_fusion.4
  247.2 1.1 constant_dynamic-slice_fusion.4
  249.6 1.1 constant_dynamic-slice_fusion.4
  252.0 1.1 constant_dynamic-slice_fusion.4
  254.3 1.1 constant_dynamic-slice_fusion.4
  294.9 1.2 convolution_bitcast_fusion.7
  296.1 1.5 convolution_bitcast_fusion.6
  298.8 5.3 %convolution_bitcast_fusion = f32[2048,1280]{0,1:T(8,128)} fusion(bf16[1,128,2048]{2,1,0:T(8,128)(2,1)S(1)} %copy-done, bf16[128,128]{0,1:T(8,128)(2,1)S(1)} %fusion.12, bf16[128,128]{0,1:T(8,128)(2,1)S(1)} %fusion.11, bf16[128,1024]{0,1:T(8,128)(2,1)S(1)} %bitcast.132), kind=kOutput, calls=%fused_computation.8 | convolution fusion | flops 672071680 | bytes 11337728 | tf_op jit(solution)/shard_map/dot_general | solution.py:154
  304.2 11.3 %copy.89 = f32[2048,1280]{1,0:T(8,128)} copy(f32[2048,1280]{0,1:T(8,128)} %convolution_bitcast_fusion) | data formatting | bytes 20971520
  315.5 121.3 %reduce-scatter.4.cloned.1.call-done = f32[64,1280]{1,0:T(8,128)} async-done(((f32[2048,1280]{1,0:T(8,128)}), f32[64,1280]{1,0:T(8,128)}) %reduce-scatter.4.cloned.1.call-update) | async-done | bytes 327696
  436.9 2.1 copy.90
  438.9 4.3 convolution_bitcast_fusion.1
  443.3 69.7 %all-reduce.2.cloned.1.call-done = f32[64,1280]{0,1:T(8,128)} async-done(((f32[64,1280]{0,1:T(8,128)}), f32[64,1280]{0,1:T(8,128)}) %all-reduce.2.cloned.1.call-update) | async-done | bytes 327696 | tf_op jit(solution)/shard_map/psum | solution.py:161
  513.0 1.1 broadcast_multiply_fusion
  (170 shorter events, 72.5 us)
Async XLA Ops:
  7.2 72.7 %copy-start = (bf16[1,128,2048]{2,1,0:T(8,128)(2,1)S(1)}, bf16[1,128,2048]{2,1,0:T(8,128)(2,1)}, u32[]{:S(2)}) copy-start(bf16[1,128,2048]{2,1,0:T(8,128)(2,1)} %param.9) | copy-start | bytes 1572868
  7.2 58.4 %all-gather.6.cloned.1.call-start = ((), (), s32[]{:S(2)}) async-start(), calls=%async_computation.1 | async-start | bytes 5406720 | tf_op jit(solution)/shard_map/all_gather | solution.py:109
  7.9 152.4 %all-gather.10.cloned.1.call-start = ((), (), s32[]{:S(2)}) async-start(), calls=%async_computation.3 | async-start | bytes 17301504 | tf_op jit(solution)/shard_map/all_gather | solution.py:13
  77.5 2.4 copy-start.2
  79.9 3.4 copy-start.5
  83.2 156.7 %all-gather.8.cloned.1.call-start = ((), (), s32[]{:S(2)}) async-start(), calls=%async_computation.2 | async-start | bytes 17301504 | tf_op jit(solution)/shard_map/all_gather | solution.py:13
  83.5 76.8 %copy-start.3 = (bf16[1,128,1024]{1,2,0:T(8,128)(2,1)}, bf16[1,128,1024]{1,2,0:T(8,128)(2,1)S(1)}, u32[]{:S(2)}) copy-start(bf16[1,128,1024]{1,2,0:T(8,128)(2,1)S(1)} %copy.63) | copy-start | bytes 786436
  85.3 351.5 %reduce-scatter.4.cloned.1.call-start = ((), (), s32[]{:S(2)}) async-start(), calls=%async_computation.5 | async-start | bytes 10813440
  106.9 53.4 %copy-start.7 = (pred[128,128]{0,1:T(8,128)(4,1)}, pred[128,128]{0,1:T(8,128)(4,1)S(1)}, u32[]{:S(2)}) copy-start(pred[128,128]{0,1:T(8,128)(4,1)S(1)} %iota_compare_fusion) | copy-start | bytes 49156
  179.4 60.7 %copy-start.1 = (f32[16,128,64]{2,1,0:T(8,128)}, f32[16,128,64]{2,1,0:T(8,128)S(1)}, u32[]{:S(2)}) copy-start(f32[16,128,64]{2,1,0:T(8,128)S(1)} %get-tuple-element.218) | copy-start | bytes 1572868
  294.6 3.7 copy-start.4
  294.6 3.7 copy-start.6
  294.6 3.7 copy-start.8
  294.6 3.7 copy-start.9
  315.5 197.5 %all-reduce.2.cloned.1.call-start = ((), (), s32[]{:S(2)}) async-start(), calls=%async_computation.4 | async-start | bytes 1310720 | tf_op jit(solution)/shard_map/psum | solution.py:161
Sparse Core Ops, SparseCore 0:
  10.6 54.9 all-gather.5
  83.4 76.8 all-gather.9
  162.9 77.0 all-gather.7
  315.6 121.2 reduce-scatter.3
  439.2 73.7 all-reduce.1
where the time goes:
time: 525 us; the launch traced here: 522 us
  waiting for transfers between devices  332 us (63%)
  local copies, waits for them, and re-layouts  91.1 us (17%)
  blocking collectives  46 us (9%)
  matrix products  18.9 us (4%)
  other arithmetic  17.6 us (3%)
  between operations  14 us (3%)
    unnamed x6, waiting for transfers between devices  122 us
    all_gather x2, waiting for transfers between devices, entering(): gathered = jax.tree.map(lambda a: lax.all_gather(a, axis), part)  112 us
    psum x1, waiting for transfers between devices, local(): summed_grad = lax.psum(partial_grad, 'dp')  69.7 us
    dynamic_slice x62, local copies, waits for them, and re-layouts, one(): lax.dynamic_index_in_dim(a, source, 0, False)  44 us
    all_gather x1, waiting for transfers between devices, local(): lax.all_gather(weight_codes, 'seq', axis=0, tiled=True)  28.6 us
    all_gather x1, blocking collectives, local(): lax.all_gather(scales, 'seq', axis=0, tiled=True)  24.5 us
    all_gather x1, blocking collectives, entering(): gathered = jax.tree.map(lambda a: lax.all_gather(a, axis), part)  21.5 us
    mul x31, local copies, waits for them, and re-layouts, join_summary(): later[0][:, None, None] * earlier[1] + later[1]  21.4 us
  transfers between devices with their start and end apart: 5, of which 5 were waited for; matrix products, arithmetic and copies ran while one was open for 6% of the time, Pallas kernels for 0%

commit v1 on v0

--- a/solution.py
+++ b/solution.py
@@ -6,20 +6,36 @@
 from jax.sharding import PartitionSpec as P
 
 
-def entering(part, axis, combine, identity, reverse):
+def shifted(value, axis, step, reverse):
     count = lax.axis_size(axis)
-    place = lax.axis_index(axis)
-    ahead = count - 1 - place if reverse else place
-    gathered = jax.tree.map(lambda a: lax.all_gather(a, axis), part)
-    state = jax.tree.map(lambda a, e: jnp.zeros_like(a) + jnp.asarray(e, a.dtype), part, identity)
+    if reverse:
+        pairs = [(place, place - step) for place in range(step, count)]
+    else:
+        pairs = [(place, place + step) for place in range(count - step)]
+    return lax.ppermute(value, axis, pairs)
 
-    def one(hop, state):
-        source = count - 1 - hop if reverse else hop
-        return combine(
-            state, jax.tree.map(lambda a: lax.dynamic_index_in_dim(a, source, 0, False), gathered)
+
+def scan_entering(decay, state, axis, reverse):
+    head_count = state.shape[0]
+    packed = jnp.concatenate(
+        [state.reshape(head_count, -1), jnp.broadcast_to(decay[:, None], (head_count, 128))],
+        axis=1,
+    )
+    split = packed.shape[1] - 128
+    packed = shifted(packed, axis, 1, reverse)
+    step = 1
+    while step < lax.axis_size(axis):
+        earlier = shifted(packed, axis, step, reverse)
+        later_decay = packed[:, split:]
+        packed = jnp.concatenate(
+            [
+                later_decay[:, :1] * earlier[:, :split] + packed[:, :split],
+                earlier[:, split:] * later_decay,
+            ],
+            axis=1,
         )
-
-    return lax.fori_loop(0, ahead, one, state)
+        step *= 2
+    return packed[:, :split].reshape(state.shape)
 
 
 def dequantize(code_rows, scale_rows):
@@ -92,10 +108,6 @@
     return lax.scan(step, start, (decays, adds), reverse=backward)
 
 
-def join_summary(earlier, later):
-    return (earlier[0] * later[0], later[0][:, None, None] * earlier[1] + later[1])
-
-
 def local(inputs, weight_codes, scales, log_decay, cotangent):
     tok_count = inputs.shape[1]
     features = inputs[0]
@@ -105,11 +117,7 @@
     head_dim = hp_width // head_count
     proj_width = weight_codes.shape[1]
     state_width = (proj_width - hp_width) // 2
-    full_codes, full_scales = (
-        lax.all_gather(weight_codes, "seq", axis=0, tiled=True),
-        lax.all_gather(scales, "seq", axis=0, tiled=True),
-    )
-    weights = dequantize(full_codes, full_scales)
+    weights = lax.all_gather(dequantize(weight_codes, scales), "seq", axis=0, tiled=True)
     projected = jnp.dot(features, weights, preferred_element_type=jnp.float32).astype(jnp.bfloat16)
     block_len = min(128, tok_count)
     block_count = tok_count // block_len
@@ -127,9 +135,8 @@
     dev_decay = jnp.prod(decays, axis=0)
     dev_fwd, unused_a = state_chain(decays, fwd_states, zero_state, False)
     dev_back, unused_b = state_chain(decays, back_states, zero_state, True)
-    neutral = (jnp.ones((head_count,), jnp.float32), zero_state)
-    carried = entering((dev_decay, dev_fwd), "seq", join_summary, neutral, False)
-    returned = entering((dev_decay, dev_back), "seq", join_summary, neutral, True)
+    carried = (None, scan_entering(dev_decay, dev_fwd, "seq", False))
+    returned = (None, scan_entering(dev_decay, dev_back, "seq", True))
     unused_c, state_starts = state_chain(decays, fwd_states, carried[1], False)
     unused_d, back_starts = state_chain(decays, back_states, returned[1], True)
     d_x, d_b, d_c = lax.map(

time: 525 us -> 391 us (0.74)
  local copies, waits for them, and re-layouts: 91.1 us -> 21.2 us
  waiting for transfers between devices: 332 us -> 282 us
  blocking collectives: 46 us -> 0 us
  starting transfers between devices: 0.2 us -> 40.1 us
  other arithmetic: 17.6 us -> 10.7 us
    all_gather x3 -> x1, waiting for transfers between devices: 141 us -> 50.5 us  [local(): lax.all_gather(dequantize(weight_codes, scales), 'seq', axis=0, tiled=True)]
    ppermute x0 -> x12, waiting for transfers between devices: none -> 57 us  [shifted(): return lax.ppermute(value, axis, pairs)]
    all_gather x2 -> x0, blocking collectives: 46 us -> none  [the longest x1 24.5 us: local(): lax.all_gather(scales, 'seq', axis=0, tiled=True)]
    dynamic_slice x62 -> x2, local copies, waits for them, and re-layouts: 44 us -> 0.67 us  [state_chain(): return lax.scan(step, start, (decays, adds), reverse=backward)]
    ppermute x0 -> x12, starting transfers between devices: none -> 39.9 us  [shifted(): return lax.ppermute(value, axis, pairs)]
    mul x31 -> x1, local copies, waits for them, and re-layouts: 21.4 us -> 0.19 us  [dequantize(): spread = spread * scale_rows.astype(jnp.float32)[:, :, None]]
    unnamed x6 -> x4, waiting for transfers between devices: 122 us -> 106 us
    all_gather x1 -> x0, local copies, waits for them, and re-layouts: 7.95 us -> none  [local(): lax.all_gather(weight_codes, 'seq', axis=0, tiled=True)]
  transfers between devices with their start and end apart: 5 -> 15, of which waited for: 5 -> 11; matrix products, arithmetic and copies ran while one was open for 6% -> 5% of each run, Pallas kernels for 0% -> 0%
where the time goes in v1:
time: 391 us; the launch traced here: 389 us
  waiting for transfers between devices  282 us (72%)
  starting transfers between devices  40.1 us (10%)
  local copies, waits for them, and re-layouts  21.2 us (5%)
  matrix products  20.9 us (5%)
  between operations  14.2 us (4%)
  other arithmetic  10.7 us (3%)
    unnamed x4, waiting for transfers between devices  106 us
    psum x1, waiting for transfers between devices, local(): summed_grad = lax.psum(partial_grad, 'dp')  68.9 us
    ppermute x12, waiting for transfers between devices, shifted(): return lax.ppermute(value, axis, pairs)  57 us
    all_gather x1, waiting for transfers between devices, local(): lax.all_gather(dequantize(weight_codes, scales), 'seq', axis=0, tiled=True)  50.5 us
    ppermute x12, starting transfers between devices, shifted(): return lax.ppermute(value, axis, pairs)  39.9 us
    unnamed x12, local copies, waits for them, and re-layouts  15.4 us
  transfers between devices with their start and end apart: 15, of which 11 were waited for; matrix products, arithmetic and copies ran while one was open for 5% of the time, Pallas kernels for 0%

profile of v1, /device:TPU:8, one launch (start us, length us, event | category | flops | bytes accessed | tf_op | source)
XLA Modules:
  0.0 389.5 jit_solution(13289274053930057519)
XLA Ops:
  8.2 1.7 fusion.30
  14.2 1.3 fusion.48
  15.7 50.5 %all-gather.2.cloned.1.call-done = bf16[2048,1280]{1,0:T(8,128)(2,1)} async-done(((bf16[64,1280]{1,0:T(8,128)(2,1)}), bf16[2048,1280]{1,0:T(8,128)(2,1)}) %all-gather.2.cloned.1.call-update) | async-done | bytes 5242896 | tf_op jit(solution)/shard_map/all_gather | solution.py:120
  66.1 4.1 %fusion = bf16[128,1280]{0,1:T(8,128)(2,1)S(1)} fusion(bf16[2048,1280]{1,0:T(8,128)(2,1)} %all-gather.2.cloned.1.call-done, bf16[1,128,2048]{2,1,0:T(8,128)(2,1)S(1)} %copy-done), kind=kOutput, calls=%fused_computation.3 | convolution fusion | flops 671252480 | bytes 6094848 | tf_op jit(solution)/shard_map/dot_general | solution.py:121
  73.2 4.4 %collective-permute-start = (f32[16,8320]{1,0:T(8,128)S(1)}, f32[16,8320]{1,0:T(8,128)S(1)}, u32[]{:S(2)}, u32[]{:S(2)}) collective-permute-start(f32[16,8320]{1,0:T(8,128)S(1)} %get-tuple-element.94), channel_id=1, source_target_pairs={{1,0},{2,1},{3,2},{4,3},{5,4},{6,5},{7,6},{8,7},{9,8},{10,9},{11,1... | collective-permute-start | bytes 1597448 | tf_op jit(solution)/shard_map/ppermute | solution.py:15
  77.6 1.9 collective-permute-start.6
  79.5 4.8 %collective-permute-done = f32[16,8320]{1,0:T(8,128)S(1)} collective-permute-done((f32[16,8320]{1,0:T(8,128)S(1)}, f32[16,8320]{1,0:T(8,128)S(1)}, u32[]{:S(2)}, u32[]{:S(2)}) %collective-permute-start) | collective-permute-done | bytes 532512 | tf_op jit(solution)/shard_map/ppermute | solution.py:15
  84.3 5.9 %collective-permute-start.1 = (f32[16,8320]{1,0:T(8,128)S(1)}, f32[16,8320]{1,0:T(8,128)S(1)}, u32[]{:S(2)}, u32[]{:S(2)}) collective-permute-start(f32[16,8320]{1,0:T(8,128)S(1)} %collective-permute-done), channel_id=1, source_target_pairs={{1,0},{2,1},{3,2},{4,3},{5,4},{6,5},{7,6},{8,7},{9,8},{10,9},{11,1... | collective-permute-start | bytes 1597448 | tf_op jit(solution)/shard_map/ppermute | solution.py:15
  92.0 1.9 collective-permute-start.7
  94.2 2.8 collective-permute-done.1
  97.2 1.9 collective-permute-start.2
  99.1 5.6 %collective-permute-done.7 = f32[16,8320]{1,0:T(8,128)S(1)} collective-permute-done((f32[16,8320]{1,0:T(8,128)S(1)}, f32[16,8320]{1,0:T(8,128)S(1)}, u32[]{:S(2)}, u32[]{:S(2)}) %collective-permute-start.7) | collective-permute-done | bytes 532512 | tf_op jit(solution)/shard_map/ppermute | solution.py:15
  104.9 1.9 collective-permute-start.8
  107.0 3.6 collective-permute-done.2
  110.8 1.9 collective-permute-start.3
  112.8 20.1 %collective-permute-done.8 = f32[16,8320]{1,0:T(8,128)S(1)} collective-permute-done((f32[16,8320]{1,0:T(8,128)S(1)}, f32[16,8320]{1,0:T(8,128)S(1)}, u32[]{:S(2)}, u32[]{:S(2)}) %collective-permute-start.8) | collective-permute-done | bytes 532512 | tf_op jit(solution)/shard_map/ppermute | solution.py:15
  133.0 1.9 collective-permute-start.9
  135.4 1.9 collective-permute-start.4
  137.3 11.6 %collective-permute-done.9 = f32[16,8320]{1,0:T(8,128)S(1)} collective-permute-done((f32[16,8320]{1,0:T(8,128)S(1)}, f32[16,8320]{1,0:T(8,128)S(1)}, u32[]{:S(2)}, u32[]{:S(2)}) %collective-permute-start.9) | collective-permute-done | bytes 532512 | tf_op jit(solution)/shard_map/ppermute | solution.py:15
  149.1 5.6 %collective-permute-start.10 = (f32[16,8320]{1,0:T(8,128)S(1)}, f32[16,8320]{1,0:T(8,128)S(1)}, u32[]{:S(2)}, u32[]{:S(2)}) collective-permute-start(f32[16,8320]{1,0:T(8,128)S(1)} %pad_maximum_fusion.8), channel_id=1, source_target_pairs={{0,8},{1,9},{2,10},{3,11},{4,12},{5,13},{6,14},{7,15},{8,16},{9,17... | collective-permute-start | bytes 1597448 | tf_op jit(solution)/shard_map/ppermute | solution.py:15
  155.1 1.3 collective-permute-start.5
  156.4 5.3 %collective-permute-done.10 = f32[16,8320]{1,0:T(8,128)S(1)} collective-permute-done((f32[16,8320]{1,0:T(8,128)S(1)}, f32[16,8320]{1,0:T(8,128)S(1)}, u32[]{:S(2)}, u32[]{:S(2)}) %collective-permute-start.10) | collective-permute-done | bytes 532512 | tf_op jit(solution)/shard_map/ppermute | solution.py:15
  161.9 9.4 %collective-permute-start.11 = (f32[16,8320]{1,0:T(8,128)S(1)}, f32[16,8320]{1,0:T(8,128)}, u32[]{:S(2)}, u32[]{:S(2)}) collective-permute-start(f32[16,8320]{1,0:T(8,128)S(1)} %pad_maximum_fusion.9), channel_id=1, source_target_pairs={{0,16},{1,17},{2,18},{3,19},{4,20},{5,21},{6,22},{7,23},{8,24},{9,... | collective-permute-start | bytes 1597448 | tf_op jit(solution)/shard_map/ppermute | solution.py:15
  174.0 3.2 collective-permute-done.11
  177.2 1.2 fusion.13
  180.3 1.4 fusion.5
  181.8 5.3 %convolution_bitcast_fusion = f32[2048,1280]{0,1:T(8,128)} fusion(bf16[1,128,2048]{2,1,0:T(8,128)(2,1)S(1)} %copy-done, bf16[128,128]{0,1:T(8,128)(2,1)S(1)} %fusion.7, bf16[128,128]{0,1:T(8,128)(2,1)S(1)} %fusion.6, bf16[128,1024]{0,1:T(8,128)(2,1)S(1)} %bitcast.105), kind=kOutput, calls=%fused_computation | convolution fusion | flops 672071680 | bytes 11337728 | tf_op jit(solution)/shard_map/dot_general | solution.py:161
  187.1 11.3 %copy.72 = f32[2048,1280]{1,0:T(8,128)} copy(f32[2048,1280]{0,1:T(8,128)} %convolution_bitcast_fusion) | data formatting | bytes 20971520
  198.5 106.1 %reduce-scatter.4.cloned.1.call-done = f32[64,1280]{1,0:T(8,128)} async-done(((f32[2048,1280]{1,0:T(8,128)}), f32[64,1280]{1,0:T(8,128)}) %reduce-scatter.4.cloned.1.call-update) | async-done | bytes 327696
  304.6 2.0 copy.73
  306.7 5.3 %convolution_bitcast_fusion.1 = f32[1,128,2048]{2,1,0:T(8,128)} fusion(bf16[2048,1280]{1,0:T(8,128)(2,1)} %all-gather.2.cloned.1.call-done, bf16[128,128]{0,1:T(8,128)(2,1)S(1)} %fusion.7, bf16[128,128]{0,1:T(8,128)(2,1)S(1)} %fusion.6, bf16[128,1024]{0,1:T(8,128)(2,1)S(1)} %bitcast.106), kind=kOutput, calls=%fused_computation.1 | convolution fusion | flops 672071680 | bytes 6619136 | tf_op jit(solution)/shard_map/dot_general | solution.py:154
  312.0 68.9 %all-reduce.2.cloned.1.call-done = f32[64,1280]{0,1:T(8,128)} async-done(((f32[64,1280]{0,1:T(8,128)}), f32[64,1280]{0,1:T(8,128)}) %all-reduce.2.cloned.1.call-update) | async-done | bytes 327696 | tf_op jit(solution)/shard_map/psum | solution.py:168
  (87 shorter events, 19.3 us)
Async XLA Ops:
  7.2 59.0 %copy-start = (bf16[1,128,2048]{2,1,0:T(8,128)(2,1)S(1)}, bf16[1,128,2048]{2,1,0:T(8,128)(2,1)}, u32[]{:S(2)}) copy-start(bf16[1,128,2048]{2,1,0:T(8,128)(2,1)} %param.5) | copy-start | bytes 1572868
  7.2 59.0 %all-gather.2.cloned.1.call-start = ((), (), s32[]{:S(2)}) async-start(), calls=%async_computation.1 | async-start | bytes 5406720 | tf_op jit(solution)/shard_map/all_gather | solution.py:120
  10.0 294.6 %reduce-scatter.4.cloned.1.call-start = ((), (), s32[]{:S(2)}) async-start(), calls=%async_computation.3 | async-start | bytes 10813440
  15.6 55.7 %copy-start.2 = (f32[128,16]{0,1:T(8,128)}, f32[128,16]{0,1:T(8,128)S(1)}, u32[]{:S(2)}) copy-start(f32[128,16]{0,1:T(8,128)S(1)} %get-tuple-element.80) | copy-start | bytes 24580
  73.2 11.2 %collective-permute-start = (f32[16,8320]{1,0:T(8,128)S(1)}, f32[16,8320]{1,0:T(8,128)S(1)}, u32[]{:S(2)}, u32[]{:S(2)}) collective-permute-start(f32[16,8320]{1,0:T(8,128)S(1)} %get-tuple-element.94), channel_id=1, source_target_pairs={{1,0},{2,1},{3,2},{4,3},{5,4},{6,5},{7,6},{8,7},{9,8},{10,9},{11,1... | collective-permute-start | bytes 1597448 | tf_op jit(solution)/shard_map/ppermute | solution.py:15
  77.6 14.5 %collective-permute-start.6 = (f32[16,8320]{1,0:T(8,128)S(1)}, f32[16,8320]{1,0:T(8,128)S(1)}, u32[]{:S(2)}, u32[]{:S(2)}) collective-permute-start(f32[16,8320]{1,0:T(8,128)S(1)} %get-tuple-element.95), channel_id=1, source_target_pairs={{0,1},{1,2},{2,3},{3,4},{4,5},{5,6},{6,7},{7,8},{8,9},{9,10},{10,1... | collective-permute-start | bytes 1597448 | tf_op jit(solution)/shard_map/ppermute | solution.py:15
  79.5 31.3 %copy-start.3 = (pred[128,128]{0,1:T(8,128)(4,1)}, pred[128,128]{0,1:T(8,128)(4,1)S(1)}, u32[]{:S(2)}) copy-start(pred[128,128]{0,1:T(8,128)(4,1)S(1)} %iota_compare_fusion) | copy-start | bytes 49156
  84.3 12.7 %collective-permute-start.1 = (f32[16,8320]{1,0:T(8,128)S(1)}, f32[16,8320]{1,0:T(8,128)S(1)}, u32[]{:S(2)}, u32[]{:S(2)}) collective-permute-start(f32[16,8320]{1,0:T(8,128)S(1)} %collective-permute-done), channel_id=1, source_target_pairs={{1,0},{2,1},{3,2},{4,3},{5,4},{6,5},{7,6},{8,7},{9,8},{10,9},{11,1... | collective-permute-start | bytes 1597448 | tf_op jit(solution)/shard_map/ppermute | solution.py:15
  92.0 12.7 %collective-permute-start.7 = (f32[16,8320]{1,0:T(8,128)S(1)}, f32[16,8320]{1,0:T(8,128)S(1)}, u32[]{:S(2)}, u32[]{:S(2)}) collective-permute-start(f32[16,8320]{1,0:T(8,128)S(1)} %collective-permute-done.6), channel_id=1, source_target_pairs={{0,1},{1,2},{2,3},{3,4},{4,5},{5,6},{6,7},{7,8},{8,9},{9,10},{10,1... | collective-permute-start | bytes 1597448 | tf_op jit(solution)/shard_map/ppermute | solution.py:15
  97.2 13.5 %collective-permute-start.2 = (f32[16,8320]{1,0:T(8,128)S(1)}, f32[16,8320]{1,0:T(8,128)S(1)}, u32[]{:S(2)}, u32[]{:S(2)}) collective-permute-start(f32[16,8320]{1,0:T(8,128)S(1)} %pad_maximum_fusion.2), channel_id=1, source_target_pairs={{2,0},{3,1},{4,2},{5,3},{6,4},{7,5},{8,6},{9,7},{10,8},{11,9},{12,... | collective-permute-start | bytes 1597448 | tf_op jit(solution)/shard_map/ppermute | solution.py:15
  104.9 28.0 %collective-permute-start.8 = (f32[16,8320]{1,0:T(8,128)S(1)}, f32[16,8320]{1,0:T(8,128)S(1)}, u32[]{:S(2)}, u32[]{:S(2)}) collective-permute-start(f32[16,8320]{1,0:T(8,128)S(1)} %pad_maximum_fusion.6), channel_id=1, source_target_pairs={{0,2},{1,3},{2,4},{3,5},{4,6},{5,7},{6,8},{7,9},{8,10},{9,11},{10,... | collective-permute-start | bytes 1597448 | tf_op jit(solution)/shard_map/ppermute | solution.py:15
  110.8 24.3 %collective-permute-start.3 = (f32[16,8320]{1,0:T(8,128)S(1)}, f32[16,8320]{1,0:T(8,128)S(1)}, u32[]{:S(2)}, u32[]{:S(2)}) collective-permute-start(f32[16,8320]{1,0:T(8,128)S(1)} %pad_maximum_fusion.3), channel_id=1, source_target_pairs={{4,0},{5,1},{6,2},{7,3},{8,4},{9,5},{10,6},{11,7},{12,8},{13,9},{1... | collective-permute-start | bytes 1597448 | tf_op jit(solution)/shard_map/ppermute | solution.py:15
  133.0 15.9 %collective-permute-start.9 = (f32[16,8320]{1,0:T(8,128)S(1)}, f32[16,8320]{1,0:T(8,128)S(1)}, u32[]{:S(2)}, u32[]{:S(2)}) collective-permute-start(f32[16,8320]{1,0:T(8,128)S(1)} %pad_maximum_fusion.7), channel_id=1, source_target_pairs={{0,4},{1,5},{2,6},{3,7},{4,8},{5,9},{6,10},{7,11},{8,12},{9,13},{1... | collective-permute-start | bytes 1597448 | tf_op jit(solution)/shard_map/ppermute | solution.py:15
  135.4 19.5 %collective-permute-start.4 = (f32[16,8320]{1,0:T(8,128)S(1)}, f32[16,8320]{1,0:T(8,128)S(1)}, u32[]{:S(2)}, u32[]{:S(2)}) collective-permute-start(f32[16,8320]{1,0:T(8,128)S(1)} %pad_maximum_fusion.4), channel_id=1, source_target_pairs={{8,0},{9,1},{10,2},{11,3},{12,4},{13,5},{14,6},{15,7},{16,8},{17,9... | collective-permute-start | bytes 1597448 | tf_op jit(solution)/shard_map/ppermute | solution.py:15
  148.9 23.9 %copy-start.1 = (bf16[128,1024]{0,1:T(8,128)(2,1)S(1)}, bf16[128,1024]{0,1:T(8,128)(2,1)}, u32[]{:S(2)}) copy-start(bf16[128,1024]{0,1:T(8,128)(2,1)} %get-tuple-element.75) | copy-start | bytes 786436
  149.1 12.6 %collective-permute-start.10 = (f32[16,8320]{1,0:T(8,128)S(1)}, f32[16,8320]{1,0:T(8,128)S(1)}, u32[]{:S(2)}, u32[]{:S(2)}) collective-permute-start(f32[16,8320]{1,0:T(8,128)S(1)} %pad_maximum_fusion.8), channel_id=1, source_target_pairs={{0,8},{1,9},{2,10},{3,11},{4,12},{5,13},{6,14},{7,15},{8,16},{9,17... | collective-permute-start | bytes 1597448 | tf_op jit(solution)/shard_map/ppermute | solution.py:15
  155.1 16.9 %collective-permute-start.5 = (f32[16,8320]{1,0:T(8,128)S(1)}, f32[16,8320]{1,0:T(8,128)S(1)}, u32[]{:S(2)}, u32[]{:S(2)}) collective-permute-start(f32[16,8320]{1,0:T(8,128)S(1)} %pad_maximum_fusion.5), channel_id=1, source_target_pairs={{16,0},{17,1},{18,2},{19,3},{20,4},{21,5},{22,6},{23,7},{24,8},{25... | collective-permute-start | bytes 1597448 | tf_op jit(solution)/shard_map/ppermute | solution.py:15
  161.9 15.3 %collective-permute-start.11 = (f32[16,8320]{1,0:T(8,128)S(1)}, f32[16,8320]{1,0:T(8,128)}, u32[]{:S(2)}, u32[]{:S(2)}) collective-permute-start(f32[16,8320]{1,0:T(8,128)S(1)} %pad_maximum_fusion.9), channel_id=1, source_target_pairs={{0,16},{1,17},{2,18},{3,19},{4,20},{5,21},{6,22},{7,23},{8,24},{9,... | collective-permute-start | bytes 1597448 | tf_op jit(solution)/shard_map/ppermute | solution.py:15
  198.5 182.4 %all-reduce.2.cloned.1.call-start = ((), (), s32[]{:S(2)}) async-start(), calls=%async_computation.2 | async-start | bytes 1310720 | tf_op jit(solution)/shard_map/psum | solution.py:168
Sparse Core Ops, SparseCore 0:
  11.1 54.9 all-gather.1
  198.6 105.9 reduce-scatter.3
  307.1 73.7 all-reduce.1

commit v2 on v1

--- a/solution.py
+++ b/solution.py
@@ -12,7 +12,7 @@
         pairs = [(place, place - step) for place in range(step, count)]
     else:
         pairs = [(place, place + step) for place in range(count - step)]
-    return lax.ppermute(value, axis, pairs)
+    return lax.ppermute(value.astype(jnp.bfloat16), axis, pairs).astype(value.dtype)
 
 
 def scan_entering(decay, state, axis, reverse):
@@ -36,6 +36,16 @@
         )
         step *= 2
     return packed[:, :split].reshape(state.shape)
+
+
+def butterfly_sum(value, axis):
+    count = lax.axis_size(axis)
+    step = 1
+    while step < count:
+        pairs = [(place, place ^ step) for place in range(count)]
+        value = value + lax.ppermute(value, axis, pairs)
+        step *= 2
+    return value
 
 
 def dequantize(code_rows, scale_rows):
@@ -165,7 +175,7 @@
         scatter_dimension=0,
         tiled=True,
     )
-    summed_grad = lax.psum(partial_grad, "dp")
+    summed_grad = butterfly_sum(partial_grad, "dp")
     return (grad_in[None], summed_grad * norm_factor)
 
 

time: 391 us -> 330 us (0.84)
  waiting for transfers between devices: 282 us -> 219 us
  starting transfers between devices: 40.1 us -> 45.6 us
    reduce_scatter x0 -> x1, waiting for transfers between devices: none -> 109 us  [local(): lax.psum_scatter(lax.dot_general(features, d_proj, (((0,), (0,)), ((), ()...]
    unnamed x4 -> x2, waiting for transfers between devices: 106 us -> 0.03 us
    psum x1 -> x0, waiting for transfers between devices: 68.9 us -> none  [local(): summed_grad = lax.psum(partial_grad, 'dp')]
    ppermute x12 -> x15, starting transfers between devices: 39.9 us -> 45.5 us  [the longest x12 35.7 us: shifted(): lax.ppermute(value.astype(jnp.bfloat16), axis, pairs).astype(value.dtype)]
    ppermute x12 -> x15, waiting for transfers between devices: 57 us -> 59.6 us  [the longest x12 30.5 us: shifted(): lax.ppermute(value.astype(jnp.bfloat16), axis, pairs).astype(value.dtype)]
  transfers between devices with their start and end apart: 15 -> 17, of which waited for: 11 -> 15; matrix products, arithmetic and copies ran while one was open for 5% -> 5% of each run, Pallas kernels for 0% -> 0%
where the time goes in v2:
time: 330 us; the launch traced here: 329 us
  waiting for transfers between devices  219 us (66%)
  starting transfers between devices  45.6 us (14%)
  matrix products  19.4 us (6%)
  local copies, waits for them, and re-layouts  18.3 us (6%)
  between operations  14.6 us (4%)
  other arithmetic  12.3 us (4%)
    reduce_scatter x1, waiting for transfers between devices, local(): lax.psum_scatter(lax.dot_general(features, d_proj, (((0,), (0,)), ((), ()...  109 us
    all_gather x1, waiting for transfers between devices, local(): lax.all_gather(dequantize(weight_codes, scales), 'seq', axis=0, tiled=True)  50.5 us
    ppermute x12, starting transfers between devices, shifted(): lax.ppermute(value.astype(jnp.bfloat16), axis, pairs).astype(value.dtype)  35.7 us
    ppermute x12, waiting for transfers between devices, shifted(): lax.ppermute(value.astype(jnp.bfloat16), axis, pairs).astype(value.dtype)  30.5 us
    ppermute x3, waiting for transfers between devices, butterfly_sum(): value = value + lax.ppermute(value, axis, pairs)  29.1 us
    unnamed x12, local copies, waits for them, and re-layouts  12.4 us
    ppermute x3, starting transfers between devices, butterfly_sum(): value = value + lax.ppermute(value, axis, pairs)  9.81 us
  transfers between devices with their start and end apart: 17, of which 15 were waited for; matrix products, arithmetic and copies ran while one was open for 5% of the time, Pallas kernels for 0%

profile of v2, /device:TPU:8, one launch (start us, length us, event | category | flops | bytes accessed | tf_op | source)
XLA Modules:
  0.0 329.0 jit_solution(9550839157973107413)
XLA Ops:
  8.2 1.7 fusion.26
  14.2 1.3 fusion.48
  15.7 50.5 %all-gather.2.cloned.1.call-done = bf16[2048,1280]{1,0:T(8,128)(2,1)} async-done(((bf16[64,1280]{1,0:T(8,128)(2,1)}), bf16[2048,1280]{1,0:T(8,128)(2,1)}) %all-gather.2.cloned.1.call-update) | async-done | bytes 5242896 | tf_op jit(solution)/shard_map/all_gather | solution.py:130
  66.1 4.1 %fusion = bf16[128,1280]{0,1:T(8,128)(2,1)S(1)} fusion(bf16[2048,1280]{1,0:T(8,128)(2,1)} %all-gather.2.cloned.1.call-done, bf16[1,128,2048]{2,1,0:T(8,128)(2,1)S(1)} %copy-done), kind=kOutput, calls=%fused_computation.3 | convolution fusion | flops 671252480 | bytes 6094848 | tf_op jit(solution)/shard_map/dot_general | solution.py:131
  73.1 2.2 collective-permute-start.6
  75.3 5.5 %collective-permute-start = (bf16[16,8320]{1,0:T(8,128)(2,1)S(1)}, bf16[16,8320]{1,0:T(8,128)(2,1)S(1)}, u32[]{:S(2)}, u32[]{:S(2)}) collective-permute-start(bf16[16,8320]{1,0:T(8,128)(2,1)S(1)} %get-tuple-element.131), channel_id=1, source_target_pairs={{1,0},{2,1},{3,2},{4,3},{5,4},{6,5},{7,6},{8,7},{9,8},{10,9},{11,1... | collective-permute-start | bytes 798728 | tf_op jit(solution)/shard_map/ppermute | solution.py:15
  83.0 1.9 collective-permute-start.7
  85.9 5.8 %collective-permute-start.1 = (bf16[16,8320]{1,0:T(8,128)(2,1)S(1)}, bf16[16,8320]{1,0:T(8,128)(2,1)S(1)}, u32[]{:S(2)}, u32[]{:S(2)}) collective-permute-start(bf16[16,8320]{1,0:T(8,128)(2,1)S(1)} %collective-permute-done), channel_id=1, source_target_pairs={{1,0},{2,1},{3,2},{4,3},{5,4},{6,5},{7,6},{8,7},{9,8},{10,9},{11,1... | collective-permute-start | bytes 798728 | tf_op jit(solution)/shard_map/ppermute | solution.py:15
  93.0 1.9 collective-permute-start.8
  95.8 5.5 %collective-permute-start.2 = (bf16[16,8320]{1,0:T(8,128)(2,1)S(1)}, bf16[16,8320]{1,0:T(8,128)(2,1)S(1)}, u32[]{:S(2)}, u32[]{:S(2)}) collective-permute-start(bf16[16,8320]{1,0:T(8,128)(2,1)S(1)} %pad_maximum_fusion.3), channel_id=1, source_target_pairs={{2,0},{3,1},{4,2},{5,3},{6,4},{7,5},{8,6},{9,7},{10,8},{11,9},{12,... | collective-permute-start | bytes 798728 | tf_op jit(solution)/shard_map/ppermute | solution.py:15
  101.5 2.0 collective-permute-done.8
  103.7 1.9 collective-permute-start.9
  105.6 8.0 %collective-permute-done.2 = bf16[16,8320]{1,0:T(8,128)(2,1)S(1)} collective-permute-done((bf16[16,8320]{1,0:T(8,128)(2,1)S(1)}, bf16[16,8320]{1,0:T(8,128)(2,1)S(1)}, u32[]{:S(2)}, u32[]{:S(2)}) %collective-permute-start.2) | collective-permute-done | bytes 266272 | tf_op jit(solution)/shard_map/ppermute | solution.py:15
  113.8 1.9 collective-permute-start.3
  117.0 1.9 collective-permute-start.10
  118.9 6.6 %collective-permute-done.3 = bf16[16,8320]{1,0:T(8,128)(2,1)S(1)} collective-permute-done((bf16[16,8320]{1,0:T(8,128)(2,1)S(1)}, bf16[16,8320]{1,0:T(8,128)(2,1)S(1)}, u32[]{:S(2)}, u32[]{:S(2)}) %collective-permute-start.3) | collective-permute-done | bytes 266272 | tf_op jit(solution)/shard_map/ppermute | solution.py:15
  125.8 1.9 collective-permute-start.4
  128.2 4.0 %collective-permute-start.11 = (bf16[16,8320]{1,0:T(8,128)(2,1)S(1)}, bf16[16,8320]{1,0:T(8,128)(2,1)S(1)}, u32[]{:S(2)}, u32[]{:S(2)}) collective-permute-start(bf16[16,8320]{1,0:T(8,128)(2,1)S(1)} %pad_maximum_fusion.10), channel_id=1, source_target_pairs={{0,16},{1,17},{2,18},{3,19},{4,20},{5,21},{6,22},{7,23},{8,24},{9,... | collective-permute-start | bytes 798728 | tf_op jit(solution)/shard_map/ppermute | solution.py:15
  132.2 2.9 collective-permute-done.4
  136.0 1.3 collective-permute-start.5
  139.3 6.9 %collective-permute-done.5 = bf16[16,8320]{1,0:T(8,128)(2,1)} collective-permute-done((bf16[16,8320]{1,0:T(8,128)(2,1)}, bf16[16,8320]{1,0:T(8,128)(2,1)}, u32[]{:S(2)}, u32[]{:S(2)}) %collective-permute-start.5) | collective-permute-done | bytes 266272 | tf_op jit(solution)/shard_map/ppermute | solution.py:15
  149.3 1.4 fusion.5
  150.7 5.3 %convolution_bitcast_fusion = f32[2048,1280]{0,1:T(8,128)} fusion(bf16[1,128,2048]{2,1,0:T(8,128)(2,1)S(1)} %copy-done, bf16[128,128]{0,1:T(8,128)(2,1)S(1)} %fusion.7, bf16[128,128]{0,1:T(8,128)(2,1)S(1)} %fusion.6, bf16[128,1024]{0,1:T(8,128)(2,1)S(1)} %bitcast.105), kind=kOutput, calls=%fused_computation | convolution fusion | flops 672071680 | bytes 11337728 | tf_op jit(solution)/shard_map/dot_general | solution.py:171
  156.0 11.3 %copy.93 = f32[2048,1280]{1,0:T(8,128)} copy(f32[2048,1280]{0,1:T(8,128)} %convolution_bitcast_fusion) | data formatting | bytes 20971520
  167.4 108.7 %reduce-scatter.4.cloned.1.call-done = f32[64,1280]{1,0:T(8,128)} async-done(((f32[2048,1280]{1,0:T(8,128)}), f32[64,1280]{1,0:T(8,128)}) %reduce-scatter.4.cloned.1.call-update) | async-done | bytes 327696 | tf_op jit(solution)/shard_map/reduce_scatter | solution.py:170
  276.1 1.6 collective-permute-start.12
  277.7 6.9 %collective-permute-done.12 = f32[64,1280]{1,0:T(8,128)S(1)} collective-permute-done((f32[64,1280]{1,0:T(8,128)}, f32[64,1280]{1,0:T(8,128)S(1)}, u32[]{:S(2)}, u32[]{:S(2)}) %collective-permute-start.12) | collective-permute-done | bytes 327712 | tf_op jit(solution)/shard_map/ppermute | solution.py:46
  285.6 2.6 collective-permute-start.13
  288.2 12.7 %collective-permute-done.13 = f32[64,1280]{1,0:T(8,128)S(1)} collective-permute-done((f32[64,1280]{1,0:T(8,128)S(1)}, f32[64,1280]{1,0:T(8,128)S(1)}, u32[]{:S(2)}, u32[]{:S(2)}) %collective-permute-start.13) | collective-permute-done | bytes 327712 | tf_op jit(solution)/shard_map/ppermute | solution.py:46
  301.0 5.7 %collective-permute-start.14 = (f32[64,1280]{1,0:T(8,128)S(1)}, f32[64,1280]{1,0:T(8,128)S(1)}, u32[]{:S(2)}, u32[]{:S(2)}) collective-permute-start(f32[64,1280]{1,0:T(8,128)S(1)} %add.93), channel_id=1, source_target_pairs={{0,128},{32,160},{64,192},{96,224},{128,0},{160,32},{192,64},{224,... | collective-permute-start | bytes 983048 | tf_op jit(solution)/shard_map/ppermute | solution.py:46
  306.6 5.3 %convolution_bitcast_fusion.1 = f32[1,128,2048]{2,1,0:T(8,128)} fusion(bf16[2048,1280]{1,0:T(8,128)(2,1)} %all-gather.2.cloned.1.call-done, bf16[128,128]{0,1:T(8,128)(2,1)S(1)} %fusion.7, bf16[128,128]{0,1:T(8,128)(2,1)S(1)} %fusion.6, bf16[128,1024]{0,1:T(8,128)(2,1)S(1)} %bitcast.106), kind=kOutput, calls=%fused_computation.1 | convolution fusion | flops 672071680 | bytes 6619136 | tf_op jit(solution)/shard_map/dot_general | solution.py:164
  311.9 9.5 %collective-permute-done.14 = f32[64,1280]{1,0:T(8,128)S(1)} collective-permute-done((f32[64,1280]{1,0:T(8,128)S(1)}, f32[64,1280]{1,0:T(8,128)S(1)}, u32[]{:S(2)}, u32[]{:S(2)}) %collective-permute-start.14) | collective-permute-done | bytes 327712 | tf_op jit(solution)/shard_map/ppermute | solution.py:46
  (102 shorter events, 23.7 us)
Async XLA Ops:
  7.2 59.0 %copy-start = (bf16[1,128,2048]{2,1,0:T(8,128)(2,1)S(1)}, bf16[1,128,2048]{2,1,0:T(8,128)(2,1)}, u32[]{:S(2)}) copy-start(bf16[1,128,2048]{2,1,0:T(8,128)(2,1)} %param.5) | copy-start | bytes 1572868
  7.2 59.0 %all-gather.2.cloned.1.call-start = ((), (), s32[]{:S(2)}) async-start(), calls=%async_computation.1 | async-start | bytes 5406720 | tf_op jit(solution)/shard_map/all_gather | solution.py:130
  10.0 266.1 %reduce-scatter.4.cloned.1.call-start = ((), (), s32[]{:S(2)}) async-start(), calls=%async_computation.2 | async-start | bytes 10813440 | tf_op jit(solution)/shard_map/reduce_scatter | solution.py:170
  15.6 55.7 %copy-start.2 = (f32[128,16]{0,1:T(8,128)}, f32[128,16]{0,1:T(8,128)S(1)}, u32[]{:S(2)}) copy-start(f32[128,16]{0,1:T(8,128)S(1)} %get-tuple-element.126) | copy-start | bytes 24580
  73.1 9.8 %collective-permute-start.6 = (bf16[16,8320]{1,0:T(8,128)(2,1)S(1)}, bf16[16,8320]{1,0:T(8,128)(2,1)S(1)}, u32[]{:S(2)}, u32[]{:S(2)}) collective-permute-start(bf16[16,8320]{1,0:T(8,128)(2,1)S(1)} %get-tuple-element.132), channel_id=1, source_target_pairs={{0,1},{1,2},{2,3},{3,4},{4,5},{5,6},{6,7},{7,8},{8,9},{9,10},{10,1... | collective-permute-start | bytes 798728 | tf_op jit(solution)/shard_map/ppermute | solution.py:15
  75.3 9.6 %copy-start.3 = (pred[128,128]{0,1:T(8,128)(4,1)}, pred[128,128]{0,1:T(8,128)(4,1)S(1)}, u32[]{:S(2)}) copy-start(pred[128,128]{0,1:T(8,128)(4,1)S(1)} %iota_compare_fusion) | copy-start | bytes 49156
  75.3 10.5 %collective-permute-start = (bf16[16,8320]{1,0:T(8,128)(2,1)S(1)}, bf16[16,8320]{1,0:T(8,128)(2,1)S(1)}, u32[]{:S(2)}, u32[]{:S(2)}) collective-permute-start(bf16[16,8320]{1,0:T(8,128)(2,1)S(1)} %get-tuple-element.131), channel_id=1, source_target_pairs={{1,0},{2,1},{3,2},{4,3},{5,4},{6,5},{7,6},{8,7},{9,8},{10,9},{11,1... | collective-permute-start | bytes 798728 | tf_op jit(solution)/shard_map/ppermute | solution.py:15
  83.0 9.8 %collective-permute-start.7 = (bf16[16,8320]{1,0:T(8,128)(2,1)S(1)}, bf16[16,8320]{1,0:T(8,128)(2,1)S(1)}, u32[]{:S(2)}, u32[]{:S(2)}) collective-permute-start(bf16[16,8320]{1,0:T(8,128)(2,1)S(1)} %collective-permute-done.6), channel_id=1, source_target_pairs={{0,1},{1,2},{2,3},{3,4},{4,5},{5,6},{6,7},{7,8},{8,9},{9,10},{10,1... | collective-permute-start | bytes 798728 | tf_op jit(solution)/shard_map/ppermute | solution.py:15
  85.9 9.7 %collective-permute-start.1 = (bf16[16,8320]{1,0:T(8,128)(2,1)S(1)}, bf16[16,8320]{1,0:T(8,128)(2,1)S(1)}, u32[]{:S(2)}, u32[]{:S(2)}) collective-permute-start(bf16[16,8320]{1,0:T(8,128)(2,1)S(1)} %collective-permute-done), channel_id=1, source_target_pairs={{1,0},{2,1},{3,2},{4,3},{5,4},{6,5},{7,6},{8,7},{9,8},{10,9},{11,1... | collective-permute-start | bytes 798728 | tf_op jit(solution)/shard_map/ppermute | solution.py:15
  93.0 10.4 %collective-permute-start.8 = (bf16[16,8320]{1,0:T(8,128)(2,1)S(1)}, bf16[16,8320]{1,0:T(8,128)(2,1)S(1)}, u32[]{:S(2)}, u32[]{:S(2)}) collective-permute-start(bf16[16,8320]{1,0:T(8,128)(2,1)S(1)} %pad_maximum_fusion.7), channel_id=1, source_target_pairs={{0,2},{1,3},{2,4},{3,5},{4,6},{5,7},{6,8},{7,9},{8,10},{9,11},{10,... | collective-permute-start | bytes 798728 | tf_op jit(solution)/shard_map/ppermute | solution.py:15
  95.8 17.8 %collective-permute-start.2 = (bf16[16,8320]{1,0:T(8,128)(2,1)S(1)}, bf16[16,8320]{1,0:T(8,128)(2,1)S(1)}, u32[]{:S(2)}, u32[]{:S(2)}) collective-permute-start(bf16[16,8320]{1,0:T(8,128)(2,1)S(1)} %pad_maximum_fusion.3), channel_id=1, source_target_pairs={{2,0},{3,1},{4,2},{5,3},{6,4},{7,5},{8,6},{9,7},{10,8},{11,9},{12,... | collective-permute-start | bytes 798728 | tf_op jit(solution)/shard_map/ppermute | solution.py:15
  103.7 13.0 %collective-permute-start.9 = (bf16[16,8320]{1,0:T(8,128)(2,1)S(1)}, bf16[16,8320]{1,0:T(8,128)(2,1)S(1)}, u32[]{:S(2)}, u32[]{:S(2)}) collective-permute-start(bf16[16,8320]{1,0:T(8,128)(2,1)S(1)} %pad_maximum_fusion.8), channel_id=1, source_target_pairs={{0,4},{1,5},{2,6},{3,7},{4,8},{5,9},{6,10},{7,11},{8,12},{9,13},{1... | collective-permute-start | bytes 798728 | tf_op jit(solution)/shard_map/ppermute | solution.py:15
  113.8 11.7 %collective-permute-start.3 = (bf16[16,8320]{1,0:T(8,128)(2,1)S(1)}, bf16[16,8320]{1,0:T(8,128)(2,1)S(1)}, u32[]{:S(2)}, u32[]{:S(2)}) collective-permute-start(bf16[16,8320]{1,0:T(8,128)(2,1)S(1)} %pad_maximum_fusion.4), channel_id=1, source_target_pairs={{4,0},{5,1},{6,2},{7,3},{8,4},{9,5},{10,6},{11,7},{12,8},{13,9},{1... | collective-permute-start | bytes 798728 | tf_op jit(solution)/shard_map/ppermute | solution.py:15
  117.0 11.0 %collective-permute-start.10 = (bf16[16,8320]{1,0:T(8,128)(2,1)S(1)}, bf16[16,8320]{1,0:T(8,128)(2,1)S(1)}, u32[]{:S(2)}, u32[]{:S(2)}) collective-permute-start(bf16[16,8320]{1,0:T(8,128)(2,1)S(1)} %pad_maximum_fusion.9), channel_id=1, source_target_pairs={{0,8},{1,9},{2,10},{3,11},{4,12},{5,13},{6,14},{7,15},{8,16},{9,17... | collective-permute-start | bytes 798728 | tf_op jit(solution)/shard_map/ppermute | solution.py:15
  125.8 9.4 %collective-permute-start.4 = (bf16[16,8320]{1,0:T(8,128)(2,1)S(1)}, bf16[16,8320]{1,0:T(8,128)(2,1)S(1)}, u32[]{:S(2)}, u32[]{:S(2)}) collective-permute-start(bf16[16,8320]{1,0:T(8,128)(2,1)S(1)} %pad_maximum_fusion.5), channel_id=1, source_target_pairs={{8,0},{9,1},{10,2},{11,3},{12,4},{13,5},{14,6},{15,7},{16,8},{17,9... | collective-permute-start | bytes 798728 | tf_op jit(solution)/shard_map/ppermute | solution.py:15
  127.9 10.7 %copy-start.4 = (f32[16]{0:T(128)}, f32[16]{0:T(128)S(1)}, u32[]{:S(2)}) copy-start(f32[16]{0:T(128)S(1)} %slice_reduce_fusion.6) | copy-start | bytes 196
  127.9 20.2 %copy-start.1 = (bf16[128,1024]{0,1:T(8,128)(2,1)S(1)}, bf16[128,1024]{0,1:T(8,128)(2,1)}, u32[]{:S(2)}) copy-start(bf16[128,1024]{0,1:T(8,128)(2,1)} %get-tuple-element.121) | copy-start | bytes 786436
  128.2 10.5 %collective-permute-start.11 = (bf16[16,8320]{1,0:T(8,128)(2,1)S(1)}, bf16[16,8320]{1,0:T(8,128)(2,1)S(1)}, u32[]{:S(2)}, u32[]{:S(2)}) collective-permute-start(bf16[16,8320]{1,0:T(8,128)(2,1)S(1)} %pad_maximum_fusion.10), channel_id=1, source_target_pairs={{0,16},{1,17},{2,18},{3,19},{4,20},{5,21},{6,22},{7,23},{8,24},{9,... | collective-permute-start | bytes 798728 | tf_op jit(solution)/shard_map/ppermute | solution.py:15
  136.0 10.2 %collective-permute-start.5 = (bf16[16,8320]{1,0:T(8,128)(2,1)}, bf16[16,8320]{1,0:T(8,128)(2,1)}, u32[]{:S(2)}, u32[]{:S(2)}) collective-permute-start(bf16[16,8320]{1,0:T(8,128)(2,1)} %pad_maximum_fusion.6), channel_id=1, source_target_pairs={{16,0},{17,1},{18,2},{19,3},{20,4},{21,5},{22,6},{23,7},{24,8},{25... | collective-permute-start | bytes 798728 | tf_op jit(solution)/shard_map/ppermute | solution.py:15
  276.1 8.5 %collective-permute-start.12 = (f32[64,1280]{1,0:T(8,128)}, f32[64,1280]{1,0:T(8,128)S(1)}, u32[]{:S(2)}, u32[]{:S(2)}) collective-permute-start(f32[64,1280]{1,0:T(8,128)} %reduce-scatter.4.cloned.1.call-done), channel_id=1, source_target_pairs={{0,32},{32,0},{64,96},{96,64},{128,160},{160,128},{192,224},{224,1... | collective-permute-start | bytes 983048 | tf_op jit(solution)/shard_map/ppermute | solution.py:46
  285.6 15.3 %collective-permute-start.13 = (f32[64,1280]{1,0:T(8,128)S(1)}, f32[64,1280]{1,0:T(8,128)S(1)}, u32[]{:S(2)}, u32[]{:S(2)}) collective-permute-start(f32[64,1280]{1,0:T(8,128)S(1)} %add.92), channel_id=1, source_target_pairs={{0,64},{32,96},{64,0},{96,32},{128,192},{160,224},{192,128},{224,1... | collective-permute-start | bytes 983048 | tf_op jit(solution)/shard_map/ppermute | solution.py:46
  301.0 20.4 %collective-permute-start.14 = (f32[64,1280]{1,0:T(8,128)S(1)}, f32[64,1280]{1,0:T(8,128)S(1)}, u32[]{:S(2)}, u32[]{:S(2)}) collective-permute-start(f32[64,1280]{1,0:T(8,128)S(1)} %add.93), channel_id=1, source_target_pairs={{0,128},{32,160},{64,192},{96,224},{128,0},{160,32},{192,64},{224,... | collective-permute-start | bytes 983048 | tf_op jit(solution)/shard_map/ppermute | solution.py:46
Sparse Core Ops, SparseCore 0:
  11.1 54.9 all-gather.1
  167.5 108.5 reduce-scatter.3

commit v3 on v2

--- a/solution.py
+++ b/solution.py
@@ -17,25 +17,24 @@
 
 def scan_entering(decay, state, axis, reverse):
     head_count = state.shape[0]
-    packed = jnp.concatenate(
-        [state.reshape(head_count, -1), jnp.broadcast_to(decay[:, None], (head_count, 128))],
-        axis=1,
-    )
-    split = packed.shape[1] - 128
-    packed = shifted(packed, axis, 1, reverse)
+    flat = state.reshape(head_count, -1)
+    split = flat.shape[1]
+
+    def send(flat, decay, step):
+        high = lax.reduce_precision(decay, exponent_bits=8, mantissa_bits=7)
+        lanes = lambda part: jnp.broadcast_to(part[:, None], (head_count, 128))
+        packed = jnp.concatenate([flat, lanes(high), lanes(decay - high)], axis=1)
+        got = shifted(packed, axis, step, reverse)
+        return got[:, :split], got[:, split] + got[:, split + 128]
+
+    flat, decay = send(flat, decay, 1)
     step = 1
     while step < lax.axis_size(axis):
-        earlier = shifted(packed, axis, step, reverse)
-        later_decay = packed[:, split:]
-        packed = jnp.concatenate(
-            [
-                later_decay[:, :1] * earlier[:, :split] + packed[:, :split],
-                earlier[:, split:] * later_decay,
-            ],
-            axis=1,
-        )
+        earlier_flat, earlier_decay = send(flat, decay, step)
+        flat = decay[:, None] * earlier_flat + flat
+        decay = earlier_decay * decay
         step *= 2
-    return packed[:, :split].reshape(state.shape)
+    return flat.reshape(state.shape)
 
 
 def butterfly_sum(value, axis):
@@ -170,11 +169,11 @@
     partial_grad = lax.psum_scatter(
         lax.dot_general(
             features, d_proj, (((0,), (0,)), ((), ())), preferred_element_type=jnp.float32
-        ),
+        ).astype(jnp.bfloat16),
         "seq",
         scatter_dimension=0,
         tiled=True,
-    )
+    ).astype(jnp.float32)
     summed_grad = butterfly_sum(partial_grad, "dp")
     return (grad_in[None], summed_grad * norm_factor)
 

time: 330 us -> 314 us (0.952)
  waiting for transfers between devices: 219 us -> 211 us
  starting transfers between devices: 45.6 us -> 39.8 us
  local copies, waits for them, and re-layouts: 18.3 us -> 14.7 us
    reduce_scatter x1, waiting for transfers between devices: 109 us -> 90.1 us  [local(): lax.psum_scatter(lax.dot_general(features, d_proj, (((0,), (0,)), ((), ()...]
    ppermute x12, waiting for transfers between devices: 30.5 us -> 43.2 us  [shifted(): lax.ppermute(value.astype(jnp.bfloat16), axis, pairs).astype(value.dtype)]
    ppermute x12, starting transfers between devices: 35.7 us -> 29.6 us  [shifted(): lax.ppermute(value.astype(jnp.bfloat16), axis, pairs).astype(value.dtype)]
    unnamed x12 -> x14, local copies, waits for them, and re-layouts: 12.4 us -> 9.02 us
  transfers between devices with their start and end apart: 17 -> 17, of which waited for: 15 -> 13; matrix products, arithmetic and copies ran while one was open for 5% -> 6% of each run, Pallas kernels for 0% -> 0%
where the time goes in v3:
time: 314 us; the launch traced here: 312 us
  waiting for transfers between devices  211 us (67%)
  starting transfers between devices  39.8 us (13%)
  matrix products  17.4 us (6%)
  other arithmetic  15.3 us (5%)
  local copies, waits for them, and re-layouts  14.7 us (5%)
  between operations  14.7 us (5%)
    reduce_scatter x1, waiting for transfers between devices, local(): lax.psum_scatter(lax.dot_general(features, d_proj, (((0,), (0,)), ((), ()...  90.1 us
    all_gather x1, waiting for transfers between devices, local(): lax.all_gather(dequantize(weight_codes, scales), 'seq', axis=0, tiled=True)  50.5 us
    ppermute x12, waiting for transfers between devices, shifted(): lax.ppermute(value.astype(jnp.bfloat16), axis, pairs).astype(value.dtype)  43.2 us
    ppermute x12, starting transfers between devices, shifted(): lax.ppermute(value.astype(jnp.bfloat16), axis, pairs).astype(value.dtype)  29.6 us
    ppermute x3, waiting for transfers between devices, butterfly_sum(): value = value + lax.ppermute(value, axis, pairs)  26.8 us
    ppermute x3, starting transfers between devices, butterfly_sum(): value = value + lax.ppermute(value, axis, pairs)  10.1 us
    unnamed x14, local copies, waits for them, and re-layouts  9.02 us
  transfers between devices with their start and end apart: 17, of which 13 were waited for; matrix products, arithmetic and copies ran while one was open for 6% of the time, Pallas kernels for 0%

profile of v3, /device:TPU:8, one launch (start us, length us, event | category | flops | bytes accessed | tf_op | source)
XLA Modules:
  0.0 312.5 jit_solution(16432688883578511530)
XLA Ops:
  8.2 1.7 fusion.29
  15.7 50.5 %all-gather.2.cloned.1.call-done = bf16[2048,1280]{1,0:T(8,128)(2,1)} async-done(((bf16[64,1280]{1,0:T(8,128)(2,1)}), bf16[2048,1280]{1,0:T(8,128)(2,1)}) %all-gather.2.cloned.1.call-update) | async-done | bytes 5242896 | tf_op jit(solution)/shard_map/all_gather | solution.py:129
  66.2 4.1 %fusion.1 = bf16[128,1280]{0,1:T(8,128)(2,1)S(1)} fusion(bf16[2048,1280]{1,0:T(8,128)(2,1)} %all-gather.2.cloned.1.call-done, bf16[1,128,2048]{2,1,0:T(8,128)(2,1)S(1)} %copy-done), kind=kOutput, calls=%fused_computation.4 | convolution fusion | flops 671252480 | bytes 6094848 | tf_op jit(solution)/shard_map/dot_general | solution.py:130
  73.2 4.4 %collective-permute-start = (bf16[16,8448]{1,0:T(8,128)(2,1)S(1)}, bf16[16,8448]{1,0:T(8,128)(2,1)S(1)}, u32[]{:S(2)}, u32[]{:S(2)}) collective-permute-start(bf16[16,8448]{1,0:T(8,128)(2,1)S(1)} %get-tuple-element.153), channel_id=1, source_target_pairs={{1,0},{2,1},{3,2},{4,3},{5,4},{6,5},{7,6},{8,7},{9,8},{10,9},{11,1... | collective-permute-start | bytes 811016 | tf_op jit(solution)/shard_map/ppermute | solution.py:15
  77.7 1.9 collective-permute-start.6
  79.6 2.0 collective-permute-done
  82.0 5.9 %collective-permute-start.1 = (bf16[16,8448]{1,0:T(8,128)(2,1)S(1)}, bf16[16,8448]{1,0:T(8,128)(2,1)S(1)}, u32[]{:S(2)}, u32[]{:S(2)}) collective-permute-start(bf16[16,8448]{1,0:T(8,128)(2,1)S(1)} %pad_maximum_fusion.5), channel_id=1, source_target_pairs={{1,0},{2,1},{3,2},{4,3},{5,4},{6,5},{7,6},{8,7},{9,8},{10,9},{11,1... | collective-permute-start | bytes 811016 | tf_op jit(solution)/shard_map/ppermute | solution.py:15
  88.5 1.9 collective-permute-start.7
  90.4 1.5 collective-permute-done.1
  92.5 1.9 collective-permute-start.2
  94.4 3.9 %collective-permute-done.7 = bf16[16,8448]{1,0:T(8,128)(2,1)S(1)} collective-permute-done((bf16[16,8448]{1,0:T(8,128)(2,1)S(1)}, bf16[16,8448]{1,0:T(8,128)(2,1)S(1)}, u32[]{:S(2)}, u32[]{:S(2)}) %collective-permute-start.7) | collective-permute-done | bytes 270368 | tf_op jit(solution)/shard_map/ppermute | solution.py:15
  98.9 1.9 collective-permute-start.8
  101.5 2.1 collective-permute-start.3
  103.5 13.8 %collective-permute-done.8 = bf16[16,8448]{1,0:T(8,128)(2,1)S(1)} collective-permute-done((bf16[16,8448]{1,0:T(8,128)(2,1)S(1)}, bf16[16,8448]{1,0:T(8,128)(2,1)S(1)}, u32[]{:S(2)}, u32[]{:S(2)}) %collective-permute-start.8) | collective-permute-done | bytes 270368 | tf_op jit(solution)/shard_map/ppermute | solution.py:15
  117.9 2.1 collective-permute-start.9
  120.6 1.9 collective-permute-start.4
  122.6 8.0 %collective-permute-done.9 = bf16[16,8448]{1,0:T(8,128)(2,1)S(1)} collective-permute-done((bf16[16,8448]{1,0:T(8,128)(2,1)S(1)}, bf16[16,8448]{1,0:T(8,128)(2,1)S(1)}, u32[]{:S(2)}, u32[]{:S(2)}) %collective-permute-start.9) | collective-permute-done | bytes 270368 | tf_op jit(solution)/shard_map/ppermute | solution.py:15
  131.1 1.9 collective-permute-start.10
  134.3 6.0 %collective-permute-done.10 = bf16[16,8448]{1,0:T(8,128)(2,1)S(1)} collective-permute-done((bf16[16,8448]{1,0:T(8,128)(2,1)S(1)}, bf16[16,8448]{1,0:T(8,128)(2,1)S(1)}, u32[]{:S(2)}, u32[]{:S(2)}) %collective-permute-start.10) | collective-permute-done | bytes 270368 | tf_op jit(solution)/shard_map/ppermute | solution.py:15
  141.0 2.2 collective-permute-start.11
  145.7 1.5 collective-permute-done.11
  147.9 6.5 %collective-permute-done.5 = bf16[16,8448]{1,0:T(8,128)(2,1)} collective-permute-done((bf16[16,8448]{1,0:T(8,128)(2,1)}, bf16[16,8448]{1,0:T(8,128)(2,1)}, u32[]{:S(2)}, u32[]{:S(2)}) %collective-permute-start.5) | collective-permute-done | bytes 270368 | tf_op jit(solution)/shard_map/ppermute | solution.py:15
  158.9 3.9 %fusion = bf16[2048,1280]{0,1:T(8,128)(2,1)} fusion(bf16[1,128,2048]{2,1,0:T(8,128)(2,1)S(1)} %copy-done, bf16[128,128]{0,1:T(8,128)(2,1)S(1)} %fusion.8, bf16[128,128]{0,1:T(8,128)(2,1)S(1)} %fusion.7, bf16[128,1024]{0,1:T(8,128)(2,1)S(1)} %bitcast.106), kind=kOutput, calls=%fused_computation.1 | convolution fusion | flops 674693120 | bytes 6094848 | tf_op jit(solution)/shard_map/dot_general | solution.py:170
  162.8 7.9 %copy.92 = bf16[2048,1280]{1,0:T(8,128)(2,1)} copy(bf16[2048,1280]{0,1:T(8,128)(2,1)} %fusion) | data formatting | bytes 10485760
  170.7 90.1 %reduce-scatter.4.cloned.1.call-done = bf16[64,1280]{1,0:T(8,128)(2,1)} async-done(((bf16[2048,1280]{1,0:T(8,128)(2,1)}), bf16[64,1280]{1,0:T(8,128)(2,1)}) %reduce-scatter.4.cloned.1.call-update) | async-done | bytes 163856 | tf_op jit(solution)/shard_map/reduce_scatter | solution.py:169
  261.7 1.6 collective-permute-start.12
  263.3 5.9 %collective-permute-done.12 = f32[64,1280]{1,0:T(8,128)S(1)} collective-permute-done((f32[64,1280]{1,0:T(8,128)S(1)}, f32[64,1280]{1,0:T(8,128)S(1)}, u32[]{:S(2)}, u32[]{:S(2)}) %collective-permute-start.12) | collective-permute-done | bytes 327712 | tf_op jit(solution)/shard_map/ppermute | solution.py:45
  270.1 2.6 collective-permute-start.13
  272.8 11.9 %collective-permute-done.13 = f32[64,1280]{1,0:T(8,128)S(1)} collective-permute-done((f32[64,1280]{1,0:T(8,128)S(1)}, f32[64,1280]{1,0:T(8,128)S(1)}, u32[]{:S(2)}, u32[]{:S(2)}) %collective-permute-start.13) | collective-permute-done | bytes 327712 | tf_op jit(solution)/shard_map/ppermute | solution.py:45
  284.7 5.8 %collective-permute-start.14 = (f32[64,1280]{1,0:T(8,128)S(1)}, f32[64,1280]{1,0:T(8,128)S(1)}, u32[]{:S(2)}, u32[]{:S(2)}) collective-permute-start(f32[64,1280]{1,0:T(8,128)S(1)} %add.223), channel_id=1, source_target_pairs={{0,128},{32,160},{64,192},{96,224},{128,0},{160,32},{192,64},{224,... | collective-permute-start | bytes 983048 | tf_op jit(solution)/shard_map/ppermute | solution.py:45
  290.5 5.3 %convolution_bitcast_fusion = f32[1,128,2048]{2,1,0:T(8,128)} fusion(bf16[2048,1280]{1,0:T(8,128)(2,1)} %all-gather.2.cloned.1.call-done, bf16[128,128]{0,1:T(8,128)(2,1)S(1)} %fusion.8, bf16[128,128]{0,1:T(8,128)(2,1)S(1)} %fusion.7, bf16[128,1024]{0,1:T(8,128)(2,1)S(1)} %bitcast.107), kind=kOutput, calls=%fused_computation.2 | convolution fusion | flops 672071680 | bytes 6619136 | tf_op jit(solution)/shard_map/dot_general | solution.py:163
  295.8 9.1 %collective-permute-done.14 = f32[64,1280]{1,0:T(8,128)S(1)} collective-permute-done((f32[64,1280]{1,0:T(8,128)S(1)}, f32[64,1280]{1,0:T(8,128)S(1)}, u32[]{:S(2)}, u32[]{:S(2)}) %collective-permute-start.14) | collective-permute-done | bytes 327712 | tf_op jit(solution)/shard_map/ppermute | solution.py:45
  (132 shorter events, 26.2 us)
Async XLA Ops:
  7.2 59.0 %copy-start = (bf16[1,128,2048]{2,1,0:T(8,128)(2,1)S(1)}, bf16[1,128,2048]{2,1,0:T(8,128)(2,1)}, u32[]{:S(2)}) copy-start(bf16[1,128,2048]{2,1,0:T(8,128)(2,1)} %param.5) | copy-start | bytes 1572868
  7.2 59.0 %all-gather.2.cloned.1.call-start = ((), (), s32[]{:S(2)}) async-start(), calls=%async_computation.1 | async-start | bytes 5406720 | tf_op jit(solution)/shard_map/all_gather | solution.py:129
  10.0 250.8 %reduce-scatter.4.cloned.1.call-start = ((), (), s32[]{:S(2)}) async-start(), calls=%async_computation.2 | async-start | bytes 5406720 | tf_op jit(solution)/shard_map/reduce_scatter | solution.py:169
  70.2 7.4 %copy-start.1 = (bf16[128,1280]{0,1:T(8,128)(2,1)}, bf16[128,1280]{0,1:T(8,128)(2,1)S(1)}, u32[]{:S(2)}) copy-start(bf16[128,1280]{0,1:T(8,128)(2,1)S(1)} %fusion.1) | copy-start | bytes 983044
  73.2 8.4 %collective-permute-start = (bf16[16,8448]{1,0:T(8,128)(2,1)S(1)}, bf16[16,8448]{1,0:T(8,128)(2,1)S(1)}, u32[]{:S(2)}, u32[]{:S(2)}) collective-permute-start(bf16[16,8448]{1,0:T(8,128)(2,1)S(1)} %get-tuple-element.153), channel_id=1, source_target_pairs={{1,0},{2,1},{3,2},{4,3},{5,4},{6,5},{7,6},{8,7},{9,8},{10,9},{11,1... | collective-permute-start | bytes 811016 | tf_op jit(solution)/shard_map/ppermute | solution.py:15
  77.6 55.4 %copy-start.3 = (pred[128,128]{0,1:T(8,128)(4,1)}, pred[128,128]{0,1:T(8,128)(4,1)S(1)}, u32[]{:S(2)}) copy-start(pred[128,128]{0,1:T(8,128)(4,1)S(1)} %iota_compare_fusion) | copy-start | bytes 49156
  77.7 10.3 %collective-permute-start.6 = (bf16[16,8448]{1,0:T(8,128)(2,1)S(1)}, bf16[16,8448]{1,0:T(8,128)(2,1)S(1)}, u32[]{:S(2)}, u32[]{:S(2)}) collective-permute-start(bf16[16,8448]{1,0:T(8,128)(2,1)S(1)} %get-tuple-element.154), channel_id=1, source_target_pairs={{0,1},{1,2},{2,3},{3,4},{4,5},{5,6},{6,7},{7,8},{8,9},{9,10},{10,1... | collective-permute-start | bytes 811016 | tf_op jit(solution)/shard_map/ppermute | solution.py:15
  82.0 9.9 %collective-permute-start.1 = (bf16[16,8448]{1,0:T(8,128)(2,1)S(1)}, bf16[16,8448]{1,0:T(8,128)(2,1)S(1)}, u32[]{:S(2)}, u32[]{:S(2)}) collective-permute-start(bf16[16,8448]{1,0:T(8,128)(2,1)S(1)} %pad_maximum_fusion.5), channel_id=1, source_target_pairs={{1,0},{2,1},{3,2},{4,3},{5,4},{6,5},{7,6},{8,7},{9,8},{10,9},{11,1... | collective-permute-start | bytes 811016 | tf_op jit(solution)/shard_map/ppermute | solution.py:15
  88.5 9.9 %collective-permute-start.7 = (bf16[16,8448]{1,0:T(8,128)(2,1)S(1)}, bf16[16,8448]{1,0:T(8,128)(2,1)S(1)}, u32[]{:S(2)}, u32[]{:S(2)}) collective-permute-start(bf16[16,8448]{1,0:T(8,128)(2,1)S(1)} %pad_maximum_fusion.10), channel_id=1, source_target_pairs={{0,1},{1,2},{2,3},{3,4},{4,5},{5,6},{6,7},{7,8},{8,9},{9,10},{10,1... | collective-permute-start | bytes 811016 | tf_op jit(solution)/shard_map/ppermute | solution.py:15
  92.5 8.4 %collective-permute-start.2 = (bf16[16,8448]{1,0:T(8,128)(2,1)S(1)}, bf16[16,8448]{1,0:T(8,128)(2,1)S(1)}, u32[]{:S(2)}, u32[]{:S(2)}) collective-permute-start(bf16[16,8448]{1,0:T(8,128)(2,1)S(1)} %pad_maximum_fusion.6), channel_id=1, source_target_pairs={{2,0},{3,1},{4,2},{5,3},{6,4},{7,5},{8,6},{9,7},{10,8},{11,9},{12,... | collective-permute-start | bytes 811016 | tf_op jit(solution)/shard_map/ppermute | solution.py:15
  98.9 18.4 %collective-permute-start.8 = (bf16[16,8448]{1,0:T(8,128)(2,1)S(1)}, bf16[16,8448]{1,0:T(8,128)(2,1)S(1)}, u32[]{:S(2)}, u32[]{:S(2)}) collective-permute-start(bf16[16,8448]{1,0:T(8,128)(2,1)S(1)} %pad_maximum_fusion.11), channel_id=1, source_target_pairs={{0,2},{1,3},{2,4},{3,5},{4,6},{5,7},{6,8},{7,9},{8,10},{9,11},{10,... | collective-permute-start | bytes 811016 | tf_op jit(solution)/shard_map/ppermute | solution.py:15
  101.5 31.6 %slice-start = ((bf16[128,1280]{0,1:T(8,128)(2,1)}), bf16[128,1024]{0,1:T(8,128)(2,1)S(1)}, s32[]{:S(2)}) async-start(bf16[128,1280]{0,1:T(8,128)(2,1)} %copy-done.1), calls=%async_computation.3 | async-start | bytes 524288 | tf_op jit(solution)/shard_map/slice | solution.py:133
  101.5 18.5 %collective-permute-start.3 = (bf16[16,8448]{1,0:T(8,128)(2,1)S(1)}, bf16[16,8448]{1,0:T(8,128)(2,1)S(1)}, u32[]{:S(2)}, u32[]{:S(2)}) collective-permute-start(bf16[16,8448]{1,0:T(8,128)(2,1)S(1)} %pad_maximum_fusion.7), channel_id=1, source_target_pairs={{4,0},{5,1},{6,2},{7,3},{8,4},{9,5},{10,6},{11,7},{12,8},{13,9},{1... | collective-permute-start | bytes 811016 | tf_op jit(solution)/shard_map/ppermute | solution.py:15
  117.9 16.1 %copy-start.2 = (bf16[128,1280]{0,1:T(8,128)(2,1)S(1)}, bf16[128,1280]{0,1:T(8,128)(2,1)}, u32[]{:S(2)}) copy-start(bf16[128,1280]{0,1:T(8,128)(2,1)} %copy-done.1) | copy-start | bytes 983044
  117.9 12.6 %collective-permute-start.9 = (bf16[16,8448]{1,0:T(8,128)(2,1)S(1)}, bf16[16,8448]{1,0:T(8,128)(2,1)S(1)}, u32[]{:S(2)}, u32[]{:S(2)}) collective-permute-start(bf16[16,8448]{1,0:T(8,128)(2,1)S(1)} %pad_maximum_fusion.12), channel_id=1, source_target_pairs={{0,4},{1,5},{2,6},{3,7},{4,8},{5,9},{6,10},{7,11},{8,12},{9,13},{1... | collective-permute-start | bytes 811016 | tf_op jit(solution)/shard_map/ppermute | solution.py:15
  120.6 13.6 %collective-permute-start.4 = (bf16[16,8448]{1,0:T(8,128)(2,1)S(1)}, bf16[16,8448]{1,0:T(8,128)(2,1)S(1)}, u32[]{:S(2)}, u32[]{:S(2)}) collective-permute-start(bf16[16,8448]{1,0:T(8,128)(2,1)S(1)} %pad_maximum_fusion.8), channel_id=1, source_target_pairs={{8,0},{9,1},{10,2},{11,3},{12,4},{13,5},{14,6},{15,7},{16,8},{17,9... | collective-permute-start | bytes 811016 | tf_op jit(solution)/shard_map/ppermute | solution.py:15
  131.1 9.2 %collective-permute-start.10 = (bf16[16,8448]{1,0:T(8,128)(2,1)S(1)}, bf16[16,8448]{1,0:T(8,128)(2,1)S(1)}, u32[]{:S(2)}, u32[]{:S(2)}) collective-permute-start(bf16[16,8448]{1,0:T(8,128)(2,1)S(1)} %pad_maximum_fusion.13), channel_id=1, source_target_pairs={{0,8},{1,9},{2,10},{3,11},{4,12},{5,13},{6,14},{7,15},{8,16},{9,17... | collective-permute-start | bytes 811016 | tf_op jit(solution)/shard_map/ppermute | solution.py:15
  141.0 17.3 %copy-start.4 = (pred[128,128]{0,1:T(8,128)(4,1)S(1)}, pred[128,128]{0,1:T(8,128)(4,1)}, u32[]{:S(2)}) copy-start(pred[128,128]{0,1:T(8,128)(4,1)} %copy-done.3) | copy-start | bytes 49156
  141.0 17.3 %copy-start.5 = (f32[128,16]{0,1:T(8,128)S(1)}, f32[128,16]{0,1:T(8,128)}, u32[]{:S(2)}) copy-start(f32[128,16]{0,1:T(8,128)} %get-tuple-element.149) | copy-start | bytes 24580
  141.0 6.2 %collective-permute-start.11 = (bf16[16,8448]{1,0:T(8,128)(2,1)S(1)}, bf16[16,8448]{1,0:T(8,128)(2,1)S(1)}, u32[]{:S(2)}, u32[]{:S(2)}) collective-permute-start(bf16[16,8448]{1,0:T(8,128)(2,1)S(1)} %pad_maximum_fusion.14), channel_id=1, source_target_pairs={{0,16},{1,17},{2,18},{3,19},{4,20},{5,21},{6,22},{7,23},{8,24},{9,... | collective-permute-start | bytes 811016 | tf_op jit(solution)/shard_map/ppermute | solution.py:15
  144.2 10.2 %collective-permute-start.5 = (bf16[16,8448]{1,0:T(8,128)(2,1)}, bf16[16,8448]{1,0:T(8,128)(2,1)}, u32[]{:S(2)}, u32[]{:S(2)}) collective-permute-start(bf16[16,8448]{1,0:T(8,128)(2,1)} %pad_maximum_fusion.9), channel_id=1, source_target_pairs={{16,0},{17,1},{18,2},{19,3},{20,4},{21,5},{22,6},{23,7},{24,8},{25... | collective-permute-start | bytes 811016 | tf_op jit(solution)/shard_map/ppermute | solution.py:15
  261.7 7.5 %collective-permute-start.12 = (f32[64,1280]{1,0:T(8,128)S(1)}, f32[64,1280]{1,0:T(8,128)S(1)}, u32[]{:S(2)}, u32[]{:S(2)}) collective-permute-start(f32[64,1280]{1,0:T(8,128)S(1)} %convert_element_type.177), channel_id=1, source_target_pairs={{0,32},{32,0},{64,96},{96,64},{128,160},{160,128},{192,224},{224,1... | collective-permute-start | bytes 983048 | tf_op jit(solution)/shard_map/ppermute | solution.py:45
  270.1 14.5 %collective-permute-start.13 = (f32[64,1280]{1,0:T(8,128)S(1)}, f32[64,1280]{1,0:T(8,128)S(1)}, u32[]{:S(2)}, u32[]{:S(2)}) collective-permute-start(f32[64,1280]{1,0:T(8,128)S(1)} %convert_add_fusion), channel_id=1, source_target_pairs={{0,64},{32,96},{64,0},{96,32},{128,192},{160,224},{192,128},{224,1... | collective-permute-start | bytes 983048 | tf_op jit(solution)/shard_map/ppermute | solution.py:45
  284.7 20.2 %collective-permute-start.14 = (f32[64,1280]{1,0:T(8,128)S(1)}, f32[64,1280]{1,0:T(8,128)S(1)}, u32[]{:S(2)}, u32[]{:S(2)}) collective-permute-start(f32[64,1280]{1,0:T(8,128)S(1)} %add.223), channel_id=1, source_target_pairs={{0,128},{32,160},{64,192},{96,224},{128,0},{160,32},{192,64},{224,... | collective-permute-start | bytes 983048 | tf_op jit(solution)/shard_map/ppermute | solution.py:45
Sparse Core Ops, SparseCore 0:
  11.1 54.9 all-gather.1
  170.8 89.8 reduce-scatter.3

commit v4 on v3

--- a/solution.py
+++ b/solution.py
@@ -45,6 +45,53 @@
         value = value + lax.ppermute(value, axis, pairs)
         step *= 2
     return value
+
+
+def digit_reduce(value, axis, where, stride, radix):
+    count = lax.axis_size(axis)
+    digit = (lax.axis_index(axis) // stride) % radix
+    total = lax.dynamic_index_in_dim(value, digit, where, False)
+    for offset in range(1, radix):
+        piece = lax.dynamic_index_in_dim(value, (digit + offset) % radix, where, False)
+        pairs = [
+            (place, place + (((place // stride) % radix + offset) % radix - (place // stride) % radix) * stride)
+            for place in range(count)
+        ]
+        got = lax.ppermute(piece.astype(jnp.bfloat16), axis, pairs)
+        total = total + got.astype(jnp.float32)
+    return total
+
+
+def seq_reduce_scatter(partial, axis):
+    rows, cols = partial.shape
+    count = lax.axis_size(axis)
+    block = rows // count
+    value = partial.reshape(count // 8, 4, 2, block, cols)
+    value = digit_reduce(value, axis, 2, 1, 2)
+    half = cols // 2
+    first = digit_reduce(value[..., :half], axis, 1, 2, 4)
+    first = digit_reduce(first, axis, 0, 8, count // 8)
+    second = digit_reduce(value[..., half:], axis, 0, 8, count // 8)
+    second = digit_reduce(second, axis, 0, 2, 4)
+    return jnp.concatenate([first, second], axis=1)
+
+
+def replicated_sum(value, axis):
+    count = lax.axis_size(axis)
+    me = lax.axis_index(axis)
+    slabs = value.reshape(count, value.shape[0] // count, value.shape[1])
+    total = lax.dynamic_index_in_dim(slabs, me, 0, False)
+    for offset in range(1, count):
+        piece = lax.dynamic_index_in_dim(slabs, (me + offset) % count, 0, False)
+        pairs = [(place, (place + offset) % count) for place in range(count)]
+        total = total + lax.ppermute(piece, axis, pairs)
+    gathered = [total]
+    for offset in range(1, count):
+        pairs = [(place, (place + offset) % count) for place in range(count)]
+        gathered.append(lax.ppermute(total, axis, pairs))
+    stacked = jnp.stack(gathered)
+    order = (me - jnp.arange(count)) % count
+    return jnp.take(stacked, order, axis=0).reshape(value.shape)
 
 
 def dequantize(code_rows, scale_rows):
@@ -166,15 +213,13 @@
     seq_count = lax.axis_size("seq")
     group_count = lax.axis_size("dp")
     norm_factor = 1.0 / math.sqrt(group_count * seq_count * tok_count)
-    partial_grad = lax.psum_scatter(
+    partial_grad = seq_reduce_scatter(
         lax.dot_general(
             features, d_proj, (((0,), (0,)), ((), ())), preferred_element_type=jnp.float32
-        ).astype(jnp.bfloat16),
+        ),
         "seq",
-        scatter_dimension=0,
-        tiled=True,
-    ).astype(jnp.float32)
-    summed_grad = butterfly_sum(partial_grad, "dp")
+    )
+    summed_grad = replicated_sum(partial_grad, "dp")
     return (grad_in[None], summed_grad * norm_factor)
 
 

time: 314 us -> 281 us (0.89)
  waiting for transfers between devices: 211 us -> 130 us
  starting transfers between devices: 39.8 us -> 68.8 us
  local copies, waits for them, and re-layouts: 14.7 us -> 26.4 us
    reduce_scatter x1 -> x0, waiting for transfers between devices: 90.1 us -> none  [local(): lax.psum_scatter(lax.dot_general(features, d_proj, (((0,), (0,)), ((), ()...]
    ppermute x3 -> x27, starting transfers between devices: 10.1 us -> 39.2 us  [the longest x7 16.5 us: replicated_sum(): total = total + lax.ppermute(piece, axis, pairs)]
    dot_general x0 -> x1, local copies, waits for them, and re-layouts: none -> 11.3 us  [local(): lax.dot_general(features, d_proj, (((0,), (0,)), ((), ())), preferred_ele...]
    ppermute x3 -> x27, waiting for transfers between devices: 26.8 us -> 37.2 us  [the longest x13 30.5 us: digit_reduce(): got = lax.ppermute(piece.astype(jnp.bfloat16), axis, pairs)]
    unnamed x14 -> x31, local copies, waits for them, and re-layouts: 9.02 us -> 2.7 us
    convert_element_type x0 -> x5, local copies, waits for them, and re-layouts: none -> 5.5 us  [digit_reduce(): got = lax.ppermute(piece.astype(jnp.bfloat16), axis, pairs)]
    add x2 -> x5, other arithmetic: 0.99 us -> 4.66 us  [digit_reduce(): total = total + got.astype(jnp.float32)]
  transfers between devices with their start and end apart: 17 -> 40, of which waited for: 13 -> 22; matrix products, arithmetic and copies ran while one was open for 6% -> 8% of each run, Pallas kernels for 0% -> 0%
where the time goes in v4:
time: 281 us; the launch traced here: 279 us
  waiting for transfers between devices  130 us (46%)
  starting transfers between devices  68.8 us (24%)
  local copies, waits for them, and re-layouts  26.4 us (9%)
  matrix products  20.4 us (7%)
  other arithmetic  18.2 us (6%)
  between operations  14.9 us (5%)
    all_gather x1, waiting for transfers between devices, local(): lax.all_gather(dequantize(weight_codes, scales), 'seq', axis=0, tiled=True)  50.5 us
    ppermute x12, waiting for transfers between devices, shifted(): lax.ppermute(value.astype(jnp.bfloat16), axis, pairs).astype(value.dtype)  42.5 us
    ppermute x13, waiting for transfers between devices, digit_reduce(): got = lax.ppermute(piece.astype(jnp.bfloat16), axis, pairs)  30.5 us
    ppermute x12, starting transfers between devices, shifted(): lax.ppermute(value.astype(jnp.bfloat16), axis, pairs).astype(value.dtype)  29.6 us
    ppermute x7, starting transfers between devices, replicated_sum(): total = total + lax.ppermute(piece, axis, pairs)  16.5 us
    ppermute x7, starting transfers between devices, replicated_sum(): gathered.append(lax.ppermute(total, axis, pairs))  14.4 us
    dot_general x1, local copies, waits for them, and re-layouts, local(): lax.dot_general(features, d_proj, (((0,), (0,)), ((), ())), preferred_ele...  11.3 us
    ppermute x13, starting transfers between devices, digit_reduce(): got = lax.ppermute(piece.astype(jnp.bfloat16), axis, pairs)  8.28 us
  transfers between devices with their start and end apart: 40, of which 22 were waited for; matrix products, arithmetic and copies ran while one was open for 8% of the time, Pallas kernels for 0%

profile of v4, /device:TPU:8, one launch (start us, length us, event | category | flops | bytes accessed | tf_op | source)
XLA Modules:
  0.0 279.0 jit_solution(9331531253662491544)
XLA Ops:
  15.7 50.5 %all-gather.2.cloned.1.call-done = bf16[2048,1280]{1,0:T(8,128)(2,1)} async-done(((bf16[64,1280]{1,0:T(8,128)(2,1)}), bf16[2048,1280]{1,0:T(8,128)(2,1)}) %all-gather.2.cloned.1.call-update) | async-done | bytes 5242896 | tf_op jit(solution)/shard_map/all_gather | solution.py:176
  66.2 4.1 %fusion.1 = bf16[128,1280]{0,1:T(8,128)(2,1)S(1)} fusion(bf16[2048,1280]{1,0:T(8,128)(2,1)} %all-gather.2.cloned.1.call-done, bf16[1,128,2048]{2,1,0:T(8,128)(2,1)S(1)} %copy-done), kind=kOutput, calls=%fused_computation.7 | convolution fusion | flops 671252480 | bytes 6094848 | tf_op jit(solution)/shard_map/dot_general | solution.py:177
  73.2 4.4 %collective-permute-start = (bf16[16,8448]{1,0:T(8,128)(2,1)S(1)}, bf16[16,8448]{1,0:T(8,128)(2,1)S(1)}, u32[]{:S(2)}, u32[]{:S(2)}) collective-permute-start(bf16[16,8448]{1,0:T(8,128)(2,1)S(1)} %get-tuple-element.168), channel_id=1, source_target_pairs={{1,0},{2,1},{3,2},{4,3},{5,4},{6,5},{7,6},{8,7},{9,8},{10,9},{11,1... | collective-permute-start | bytes 811016 | tf_op jit(solution)/shard_map/ppermute | solution.py:15
  79.6 2.0 collective-permute-done
  82.0 5.9 %collective-permute-start.1 = (bf16[16,8448]{1,0:T(8,128)(2,1)S(1)}, bf16[16,8448]{1,0:T(8,128)(2,1)S(1)}, u32[]{:S(2)}, u32[]{:S(2)}) collective-permute-start(bf16[16,8448]{1,0:T(8,128)(2,1)S(1)} %pad_maximum_fusion.5), channel_id=1, source_target_pairs={{1,0},{2,1},{3,2},{4,3},{5,4},{6,5},{7,6},{8,7},{9,8},{10,9},{11,1... | collective-permute-start | bytes 811016 | tf_op jit(solution)/shard_map/ppermute | solution.py:15
  94.4 3.9 %collective-permute-done.7 = bf16[16,8448]{1,0:T(8,128)(2,1)S(1)} collective-permute-done((bf16[16,8448]{1,0:T(8,128)(2,1)S(1)}, bf16[16,8448]{1,0:T(8,128)(2,1)S(1)}, u32[]{:S(2)}, u32[]{:S(2)}) %collective-permute-start.7) | collective-permute-done | bytes 270368 | tf_op jit(solution)/shard_map/ppermute | solution.py:15
  101.5 2.1 collective-permute-start.3
  103.5 13.8 %collective-permute-done.8 = bf16[16,8448]{1,0:T(8,128)(2,1)S(1)} collective-permute-done((bf16[16,8448]{1,0:T(8,128)(2,1)S(1)}, bf16[16,8448]{1,0:T(8,128)(2,1)S(1)}, u32[]{:S(2)}, u32[]{:S(2)}) %collective-permute-start.8) | collective-permute-done | bytes 270368 | tf_op jit(solution)/shard_map/ppermute | solution.py:15
  117.9 2.1 collective-permute-start.9
  122.5 8.0 %collective-permute-done.9 = bf16[16,8448]{1,0:T(8,128)(2,1)S(1)} collective-permute-done((bf16[16,8448]{1,0:T(8,128)(2,1)S(1)}, bf16[16,8448]{1,0:T(8,128)(2,1)S(1)}, u32[]{:S(2)}, u32[]{:S(2)}) %collective-permute-start.9) | collective-permute-done | bytes 270368 | tf_op jit(solution)/shard_map/ppermute | solution.py:15
  134.9 5.4 %collective-permute-done.10 = bf16[16,8448]{1,0:T(8,128)(2,1)S(1)} collective-permute-done((bf16[16,8448]{1,0:T(8,128)(2,1)S(1)}, bf16[16,8448]{1,0:T(8,128)(2,1)S(1)}, u32[]{:S(2)}, u32[]{:S(2)}) %collective-permute-start.10) | collective-permute-done | bytes 270368 | tf_op jit(solution)/shard_map/ppermute | solution.py:15
  140.9 2.2 collective-permute-start.11
  147.8 6.6 %collective-permute-done.5 = bf16[16,8448]{1,0:T(8,128)(2,1)} collective-permute-done((bf16[16,8448]{1,0:T(8,128)(2,1)}, bf16[16,8448]{1,0:T(8,128)(2,1)}, u32[]{:S(2)}, u32[]{:S(2)}) %collective-permute-start.5) | collective-permute-done | bytes 270368 | tf_op jit(solution)/shard_map/ppermute | solution.py:15
  159.8 5.3 %convolution_bitcast_fusion = f32[2048,1280]{0,1:T(8,128)} fusion(bf16[1,128,2048]{2,1,0:T(8,128)(2,1)S(1)} %copy-done, bf16[128,128]{0,1:T(8,128)(2,1)S(1)} %fusion.8, bf16[128,128]{0,1:T(8,128)(2,1)S(1)} %fusion.7, bf16[128,1024]{0,1:T(8,128)(2,1)S(1)} %bitcast.227), kind=kOutput, calls=%fused_computation.1 | convolution fusion | flops 672071680 | bytes 11337728 | tf_op jit(solution)/shard_map/dot_general | solution.py:217
  165.1 11.3 %copy.68 = f32[2048,1280]{1,0:T(8,128)} copy(f32[2048,1280]{0,1:T(8,128)} %convolution_bitcast_fusion) | data formatting | bytes 20971520 | tf_op jit(solution)/shard_map/dot_general | solution.py:217
  176.4 4.3 %fusion = bf16[4,4,64,1280]{3,2,1,0:T(8,128)(2,1)} fusion(f32[4,4,2,64,1280]{4,3,2,1,0:T(8,128)} %bitcast.223, s32[]{:T(128)S(6)} %select_n.218), kind=kLoop, calls=%fused_computation.4 | loop fusion | bytes 5242884 | tf_op jit(solution)/shard_map/convert_element_type | solution.py:60
  180.8 5.1 %collective-permute-done.12 = bf16[4,4,64,1280]{3,2,1,0:T(8,128)(2,1)S(1)} collective-permute-done((bf16[4,4,64,1280]{3,2,1,0:T(8,128)(2,1)}, bf16[4,4,64,1280]{3,2,1,0:T(8,128)(2,1)S(1)}, u32[]{:S(2)}, u32[]{:S(2)}) %collective-permute-start.12) | collective-permute-done | bytes 2621472 | tf_op jit(solution)/shard_map/ppermute | solution.py:60
  185.9 3.0 %bitcast_add_fusion = f32[4,4,64,1280]{3,2,1,0:T(8,128)S(1)} fusion(bf16[4,4,64,1280]{3,2,1,0:T(8,128)(2,1)S(1)} %collective-permute-done.12, f32[4,4,2,64,1280]{4,3,2,1,0:T(8,128)} %bitcast.224, s32[]{:T(128)S(6)} %select_n.216), kind=kLoop, calls=%fused_computation.2 | loop fusion | flops 2621440 | bytes 13107204 | tf_op jit(solution)/shard_map/add | solution.py:61
  191.8 2.2 collective-permute-start.21
  195.8 13.0 %collective-permute-done.21 = bf16[4,64,640]{2,1,0:T(8,128)(2,1)S(1)} collective-permute-done((bf16[4,64,640]{2,1,0:T(8,128)(2,1)}, bf16[4,64,640]{2,1,0:T(8,128)(2,1)S(1)}, u32[]{:S(2)}, u32[]{:S(2)}) %collective-permute-start.21) | collective-permute-done | bytes 327712 | tf_op jit(solution)/shard_map/ppermute | solution.py:60
  214.6 5.2 %collective-permute-done.13 = bf16[4,64,640]{2,1,0:T(8,128)(2,1)S(1)} collective-permute-done((bf16[4,64,640]{2,1,0:T(8,128)(2,1)S(1)}, bf16[4,64,640]{2,1,0:T(8,128)(2,1)S(1)}, u32[]{:S(2)}, u32[]{:S(2)}) %collective-permute-start.13) | collective-permute-done | bytes 327712 | tf_op jit(solution)/shard_map/ppermute | solution.py:60
  222.1 2.3 collective-permute-done.18
  227.5 5.4 %collective-permute-start.31 = (f32[8,1280]{1,0:T(8,128)S(1)}, f32[8,1280]{1,0:T(8,128)S(1)}, u32[]{:S(2)}, u32[]{:S(2)}) collective-permute-start(f32[8,1280]{1,0:T(8,128)S(1)} %get-tuple-element.154), channel_id=1, source_target_pairs={{0,224},{32,0},{64,32},{96,64},{128,96},{160,128},{192,160},{224,1... | collective-permute-start | bytes 122888 | tf_op jit(solution)/shard_map/ppermute | solution.py:87
  232.8 2.2 collective-permute-start.30
  236.2 2.7 collective-permute-start.28
  240.0 3.7 %collective-permute-start.26 = (f32[8,1280]{1,0:T(8,128)S(1)}, f32[8,1280]{1,0:T(8,128)S(1)}, u32[]{:S(2)}, u32[]{:S(2)}) collective-permute-start(f32[8,1280]{1,0:T(8,128)S(1)} %get-tuple-element.159), channel_id=1, source_target_pairs={{0,64},{32,96},{64,128},{96,160},{128,192},{160,224},{192,0},{224,... | collective-permute-start | bytes 122888 | tf_op jit(solution)/shard_map/ppermute | solution.py:87
  249.7 5.3 %convolution_bitcast_fusion.1 = f32[1,128,2048]{2,1,0:T(8,128)} fusion(bf16[2048,1280]{1,0:T(8,128)(2,1)} %all-gather.2.cloned.1.call-done, bf16[128,128]{0,1:T(8,128)(2,1)S(1)} %fusion.8, bf16[128,128]{0,1:T(8,128)(2,1)S(1)} %fusion.7, bf16[128,1024]{0,1:T(8,128)(2,1)S(1)} %bitcast.228), kind=kOutput, calls=%fused_computation.5 | convolution fusion | flops 672071680 | bytes 6619136 | tf_op jit(solution)/shard_map/dot_general | solution.py:210
  255.4 2.7 collective-permute-start.34
  258.1 3.2 %collective-permute-start.35 = (f32[8,1280]{1,0:T(8,128)S(1)}, f32[8,1280]{1,0:T(8,128)S(1)}, u32[]{:S(2)}, u32[]{:S(2)}) collective-permute-start(f32[8,1280]{1,0:T(8,128)S(1)} %get-tuple-element.99), channel_id=1, source_target_pairs={{0,128},{32,160},{64,192},{96,224},{128,0},{160,32},{192,64},{224,... | collective-permute-start | bytes 122888 | tf_op jit(solution)/shard_map/ppermute | solution.py:91
  261.3 2.4 collective-permute-start.36
  263.7 3.0 %collective-permute-start.37 = (f32[8,1280]{1,0:T(8,128)S(1)}, f32[8,1280]{1,0:T(8,128)S(1)}, u32[]{:S(2)}, u32[]{:S(2)}) collective-permute-start(f32[8,1280]{1,0:T(8,128)S(1)} %get-tuple-element.99), channel_id=1, source_target_pairs={{0,192},{32,224},{64,0},{96,32},{128,64},{160,96},{192,128},{224,1... | collective-permute-start | bytes 122888 | tf_op jit(solution)/shard_map/ppermute | solution.py:91
  266.6 2.0 collective-permute-start.38
  (213 shorter events, 68.9 us)
Async XLA Ops:
  7.2 59.0 %all-gather.2.cloned.1.call-start = ((), (), s32[]{:S(2)}) async-start(), calls=%async_computation | async-start | bytes 5406720 | tf_op jit(solution)/shard_map/all_gather | solution.py:176
  73.2 8.4 %collective-permute-start = (bf16[16,8448]{1,0:T(8,128)(2,1)S(1)}, bf16[16,8448]{1,0:T(8,128)(2,1)S(1)}, u32[]{:S(2)}, u32[]{:S(2)}) collective-permute-start(bf16[16,8448]{1,0:T(8,128)(2,1)S(1)} %get-tuple-element.168), channel_id=1, source_target_pairs={{1,0},{2,1},{3,2},{4,3},{5,4},{6,5},{7,6},{8,7},{9,8},{10,9},{11,1... | collective-permute-start | bytes 811016 | tf_op jit(solution)/shard_map/ppermute | solution.py:15
  77.7 10.3 %collective-permute-start.6 = (bf16[16,8448]{1,0:T(8,128)(2,1)S(1)}, bf16[16,8448]{1,0:T(8,128)(2,1)S(1)}, u32[]{:S(2)}, u32[]{:S(2)}) collective-permute-start(bf16[16,8448]{1,0:T(8,128)(2,1)S(1)} %get-tuple-element.169), channel_id=1, source_target_pairs={{0,1},{1,2},{2,3},{3,4},{4,5},{5,6},{6,7},{7,8},{8,9},{9,10},{10,1... | collective-permute-start | bytes 811016 | tf_op jit(solution)/shard_map/ppermute | solution.py:15
  82.0 9.9 %collective-permute-start.1 = (bf16[16,8448]{1,0:T(8,128)(2,1)S(1)}, bf16[16,8448]{1,0:T(8,128)(2,1)S(1)}, u32[]{:S(2)}, u32[]{:S(2)}) collective-permute-start(bf16[16,8448]{1,0:T(8,128)(2,1)S(1)} %pad_maximum_fusion.5), channel_id=1, source_target_pairs={{1,0},{2,1},{3,2},{4,3},{5,4},{6,5},{7,6},{8,7},{9,8},{10,9},{11,1... | collective-permute-start | bytes 811016 | tf_op jit(solution)/shard_map/ppermute | solution.py:15
  88.5 9.9 %collective-permute-start.7 = (bf16[16,8448]{1,0:T(8,128)(2,1)S(1)}, bf16[16,8448]{1,0:T(8,128)(2,1)S(1)}, u32[]{:S(2)}, u32[]{:S(2)}) collective-permute-start(bf16[16,8448]{1,0:T(8,128)(2,1)S(1)} %pad_maximum_fusion.10), channel_id=1, source_target_pairs={{0,1},{1,2},{2,3},{3,4},{4,5},{5,6},{6,7},{7,8},{8,9},{9,10},{10,1... | collective-permute-start | bytes 811016 | tf_op jit(solution)/shard_map/ppermute | solution.py:15
  92.5 8.4 %collective-permute-start.2 = (bf16[16,8448]{1,0:T(8,128)(2,1)S(1)}, bf16[16,8448]{1,0:T(8,128)(2,1)S(1)}, u32[]{:S(2)}, u32[]{:S(2)}) collective-permute-start(bf16[16,8448]{1,0:T(8,128)(2,1)S(1)} %pad_maximum_fusion.6), channel_id=1, source_target_pairs={{2,0},{3,1},{4,2},{5,3},{6,4},{7,5},{8,6},{9,7},{10,8},{11,9},{12,... | collective-permute-start | bytes 811016 | tf_op jit(solution)/shard_map/ppermute | solution.py:15
  98.9 18.4 %collective-permute-start.8 = (bf16[16,8448]{1,0:T(8,128)(2,1)S(1)}, bf16[16,8448]{1,0:T(8,128)(2,1)S(1)}, u32[]{:S(2)}, u32[]{:S(2)}) collective-permute-start(bf16[16,8448]{1,0:T(8,128)(2,1)S(1)} %pad_maximum_fusion.11), channel_id=1, source_target_pairs={{0,2},{1,3},{2,4},{3,5},{4,6},{5,7},{6,8},{7,9},{8,10},{9,11},{10,... | collective-permute-start | bytes 811016 | tf_op jit(solution)/shard_map/ppermute | solution.py:15
  101.5 18.5 %collective-permute-start.3 = (bf16[16,8448]{1,0:T(8,128)(2,1)S(1)}, bf16[16,8448]{1,0:T(8,128)(2,1)S(1)}, u32[]{:S(2)}, u32[]{:S(2)}) collective-permute-start(bf16[16,8448]{1,0:T(8,128)(2,1)S(1)} %pad_maximum_fusion.7), channel_id=1, source_target_pairs={{4,0},{5,1},{6,2},{7,3},{8,4},{9,5},{10,6},{11,7},{12,8},{13,9},{1... | collective-permute-start | bytes 811016 | tf_op jit(solution)/shard_map/ppermute | solution.py:15
  117.9 12.6 %collective-permute-start.9 = (bf16[16,8448]{1,0:T(8,128)(2,1)S(1)}, bf16[16,8448]{1,0:T(8,128)(2,1)S(1)}, u32[]{:S(2)}, u32[]{:S(2)}) collective-permute-start(bf16[16,8448]{1,0:T(8,128)(2,1)S(1)} %pad_maximum_fusion.12), channel_id=1, source_target_pairs={{0,4},{1,5},{2,6},{3,7},{4,8},{5,9},{6,10},{7,11},{8,12},{9,13},{1... | collective-permute-start | bytes 811016 | tf_op jit(solution)/shard_map/ppermute | solution.py:15
  120.6 14.3 %collective-permute-start.4 = (bf16[16,8448]{1,0:T(8,128)(2,1)S(1)}, bf16[16,8448]{1,0:T(8,128)(2,1)S(1)}, u32[]{:S(2)}, u32[]{:S(2)}) collective-permute-start(bf16[16,8448]{1,0:T(8,128)(2,1)S(1)} %pad_maximum_fusion.8), channel_id=1, source_target_pairs={{8,0},{9,1},{10,2},{11,3},{12,4},{13,5},{14,6},{15,7},{16,8},{17,9... | collective-permute-start | bytes 811016 | tf_op jit(solution)/shard_map/ppermute | solution.py:15
  131.1 9.2 %collective-permute-start.10 = (bf16[16,8448]{1,0:T(8,128)(2,1)S(1)}, bf16[16,8448]{1,0:T(8,128)(2,1)S(1)}, u32[]{:S(2)}, u32[]{:S(2)}) collective-permute-start(bf16[16,8448]{1,0:T(8,128)(2,1)S(1)} %pad_maximum_fusion.13), channel_id=1, source_target_pairs={{0,8},{1,9},{2,10},{3,11},{4,12},{5,13},{6,14},{7,15},{8,16},{9,17... | collective-permute-start | bytes 811016 | tf_op jit(solution)/shard_map/ppermute | solution.py:15
  144.2 10.2 %collective-permute-start.5 = (bf16[16,8448]{1,0:T(8,128)(2,1)}, bf16[16,8448]{1,0:T(8,128)(2,1)}, u32[]{:S(2)}, u32[]{:S(2)}) collective-permute-start(bf16[16,8448]{1,0:T(8,128)(2,1)} %pad_maximum_fusion.9), channel_id=1, source_target_pairs={{16,0},{17,1},{18,2},{19,3},{20,4},{21,5},{22,6},{23,7},{24,8},{25... | collective-permute-start | bytes 811016 | tf_op jit(solution)/shard_map/ppermute | solution.py:15
  191.8 17.0 %collective-permute-start.21 = (bf16[4,64,640]{2,1,0:T(8,128)(2,1)}, bf16[4,64,640]{2,1,0:T(8,128)(2,1)S(1)}, u32[]{:S(2)}, u32[]{:S(2)}) collective-permute-start(bf16[4,64,640]{2,1,0:T(8,128)(2,1)} %get-tuple-element.145), channel_id=1, source_target_pairs={{0,24},{1,25},{2,26},{3,27},{4,28},{5,29},{6,30},{7,31},{8,0},{9,1... | collective-permute-start | bytes 983048 | tf_op jit(solution)/shard_map/ppermute | solution.py:60
  194.0 14.8 %collective-permute-start.20 = (bf16[4,64,640]{2,1,0:T(8,128)(2,1)}, bf16[4,64,640]{2,1,0:T(8,128)(2,1)}, u32[]{:S(2)}, u32[]{:S(2)}) collective-permute-start(bf16[4,64,640]{2,1,0:T(8,128)(2,1)} %get-tuple-element.146), channel_id=1, source_target_pairs={{0,16},{1,17},{2,18},{3,19},{4,20},{5,21},{6,22},{7,23},{8,24},{9,... | collective-permute-start | bytes 983048 | tf_op jit(solution)/shard_map/ppermute | solution.py:60
  194.0 16.7 %collective-permute-start.19 = (bf16[4,64,640]{2,1,0:T(8,128)(2,1)}, bf16[4,64,640]{2,1,0:T(8,128)(2,1)}, u32[]{:S(2)}, u32[]{:S(2)}) collective-permute-start(bf16[4,64,640]{2,1,0:T(8,128)(2,1)} %get-tuple-element.144), channel_id=1, source_target_pairs={{0,8},{1,9},{2,10},{3,11},{4,12},{5,13},{6,14},{7,15},{8,16},{9,17... | collective-permute-start | bytes 983048 | tf_op jit(solution)/shard_map/ppermute | solution.py:60
  195.6 18.0 %collective-permute-start.15 = (bf16[4,64,640]{2,1,0:T(8,128)(2,1)S(1)}, bf16[4,64,640]{2,1,0:T(8,128)(2,1)S(1)}, u32[]{:S(2)}, u32[]{:S(2)}) collective-permute-start(bf16[4,64,640]{2,1,0:T(8,128)(2,1)S(1)} %get-tuple-element.143), channel_id=1, source_target_pairs={{0,6},{1,7},{2,0},{3,1},{4,2},{5,3},{6,4},{7,5},{8,14},{9,15},{10,... | collective-permute-start | bytes 983048 | tf_op jit(solution)/shard_map/ppermute | solution.py:60
  195.7 18.8 %collective-permute-start.14 = (bf16[4,64,640]{2,1,0:T(8,128)(2,1)S(1)}, bf16[4,64,640]{2,1,0:T(8,128)(2,1)S(1)}, u32[]{:S(2)}, u32[]{:S(2)}) collective-permute-start(bf16[4,64,640]{2,1,0:T(8,128)(2,1)S(1)} %get-tuple-element.142), channel_id=1, source_target_pairs={{0,4},{1,5},{2,6},{3,7},{4,0},{5,1},{6,2},{7,3},{8,12},{9,13},{10,... | collective-permute-start | bytes 983048 | tf_op jit(solution)/shard_map/ppermute | solution.py:60
  208.8 10.9 %collective-permute-start.13 = (bf16[4,64,640]{2,1,0:T(8,128)(2,1)S(1)}, bf16[4,64,640]{2,1,0:T(8,128)(2,1)S(1)}, u32[]{:S(2)}, u32[]{:S(2)}) collective-permute-start(bf16[4,64,640]{2,1,0:T(8,128)(2,1)S(1)} %get-tuple-element.141), channel_id=1, source_target_pairs={{0,2},{1,3},{2,4},{3,5},{4,6},{5,7},{6,0},{7,1},{8,10},{9,11},{10,... | collective-permute-start | bytes 983048 | tf_op jit(solution)/shard_map/ppermute | solution.py:60
  212.2 7.9 %collective-permute-start.24 = (bf16[64,640]{1,0:T(8,128)(2,1)S(1)}, bf16[64,640]{1,0:T(8,128)(2,1)S(1)}, u32[]{:S(2)}, u32[]{:S(2)}) collective-permute-start(bf16[64,640]{1,0:T(8,128)(2,1)S(1)} %get-tuple-element.151), channel_id=1, source_target_pairs={{0,6},{1,7},{2,0},{3,1},{4,2},{5,3},{6,4},{7,5},{8,14},{9,15},{10,... | collective-permute-start | bytes 245768 | tf_op jit(solution)/shard_map/ppermute | solution.py:60
  213.6 8.4 %collective-permute-start.23 = (bf16[64,640]{1,0:T(8,128)(2,1)S(1)}, bf16[64,640]{1,0:T(8,128)(2,1)S(1)}, u32[]{:S(2)}, u32[]{:S(2)}) collective-permute-start(bf16[64,640]{1,0:T(8,128)(2,1)S(1)} %get-tuple-element.152), channel_id=1, source_target_pairs={{0,4},{1,5},{2,6},{3,7},{4,0},{5,1},{6,2},{7,3},{8,12},{9,13},{10,... | collective-permute-start | bytes 245768 | tf_op jit(solution)/shard_map/ppermute | solution.py:60
  213.6 8.4 %collective-permute-start.22 = (bf16[64,640]{1,0:T(8,128)(2,1)S(1)}, bf16[64,640]{1,0:T(8,128)(2,1)S(1)}, u32[]{:S(2)}, u32[]{:S(2)}) collective-permute-start(bf16[64,640]{1,0:T(8,128)(2,1)S(1)} %get-tuple-element.150), channel_id=1, source_target_pairs={{0,2},{1,3},{2,4},{3,5},{4,6},{5,7},{6,0},{7,1},{8,10},{9,11},{10,... | collective-permute-start | bytes 245768 | tf_op jit(solution)/shard_map/ppermute | solution.py:60
  220.1 7.3 %collective-permute-start.16 = (bf16[64,640]{1,0:T(8,128)(2,1)S(1)}, bf16[64,640]{1,0:T(8,128)(2,1)S(1)}, u32[]{:S(2)}, u32[]{:S(2)}) collective-permute-start(bf16[64,640]{1,0:T(8,128)(2,1)S(1)} %get-tuple-element.147), channel_id=1, source_target_pairs={{0,8},{1,9},{2,10},{3,11},{4,12},{5,13},{6,14},{7,15},{8,16},{9,17... | collective-permute-start | bytes 245768 | tf_op jit(solution)/shard_map/ppermute | solution.py:60
  227.5 12.5 %collective-permute-start.31 = (f32[8,1280]{1,0:T(8,128)S(1)}, f32[8,1280]{1,0:T(8,128)S(1)}, u32[]{:S(2)}, u32[]{:S(2)}) collective-permute-start(f32[8,1280]{1,0:T(8,128)S(1)} %get-tuple-element.154), channel_id=1, source_target_pairs={{0,224},{32,0},{64,32},{96,64},{128,96},{160,128},{192,160},{224,1... | collective-permute-start | bytes 122888 | tf_op jit(solution)/shard_map/ppermute | solution.py:87
  232.8 10.9 %collective-permute-start.30 = (f32[8,1280]{1,0:T(8,128)S(1)}, f32[8,1280]{1,0:T(8,128)S(1)}, u32[]{:S(2)}, u32[]{:S(2)}) collective-permute-start(f32[8,1280]{1,0:T(8,128)S(1)} %get-tuple-element.155), channel_id=1, source_target_pairs={{0,192},{32,224},{64,0},{96,32},{128,64},{160,96},{192,128},{224,1... | collective-permute-start | bytes 122888 | tf_op jit(solution)/shard_map/ppermute | solution.py:87
  235.0 9.1 %collective-permute-start.29 = (f32[8,1280]{1,0:T(8,128)S(1)}, f32[8,1280]{1,0:T(8,128)S(1)}, u32[]{:S(2)}, u32[]{:S(2)}) collective-permute-start(f32[8,1280]{1,0:T(8,128)S(1)} %get-tuple-element.156), channel_id=1, source_target_pairs={{0,160},{32,192},{64,224},{96,0},{128,32},{160,64},{192,96},{224,1... | collective-permute-start | bytes 122888 | tf_op jit(solution)/shard_map/ppermute | solution.py:87
  236.2 8.2 %collective-permute-start.28 = (f32[8,1280]{1,0:T(8,128)S(1)}, f32[8,1280]{1,0:T(8,128)S(1)}, u32[]{:S(2)}, u32[]{:S(2)}) collective-permute-start(f32[8,1280]{1,0:T(8,128)S(1)} %get-tuple-element.157), channel_id=1, source_target_pairs={{0,128},{32,160},{64,192},{96,224},{128,0},{160,32},{192,64},{224,... | collective-permute-start | bytes 122888 | tf_op jit(solution)/shard_map/ppermute | solution.py:87
  240.0 7.7 %collective-permute-start.26 = (f32[8,1280]{1,0:T(8,128)S(1)}, f32[8,1280]{1,0:T(8,128)S(1)}, u32[]{:S(2)}, u32[]{:S(2)}) collective-permute-start(f32[8,1280]{1,0:T(8,128)S(1)} %get-tuple-element.159), channel_id=1, source_target_pairs={{0,64},{32,96},{64,128},{96,160},{128,192},{160,224},{192,0},{224,... | collective-permute-start | bytes 122888 | tf_op jit(solution)/shard_map/ppermute | solution.py:87
  248.9 14.7 %collective-permute-start.32 = (f32[8,1280]{1,0:T(8,128)S(1)}, f32[8,1280]{1,0:T(8,128)S(1)}, u32[]{:S(2)}, u32[]{:S(2)}) collective-permute-start(f32[8,1280]{1,0:T(8,128)S(1)} %get-tuple-element.99), channel_id=1, source_target_pairs={{0,32},{32,64},{64,96},{96,128},{128,160},{160,192},{192,224},{224... | collective-permute-start | bytes 122888 | tf_op jit(solution)/shard_map/ppermute | solution.py:91
  255.0 11.7 %collective-permute-start.33 = (f32[8,1280]{1,0:T(8,128)S(1)}, f32[8,1280]{1,0:T(8,128)S(1)}, u32[]{:S(2)}, u32[]{:S(2)}) collective-permute-start(f32[8,1280]{1,0:T(8,128)S(1)} %get-tuple-element.99), channel_id=1, source_target_pairs={{0,64},{32,96},{64,128},{96,160},{128,192},{160,224},{192,0},{224,... | collective-permute-start | bytes 122888 | tf_op jit(solution)/shard_map/ppermute | solution.py:91
  255.4 13.3 %collective-permute-start.34 = (f32[8,1280]{1,0:T(8,128)S(1)}, f32[8,1280]{1,0:T(8,128)S(1)}, u32[]{:S(2)}, u32[]{:S(2)}) collective-permute-start(f32[8,1280]{1,0:T(8,128)S(1)} %get-tuple-element.99), channel_id=1, source_target_pairs={{0,96},{32,128},{64,160},{96,192},{128,224},{160,0},{192,32},{224,... | collective-permute-start | bytes 122888 | tf_op jit(solution)/shard_map/ppermute | solution.py:91
  258.1 10.6 %collective-permute-start.35 = (f32[8,1280]{1,0:T(8,128)S(1)}, f32[8,1280]{1,0:T(8,128)S(1)}, u32[]{:S(2)}, u32[]{:S(2)}) collective-permute-start(f32[8,1280]{1,0:T(8,128)S(1)} %get-tuple-element.99), channel_id=1, source_target_pairs={{0,128},{32,160},{64,192},{96,224},{128,0},{160,32},{192,64},{224,... | collective-permute-start | bytes 122888 | tf_op jit(solution)/shard_map/ppermute | solution.py:91
  261.3 7.4 %collective-permute-start.36 = (f32[8,1280]{1,0:T(8,128)S(1)}, f32[8,1280]{1,0:T(8,128)S(1)}, u32[]{:S(2)}, u32[]{:S(2)}) collective-permute-start(f32[8,1280]{1,0:T(8,128)S(1)} %get-tuple-element.99), channel_id=1, source_target_pairs={{0,160},{32,192},{64,224},{96,0},{128,32},{160,64},{192,96},{224,1... | collective-permute-start | bytes 122888 | tf_op jit(solution)/shard_map/ppermute | solution.py:91
  (21 other events, 494.1 us)
Sparse Core Ops, SparseCore 0:
  11.1 54.9 all-gather.1

commit v5 on v4

--- a/solution.py
+++ b/solution.py
@@ -27,8 +27,11 @@
         got = shifted(packed, axis, step, reverse)
         return got[:, :split], got[:, split] + got[:, split + 128]
 
-    flat, decay = send(flat, decay, 1)
-    step = 1
+    nearer_flat, nearer_decay = send(flat, decay, 1)
+    farther_flat, farther_decay = send(flat, decay, 2)
+    flat = nearer_decay[:, None] * farther_flat + nearer_flat
+    decay = farther_decay * nearer_decay
+    step = 2
     while step < lax.axis_size(axis):
         earlier_flat, earlier_decay = send(flat, decay, step)
         flat = decay[:, None] * earlier_flat + flat
@@ -50,7 +53,7 @@
 def digit_reduce(value, axis, where, stride, radix):
     count = lax.axis_size(axis)
     digit = (lax.axis_index(axis) // stride) % radix
-    total = lax.dynamic_index_in_dim(value, digit, where, False)
+    total = lax.dynamic_index_in_dim(value, digit, where, False).astype(jnp.float32)
     for offset in range(1, radix):
         piece = lax.dynamic_index_in_dim(value, (digit + offset) % radix, where, False)
         pairs = [
@@ -216,7 +219,7 @@
     partial_grad = seq_reduce_scatter(
         lax.dot_general(
             features, d_proj, (((0,), (0,)), ((), ())), preferred_element_type=jnp.float32
-        ),
+        ).astype(jnp.bfloat16),
         "seq",
     )
     summed_grad = replicated_sum(partial_grad, "dp")

time: 281 us -> 271 us (0.964)
  local copies, waits for them, and re-layouts: 26.4 us -> 20.2 us
  waiting for transfers between devices: 130 us -> 125 us
  starting transfers between devices: 68.8 us -> 73.4 us
    dot_general x1 -> x0, local copies, waits for them, and re-layouts: 11.3 us -> none  [local(): lax.dot_general(features, d_proj, (((0,), (0,)), ((), ())), preferred_ele...]
    ppermute x12, waiting for transfers between devices: 42.5 us -> 34.5 us  [shifted(): lax.ppermute(value.astype(jnp.bfloat16), axis, pairs).astype(value.dtype)]
    convert_element_type x0 -> x1, local copies, waits for them, and re-layouts: none -> 7.87 us  [local(): partial_grad = seq_reduce_scatter(lax.dot_general(features, d_proj, (((0,...]
    ppermute x12, starting transfers between devices: 29.6 us -> 35.8 us  [shifted(): lax.ppermute(value.astype(jnp.bfloat16), axis, pairs).astype(value.dtype)]
    convert_element_type x5 -> x4, local copies, waits for them, and re-layouts: 5.5 us -> 1.21 us  [digit_reduce(): got = lax.ppermute(piece.astype(jnp.bfloat16), axis, pairs)]
  transfers between devices with their start and end apart: 40 -> 40, of which waited for: 22 -> 21; matrix products, arithmetic and copies ran while one was open for 8% -> 7% of each run, Pallas kernels for 0% -> 0%
where the time goes in v5:
time: 271 us; the launch traced here: 270 us
  waiting for transfers between devices  125 us (46%)
  starting transfers between devices  73.4 us (27%)
  local copies, waits for them, and re-layouts  20.2 us (7%)
  matrix products  18.9 us (7%)
  other arithmetic  17.9 us (7%)
  between operations  15 us (6%)
    all_gather x1, waiting for transfers between devices, local(): lax.all_gather(dequantize(weight_codes, scales), 'seq', axis=0, tiled=True)  50.5 us
    ppermute x12, starting transfers between devices, shifted(): lax.ppermute(value.astype(jnp.bfloat16), axis, pairs).astype(value.dtype)  35.8 us
    ppermute x12, waiting for transfers between devices, shifted(): lax.ppermute(value.astype(jnp.bfloat16), axis, pairs).astype(value.dtype)  34.5 us
    ppermute x13, waiting for transfers between devices, digit_reduce(): got = lax.ppermute(piece.astype(jnp.bfloat16), axis, pairs)  33.3 us
    ppermute x7, starting transfers between devices, replicated_sum(): total = total + lax.ppermute(piece, axis, pairs)  15.8 us
    ppermute x7, starting transfers between devices, replicated_sum(): gathered.append(lax.ppermute(total, axis, pairs))  14.4 us
    convert_element_type x1, local copies, waits for them, and re-layouts, local(): partial_grad = seq_reduce_scatter(lax.dot_general(features, d_proj, (((0,...  7.87 us
    ppermute x13, starting transfers between devices, digit_reduce(): got = lax.ppermute(piece.astype(jnp.bfloat16), axis, pairs)  7.4 us
  transfers between devices with their start and end apart: 40, of which 21 were waited for; matrix products, arithmetic and copies ran while one was open for 7% of the time, Pallas kernels for 0%

profile of v5, /device:TPU:8, one launch (start us, length us, event | category | flops | bytes accessed | tf_op | source)
XLA Modules:
  0.0 270.0 jit_solution(3635966980422640331)
XLA Ops:
  15.7 50.5 %all-gather.2.cloned.1.call-done = bf16[2048,1280]{1,0:T(8,128)(2,1)} async-done(((bf16[64,1280]{1,0:T(8,128)(2,1)}), bf16[2048,1280]{1,0:T(8,128)(2,1)}) %all-gather.2.cloned.1.call-update) | async-done | bytes 5242896 | tf_op jit(solution)/shard_map/all_gather | solution.py:179
  66.2 4.1 %fusion.1 = bf16[128,1280]{0,1:T(8,128)(2,1)S(1)} fusion(bf16[2048,1280]{1,0:T(8,128)(2,1)} %all-gather.2.cloned.1.call-done, bf16[1,128,2048]{2,1,0:T(8,128)(2,1)S(1)} %copy-done), kind=kOutput, calls=%fused_computation.7 | convolution fusion | flops 671252480 | bytes 6094848 | tf_op jit(solution)/shard_map/dot_general | solution.py:180
  73.2 4.4 %collective-permute-start = (bf16[16,8448]{1,0:T(8,128)(2,1)S(1)}, bf16[16,8448]{1,0:T(8,128)(2,1)S(1)}, u32[]{:S(2)}, u32[]{:S(2)}) collective-permute-start(bf16[16,8448]{1,0:T(8,128)(2,1)S(1)} %get-tuple-element.162), channel_id=1, source_target_pairs={{1,0},{2,1},{3,2},{4,3},{5,4},{6,5},{7,6},{8,7},{9,8},{10,9},{11,1... | collective-permute-start | bytes 811016 | tf_op jit(solution)/shard_map/ppermute | solution.py:15
  77.6 2.1 collective-permute-start.1
  79.8 2.1 collective-permute-start.6
  81.9 3.5 %collective-permute-start.7 = (bf16[16,8448]{1,0:T(8,128)(2,1)S(1)}, bf16[16,8448]{1,0:T(8,128)(2,1)S(1)}, u32[]{:S(2)}, u32[]{:S(2)}) collective-permute-start(bf16[16,8448]{1,0:T(8,128)(2,1)S(1)} %get-tuple-element.163), channel_id=1, source_target_pairs={{0,2},{1,3},{2,4},{3,5},{4,6},{5,7},{6,8},{7,9},{8,10},{9,11},{10,... | collective-permute-start | bytes 811016 | tf_op jit(solution)/shard_map/ppermute | solution.py:15
  87.9 6.5 %collective-permute-start.2 = (bf16[16,8448]{1,0:T(8,128)(2,1)S(1)}, bf16[16,8448]{1,0:T(8,128)(2,1)S(1)}, u32[]{:S(2)}, u32[]{:S(2)}) collective-permute-start(bf16[16,8448]{1,0:T(8,128)(2,1)S(1)} %pad_maximum_fusion.5), channel_id=1, source_target_pairs={{2,0},{3,1},{4,2},{5,3},{6,4},{7,5},{8,6},{9,7},{10,8},{11,9},{12,... | collective-permute-start | bytes 811016 | tf_op jit(solution)/shard_map/ppermute | solution.py:15
  99.8 4.3 %collective-permute-start.3 = (bf16[16,8448]{1,0:T(8,128)(2,1)S(1)}, bf16[16,8448]{1,0:T(8,128)(2,1)S(1)}, u32[]{:S(2)}, u32[]{:S(2)}) collective-permute-start(bf16[16,8448]{1,0:T(8,128)(2,1)S(1)} %pad_maximum_fusion.6), channel_id=1, source_target_pairs={{4,0},{5,1},{6,2},{7,3},{8,4},{9,5},{10,6},{11,7},{12,8},{13,9},{1... | collective-permute-start | bytes 811016 | tf_op jit(solution)/shard_map/ppermute | solution.py:15
  104.1 9.9 %collective-permute-done.8 = bf16[16,8448]{1,0:T(8,128)(2,1)S(1)} collective-permute-done((bf16[16,8448]{1,0:T(8,128)(2,1)S(1)}, bf16[16,8448]{1,0:T(8,128)(2,1)S(1)}, u32[]{:S(2)}, u32[]{:S(2)}) %collective-permute-start.8) | collective-permute-done | bytes 270368 | tf_op jit(solution)/shard_map/ppermute | solution.py:15
  114.6 2.1 collective-permute-start.9
  119.2 7.7 %collective-permute-done.9 = bf16[16,8448]{1,0:T(8,128)(2,1)S(1)} collective-permute-done((bf16[16,8448]{1,0:T(8,128)(2,1)S(1)}, bf16[16,8448]{1,0:T(8,128)(2,1)S(1)}, u32[]{:S(2)}, u32[]{:S(2)}) %collective-permute-start.9) | collective-permute-done | bytes 270368 | tf_op jit(solution)/shard_map/ppermute | solution.py:15
  127.6 2.3 collective-permute-start.10
  131.8 4.7 %collective-permute-done.10 = bf16[16,8448]{1,0:T(8,128)(2,1)S(1)} collective-permute-done((bf16[16,8448]{1,0:T(8,128)(2,1)S(1)}, bf16[16,8448]{1,0:T(8,128)(2,1)S(1)}, u32[]{:S(2)}, u32[]{:S(2)}) %collective-permute-start.10) | collective-permute-done | bytes 270368 | tf_op jit(solution)/shard_map/ppermute | solution.py:15
  137.1 3.2 %collective-permute-start.11 = (bf16[16,8448]{1,0:T(8,128)(2,1)S(1)}, bf16[16,8448]{1,0:T(8,128)(2,1)S(1)}, u32[]{:S(2)}, u32[]{:S(2)}) collective-permute-start(bf16[16,8448]{1,0:T(8,128)(2,1)S(1)} %pad_maximum_fusion.12), channel_id=1, source_target_pairs={{0,16},{1,17},{2,18},{3,19},{4,20},{5,21},{6,22},{7,23},{8,24},{9,... | collective-permute-start | bytes 811016 | tf_op jit(solution)/shard_map/ppermute | solution.py:15
  145.0 6.6 %collective-permute-done.5 = bf16[16,8448]{1,0:T(8,128)(2,1)} collective-permute-done((bf16[16,8448]{1,0:T(8,128)(2,1)}, bf16[16,8448]{1,0:T(8,128)(2,1)}, u32[]{:S(2)}, u32[]{:S(2)}) %collective-permute-start.5) | collective-permute-done | bytes 270368 | tf_op jit(solution)/shard_map/ppermute | solution.py:15
  157.0 3.9 %fusion = bf16[2048,1280]{0,1:T(8,128)(2,1)} fusion(bf16[1,128,2048]{2,1,0:T(8,128)(2,1)S(1)} %copy-done, bf16[128,128]{0,1:T(8,128)(2,1)S(1)} %fusion.8, bf16[128,128]{0,1:T(8,128)(2,1)S(1)} %fusion.7, bf16[128,1024]{0,1:T(8,128)(2,1)S(1)} %bitcast.228), kind=kOutput, calls=%fused_computation.2 | convolution fusion | flops 674693120 | bytes 6094848 | tf_op jit(solution)/shard_map/dot_general | solution.py:220
  160.9 7.9 %copy.68 = bf16[2048,1280]{1,0:T(8,128)(2,1)} copy(bf16[2048,1280]{0,1:T(8,128)(2,1)} %fusion) | data formatting | bytes 10485760 | tf_op jit(solution)/shard_map/convert_element_type | solution.py:222
  170.8 4.9 %collective-permute-done.12 = bf16[4,4,64,1280]{3,2,1,0:T(8,128)(2,1)} collective-permute-done((bf16[4,4,64,1280]{3,2,1,0:T(8,128)(2,1)S(1)}, bf16[4,4,64,1280]{3,2,1,0:T(8,128)(2,1)}, u32[]{:S(2)}, u32[]{:S(2)}) %collective-permute-start.12) | collective-permute-done | bytes 2621472 | tf_op jit(solution)/shard_map/ppermute | solution.py:63
  175.8 3.2 %convert_add_fusion = f32[4,4,64,1280]{3,2,1,0:T(8,128)S(1)} fusion(bf16[4,4,64,1280]{3,2,1,0:T(8,128)(2,1)} %collective-permute-done.12, bf16[4,4,2,64,1280]{4,3,2,1,0:T(8,128)(2,1)} %bitcast.225, s32[]{:T(128)S(6)} %select_n.216), kind=kLoop, calls=%fused_computation.3 | loop fusion | flops 3932160 | bytes 10485764 | tf_op jit(solution)/shard_map/add | solution.py:64
  185.0 14.0 %collective-permute-done.21 = bf16[4,64,640]{2,1,0:T(8,128)(2,1)S(1)} collective-permute-done((bf16[4,64,640]{2,1,0:T(8,128)(2,1)}, bf16[4,64,640]{2,1,0:T(8,128)(2,1)S(1)}, u32[]{:S(2)}, u32[]{:S(2)}) %collective-permute-start.21) | collective-permute-done | bytes 327712 | tf_op jit(solution)/shard_map/ppermute | solution.py:63
  204.7 7.1 %collective-permute-done.13 = bf16[4,64,640]{2,1,0:T(8,128)(2,1)S(1)} collective-permute-done((bf16[4,64,640]{2,1,0:T(8,128)(2,1)S(1)}, bf16[4,64,640]{2,1,0:T(8,128)(2,1)S(1)}, u32[]{:S(2)}, u32[]{:S(2)}) %collective-permute-start.13) | collective-permute-done | bytes 327712 | tf_op jit(solution)/shard_map/ppermute | solution.py:63
  214.2 2.3 collective-permute-done.18
  219.6 3.4 %collective-permute-start.31 = (f32[8,1280]{1,0:T(8,128)S(1)}, f32[8,1280]{1,0:T(8,128)S(1)}, u32[]{:S(2)}, u32[]{:S(2)}) collective-permute-start(f32[8,1280]{1,0:T(8,128)S(1)} %get-tuple-element.148), channel_id=1, source_target_pairs={{0,224},{32,0},{64,32},{96,64},{128,96},{160,128},{192,160},{224,1... | collective-permute-start | bytes 122888 | tf_op jit(solution)/shard_map/ppermute | solution.py:90
  223.0 2.2 collective-permute-start.30
  226.3 4.0 %collective-permute-start.28 = (f32[8,1280]{1,0:T(8,128)S(1)}, f32[8,1280]{1,0:T(8,128)S(1)}, u32[]{:S(2)}, u32[]{:S(2)}) collective-permute-start(f32[8,1280]{1,0:T(8,128)S(1)} %get-tuple-element.151), channel_id=1, source_target_pairs={{0,128},{32,160},{64,192},{96,224},{128,0},{160,32},{192,64},{224,... | collective-permute-start | bytes 122888 | tf_op jit(solution)/shard_map/ppermute | solution.py:90
  230.3 3.5 %collective-permute-start.26 = (f32[8,1280]{1,0:T(8,128)S(1)}, f32[8,1280]{1,0:T(8,128)S(1)}, u32[]{:S(2)}, u32[]{:S(2)}) collective-permute-start(f32[8,1280]{1,0:T(8,128)S(1)} %get-tuple-element.153), channel_id=1, source_target_pairs={{0,64},{32,96},{64,128},{96,160},{128,192},{160,224},{192,0},{224,... | collective-permute-start | bytes 122888 | tf_op jit(solution)/shard_map/ppermute | solution.py:90
  239.8 5.3 %convolution_bitcast_fusion = f32[1,128,2048]{2,1,0:T(8,128)} fusion(bf16[2048,1280]{1,0:T(8,128)(2,1)} %all-gather.2.cloned.1.call-done, bf16[128,128]{0,1:T(8,128)(2,1)S(1)} %fusion.8, bf16[128,128]{0,1:T(8,128)(2,1)S(1)} %fusion.7, bf16[128,1024]{0,1:T(8,128)(2,1)S(1)} %bitcast.229), kind=kOutput, calls=%fused_computation.5 | convolution fusion | flops 672071680 | bytes 6619136 | tf_op jit(solution)/shard_map/dot_general | solution.py:213
  246.8 2.7 %collective-permute-start.34 = (f32[8,1280]{1,0:T(8,128)S(1)}, f32[8,1280]{1,0:T(8,128)S(1)}, u32[]{:S(2)}, u32[]{:S(2)}) collective-permute-start(f32[8,1280]{1,0:T(8,128)S(1)} %get-tuple-element.95), channel_id=1, source_target_pairs={{0,96},{32,128},{64,160},{96,192},{128,224},{160,0},{192,32},{224,... | collective-permute-start | bytes 122888 | tf_op jit(solution)/shard_map/ppermute | solution.py:94
  249.5 2.0 collective-permute-start.35
  251.5 2.5 collective-permute-start.36
  254.0 3.6 %collective-permute-start.37 = (f32[8,1280]{1,0:T(8,128)S(1)}, f32[8,1280]{1,0:T(8,128)S(1)}, u32[]{:S(2)}, u32[]{:S(2)}) collective-permute-start(f32[8,1280]{1,0:T(8,128)S(1)} %get-tuple-element.95), channel_id=1, source_target_pairs={{0,192},{32,224},{64,0},{96,32},{128,64},{160,96},{192,128},{224,1... | collective-permute-start | bytes 122888 | tf_op jit(solution)/shard_map/ppermute | solution.py:94
  259.3 2.4 collective-permute-done.38
  (201 shorter events, 66.0 us)
Async XLA Ops:
  7.2 59.0 %all-gather.2.cloned.1.call-start = ((), (), s32[]{:S(2)}) async-start(), calls=%async_computation | async-start | bytes 5406720 | tf_op jit(solution)/shard_map/all_gather | solution.py:179
  73.2 12.3 %collective-permute-start = (bf16[16,8448]{1,0:T(8,128)(2,1)S(1)}, bf16[16,8448]{1,0:T(8,128)(2,1)S(1)}, u32[]{:S(2)}, u32[]{:S(2)}) collective-permute-start(bf16[16,8448]{1,0:T(8,128)(2,1)S(1)} %get-tuple-element.162), channel_id=1, source_target_pairs={{1,0},{2,1},{3,2},{4,3},{5,4},{6,5},{7,6},{8,7},{9,8},{10,9},{11,1... | collective-permute-start | bytes 811016 | tf_op jit(solution)/shard_map/ppermute | solution.py:15
  77.6 9.7 %collective-permute-start.1 = (bf16[16,8448]{1,0:T(8,128)(2,1)S(1)}, bf16[16,8448]{1,0:T(8,128)(2,1)S(1)}, u32[]{:S(2)}, u32[]{:S(2)}) collective-permute-start(bf16[16,8448]{1,0:T(8,128)(2,1)S(1)} %get-tuple-element.162), channel_id=1, source_target_pairs={{2,0},{3,1},{4,2},{5,3},{6,4},{7,5},{8,6},{9,7},{10,8},{11,9},{12,... | collective-permute-start | bytes 811016 | tf_op jit(solution)/shard_map/ppermute | solution.py:15
  79.8 14.7 %collective-permute-start.6 = (bf16[16,8448]{1,0:T(8,128)(2,1)S(1)}, bf16[16,8448]{1,0:T(8,128)(2,1)S(1)}, u32[]{:S(2)}, u32[]{:S(2)}) collective-permute-start(bf16[16,8448]{1,0:T(8,128)(2,1)S(1)} %get-tuple-element.163), channel_id=1, source_target_pairs={{0,1},{1,2},{2,3},{3,4},{4,5},{5,6},{6,7},{7,8},{8,9},{9,10},{10,1... | collective-permute-start | bytes 811016 | tf_op jit(solution)/shard_map/ppermute | solution.py:15
  81.9 13.0 %collective-permute-start.7 = (bf16[16,8448]{1,0:T(8,128)(2,1)S(1)}, bf16[16,8448]{1,0:T(8,128)(2,1)S(1)}, u32[]{:S(2)}, u32[]{:S(2)}) collective-permute-start(bf16[16,8448]{1,0:T(8,128)(2,1)S(1)} %get-tuple-element.163), channel_id=1, source_target_pairs={{0,2},{1,3},{2,4},{3,5},{4,6},{5,7},{6,8},{7,9},{8,10},{9,11},{10,... | collective-permute-start | bytes 811016 | tf_op jit(solution)/shard_map/ppermute | solution.py:15
  87.9 11.3 %collective-permute-start.2 = (bf16[16,8448]{1,0:T(8,128)(2,1)S(1)}, bf16[16,8448]{1,0:T(8,128)(2,1)S(1)}, u32[]{:S(2)}, u32[]{:S(2)}) collective-permute-start(bf16[16,8448]{1,0:T(8,128)(2,1)S(1)} %pad_maximum_fusion.5), channel_id=1, source_target_pairs={{2,0},{3,1},{4,2},{5,3},{6,4},{7,5},{8,6},{9,7},{10,8},{11,9},{12,... | collective-permute-start | bytes 811016 | tf_op jit(solution)/shard_map/ppermute | solution.py:15
  95.5 18.5 %collective-permute-start.8 = (bf16[16,8448]{1,0:T(8,128)(2,1)S(1)}, bf16[16,8448]{1,0:T(8,128)(2,1)S(1)}, u32[]{:S(2)}, u32[]{:S(2)}) collective-permute-start(bf16[16,8448]{1,0:T(8,128)(2,1)S(1)} %pad_maximum_fusion.9), channel_id=1, source_target_pairs={{0,2},{1,3},{2,4},{3,5},{4,6},{5,7},{6,8},{7,9},{8,10},{9,11},{10,... | collective-permute-start | bytes 811016 | tf_op jit(solution)/shard_map/ppermute | solution.py:15
  99.8 16.9 %collective-permute-start.3 = (bf16[16,8448]{1,0:T(8,128)(2,1)S(1)}, bf16[16,8448]{1,0:T(8,128)(2,1)S(1)}, u32[]{:S(2)}, u32[]{:S(2)}) collective-permute-start(bf16[16,8448]{1,0:T(8,128)(2,1)S(1)} %pad_maximum_fusion.6), channel_id=1, source_target_pairs={{4,0},{5,1},{6,2},{7,3},{8,4},{9,5},{10,6},{11,7},{12,8},{13,9},{1... | collective-permute-start | bytes 811016 | tf_op jit(solution)/shard_map/ppermute | solution.py:15
  114.6 12.4 %collective-permute-start.9 = (bf16[16,8448]{1,0:T(8,128)(2,1)S(1)}, bf16[16,8448]{1,0:T(8,128)(2,1)S(1)}, u32[]{:S(2)}, u32[]{:S(2)}) collective-permute-start(bf16[16,8448]{1,0:T(8,128)(2,1)S(1)} %pad_maximum_fusion.10), channel_id=1, source_target_pairs={{0,4},{1,5},{2,6},{3,7},{4,8},{5,9},{6,10},{7,11},{8,12},{9,13},{1... | collective-permute-start | bytes 811016 | tf_op jit(solution)/shard_map/ppermute | solution.py:15
  117.3 14.4 %collective-permute-start.4 = (bf16[16,8448]{1,0:T(8,128)(2,1)S(1)}, bf16[16,8448]{1,0:T(8,128)(2,1)S(1)}, u32[]{:S(2)}, u32[]{:S(2)}) collective-permute-start(bf16[16,8448]{1,0:T(8,128)(2,1)S(1)} %pad_maximum_fusion.7), channel_id=1, source_target_pairs={{8,0},{9,1},{10,2},{11,3},{12,4},{13,5},{14,6},{15,7},{16,8},{17,9... | collective-permute-start | bytes 811016 | tf_op jit(solution)/shard_map/ppermute | solution.py:15
  127.6 8.9 %collective-permute-start.10 = (bf16[16,8448]{1,0:T(8,128)(2,1)S(1)}, bf16[16,8448]{1,0:T(8,128)(2,1)S(1)}, u32[]{:S(2)}, u32[]{:S(2)}) collective-permute-start(bf16[16,8448]{1,0:T(8,128)(2,1)S(1)} %pad_maximum_fusion.11), channel_id=1, source_target_pairs={{0,8},{1,9},{2,10},{3,11},{4,12},{5,13},{6,14},{7,15},{8,16},{9,17... | collective-permute-start | bytes 811016 | tf_op jit(solution)/shard_map/ppermute | solution.py:15
  141.4 10.2 %collective-permute-start.5 = (bf16[16,8448]{1,0:T(8,128)(2,1)}, bf16[16,8448]{1,0:T(8,128)(2,1)}, u32[]{:S(2)}, u32[]{:S(2)}) collective-permute-start(bf16[16,8448]{1,0:T(8,128)(2,1)} %pad_maximum_fusion.8), channel_id=1, source_target_pairs={{16,0},{17,1},{18,2},{19,3},{20,4},{21,5},{22,6},{23,7},{24,8},{25... | collective-permute-start | bytes 811016 | tf_op jit(solution)/shard_map/ppermute | solution.py:15
  182.0 17.0 %collective-permute-start.21 = (bf16[4,64,640]{2,1,0:T(8,128)(2,1)}, bf16[4,64,640]{2,1,0:T(8,128)(2,1)S(1)}, u32[]{:S(2)}, u32[]{:S(2)}) collective-permute-start(bf16[4,64,640]{2,1,0:T(8,128)(2,1)} %get-tuple-element.137), channel_id=1, source_target_pairs={{0,24},{1,25},{2,26},{3,27},{4,28},{5,29},{6,30},{7,31},{8,0},{9,1... | collective-permute-start | bytes 983048 | tf_op jit(solution)/shard_map/ppermute | solution.py:63
  183.2 15.8 %collective-permute-start.20 = (bf16[4,64,640]{2,1,0:T(8,128)(2,1)}, bf16[4,64,640]{2,1,0:T(8,128)(2,1)}, u32[]{:S(2)}, u32[]{:S(2)}) collective-permute-start(bf16[4,64,640]{2,1,0:T(8,128)(2,1)} %get-tuple-element.138), channel_id=1, source_target_pairs={{0,16},{1,17},{2,18},{3,19},{4,20},{5,21},{6,22},{7,23},{8,24},{9,... | collective-permute-start | bytes 983048 | tf_op jit(solution)/shard_map/ppermute | solution.py:63
  183.2 17.7 %collective-permute-start.19 = (bf16[4,64,640]{2,1,0:T(8,128)(2,1)}, bf16[4,64,640]{2,1,0:T(8,128)(2,1)}, u32[]{:S(2)}, u32[]{:S(2)}) collective-permute-start(bf16[4,64,640]{2,1,0:T(8,128)(2,1)} %get-tuple-element.136), channel_id=1, source_target_pairs={{0,8},{1,9},{2,10},{3,11},{4,12},{5,13},{6,14},{7,15},{8,16},{9,17... | collective-permute-start | bytes 983048 | tf_op jit(solution)/shard_map/ppermute | solution.py:63
  184.8 19.0 %collective-permute-start.15 = (bf16[4,64,640]{2,1,0:T(8,128)(2,1)S(1)}, bf16[4,64,640]{2,1,0:T(8,128)(2,1)S(1)}, u32[]{:S(2)}, u32[]{:S(2)}) collective-permute-start(bf16[4,64,640]{2,1,0:T(8,128)(2,1)S(1)} %get-tuple-element.135), channel_id=1, source_target_pairs={{0,6},{1,7},{2,0},{3,1},{4,2},{5,3},{6,4},{7,5},{8,14},{9,15},{10,... | collective-permute-start | bytes 983048 | tf_op jit(solution)/shard_map/ppermute | solution.py:63
  184.9 19.8 %collective-permute-start.14 = (bf16[4,64,640]{2,1,0:T(8,128)(2,1)S(1)}, bf16[4,64,640]{2,1,0:T(8,128)(2,1)S(1)}, u32[]{:S(2)}, u32[]{:S(2)}) collective-permute-start(bf16[4,64,640]{2,1,0:T(8,128)(2,1)S(1)} %get-tuple-element.134), channel_id=1, source_target_pairs={{0,4},{1,5},{2,6},{3,7},{4,0},{5,1},{6,2},{7,3},{8,12},{9,13},{10,... | collective-permute-start | bytes 983048 | tf_op jit(solution)/shard_map/ppermute | solution.py:63
  198.9 12.9 %collective-permute-start.13 = (bf16[4,64,640]{2,1,0:T(8,128)(2,1)S(1)}, bf16[4,64,640]{2,1,0:T(8,128)(2,1)S(1)}, u32[]{:S(2)}, u32[]{:S(2)}) collective-permute-start(bf16[4,64,640]{2,1,0:T(8,128)(2,1)S(1)} %get-tuple-element.133), channel_id=1, source_target_pairs={{0,2},{1,3},{2,4},{3,5},{4,6},{5,7},{6,0},{7,1},{8,10},{9,11},{10,... | collective-permute-start | bytes 983048 | tf_op jit(solution)/shard_map/ppermute | solution.py:63
  202.3 10.7 %collective-permute-start.24 = (bf16[64,640]{1,0:T(8,128)(2,1)S(1)}, bf16[64,640]{1,0:T(8,128)(2,1)S(1)}, u32[]{:S(2)}, u32[]{:S(2)}) collective-permute-start(bf16[64,640]{1,0:T(8,128)(2,1)S(1)} %get-tuple-element.143), channel_id=1, source_target_pairs={{0,6},{1,7},{2,0},{3,1},{4,2},{5,3},{6,4},{7,5},{8,14},{9,15},{10,... | collective-permute-start | bytes 245768 | tf_op jit(solution)/shard_map/ppermute | solution.py:63
  203.7 10.4 %collective-permute-start.23 = (bf16[64,640]{1,0:T(8,128)(2,1)S(1)}, bf16[64,640]{1,0:T(8,128)(2,1)S(1)}, u32[]{:S(2)}, u32[]{:S(2)}) collective-permute-start(bf16[64,640]{1,0:T(8,128)(2,1)S(1)} %get-tuple-element.144), channel_id=1, source_target_pairs={{0,4},{1,5},{2,6},{3,7},{4,0},{5,1},{6,2},{7,3},{8,12},{9,13},{10,... | collective-permute-start | bytes 245768 | tf_op jit(solution)/shard_map/ppermute | solution.py:63
  203.7 10.4 %collective-permute-start.22 = (bf16[64,640]{1,0:T(8,128)(2,1)S(1)}, bf16[64,640]{1,0:T(8,128)(2,1)S(1)}, u32[]{:S(2)}, u32[]{:S(2)}) collective-permute-start(bf16[64,640]{1,0:T(8,128)(2,1)S(1)} %get-tuple-element.142), channel_id=1, source_target_pairs={{0,2},{1,3},{2,4},{3,5},{4,6},{5,7},{6,0},{7,1},{8,10},{9,11},{10,... | collective-permute-start | bytes 245768 | tf_op jit(solution)/shard_map/ppermute | solution.py:63
  219.6 10.7 %collective-permute-start.31 = (f32[8,1280]{1,0:T(8,128)S(1)}, f32[8,1280]{1,0:T(8,128)S(1)}, u32[]{:S(2)}, u32[]{:S(2)}) collective-permute-start(f32[8,1280]{1,0:T(8,128)S(1)} %get-tuple-element.148), channel_id=1, source_target_pairs={{0,224},{32,0},{64,32},{96,64},{128,96},{160,128},{192,160},{224,1... | collective-permute-start | bytes 122888 | tf_op jit(solution)/shard_map/ppermute | solution.py:90
  223.0 10.9 %collective-permute-start.30 = (f32[8,1280]{1,0:T(8,128)S(1)}, f32[8,1280]{1,0:T(8,128)S(1)}, u32[]{:S(2)}, u32[]{:S(2)}) collective-permute-start(f32[8,1280]{1,0:T(8,128)S(1)} %get-tuple-element.149), channel_id=1, source_target_pairs={{0,192},{32,224},{64,0},{96,32},{128,64},{160,96},{192,128},{224,1... | collective-permute-start | bytes 122888 | tf_op jit(solution)/shard_map/ppermute | solution.py:90
  225.1 10.4 %collective-permute-start.29 = (f32[8,1280]{1,0:T(8,128)S(1)}, f32[8,1280]{1,0:T(8,128)S(1)}, u32[]{:S(2)}, u32[]{:S(2)}) collective-permute-start(f32[8,1280]{1,0:T(8,128)S(1)} %get-tuple-element.150), channel_id=1, source_target_pairs={{0,160},{32,192},{64,224},{96,0},{128,32},{160,64},{192,96},{224,1... | collective-permute-start | bytes 122888 | tf_op jit(solution)/shard_map/ppermute | solution.py:90
  226.3 9.3 %collective-permute-start.28 = (f32[8,1280]{1,0:T(8,128)S(1)}, f32[8,1280]{1,0:T(8,128)S(1)}, u32[]{:S(2)}, u32[]{:S(2)}) collective-permute-start(f32[8,1280]{1,0:T(8,128)S(1)} %get-tuple-element.151), channel_id=1, source_target_pairs={{0,128},{32,160},{64,192},{96,224},{128,0},{160,32},{192,64},{224,... | collective-permute-start | bytes 122888 | tf_op jit(solution)/shard_map/ppermute | solution.py:90
  230.3 7.2 %collective-permute-start.27 = (f32[8,1280]{1,0:T(8,128)S(1)}, f32[8,1280]{1,0:T(8,128)S(1)}, u32[]{:S(2)}, u32[]{:S(2)}) collective-permute-start(f32[8,1280]{1,0:T(8,128)S(1)} %get-tuple-element.152), channel_id=1, source_target_pairs={{0,96},{32,128},{64,160},{96,192},{128,224},{160,0},{192,32},{224,... | collective-permute-start | bytes 122888 | tf_op jit(solution)/shard_map/ppermute | solution.py:90
  230.3 7.9 %collective-permute-start.26 = (f32[8,1280]{1,0:T(8,128)S(1)}, f32[8,1280]{1,0:T(8,128)S(1)}, u32[]{:S(2)}, u32[]{:S(2)}) collective-permute-start(f32[8,1280]{1,0:T(8,128)S(1)} %get-tuple-element.153), channel_id=1, source_target_pairs={{0,64},{32,96},{64,128},{96,160},{128,192},{160,224},{192,0},{224,... | collective-permute-start | bytes 122888 | tf_op jit(solution)/shard_map/ppermute | solution.py:90
  239.1 14.9 %collective-permute-start.32 = (f32[8,1280]{1,0:T(8,128)S(1)}, f32[8,1280]{1,0:T(8,128)S(1)}, u32[]{:S(2)}, u32[]{:S(2)}) collective-permute-start(f32[8,1280]{1,0:T(8,128)S(1)} %get-tuple-element.95), channel_id=1, source_target_pairs={{0,32},{32,64},{64,96},{96,128},{128,160},{160,192},{192,224},{224... | collective-permute-start | bytes 122888 | tf_op jit(solution)/shard_map/ppermute | solution.py:94
  245.1 12.5 %collective-permute-start.33 = (f32[8,1280]{1,0:T(8,128)S(1)}, f32[8,1280]{1,0:T(8,128)S(1)}, u32[]{:S(2)}, u32[]{:S(2)}) collective-permute-start(f32[8,1280]{1,0:T(8,128)S(1)} %get-tuple-element.95), channel_id=1, source_target_pairs={{0,64},{32,96},{64,128},{96,160},{128,192},{160,224},{192,0},{224,... | collective-permute-start | bytes 122888 | tf_op jit(solution)/shard_map/ppermute | solution.py:94
  246.8 12.0 %collective-permute-start.34 = (f32[8,1280]{1,0:T(8,128)S(1)}, f32[8,1280]{1,0:T(8,128)S(1)}, u32[]{:S(2)}, u32[]{:S(2)}) collective-permute-start(f32[8,1280]{1,0:T(8,128)S(1)} %get-tuple-element.95), channel_id=1, source_target_pairs={{0,96},{32,128},{64,160},{96,192},{128,224},{160,0},{192,32},{224,... | collective-permute-start | bytes 122888 | tf_op jit(solution)/shard_map/ppermute | solution.py:94
  249.5 9.3 %collective-permute-start.35 = (f32[8,1280]{1,0:T(8,128)S(1)}, f32[8,1280]{1,0:T(8,128)S(1)}, u32[]{:S(2)}, u32[]{:S(2)}) collective-permute-start(f32[8,1280]{1,0:T(8,128)S(1)} %get-tuple-element.95), channel_id=1, source_target_pairs={{0,128},{32,160},{64,192},{96,224},{128,0},{160,32},{192,64},{224,... | collective-permute-start | bytes 122888 | tf_op jit(solution)/shard_map/ppermute | solution.py:94
  251.5 7.3 %collective-permute-start.36 = (f32[8,1280]{1,0:T(8,128)S(1)}, f32[8,1280]{1,0:T(8,128)S(1)}, u32[]{:S(2)}, u32[]{:S(2)}) collective-permute-start(f32[8,1280]{1,0:T(8,128)S(1)} %get-tuple-element.95), channel_id=1, source_target_pairs={{0,160},{32,192},{64,224},{96,0},{128,32},{160,64},{192,96},{224,1... | collective-permute-start | bytes 122888 | tf_op jit(solution)/shard_map/ppermute | solution.py:94
  (21 other events, 493.1 us)
Sparse Core Ops, SparseCore 0:
  11.1 54.9 all-gather.1

commit v6 on v5

--- a/solution.py
+++ b/solution.py
@@ -19,24 +19,32 @@
     head_count = state.shape[0]
     flat = state.reshape(head_count, -1)
     split = flat.shape[1]
-
-    def send(flat, decay, step):
+    count = lax.axis_size(axis)
+
+    def send(part, step):
+        flat, decay = part
         high = lax.reduce_precision(decay, exponent_bits=8, mantissa_bits=7)
-        lanes = lambda part: jnp.broadcast_to(part[:, None], (head_count, 128))
+        lanes = lambda piece: jnp.broadcast_to(piece[:, None], (head_count, 128))
         packed = jnp.concatenate([flat, lanes(high), lanes(decay - high)], axis=1)
         got = shifted(packed, axis, step, reverse)
         return got[:, :split], got[:, split] + got[:, split + 128]
 
-    nearer_flat, nearer_decay = send(flat, decay, 1)
-    farther_flat, farther_decay = send(flat, decay, 2)
-    flat = nearer_decay[:, None] * farther_flat + nearer_flat
-    decay = farther_decay * nearer_decay
-    step = 2
-    while step < lax.axis_size(axis):
-        earlier_flat, earlier_decay = send(flat, decay, step)
-        flat = decay[:, None] * earlier_flat + flat
-        decay = earlier_decay * decay
-        step *= 2
+    def chain(parts):
+        flat, decay = parts[0]
+        for later_flat, later_decay in parts[1:]:
+            flat = later_decay[:, None] * flat + later_flat
+            decay = decay * later_decay
+        return flat, decay
+
+    radix = 4
+    own = (flat, decay)
+    part = chain([send(own, step) for step in range(radix, 0, -1)])
+    width = radix
+    while width < count:
+        pieces = min(radix, -(-count // width))
+        part = chain([send(part, width * m) for m in range(pieces - 1, 0, -1)] + [part])
+        width *= pieces
+    flat = part[0]
     return flat.reshape(state.shape)
 
 

time: 271 us -> 270 us (level)
  starting transfers between devices: 73.4 us -> 104 us
  waiting for transfers between devices: 125 us -> 94.6 us
    ppermute x12 -> x16, waiting for transfers between devices: 34.5 us -> 15.4 us  [shifted(): lax.ppermute(value.astype(jnp.bfloat16), axis, pairs).astype(value.dtype)]
    ppermute x13, starting transfers between devices: 7.4 us -> 24.1 us  [digit_reduce(): got = lax.ppermute(piece.astype(jnp.bfloat16), axis, pairs)]
    ppermute x12 -> x16, starting transfers between devices: 35.8 us -> 50.1 us  [shifted(): lax.ppermute(value.astype(jnp.bfloat16), axis, pairs).astype(value.dtype)]
    ppermute x13, waiting for transfers between devices: 33.3 us -> 22.4 us  [digit_reduce(): got = lax.ppermute(piece.astype(jnp.bfloat16), axis, pairs)]
  transfers between devices with their start and end apart: 40 -> 44, of which waited for: 21 -> 19; matrix products, arithmetic and copies ran while one was open for 7% -> 7% of each run, Pallas kernels for 0% -> 0%
where the time goes in v6:
time: 270 us; the launch traced here: 268 us
  starting transfers between devices  104 us (39%)
  waiting for transfers between devices  94.6 us (35%)
  local copies, waits for them, and re-layouts  19.6 us (7%)
  matrix products  17.2 us (6%)
  other arithmetic  17 us (6%)
  between operations  14.8 us (5%)
    all_gather x1, waiting for transfers between devices, local(): lax.all_gather(dequantize(weight_codes, scales), 'seq', axis=0, tiled=True)  50.4 us
    ppermute x16, starting transfers between devices, shifted(): lax.ppermute(value.astype(jnp.bfloat16), axis, pairs).astype(value.dtype)  50.1 us
    ppermute x13, starting transfers between devices, digit_reduce(): got = lax.ppermute(piece.astype(jnp.bfloat16), axis, pairs)  24.1 us
    ppermute x13, waiting for transfers between devices, digit_reduce(): got = lax.ppermute(piece.astype(jnp.bfloat16), axis, pairs)  22.4 us
    ppermute x7, starting transfers between devices, replicated_sum(): total = total + lax.ppermute(piece, axis, pairs)  15.8 us
    ppermute x16, waiting for transfers between devices, shifted(): lax.ppermute(value.astype(jnp.bfloat16), axis, pairs).astype(value.dtype)  15.4 us
    ppermute x7, starting transfers between devices, replicated_sum(): gathered.append(lax.ppermute(total, axis, pairs))  14.4 us
    convert_element_type x1, local copies, waits for them, and re-layouts, local(): partial_grad = seq_reduce_scatter(lax.dot_general(features, d_proj, (((0,...  7.87 us
  transfers between devices with their start and end apart: 44, of which 19 were waited for; matrix products, arithmetic and copies ran while one was open for 7% of the time, Pallas kernels for 0%

profile of v6, /device:TPU:8, one launch (start us, length us, event | category | flops | bytes accessed | tf_op | source)
XLA Modules:
  0.0 267.7 jit_solution(5589358289186387737)
XLA Ops:
  15.7 50.4 %all-gather.2.cloned.1.call-done = bf16[2048,1280]{1,0:T(8,128)(2,1)} async-done(((bf16[64,1280]{1,0:T(8,128)(2,1)}), bf16[2048,1280]{1,0:T(8,128)(2,1)}) %all-gather.2.cloned.1.call-update) | async-done | bytes 5242896 | tf_op jit(solution)/shard_map/all_gather | solution.py:187
  66.2 4.1 %fusion.1 = bf16[128,1280]{0,1:T(8,128)(2,1)S(1)} fusion(bf16[2048,1280]{1,0:T(8,128)(2,1)} %all-gather.2.cloned.1.call-done, bf16[1,128,2048]{2,1,0:T(8,128)(2,1)S(1)} %copy-done), kind=kOutput, calls=%fused_computation.7 | convolution fusion | flops 671252480 | bytes 6094848 | tf_op jit(solution)/shard_map/dot_general | solution.py:188
  77.5 3.7 %collective-permute-start.10 = (bf16[16,8448]{1,0:T(8,128)(2,1)S(1)}, bf16[16,8448]{1,0:T(8,128)(2,1)S(1)}, u32[]{:S(2)}, u32[]{:S(2)}) collective-permute-start(bf16[16,8448]{1,0:T(8,128)(2,1)S(1)} %get-tuple-element.155), channel_id=1, source_target_pairs={{0,3},{1,4},{2,5},{3,6},{4,7},{5,8},{6,9},{7,10},{8,11},{9,12},{10... | collective-permute-start | bytes 811016 | tf_op jit(solution)/shard_map/ppermute | solution.py:15
  81.2 4.7 %collective-permute-start.11 = (bf16[16,8448]{1,0:T(8,128)(2,1)S(1)}, bf16[16,8448]{1,0:T(8,128)(2,1)S(1)}, u32[]{:S(2)}, u32[]{:S(2)}) collective-permute-start(bf16[16,8448]{1,0:T(8,128)(2,1)S(1)} %get-tuple-element.155), channel_id=1, source_target_pairs={{0,4},{1,5},{2,6},{3,7},{4,8},{5,9},{6,10},{7,11},{8,12},{9,13},{1... | collective-permute-start | bytes 811016 | tf_op jit(solution)/shard_map/ppermute | solution.py:15
  85.9 4.3 %collective-permute-start = (bf16[16,8448]{1,0:T(8,128)(2,1)S(1)}, bf16[16,8448]{1,0:T(8,128)(2,1)S(1)}, u32[]{:S(2)}, u32[]{:S(2)}) collective-permute-start(bf16[16,8448]{1,0:T(8,128)(2,1)S(1)} %get-tuple-element.154), channel_id=1, source_target_pairs={{1,0},{2,1},{3,2},{4,3},{5,4},{6,5},{7,6},{8,7},{9,8},{10,9},{11,1... | collective-permute-start | bytes 811016 | tf_op jit(solution)/shard_map/ppermute | solution.py:15
  95.7 3.0 %collective-permute-start.3 = (bf16[16,8448]{1,0:T(8,128)(2,1)S(1)}, bf16[16,8448]{1,0:T(8,128)(2,1)S(1)}, u32[]{:S(2)}, u32[]{:S(2)}) collective-permute-start(bf16[16,8448]{1,0:T(8,128)(2,1)S(1)} %get-tuple-element.154), channel_id=1, source_target_pairs={{4,0},{5,1},{6,2},{7,3},{8,4},{9,5},{10,6},{11,7},{12,8},{13,9},{1... | collective-permute-start | bytes 811016 | tf_op jit(solution)/shard_map/ppermute | solution.py:15
  100.9 2.9 %collective-permute-start.14 = (bf16[16,8448]{1,0:T(8,128)(2,1)S(1)}, bf16[16,8448]{1,0:T(8,128)(2,1)S(1)}, u32[]{:S(2)}, u32[]{:S(2)}) collective-permute-start(bf16[16,8448]{1,0:T(8,128)(2,1)S(1)} %pad_maximum_fusion.7), channel_id=1, source_target_pairs={{0,4},{1,5},{2,6},{3,7},{4,8},{5,9},{6,10},{7,11},{8,12},{9,13},{1... | collective-permute-start | bytes 811016 | tf_op jit(solution)/shard_map/ppermute | solution.py:15
  103.8 3.9 %collective-permute-start.13 = (bf16[16,8448]{1,0:T(8,128)(2,1)S(1)}, bf16[16,8448]{1,0:T(8,128)(2,1)S(1)}, u32[]{:S(2)}, u32[]{:S(2)}) collective-permute-start(bf16[16,8448]{1,0:T(8,128)(2,1)S(1)} %pad_maximum_fusion.7), channel_id=1, source_target_pairs={{0,8},{1,9},{2,10},{3,11},{4,12},{5,13},{6,14},{7,15},{8,16},{9,17... | collective-permute-start | bytes 811016 | tf_op jit(solution)/shard_map/ppermute | solution.py:15
  107.8 5.6 %collective-permute-start.12 = (bf16[16,8448]{1,0:T(8,128)(2,1)S(1)}, bf16[16,8448]{1,0:T(8,128)(2,1)S(1)}, u32[]{:S(2)}, u32[]{:S(2)}) collective-permute-start(bf16[16,8448]{1,0:T(8,128)(2,1)S(1)} %pad_maximum_fusion.7), channel_id=1, source_target_pairs={{0,12},{1,13},{2,14},{3,15},{4,16},{5,17},{6,18},{7,19},{8,20},{9,... | collective-permute-start | bytes 811016 | tf_op jit(solution)/shard_map/ppermute | solution.py:15
  114.2 4.0 %collective-permute-start.6 = (bf16[16,8448]{1,0:T(8,128)(2,1)S(1)}, bf16[16,8448]{1,0:T(8,128)(2,1)S(1)}, u32[]{:S(2)}, u32[]{:S(2)}) collective-permute-start(bf16[16,8448]{1,0:T(8,128)(2,1)S(1)} %pad_maximum_fusion.5), channel_id=1, source_target_pairs={{4,0},{5,1},{6,2},{7,3},{8,4},{9,5},{10,6},{11,7},{12,8},{13,9},{1... | collective-permute-start | bytes 811016 | tf_op jit(solution)/shard_map/ppermute | solution.py:15
  121.5 4.2 %collective-permute-done.13 = bf16[16,8448]{1,0:T(8,128)(2,1)S(1)} collective-permute-done((bf16[16,8448]{1,0:T(8,128)(2,1)S(1)}, bf16[16,8448]{1,0:T(8,128)(2,1)S(1)}, u32[]{:S(2)}, u32[]{:S(2)}) %collective-permute-start.13) | collective-permute-done | bytes 270368 | tf_op jit(solution)/shard_map/ppermute | solution.py:15
  126.4 4.9 %collective-permute-start.15 = (bf16[16,8448]{1,0:T(8,128)(2,1)S(1)}, bf16[16,8448]{1,0:T(8,128)(2,1)S(1)}, u32[]{:S(2)}, u32[]{:S(2)}) collective-permute-start(bf16[16,8448]{1,0:T(8,128)(2,1)S(1)} %pad_maximum_fusion.8), channel_id=1, source_target_pairs={{0,16},{1,17},{2,18},{3,19},{4,20},{5,21},{6,22},{7,23},{8,24},{9,... | collective-permute-start | bytes 811016 | tf_op jit(solution)/shard_map/ppermute | solution.py:15
  135.1 3.2 %collective-permute-done.15 = bf16[16,8448]{1,0:T(8,128)(2,1)S(1)} collective-permute-done((bf16[16,8448]{1,0:T(8,128)(2,1)S(1)}, bf16[16,8448]{1,0:T(8,128)(2,1)S(1)}, u32[]{:S(2)}, u32[]{:S(2)}) %collective-permute-start.15) | collective-permute-done | bytes 270368 | tf_op jit(solution)/shard_map/ppermute | solution.py:15
  139.0 5.8 %collective-permute-done.7 = bf16[16,8448]{1,0:T(8,128)(2,1)} collective-permute-done((bf16[16,8448]{1,0:T(8,128)(2,1)}, bf16[16,8448]{1,0:T(8,128)(2,1)}, u32[]{:S(2)}, u32[]{:S(2)}) %collective-permute-start.7) | collective-permute-done | bytes 270368 | tf_op jit(solution)/shard_map/ppermute | solution.py:15
  149.0 3.9 %fusion = bf16[2048,1280]{0,1:T(8,128)(2,1)} fusion(bf16[1,128,2048]{2,1,0:T(8,128)(2,1)S(1)} %copy-done, bf16[128,128]{0,1:T(8,128)(2,1)S(1)} %fusion.8, bf16[128,128]{0,1:T(8,128)(2,1)S(1)} %fusion.7, bf16[128,1024]{0,1:T(8,128)(2,1)S(1)} %bitcast.227), kind=kOutput, calls=%fused_computation.2 | convolution fusion | flops 674693120 | bytes 6094848 | tf_op jit(solution)/shard_map/dot_general | solution.py:228
  152.9 7.9 %copy.68 = bf16[2048,1280]{1,0:T(8,128)(2,1)} copy(bf16[2048,1280]{0,1:T(8,128)(2,1)} %fusion) | data formatting | bytes 10485760 | tf_op jit(solution)/shard_map/convert_element_type | solution.py:230
  164.5 4.7 %collective-permute-done.16 = bf16[4,4,64,1280]{3,2,1,0:T(8,128)(2,1)} collective-permute-done((bf16[4,4,64,1280]{3,2,1,0:T(8,128)(2,1)S(1)}, bf16[4,4,64,1280]{3,2,1,0:T(8,128)(2,1)}, u32[]{:S(2)}, u32[]{:S(2)}) %collective-permute-start.16) | collective-permute-done | bytes 2621472 | tf_op jit(solution)/shard_map/ppermute | solution.py:71
  169.2 3.2 %convert_add_fusion = f32[4,4,64,1280]{3,2,1,0:T(8,128)S(1)} fusion(bf16[4,4,64,1280]{3,2,1,0:T(8,128)(2,1)} %collective-permute-done.16, bf16[4,4,2,64,1280]{4,3,2,1,0:T(8,128)(2,1)} %bitcast.225, s32[]{:T(128)S(6)} %select_n.216), kind=kLoop, calls=%fused_computation.3 | loop fusion | flops 3932160 | bytes 10485764 | tf_op jit(solution)/shard_map/add | solution.py:72
  175.4 2.7 %collective-permute-start.25 = (bf16[4,64,640]{2,1,0:T(8,128)(2,1)}, bf16[4,64,640]{2,1,0:T(8,128)(2,1)S(1)}, u32[]{:S(2)}, u32[]{:S(2)}) collective-permute-start(bf16[4,64,640]{2,1,0:T(8,128)(2,1)} %get-tuple-element.121), channel_id=1, source_target_pairs={{0,24},{1,25},{2,26},{3,27},{4,28},{5,29},{6,30},{7,31},{8,0},{9,1... | collective-permute-start | bytes 983048 | tf_op jit(solution)/shard_map/ppermute | solution.py:71
  179.7 6.2 %collective-permute-start.19 = (bf16[4,64,640]{2,1,0:T(8,128)(2,1)S(1)}, bf16[4,64,640]{2,1,0:T(8,128)(2,1)S(1)}, u32[]{:S(2)}, u32[]{:S(2)}) collective-permute-start(bf16[4,64,640]{2,1,0:T(8,128)(2,1)S(1)} %get-tuple-element.119), channel_id=1, source_target_pairs={{0,6},{1,7},{2,0},{3,1},{4,2},{5,3},{6,4},{7,5},{8,14},{9,15},{10,... | collective-permute-start | bytes 983048 | tf_op jit(solution)/shard_map/ppermute | solution.py:71
  186.2 6.4 %collective-permute-done.25 = bf16[4,64,640]{2,1,0:T(8,128)(2,1)S(1)} collective-permute-done((bf16[4,64,640]{2,1,0:T(8,128)(2,1)}, bf16[4,64,640]{2,1,0:T(8,128)(2,1)S(1)}, u32[]{:S(2)}, u32[]{:S(2)}) %collective-permute-start.25) | collective-permute-done | bytes 327712 | tf_op jit(solution)/shard_map/ppermute | solution.py:71
  196.0 8.0 %collective-permute-start.28 = (bf16[64,640]{1,0:T(8,128)(2,1)S(1)}, bf16[64,640]{1,0:T(8,128)(2,1)S(1)}, u32[]{:S(2)}, u32[]{:S(2)}) collective-permute-start(bf16[64,640]{1,0:T(8,128)(2,1)S(1)} %get-tuple-element.127), channel_id=1, source_target_pairs={{0,6},{1,7},{2,0},{3,1},{4,2},{5,3},{6,4},{7,5},{8,14},{9,15},{10,... | collective-permute-start | bytes 245768 | tf_op jit(solution)/shard_map/ppermute | solution.py:71
  205.5 4.1 %collective-permute-done.17 = bf16[4,64,640]{2,1,0:T(8,128)(2,1)S(1)} collective-permute-done((bf16[4,64,640]{2,1,0:T(8,128)(2,1)S(1)}, bf16[4,64,640]{2,1,0:T(8,128)(2,1)S(1)}, u32[]{:S(2)}, u32[]{:S(2)}) %collective-permute-start.17) | collective-permute-done | bytes 327712 | tf_op jit(solution)/shard_map/ppermute | solution.py:71
  211.9 2.3 collective-permute-done.22
  217.3 3.4 %collective-permute-start.35 = (f32[8,1280]{1,0:T(8,128)S(1)}, f32[8,1280]{1,0:T(8,128)S(1)}, u32[]{:S(2)}, u32[]{:S(2)}) collective-permute-start(f32[8,1280]{1,0:T(8,128)S(1)} %get-tuple-element.140), channel_id=1, source_target_pairs={{0,224},{32,0},{64,32},{96,64},{128,96},{160,128},{192,160},{224,1... | collective-permute-start | bytes 122888 | tf_op jit(solution)/shard_map/ppermute | solution.py:98
  224.0 4.0 %collective-permute-start.32 = (f32[8,1280]{1,0:T(8,128)S(1)}, f32[8,1280]{1,0:T(8,128)S(1)}, u32[]{:S(2)}, u32[]{:S(2)}) collective-permute-start(f32[8,1280]{1,0:T(8,128)S(1)} %get-tuple-element.143), channel_id=1, source_target_pairs={{0,128},{32,160},{64,192},{96,224},{128,0},{160,32},{192,64},{224,... | collective-permute-start | bytes 122888 | tf_op jit(solution)/shard_map/ppermute | solution.py:98
  228.0 3.5 %collective-permute-start.30 = (f32[8,1280]{1,0:T(8,128)S(1)}, f32[8,1280]{1,0:T(8,128)S(1)}, u32[]{:S(2)}, u32[]{:S(2)}) collective-permute-start(f32[8,1280]{1,0:T(8,128)S(1)} %get-tuple-element.145), channel_id=1, source_target_pairs={{0,64},{32,96},{64,128},{96,160},{128,192},{160,224},{192,0},{224,... | collective-permute-start | bytes 122888 | tf_op jit(solution)/shard_map/ppermute | solution.py:98
  237.6 5.3 %convolution_bitcast_fusion = f32[1,128,2048]{2,1,0:T(8,128)} fusion(bf16[2048,1280]{1,0:T(8,128)(2,1)} %all-gather.2.cloned.1.call-done, bf16[128,128]{0,1:T(8,128)(2,1)S(1)} %fusion.8, bf16[128,128]{0,1:T(8,128)(2,1)S(1)} %fusion.7, bf16[128,1024]{0,1:T(8,128)(2,1)S(1)} %bitcast.228), kind=kOutput, calls=%fused_computation.5 | convolution fusion | flops 672071680 | bytes 6619136 | tf_op jit(solution)/shard_map/dot_general | solution.py:221
  246.6 2.6 collective-permute-start.39
  249.2 2.3 collective-permute-start.40
  251.5 3.9 %collective-permute-start.41 = (f32[8,1280]{1,0:T(8,128)S(1)}, f32[8,1280]{1,0:T(8,128)S(1)}, u32[]{:S(2)}, u32[]{:S(2)}) collective-permute-start(f32[8,1280]{1,0:T(8,128)S(1)} %get-tuple-element.76), channel_id=1, source_target_pairs={{0,192},{32,224},{64,0},{96,32},{128,64},{160,96},{192,128},{224,1... | collective-permute-start | bytes 122888 | tf_op jit(solution)/shard_map/ppermute | solution.py:102
  257.1 2.4 collective-permute-done.42
  (179 shorter events, 71.6 us)
Async XLA Ops:
  7.2 59.0 %all-gather.2.cloned.1.call-start = ((), (), s32[]{:S(2)}) async-start(), calls=%async_computation | async-start | bytes 5406720 | tf_op jit(solution)/shard_map/all_gather | solution.py:187
  73.2 18.2 %collective-permute-start.8 = (bf16[16,8448]{1,0:T(8,128)(2,1)S(1)}, bf16[16,8448]{1,0:T(8,128)(2,1)S(1)}, u32[]{:S(2)}, u32[]{:S(2)}) collective-permute-start(bf16[16,8448]{1,0:T(8,128)(2,1)S(1)} %get-tuple-element.155), channel_id=1, source_target_pairs={{0,1},{1,2},{2,3},{3,4},{4,5},{5,6},{6,7},{7,8},{8,9},{9,10},{10,1... | collective-permute-start | bytes 811016 | tf_op jit(solution)/shard_map/ppermute | solution.py:15
  75.4 18.3 %collective-permute-start.9 = (bf16[16,8448]{1,0:T(8,128)(2,1)S(1)}, bf16[16,8448]{1,0:T(8,128)(2,1)S(1)}, u32[]{:S(2)}, u32[]{:S(2)}) collective-permute-start(bf16[16,8448]{1,0:T(8,128)(2,1)S(1)} %get-tuple-element.155), channel_id=1, source_target_pairs={{0,2},{1,3},{2,4},{3,5},{4,6},{5,7},{6,8},{7,9},{8,10},{9,11},{10,... | collective-permute-start | bytes 811016 | tf_op jit(solution)/shard_map/ppermute | solution.py:15
  77.5 18.2 %collective-permute-start.10 = (bf16[16,8448]{1,0:T(8,128)(2,1)S(1)}, bf16[16,8448]{1,0:T(8,128)(2,1)S(1)}, u32[]{:S(2)}, u32[]{:S(2)}) collective-permute-start(bf16[16,8448]{1,0:T(8,128)(2,1)S(1)} %get-tuple-element.155), channel_id=1, source_target_pairs={{0,3},{1,4},{2,5},{3,6},{4,7},{5,8},{6,9},{7,10},{8,11},{9,12},{10... | collective-permute-start | bytes 811016 | tf_op jit(solution)/shard_map/ppermute | solution.py:15
  81.2 19.0 %collective-permute-start.11 = (bf16[16,8448]{1,0:T(8,128)(2,1)S(1)}, bf16[16,8448]{1,0:T(8,128)(2,1)S(1)}, u32[]{:S(2)}, u32[]{:S(2)}) collective-permute-start(bf16[16,8448]{1,0:T(8,128)(2,1)S(1)} %get-tuple-element.155), channel_id=1, source_target_pairs={{0,4},{1,5},{2,6},{3,7},{4,8},{5,9},{6,10},{7,11},{8,12},{9,13},{1... | collective-permute-start | bytes 811016 | tf_op jit(solution)/shard_map/ppermute | solution.py:15
  85.9 17.9 %collective-permute-start = (bf16[16,8448]{1,0:T(8,128)(2,1)S(1)}, bf16[16,8448]{1,0:T(8,128)(2,1)S(1)}, u32[]{:S(2)}, u32[]{:S(2)}) collective-permute-start(bf16[16,8448]{1,0:T(8,128)(2,1)S(1)} %get-tuple-element.154), channel_id=1, source_target_pairs={{1,0},{2,1},{3,2},{4,3},{5,4},{6,5},{7,6},{8,7},{9,8},{10,9},{11,1... | collective-permute-start | bytes 811016 | tf_op jit(solution)/shard_map/ppermute | solution.py:15
  91.4 16.4 %collective-permute-start.1 = (bf16[16,8448]{1,0:T(8,128)(2,1)S(1)}, bf16[16,8448]{1,0:T(8,128)(2,1)S(1)}, u32[]{:S(2)}, u32[]{:S(2)}) collective-permute-start(bf16[16,8448]{1,0:T(8,128)(2,1)S(1)} %get-tuple-element.154), channel_id=1, source_target_pairs={{2,0},{3,1},{4,2},{5,3},{6,4},{7,5},{8,6},{9,7},{10,8},{11,9},{12,... | collective-permute-start | bytes 811016 | tf_op jit(solution)/shard_map/ppermute | solution.py:15
  93.7 19.7 %collective-permute-start.2 = (bf16[16,8448]{1,0:T(8,128)(2,1)S(1)}, bf16[16,8448]{1,0:T(8,128)(2,1)S(1)}, u32[]{:S(2)}, u32[]{:S(2)}) collective-permute-start(bf16[16,8448]{1,0:T(8,128)(2,1)S(1)} %get-tuple-element.154), channel_id=1, source_target_pairs={{3,0},{4,1},{5,2},{6,3},{7,4},{8,5},{9,6},{10,7},{11,8},{12,9},{13... | collective-permute-start | bytes 811016 | tf_op jit(solution)/shard_map/ppermute | solution.py:15
  95.7 17.8 %collective-permute-start.3 = (bf16[16,8448]{1,0:T(8,128)(2,1)S(1)}, bf16[16,8448]{1,0:T(8,128)(2,1)S(1)}, u32[]{:S(2)}, u32[]{:S(2)}) collective-permute-start(bf16[16,8448]{1,0:T(8,128)(2,1)S(1)} %get-tuple-element.154), channel_id=1, source_target_pairs={{4,0},{5,1},{6,2},{7,3},{8,4},{9,5},{10,6},{11,7},{12,8},{13,9},{1... | collective-permute-start | bytes 811016 | tf_op jit(solution)/shard_map/ppermute | solution.py:15
  100.9 19.2 %collective-permute-start.14 = (bf16[16,8448]{1,0:T(8,128)(2,1)S(1)}, bf16[16,8448]{1,0:T(8,128)(2,1)S(1)}, u32[]{:S(2)}, u32[]{:S(2)}) collective-permute-start(bf16[16,8448]{1,0:T(8,128)(2,1)S(1)} %pad_maximum_fusion.7), channel_id=1, source_target_pairs={{0,4},{1,5},{2,6},{3,7},{4,8},{5,9},{6,10},{7,11},{8,12},{9,13},{1... | collective-permute-start | bytes 811016 | tf_op jit(solution)/shard_map/ppermute | solution.py:15
  103.8 21.8 %collective-permute-start.13 = (bf16[16,8448]{1,0:T(8,128)(2,1)S(1)}, bf16[16,8448]{1,0:T(8,128)(2,1)S(1)}, u32[]{:S(2)}, u32[]{:S(2)}) collective-permute-start(bf16[16,8448]{1,0:T(8,128)(2,1)S(1)} %pad_maximum_fusion.7), channel_id=1, source_target_pairs={{0,8},{1,9},{2,10},{3,11},{4,12},{5,13},{6,14},{7,15},{8,16},{9,17... | collective-permute-start | bytes 811016 | tf_op jit(solution)/shard_map/ppermute | solution.py:15
  107.8 17.9 %collective-permute-start.12 = (bf16[16,8448]{1,0:T(8,128)(2,1)S(1)}, bf16[16,8448]{1,0:T(8,128)(2,1)S(1)}, u32[]{:S(2)}, u32[]{:S(2)}) collective-permute-start(bf16[16,8448]{1,0:T(8,128)(2,1)S(1)} %pad_maximum_fusion.7), channel_id=1, source_target_pairs={{0,12},{1,13},{2,14},{3,15},{4,16},{5,17},{6,18},{7,19},{8,20},{9,... | collective-permute-start | bytes 811016 | tf_op jit(solution)/shard_map/ppermute | solution.py:15
  114.2 17.2 %collective-permute-start.6 = (bf16[16,8448]{1,0:T(8,128)(2,1)S(1)}, bf16[16,8448]{1,0:T(8,128)(2,1)S(1)}, u32[]{:S(2)}, u32[]{:S(2)}) collective-permute-start(bf16[16,8448]{1,0:T(8,128)(2,1)S(1)} %pad_maximum_fusion.5), channel_id=1, source_target_pairs={{4,0},{5,1},{6,2},{7,3},{8,4},{9,5},{10,6},{11,7},{12,8},{13,9},{1... | collective-permute-start | bytes 811016 | tf_op jit(solution)/shard_map/ppermute | solution.py:15
  118.2 13.2 %collective-permute-start.5 = (bf16[16,8448]{1,0:T(8,128)(2,1)S(1)}, bf16[16,8448]{1,0:T(8,128)(2,1)S(1)}, u32[]{:S(2)}, u32[]{:S(2)}) collective-permute-start(bf16[16,8448]{1,0:T(8,128)(2,1)S(1)} %pad_maximum_fusion.5), channel_id=1, source_target_pairs={{8,0},{9,1},{10,2},{11,3},{12,4},{13,5},{14,6},{15,7},{16,8},{17,9... | collective-permute-start | bytes 811016 | tf_op jit(solution)/shard_map/ppermute | solution.py:15
  120.1 12.1 %collective-permute-start.4 = (bf16[16,8448]{1,0:T(8,128)(2,1)S(1)}, bf16[16,8448]{1,0:T(8,128)(2,1)S(1)}, u32[]{:S(2)}, u32[]{:S(2)}) collective-permute-start(bf16[16,8448]{1,0:T(8,128)(2,1)S(1)} %pad_maximum_fusion.5), channel_id=1, source_target_pairs={{12,0},{13,1},{14,2},{15,3},{16,4},{17,5},{18,6},{19,7},{20,8},{21... | collective-permute-start | bytes 811016 | tf_op jit(solution)/shard_map/ppermute | solution.py:15
  126.4 11.9 %collective-permute-start.15 = (bf16[16,8448]{1,0:T(8,128)(2,1)S(1)}, bf16[16,8448]{1,0:T(8,128)(2,1)S(1)}, u32[]{:S(2)}, u32[]{:S(2)}) collective-permute-start(bf16[16,8448]{1,0:T(8,128)(2,1)S(1)} %pad_maximum_fusion.8), channel_id=1, source_target_pairs={{0,16},{1,17},{2,18},{3,19},{4,20},{5,21},{6,22},{7,23},{8,24},{9,... | collective-permute-start | bytes 811016 | tf_op jit(solution)/shard_map/ppermute | solution.py:15
  133.6 11.1 %collective-permute-start.7 = (bf16[16,8448]{1,0:T(8,128)(2,1)}, bf16[16,8448]{1,0:T(8,128)(2,1)}, u32[]{:S(2)}, u32[]{:S(2)}) collective-permute-start(bf16[16,8448]{1,0:T(8,128)(2,1)} %pad_maximum_fusion.6), channel_id=1, source_target_pairs={{16,0},{17,1},{18,2},{19,3},{20,4},{21,5},{22,6},{23,7},{24,8},{25... | collective-permute-start | bytes 811016 | tf_op jit(solution)/shard_map/ppermute | solution.py:15
  175.4 17.2 %collective-permute-start.25 = (bf16[4,64,640]{2,1,0:T(8,128)(2,1)}, bf16[4,64,640]{2,1,0:T(8,128)(2,1)S(1)}, u32[]{:S(2)}, u32[]{:S(2)}) collective-permute-start(bf16[4,64,640]{2,1,0:T(8,128)(2,1)} %get-tuple-element.121), channel_id=1, source_target_pairs={{0,24},{1,25},{2,26},{3,27},{4,28},{5,29},{6,30},{7,31},{8,0},{9,1... | collective-permute-start | bytes 983048 | tf_op jit(solution)/shard_map/ppermute | solution.py:71
  178.1 14.6 %collective-permute-start.24 = (bf16[4,64,640]{2,1,0:T(8,128)(2,1)}, bf16[4,64,640]{2,1,0:T(8,128)(2,1)}, u32[]{:S(2)}, u32[]{:S(2)}) collective-permute-start(bf16[4,64,640]{2,1,0:T(8,128)(2,1)} %get-tuple-element.122), channel_id=1, source_target_pairs={{0,16},{1,17},{2,18},{3,19},{4,20},{5,21},{6,22},{7,23},{8,24},{9,... | collective-permute-start | bytes 983048 | tf_op jit(solution)/shard_map/ppermute | solution.py:71
  178.1 16.5 %collective-permute-start.23 = (bf16[4,64,640]{2,1,0:T(8,128)(2,1)}, bf16[4,64,640]{2,1,0:T(8,128)(2,1)}, u32[]{:S(2)}, u32[]{:S(2)}) collective-permute-start(bf16[4,64,640]{2,1,0:T(8,128)(2,1)} %get-tuple-element.120), channel_id=1, source_target_pairs={{0,8},{1,9},{2,10},{3,11},{4,12},{5,13},{6,14},{7,15},{8,16},{9,17... | collective-permute-start | bytes 983048 | tf_op jit(solution)/shard_map/ppermute | solution.py:71
  179.7 24.4 %collective-permute-start.19 = (bf16[4,64,640]{2,1,0:T(8,128)(2,1)S(1)}, bf16[4,64,640]{2,1,0:T(8,128)(2,1)S(1)}, u32[]{:S(2)}, u32[]{:S(2)}) collective-permute-start(bf16[4,64,640]{2,1,0:T(8,128)(2,1)S(1)} %get-tuple-element.119), channel_id=1, source_target_pairs={{0,6},{1,7},{2,0},{3,1},{4,2},{5,3},{6,4},{7,5},{8,14},{9,15},{10,... | collective-permute-start | bytes 983048 | tf_op jit(solution)/shard_map/ppermute | solution.py:71
  185.9 19.6 %collective-permute-start.18 = (bf16[4,64,640]{2,1,0:T(8,128)(2,1)S(1)}, bf16[4,64,640]{2,1,0:T(8,128)(2,1)S(1)}, u32[]{:S(2)}, u32[]{:S(2)}) collective-permute-start(bf16[4,64,640]{2,1,0:T(8,128)(2,1)S(1)} %get-tuple-element.118), channel_id=1, source_target_pairs={{0,4},{1,5},{2,6},{3,7},{4,0},{5,1},{6,2},{7,3},{8,12},{9,13},{10,... | collective-permute-start | bytes 983048 | tf_op jit(solution)/shard_map/ppermute | solution.py:71
  192.6 16.9 %collective-permute-start.17 = (bf16[4,64,640]{2,1,0:T(8,128)(2,1)S(1)}, bf16[4,64,640]{2,1,0:T(8,128)(2,1)S(1)}, u32[]{:S(2)}, u32[]{:S(2)}) collective-permute-start(bf16[4,64,640]{2,1,0:T(8,128)(2,1)S(1)} %get-tuple-element.117), channel_id=1, source_target_pairs={{0,2},{1,3},{2,4},{3,5},{4,6},{5,7},{6,0},{7,1},{8,10},{9,11},{10,... | collective-permute-start | bytes 983048 | tf_op jit(solution)/shard_map/ppermute | solution.py:71
  196.0 14.8 %collective-permute-start.28 = (bf16[64,640]{1,0:T(8,128)(2,1)S(1)}, bf16[64,640]{1,0:T(8,128)(2,1)S(1)}, u32[]{:S(2)}, u32[]{:S(2)}) collective-permute-start(bf16[64,640]{1,0:T(8,128)(2,1)S(1)} %get-tuple-element.127), channel_id=1, source_target_pairs={{0,6},{1,7},{2,0},{3,1},{4,2},{5,3},{6,4},{7,5},{8,14},{9,15},{10,... | collective-permute-start | bytes 245768 | tf_op jit(solution)/shard_map/ppermute | solution.py:71
  217.3 10.7 %collective-permute-start.35 = (f32[8,1280]{1,0:T(8,128)S(1)}, f32[8,1280]{1,0:T(8,128)S(1)}, u32[]{:S(2)}, u32[]{:S(2)}) collective-permute-start(f32[8,1280]{1,0:T(8,128)S(1)} %get-tuple-element.140), channel_id=1, source_target_pairs={{0,224},{32,0},{64,32},{96,64},{128,96},{160,128},{192,160},{224,1... | collective-permute-start | bytes 122888 | tf_op jit(solution)/shard_map/ppermute | solution.py:98
  220.7 10.9 %collective-permute-start.34 = (f32[8,1280]{1,0:T(8,128)S(1)}, f32[8,1280]{1,0:T(8,128)S(1)}, u32[]{:S(2)}, u32[]{:S(2)}) collective-permute-start(f32[8,1280]{1,0:T(8,128)S(1)} %get-tuple-element.141), channel_id=1, source_target_pairs={{0,192},{32,224},{64,0},{96,32},{128,64},{160,96},{192,128},{224,1... | collective-permute-start | bytes 122888 | tf_op jit(solution)/shard_map/ppermute | solution.py:98
  222.9 10.4 %collective-permute-start.33 = (f32[8,1280]{1,0:T(8,128)S(1)}, f32[8,1280]{1,0:T(8,128)S(1)}, u32[]{:S(2)}, u32[]{:S(2)}) collective-permute-start(f32[8,1280]{1,0:T(8,128)S(1)} %get-tuple-element.142), channel_id=1, source_target_pairs={{0,160},{32,192},{64,224},{96,0},{128,32},{160,64},{192,96},{224,1... | collective-permute-start | bytes 122888 | tf_op jit(solution)/shard_map/ppermute | solution.py:98
  224.0 9.3 %collective-permute-start.32 = (f32[8,1280]{1,0:T(8,128)S(1)}, f32[8,1280]{1,0:T(8,128)S(1)}, u32[]{:S(2)}, u32[]{:S(2)}) collective-permute-start(f32[8,1280]{1,0:T(8,128)S(1)} %get-tuple-element.143), channel_id=1, source_target_pairs={{0,128},{32,160},{64,192},{96,224},{128,0},{160,32},{192,64},{224,... | collective-permute-start | bytes 122888 | tf_op jit(solution)/shard_map/ppermute | solution.py:98
  236.8 14.7 %collective-permute-start.36 = (f32[8,1280]{1,0:T(8,128)S(1)}, f32[8,1280]{1,0:T(8,128)S(1)}, u32[]{:S(2)}, u32[]{:S(2)}) collective-permute-start(f32[8,1280]{1,0:T(8,128)S(1)} %get-tuple-element.76), channel_id=1, source_target_pairs={{0,32},{32,64},{64,96},{96,128},{128,160},{160,192},{192,224},{224... | collective-permute-start | bytes 122888 | tf_op jit(solution)/shard_map/ppermute | solution.py:102
  242.9 12.5 %collective-permute-start.37 = (f32[8,1280]{1,0:T(8,128)S(1)}, f32[8,1280]{1,0:T(8,128)S(1)}, u32[]{:S(2)}, u32[]{:S(2)}) collective-permute-start(f32[8,1280]{1,0:T(8,128)S(1)} %get-tuple-element.76), channel_id=1, source_target_pairs={{0,64},{32,96},{64,128},{96,160},{128,192},{160,224},{192,0},{224,... | collective-permute-start | bytes 122888 | tf_op jit(solution)/shard_map/ppermute | solution.py:102
  244.5 12.0 %collective-permute-start.38 = (f32[8,1280]{1,0:T(8,128)S(1)}, f32[8,1280]{1,0:T(8,128)S(1)}, u32[]{:S(2)}, u32[]{:S(2)}) collective-permute-start(f32[8,1280]{1,0:T(8,128)S(1)} %get-tuple-element.76), channel_id=1, source_target_pairs={{0,96},{32,128},{64,160},{96,192},{128,224},{160,0},{192,32},{224,... | collective-permute-start | bytes 122888 | tf_op jit(solution)/shard_map/ppermute | solution.py:102
  246.6 9.9 %collective-permute-start.39 = (f32[8,1280]{1,0:T(8,128)S(1)}, f32[8,1280]{1,0:T(8,128)S(1)}, u32[]{:S(2)}, u32[]{:S(2)}) collective-permute-start(f32[8,1280]{1,0:T(8,128)S(1)} %get-tuple-element.76), channel_id=1, source_target_pairs={{0,128},{32,160},{64,192},{96,224},{128,0},{160,32},{192,64},{224,... | collective-permute-start | bytes 122888 | tf_op jit(solution)/shard_map/ppermute | solution.py:102
  (19 other events, 374.8 us)
Sparse Core Ops, SparseCore 0:
  11.1 54.9 all-gather.1

commit v7 on v6

--- a/solution.py
+++ b/solution.py
@@ -15,7 +15,7 @@
     return lax.ppermute(value.astype(jnp.bfloat16), axis, pairs).astype(value.dtype)
 
 
-def scan_entering(decay, state, axis, reverse):
+def scan_entering(decay, state, axis, reverse, hold=None):
     head_count = state.shape[0]
     flat = state.reshape(head_count, -1)
     split = flat.shape[1]
@@ -37,6 +37,7 @@
         return flat, decay
 
     radix = 4
+    held = hold
     own = (flat, decay)
     part = chain([send(own, step) for step in range(radix, 0, -1)])
     width = radix
@@ -44,8 +45,11 @@
         pieces = min(radix, -(-count // width))
         part = chain([send(part, width * m) for m in range(pieces - 1, 0, -1)] + [part])
         width *= pieces
+        if hold is not None:
+            part, held = lax.optimization_barrier((part, hold))
+            hold = None
     flat = part[0]
-    return flat.reshape(state.shape)
+    return flat.reshape(state.shape), held
 
 
 def butterfly_sum(value, axis):
@@ -134,6 +138,14 @@
     fwd_state = jnp.einsum("sn,shp->hnp", b_mat, weighted_x, preferred_element_type=jnp.float32)
     back_state = jnp.einsum("tn,thp->hnp", c_mat, weighted_g, preferred_element_type=jnp.float32)
     return (jnp.exp(cum_log[:, -1]), fwd_state, back_state)
+
+
+def back_summary(c_mat, grad_out, ld_block):
+    cum_log, input_scale, tail_weight = block_prep(ld_block)
+    inv_root = 1.0 / math.sqrt(c_mat.shape[1])
+    head_weight = jnp.exp(cum_log) * inv_root
+    weighted_g = (grad_out.astype(jnp.float32) * head_weight.T[:, :, None]).astype(jnp.bfloat16)
+    return jnp.einsum("tn,thp->hnp", c_mat, weighted_g, preferred_element_type=jnp.float32)
 
 
 def block_grads(x_vals, b_mat, c_mat, grad_out, ld_block, state_in, back_in):
@@ -184,26 +196,35 @@
     head_dim = hp_width // head_count
     proj_width = weight_codes.shape[1]
     state_width = (proj_width - hp_width) // 2
-    weights = lax.all_gather(dequantize(weight_codes, scales), "seq", axis=0, tiled=True)
-    projected = jnp.dot(features, weights, preferred_element_type=jnp.float32).astype(jnp.bfloat16)
+    local_weights = dequantize(weight_codes, scales)
+    state_weights = lax.all_gather(local_weights[:, hp_width:], "seq", axis=0, tiled=True)
+    head_weights = lax.all_gather(local_weights[:, :hp_width], "seq", axis=0, tiled=True)
+    state_proj = jnp.dot(features, state_weights, preferred_element_type=jnp.float32).astype(
+        jnp.bfloat16
+    )
     block_len = min(128, tok_count)
     block_count = tok_count // block_len
-    x_blocks = projected[:, :hp_width].reshape(block_count, block_len, head_count, head_dim)
-    b_blocks = projected[:, hp_width : hp_width + state_width].reshape(
-        block_count, block_len, state_width
-    )
-    c_blocks = projected[:, hp_width + state_width :].reshape(block_count, block_len, state_width)
+    b_blocks = state_proj[:, :state_width].reshape(block_count, block_len, state_width)
+    c_blocks = state_proj[:, state_width:].reshape(block_count, block_len, state_width)
     g_blocks = grad_out.reshape(block_count, block_len, head_count, head_dim)
     ld_blocks = log_decay[0].reshape(head_count, block_count, block_len).transpose(1, 0, 2)
-    decays, fwd_states, back_states = jax.vmap(summaries)(
+    zero_state = jnp.zeros((head_count, state_width, head_dim), jnp.float32)
+    back_states = jax.vmap(back_summary)(c_blocks, g_blocks, ld_blocks)
+    decays = jnp.exp(jnp.cumsum(ld_blocks, axis=2)[:, :, -1])
+    dev_decay = jnp.prod(decays, axis=0)
+    dev_back, unused_b = state_chain(decays, back_states, zero_state, True)
+    back_entering, head_weights = scan_entering(dev_decay, dev_back, "seq", True, head_weights)
+    returned = (None, back_entering)
+    weights = jnp.concatenate([head_weights, state_weights], axis=1)
+    head_proj = jnp.dot(features, head_weights, preferred_element_type=jnp.float32).astype(
+        jnp.bfloat16
+    )
+    x_blocks = head_proj.reshape(block_count, block_len, head_count, head_dim)
+    unused_e, fwd_states, unused_f = jax.vmap(summaries)(
         x_blocks, b_blocks, c_blocks, g_blocks, ld_blocks
     )
-    zero_state = jnp.zeros((head_count, state_width, head_dim), jnp.float32)
-    dev_decay = jnp.prod(decays, axis=0)
     dev_fwd, unused_a = state_chain(decays, fwd_states, zero_state, False)
-    dev_back, unused_b = state_chain(decays, back_states, zero_state, True)
-    carried = (None, scan_entering(dev_decay, dev_fwd, "seq", False))
-    returned = (None, scan_entering(dev_decay, dev_back, "seq", True))
+    carried = (None, scan_entering(dev_decay, dev_fwd, "seq", False)[0])
     unused_c, state_starts = state_chain(decays, fwd_states, carried[1], False)
     unused_d, back_starts = state_chain(decays, back_states, returned[1], True)
     d_x, d_b, d_c = lax.map(

time: 270 us -> 311 us (1.15)
  waiting for transfers between devices: 94.6 us -> 141 us
  starting transfers between devices: 104 us -> 91.8 us
    ppermute x16, waiting for transfers between devices: 15.4 us -> 45 us  [shifted(): lax.ppermute(value.astype(jnp.bfloat16), axis, pairs).astype(value.dtype)]
    all_gather x1 -> x2, waiting for transfers between devices: 50.4 us -> 67.1 us  [the longest x1 45.1 us: local(): lax.all_gather(local_weights[:, hp_width:], 'seq', axis=0, tiled=True)]
    ppermute x13, starting transfers between devices: 24.1 us -> 14.7 us  [digit_reduce(): got = lax.ppermute(piece.astype(jnp.bfloat16), axis, pairs)]
    ppermute x16, starting transfers between devices: 50.1 us -> 46.5 us  [shifted(): lax.ppermute(value.astype(jnp.bfloat16), axis, pairs).astype(value.dtype)]
  transfers between devices with their start and end apart: 44 -> 45, of which waited for: 19 -> 25; matrix products, arithmetic and copies ran while one was open for 7% -> 9% of each run, Pallas kernels for 0% -> 0%
where the time goes in v7:
time: 311 us; the launch traced here: 307 us
  waiting for transfers between devices  141 us (45%)
  starting transfers between devices  91.8 us (30%)
  local copies, waits for them, and re-layouts  20.9 us (7%)
  matrix products  19.8 us (6%)
  other arithmetic  17.9 us (6%)
  between operations  14.9 us (5%)
    ppermute x16, starting transfers between devices, shifted(): lax.ppermute(value.astype(jnp.bfloat16), axis, pairs).astype(value.dtype)  46.5 us
    all_gather x1, waiting for transfers between devices, local(): lax.all_gather(local_weights[:, hp_width:], 'seq', axis=0, tiled=True)  45.1 us
    ppermute x16, waiting for transfers between devices, shifted(): lax.ppermute(value.astype(jnp.bfloat16), axis, pairs).astype(value.dtype)  45 us
    ppermute x13, waiting for transfers between devices, digit_reduce(): got = lax.ppermute(piece.astype(jnp.bfloat16), axis, pairs)  23 us
    all_gather x1, waiting for transfers between devices, local(): lax.all_gather(local_weights[:, :hp_width], 'seq', axis=0, tiled=True)  22 us
    ppermute x7, starting transfers between devices, replicated_sum(): total = total + lax.ppermute(piece, axis, pairs)  15.8 us
    ppermute x13, starting transfers between devices, digit_reduce(): got = lax.ppermute(piece.astype(jnp.bfloat16), axis, pairs)  14.7 us
    ppermute x7, starting transfers between devices, replicated_sum(): gathered.append(lax.ppermute(total, axis, pairs))  14.6 us
  transfers between devices with their start and end apart: 45, of which 25 were waited for; matrix products, arithmetic and copies ran while one was open for 9% of the time, Pallas kernels for 0%

profile of v7, /device:TPU:8, one launch (start us, length us, event | category | flops | bytes accessed | tf_op | source)
XLA Modules:
  0.0 306.6 jit_solution(8124295409449473168)
XLA Ops:
  16.4 45.1 %all-gather.3.cloned.1.call-done = bf16[2048,256]{1,0:T(8,128)(2,1)} async-done(((bf16[64,256]{1,0:T(8,128)(2,1)}), bf16[2048,256]{1,0:T(8,128)(2,1)}) %all-gather.3.cloned.1.call-update) | async-done | bytes 1048592 | tf_op jit(solution)/shard_map/all_gather | solution.py:200
  64.4 4.5 %collective-permute-start.3 = (bf16[16,8448]{1,0:T(8,128)(2,1)S(1)}, bf16[16,8448]{1,0:T(8,128)(2,1)S(1)}, u32[]{:S(2)}, u32[]{:S(2)}) collective-permute-start(bf16[16,8448]{1,0:T(8,128)(2,1)S(1)} %pad_maximum_fusion.1), channel_id=1, source_target_pairs={{1,0},{2,1},{3,2},{4,3},{5,4},{6,5},{7,6},{8,7},{9,8},{10,9},{11,1... | collective-permute-start | bytes 811016 | tf_op jit(solution)/shard_map/ppermute | solution.py:15
  73.5 2.8 collective-permute-start
  76.5 4.4 %collective-permute-done.2 = bf16[16,8448]{1,0:T(8,128)(2,1)S(1)} collective-permute-done((bf16[16,8448]{1,0:T(8,128)(2,1)S(1)}, bf16[16,8448]{1,0:T(8,128)(2,1)S(1)}, u32[]{:S(2)}, u32[]{:S(2)}) %collective-permute-start.2) | collective-permute-done | bytes 270368 | tf_op jit(solution)/shard_map/ppermute | solution.py:15
  83.3 4.6 %collective-permute-done = bf16[16,8448]{1,0:T(8,128)(2,1)S(1)} collective-permute-done((bf16[16,8448]{1,0:T(8,128)(2,1)S(1)}, bf16[16,8448]{1,0:T(8,128)(2,1)S(1)}, u32[]{:S(2)}, u32[]{:S(2)}) %collective-permute-start) | collective-permute-done | bytes 270368 | tf_op jit(solution)/shard_map/ppermute | solution.py:15
  88.6 3.7 %collective-permute-start.4 = (bf16[16,8448]{1,0:T(8,128)(2,1)S(1)}, bf16[16,8448]{1,0:T(8,128)(2,1)S(1)}, u32[]{:S(2)}, u32[]{:S(2)}) collective-permute-start(bf16[16,8448]{1,0:T(8,128)(2,1)S(1)} %pad_maximum_fusion.5), channel_id=1, source_target_pairs={{4,0},{5,1},{6,2},{7,3},{8,4},{9,5},{10,6},{11,7},{12,8},{13,9},{1... | collective-permute-start | bytes 811016 | tf_op jit(solution)/shard_map/ppermute | solution.py:15
  98.5 3.6 %collective-permute-done.5 = bf16[16,8448]{1,0:T(8,128)(2,1)S(1)} collective-permute-done((bf16[16,8448]{1,0:T(8,128)(2,1)S(1)}, bf16[16,8448]{1,0:T(8,128)(2,1)S(1)}, u32[]{:S(2)}, u32[]{:S(2)}) %collective-permute-start.5) | collective-permute-done | bytes 270368 | tf_op jit(solution)/shard_map/ppermute | solution.py:15
  102.1 3.9 %collective-permute-done.6 = bf16[16,8448]{1,0:T(8,128)(2,1)S(1)} collective-permute-done((bf16[16,8448]{1,0:T(8,128)(2,1)S(1)}, bf16[16,8448]{1,0:T(8,128)(2,1)S(1)}, u32[]{:S(2)}, u32[]{:S(2)}) %collective-permute-start.6) | collective-permute-done | bytes 270368 | tf_op jit(solution)/shard_map/ppermute | solution.py:15
  106.4 22.0 %all-gather.5.cloned.1.call-done = bf16[2048,1024]{1,0:T(8,128)(2,1)} async-done(((bf16[64,1024]{1,0:T(8,128)(2,1)}), bf16[2048,1024]{1,0:T(8,128)(2,1)}) %all-gather.5.cloned.1.call-update) | async-done | bytes 4194320 | tf_op jit(solution)/shard_map/all_gather | solution.py:201
  128.4 4.2 %fusion.22 = (bf16[128,1024]{0,1:T(8,128)(2,1)S(1)}, bf16[128,1024]{0,1:T(8,128)(2,1)S(1)}, bf16[1024,128]{1,0:T(8,128)(2,1)}) fusion(f32[128,16]{0,1:T(8,128)S(1)} %get-tuple-element.152, f32[128,16]{0,1:T(8,128)S(1)} %get-tuple-element.155, bf16[2048,1024]{1,0:T(8,128)(2,1)} %all-gather.5.cloned.1.call-done, bf16[1,128,2048]{2,1,0:T(8,128)(2,1)S(1)} %copy-done), kind=kOutput, calls=%fused_computation.48 | convolution fusion | flops 537657344 | bytes 5521408 | tf_op jit(solution)/shard_map/dot_general | solution.py:219
  138.0 3.7 %collective-permute-start.10 = (bf16[16,8448]{1,0:T(8,128)(2,1)S(1)}, bf16[16,8448]{1,0:T(8,128)(2,1)S(1)}, u32[]{:S(2)}, u32[]{:S(2)}) collective-permute-start(bf16[16,8448]{1,0:T(8,128)(2,1)S(1)} %pad_maximum_fusion), channel_id=1, source_target_pairs={{0,3},{1,4},{2,5},{3,6},{4,7},{5,8},{6,9},{7,10},{8,11},{9,12},{10... | collective-permute-start | bytes 811016 | tf_op jit(solution)/shard_map/ppermute | solution.py:15
  141.7 4.8 %collective-permute-start.11 = (bf16[16,8448]{1,0:T(8,128)(2,1)S(1)}, bf16[16,8448]{1,0:T(8,128)(2,1)S(1)}, u32[]{:S(2)}, u32[]{:S(2)}) collective-permute-start(bf16[16,8448]{1,0:T(8,128)(2,1)S(1)} %pad_maximum_fusion), channel_id=1, source_target_pairs={{0,4},{1,5},{2,6},{3,7},{4,8},{5,9},{6,10},{7,11},{8,12},{9,13},{1... | collective-permute-start | bytes 811016 | tf_op jit(solution)/shard_map/ppermute | solution.py:15
  149.9 5.6 %collective-permute-done.10 = bf16[16,8448]{1,0:T(8,128)(2,1)S(1)} collective-permute-done((bf16[16,8448]{1,0:T(8,128)(2,1)S(1)}, bf16[16,8448]{1,0:T(8,128)(2,1)S(1)}, u32[]{:S(2)}, u32[]{:S(2)}) %collective-permute-start.10) | collective-permute-done | bytes 270368 | tf_op jit(solution)/shard_map/ppermute | solution.py:15
  159.8 4.0 %collective-permute-start.14 = (bf16[16,8448]{1,0:T(8,128)(2,1)}, bf16[16,8448]{1,0:T(8,128)(2,1)}, u32[]{:S(2)}, u32[]{:S(2)}) collective-permute-start(bf16[16,8448]{1,0:T(8,128)(2,1)} %pad_maximum_fusion.7), channel_id=1, source_target_pairs={{0,4},{1,5},{2,6},{3,7},{4,8},{5,9},{6,10},{7,11},{8,12},{9,13},{1... | collective-permute-start | bytes 811016 | tf_op jit(solution)/shard_map/ppermute | solution.py:15
  163.8 3.0 collective-permute-start.13
  166.8 5.1 %collective-permute-start.12 = (bf16[16,8448]{1,0:T(8,128)(2,1)}, bf16[16,8448]{1,0:T(8,128)(2,1)}, u32[]{:S(2)}, u32[]{:S(2)}) collective-permute-start(bf16[16,8448]{1,0:T(8,128)(2,1)} %pad_maximum_fusion.7), channel_id=1, source_target_pairs={{0,12},{1,13},{2,14},{3,15},{4,16},{5,17},{6,18},{7,19},{8,20},{9,... | collective-permute-start | bytes 811016 | tf_op jit(solution)/shard_map/ppermute | solution.py:15
  174.3 11.0 %collective-permute-done.13 = bf16[16,8448]{1,0:T(8,128)(2,1)} collective-permute-done((bf16[16,8448]{1,0:T(8,128)(2,1)}, bf16[16,8448]{1,0:T(8,128)(2,1)}, u32[]{:S(2)}, u32[]{:S(2)}) %collective-permute-start.13) | collective-permute-done | bytes 270368 | tf_op jit(solution)/shard_map/ppermute | solution.py:15
  190.3 5.2 %collective-permute-done.15 = bf16[16,8448]{1,0:T(8,128)(2,1)S(1)} collective-permute-done((bf16[16,8448]{1,0:T(8,128)(2,1)S(1)}, bf16[16,8448]{1,0:T(8,128)(2,1)S(1)}, u32[]{:S(2)}, u32[]{:S(2)}) %collective-permute-start.15) | collective-permute-done | bytes 270368 | tf_op jit(solution)/shard_map/ppermute | solution.py:15
  196.6 3.8 %fusion = bf16[2048,1280]{0,1:T(8,128)(2,1)} fusion(bf16[1,128,2048]{2,1,0:T(8,128)(2,1)S(1)} %copy-done, bf16[128,128]{0,1:T(8,128)(2,1)S(1)} %fusion.15, bf16[128,128]{0,1:T(8,128)(2,1)S(1)} %fusion.14, bf16[128,1024]{0,1:T(8,128)(2,1)S(1)} %bitcast.243), kind=kOutput, calls=%fused_computation.2 | convolution fusion | flops 674693120 | bytes 6094848 | tf_op jit(solution)/shard_map/dot_general | solution.py:249
  200.5 7.8 %copy.68 = bf16[2048,1280]{1,0:T(8,128)(2,1)} copy(bf16[2048,1280]{0,1:T(8,128)(2,1)} %fusion) | data formatting | bytes 10485760 | tf_op jit(solution)/shard_map/convert_element_type | solution.py:251
  210.4 4.9 %collective-permute-done.16 = bf16[4,4,64,1280]{3,2,1,0:T(8,128)(2,1)} collective-permute-done((bf16[4,4,64,1280]{3,2,1,0:T(8,128)(2,1)S(1)}, bf16[4,4,64,1280]{3,2,1,0:T(8,128)(2,1)}, u32[]{:S(2)}, u32[]{:S(2)}) %collective-permute-start.16) | collective-permute-done | bytes 2621472 | tf_op jit(solution)/shard_map/ppermute | solution.py:75
  215.4 3.2 %convert_add_fusion = f32[4,4,64,1280]{3,2,1,0:T(8,128)S(1)} fusion(bf16[4,4,64,1280]{3,2,1,0:T(8,128)(2,1)} %collective-permute-done.16, bf16[4,4,2,64,1280]{4,3,2,1,0:T(8,128)(2,1)} %bitcast.233, s32[]{:T(128)S(6)} %select_n.216), kind=kLoop, calls=%fused_computation.7 | loop fusion | flops 3932160 | bytes 10485764 | tf_op jit(solution)/shard_map/add | solution.py:76
  221.5 4.0 %collective-permute-start.25 = (bf16[4,64,640]{2,1,0:T(8,128)(2,1)}, bf16[4,64,640]{2,1,0:T(8,128)(2,1)S(1)}, u32[]{:S(2)}, u32[]{:S(2)}) collective-permute-start(bf16[4,64,640]{2,1,0:T(8,128)(2,1)} %get-tuple-element.124), channel_id=1, source_target_pairs={{0,24},{1,25},{2,26},{3,27},{4,28},{5,29},{6,30},{7,31},{8,0},{9,1... | collective-permute-start | bytes 983048 | tf_op jit(solution)/shard_map/ppermute | solution.py:75
  225.5 3.4 %collective-permute-start.24 = (bf16[4,64,640]{2,1,0:T(8,128)(2,1)}, bf16[4,64,640]{2,1,0:T(8,128)(2,1)S(1)}, u32[]{:S(2)}, u32[]{:S(2)}) collective-permute-start(bf16[4,64,640]{2,1,0:T(8,128)(2,1)} %get-tuple-element.125), channel_id=1, source_target_pairs={{0,16},{1,17},{2,18},{3,19},{4,20},{5,21},{6,22},{7,23},{8,24},{9,... | collective-permute-start | bytes 983048 | tf_op jit(solution)/shard_map/ppermute | solution.py:75
  229.2 6.4 %collective-permute-done.25 = bf16[4,64,640]{2,1,0:T(8,128)(2,1)S(1)} collective-permute-done((bf16[4,64,640]{2,1,0:T(8,128)(2,1)}, bf16[4,64,640]{2,1,0:T(8,128)(2,1)S(1)}, u32[]{:S(2)}, u32[]{:S(2)}) %collective-permute-start.25) | collective-permute-done | bytes 327712 | tf_op jit(solution)/shard_map/ppermute | solution.py:75
  235.6 8.2 %collective-permute-done.24 = bf16[4,64,640]{2,1,0:T(8,128)(2,1)S(1)} collective-permute-done((bf16[4,64,640]{2,1,0:T(8,128)(2,1)}, bf16[4,64,640]{2,1,0:T(8,128)(2,1)S(1)}, u32[]{:S(2)}, u32[]{:S(2)}) %collective-permute-start.24) | collective-permute-done | bytes 327712 | tf_op jit(solution)/shard_map/ppermute | solution.py:75
  256.1 3.4 %collective-permute-start.35 = (f32[8,1280]{1,0:T(8,128)S(1)}, f32[8,1280]{1,0:T(8,128)S(1)}, u32[]{:S(2)}, u32[]{:S(2)}) collective-permute-start(f32[8,1280]{1,0:T(8,128)S(1)} %get-tuple-element.141), channel_id=1, source_target_pairs={{0,224},{32,0},{64,32},{96,64},{128,96},{160,128},{192,160},{224,1... | collective-permute-start | bytes 122888 | tf_op jit(solution)/shard_map/ppermute | solution.py:102
  262.9 3.9 %collective-permute-start.32 = (f32[8,1280]{1,0:T(8,128)S(1)}, f32[8,1280]{1,0:T(8,128)S(1)}, u32[]{:S(2)}, u32[]{:S(2)}) collective-permute-start(f32[8,1280]{1,0:T(8,128)S(1)} %get-tuple-element.144), channel_id=1, source_target_pairs={{0,128},{32,160},{64,192},{96,224},{128,0},{160,32},{192,64},{224,... | collective-permute-start | bytes 122888 | tf_op jit(solution)/shard_map/ppermute | solution.py:102
  266.8 3.6 %collective-permute-start.30 = (f32[8,1280]{1,0:T(8,128)S(1)}, f32[8,1280]{1,0:T(8,128)S(1)}, u32[]{:S(2)}, u32[]{:S(2)}) collective-permute-start(f32[8,1280]{1,0:T(8,128)S(1)} %get-tuple-element.146), channel_id=1, source_target_pairs={{0,64},{32,96},{64,128},{96,160},{128,192},{160,224},{192,0},{224,... | collective-permute-start | bytes 122888 | tf_op jit(solution)/shard_map/ppermute | solution.py:102
  276.5 5.4 %fusion.5 = f32[1,128,2048]{2,1,0:T(8,128)} fusion(bf16[2048,256]{1,0:T(8,128)(2,1)} %all-gather.3.cloned.1.call-done, bf16[2048,1024]{1,0:T(8,128)(2,1)} %all-gather.5.cloned.1.call-done, bf16[128,128]{0,1:T(8,128)(2,1)S(1)} %copy-done.7, bf16[128,128]{0,1:T(8,128)(2,1)S(1)} %copy-done.5, bf16[128,1024]{0,1:T(8,128)(2,1)} %bitcast.244), kind=kOutput, calls=%fused_computation.9 | convolution fusion | flops 682557440 | bytes 6619136 | tf_op jit(solution)/shard_map/dot_general | solution.py:242
  285.3 3.1 %collective-permute-start.39 = (f32[8,1280]{1,0:T(8,128)S(1)}, f32[8,1280]{1,0:T(8,128)S(1)}, u32[]{:S(2)}, u32[]{:S(2)}) collective-permute-start(f32[8,1280]{1,0:T(8,128)S(1)} %get-tuple-element.94), channel_id=1, source_target_pairs={{0,128},{32,160},{64,192},{96,224},{128,0},{160,32},{192,64},{224,... | collective-permute-start | bytes 122888 | tf_op jit(solution)/shard_map/ppermute | solution.py:106
  290.6 3.7 %collective-permute-start.41 = (f32[8,1280]{1,0:T(8,128)S(1)}, f32[8,1280]{1,0:T(8,128)S(1)}, u32[]{:S(2)}, u32[]{:S(2)}) collective-permute-start(f32[8,1280]{1,0:T(8,128)S(1)} %get-tuple-element.94), channel_id=1, source_target_pairs={{0,192},{32,224},{64,0},{96,32},{128,64},{160,96},{192,128},{224,1... | collective-permute-start | bytes 122888 | tf_op jit(solution)/shard_map/ppermute | solution.py:106
  (199 shorter events, 85.5 us)
Async XLA Ops:
  7.2 54.3 %all-gather.3.cloned.1.call-start = ((), (), s32[]{:S(2)}) async-start(), calls=%async_computation | async-start | bytes 1081344 | tf_op jit(solution)/shard_map/all_gather | solution.py:200
  9.9 118.5 %all-gather.5.cloned.1.call-start = ((), (), s32[]{:S(2)}) async-start(), calls=%async_computation.1 | async-start | bytes 4325376 | tf_op jit(solution)/shard_map/all_gather | solution.py:201
  64.4 12.0 %collective-permute-start.3 = (bf16[16,8448]{1,0:T(8,128)(2,1)S(1)}, bf16[16,8448]{1,0:T(8,128)(2,1)S(1)}, u32[]{:S(2)}, u32[]{:S(2)}) collective-permute-start(bf16[16,8448]{1,0:T(8,128)(2,1)S(1)} %pad_maximum_fusion.1), channel_id=1, source_target_pairs={{1,0},{2,1},{3,2},{4,3},{5,4},{6,5},{7,6},{8,7},{9,8},{10,9},{11,1... | collective-permute-start | bytes 811016 | tf_op jit(solution)/shard_map/ppermute | solution.py:15
  68.9 12.0 %collective-permute-start.2 = (bf16[16,8448]{1,0:T(8,128)(2,1)S(1)}, bf16[16,8448]{1,0:T(8,128)(2,1)S(1)}, u32[]{:S(2)}, u32[]{:S(2)}) collective-permute-start(bf16[16,8448]{1,0:T(8,128)(2,1)S(1)} %pad_maximum_fusion.1), channel_id=1, source_target_pairs={{2,0},{3,1},{4,2},{5,3},{6,4},{7,5},{8,6},{9,7},{10,8},{11,9},{12,... | collective-permute-start | bytes 811016 | tf_op jit(solution)/shard_map/ppermute | solution.py:15
  71.6 11.7 %collective-permute-start.1 = (bf16[16,8448]{1,0:T(8,128)(2,1)S(1)}, bf16[16,8448]{1,0:T(8,128)(2,1)S(1)}, u32[]{:S(2)}, u32[]{:S(2)}) collective-permute-start(bf16[16,8448]{1,0:T(8,128)(2,1)S(1)} %pad_maximum_fusion.1), channel_id=1, source_target_pairs={{3,0},{4,1},{5,2},{6,3},{7,4},{8,5},{9,6},{10,7},{11,8},{12,9},{13... | collective-permute-start | bytes 811016 | tf_op jit(solution)/shard_map/ppermute | solution.py:15
  73.5 14.3 %collective-permute-start = (bf16[16,8448]{1,0:T(8,128)(2,1)S(1)}, bf16[16,8448]{1,0:T(8,128)(2,1)S(1)}, u32[]{:S(2)}, u32[]{:S(2)}) collective-permute-start(bf16[16,8448]{1,0:T(8,128)(2,1)S(1)} %pad_maximum_fusion.1), channel_id=1, source_target_pairs={{4,0},{5,1},{6,2},{7,3},{8,4},{9,5},{10,6},{11,7},{12,8},{13,9},{1... | collective-permute-start | bytes 811016 | tf_op jit(solution)/shard_map/ppermute | solution.py:15
  88.6 9.9 %collective-permute-start.4 = (bf16[16,8448]{1,0:T(8,128)(2,1)S(1)}, bf16[16,8448]{1,0:T(8,128)(2,1)S(1)}, u32[]{:S(2)}, u32[]{:S(2)}) collective-permute-start(bf16[16,8448]{1,0:T(8,128)(2,1)S(1)} %pad_maximum_fusion.5), channel_id=1, source_target_pairs={{4,0},{5,1},{6,2},{7,3},{8,4},{9,5},{10,6},{11,7},{12,8},{13,9},{1... | collective-permute-start | bytes 811016 | tf_op jit(solution)/shard_map/ppermute | solution.py:15
  92.3 9.8 %collective-permute-start.5 = (bf16[16,8448]{1,0:T(8,128)(2,1)S(1)}, bf16[16,8448]{1,0:T(8,128)(2,1)S(1)}, u32[]{:S(2)}, u32[]{:S(2)}) collective-permute-start(bf16[16,8448]{1,0:T(8,128)(2,1)S(1)} %pad_maximum_fusion.5), channel_id=1, source_target_pairs={{8,0},{9,1},{10,2},{11,3},{12,4},{13,5},{14,6},{15,7},{16,8},{17,9... | collective-permute-start | bytes 811016 | tf_op jit(solution)/shard_map/ppermute | solution.py:15
  94.2 11.8 %collective-permute-start.6 = (bf16[16,8448]{1,0:T(8,128)(2,1)S(1)}, bf16[16,8448]{1,0:T(8,128)(2,1)S(1)}, u32[]{:S(2)}, u32[]{:S(2)}) collective-permute-start(bf16[16,8448]{1,0:T(8,128)(2,1)S(1)} %pad_maximum_fusion.5), channel_id=1, source_target_pairs={{12,0},{13,1},{14,2},{15,3},{16,4},{17,5},{18,6},{19,7},{20,8},{21... | collective-permute-start | bytes 811016 | tf_op jit(solution)/shard_map/ppermute | solution.py:15
  133.7 16.1 %collective-permute-start.8 = (bf16[16,8448]{1,0:T(8,128)(2,1)S(1)}, bf16[16,8448]{1,0:T(8,128)(2,1)S(1)}, u32[]{:S(2)}, u32[]{:S(2)}) collective-permute-start(bf16[16,8448]{1,0:T(8,128)(2,1)S(1)} %pad_maximum_fusion), channel_id=1, source_target_pairs={{0,1},{1,2},{2,3},{3,4},{4,5},{5,6},{6,7},{7,8},{8,9},{9,10},{10,1... | collective-permute-start | bytes 811016 | tf_op jit(solution)/shard_map/ppermute | solution.py:15
  135.8 14.0 %collective-permute-start.9 = (bf16[16,8448]{1,0:T(8,128)(2,1)S(1)}, bf16[16,8448]{1,0:T(8,128)(2,1)S(1)}, u32[]{:S(2)}, u32[]{:S(2)}) collective-permute-start(bf16[16,8448]{1,0:T(8,128)(2,1)S(1)} %pad_maximum_fusion), channel_id=1, source_target_pairs={{0,2},{1,3},{2,4},{3,5},{4,6},{5,7},{6,8},{7,9},{8,10},{9,11},{10,... | collective-permute-start | bytes 811016 | tf_op jit(solution)/shard_map/ppermute | solution.py:15
  138.0 17.5 %collective-permute-start.10 = (bf16[16,8448]{1,0:T(8,128)(2,1)S(1)}, bf16[16,8448]{1,0:T(8,128)(2,1)S(1)}, u32[]{:S(2)}, u32[]{:S(2)}) collective-permute-start(bf16[16,8448]{1,0:T(8,128)(2,1)S(1)} %pad_maximum_fusion), channel_id=1, source_target_pairs={{0,3},{1,4},{2,5},{3,6},{4,7},{5,8},{6,9},{7,10},{8,11},{9,12},{10... | collective-permute-start | bytes 811016 | tf_op jit(solution)/shard_map/ppermute | solution.py:15
  141.7 16.7 %collective-permute-start.11 = (bf16[16,8448]{1,0:T(8,128)(2,1)S(1)}, bf16[16,8448]{1,0:T(8,128)(2,1)S(1)}, u32[]{:S(2)}, u32[]{:S(2)}) collective-permute-start(bf16[16,8448]{1,0:T(8,128)(2,1)S(1)} %pad_maximum_fusion), channel_id=1, source_target_pairs={{0,4},{1,5},{2,6},{3,7},{4,8},{5,9},{6,10},{7,11},{8,12},{9,13},{1... | collective-permute-start | bytes 811016 | tf_op jit(solution)/shard_map/ppermute | solution.py:15
  146.7 25.2 %collective-permute-start.7 = (bf16[16,8448]{1,0:T(8,128)(2,1)S(1)}, bf16[16,8448]{1,0:T(8,128)(2,1)S(1)}, u32[]{:S(2)}, u32[]{:S(2)}) collective-permute-start(bf16[16,8448]{1,0:T(8,128)(2,1)S(1)} %pad_maximum_fusion.6), channel_id=1, source_target_pairs={{16,0},{17,1},{18,2},{19,3},{20,4},{21,5},{22,6},{23,7},{24,8},{25... | collective-permute-start | bytes 811016 | tf_op jit(solution)/shard_map/ppermute | solution.py:15
  159.8 13.6 %collective-permute-start.14 = (bf16[16,8448]{1,0:T(8,128)(2,1)}, bf16[16,8448]{1,0:T(8,128)(2,1)}, u32[]{:S(2)}, u32[]{:S(2)}) collective-permute-start(bf16[16,8448]{1,0:T(8,128)(2,1)} %pad_maximum_fusion.7), channel_id=1, source_target_pairs={{0,4},{1,5},{2,6},{3,7},{4,8},{5,9},{6,10},{7,11},{8,12},{9,13},{1... | collective-permute-start | bytes 811016 | tf_op jit(solution)/shard_map/ppermute | solution.py:15
  163.8 21.5 %collective-permute-start.13 = (bf16[16,8448]{1,0:T(8,128)(2,1)}, bf16[16,8448]{1,0:T(8,128)(2,1)}, u32[]{:S(2)}, u32[]{:S(2)}) collective-permute-start(bf16[16,8448]{1,0:T(8,128)(2,1)} %pad_maximum_fusion.7), channel_id=1, source_target_pairs={{0,8},{1,9},{2,10},{3,11},{4,12},{5,13},{6,14},{7,15},{8,16},{9,17... | collective-permute-start | bytes 811016 | tf_op jit(solution)/shard_map/ppermute | solution.py:15
  166.8 19.5 %collective-permute-start.12 = (bf16[16,8448]{1,0:T(8,128)(2,1)}, bf16[16,8448]{1,0:T(8,128)(2,1)}, u32[]{:S(2)}, u32[]{:S(2)}) collective-permute-start(bf16[16,8448]{1,0:T(8,128)(2,1)} %pad_maximum_fusion.7), channel_id=1, source_target_pairs={{0,12},{1,13},{2,14},{3,15},{4,16},{5,17},{6,18},{7,19},{8,20},{9,... | collective-permute-start | bytes 811016 | tf_op jit(solution)/shard_map/ppermute | solution.py:15
  188.0 7.5 %collective-permute-start.15 = (bf16[16,8448]{1,0:T(8,128)(2,1)S(1)}, bf16[16,8448]{1,0:T(8,128)(2,1)S(1)}, u32[]{:S(2)}, u32[]{:S(2)}) collective-permute-start(bf16[16,8448]{1,0:T(8,128)(2,1)S(1)} %pad_maximum_fusion.8), channel_id=1, source_target_pairs={{0,16},{1,17},{2,18},{3,19},{4,20},{5,21},{6,22},{7,23},{8,24},{9,... | collective-permute-start | bytes 811016 | tf_op jit(solution)/shard_map/ppermute | solution.py:15
  221.5 14.1 %collective-permute-start.25 = (bf16[4,64,640]{2,1,0:T(8,128)(2,1)}, bf16[4,64,640]{2,1,0:T(8,128)(2,1)S(1)}, u32[]{:S(2)}, u32[]{:S(2)}) collective-permute-start(bf16[4,64,640]{2,1,0:T(8,128)(2,1)} %get-tuple-element.124), channel_id=1, source_target_pairs={{0,24},{1,25},{2,26},{3,27},{4,28},{5,29},{6,30},{7,31},{8,0},{9,1... | collective-permute-start | bytes 983048 | tf_op jit(solution)/shard_map/ppermute | solution.py:75
  225.5 18.3 %collective-permute-start.24 = (bf16[4,64,640]{2,1,0:T(8,128)(2,1)}, bf16[4,64,640]{2,1,0:T(8,128)(2,1)S(1)}, u32[]{:S(2)}, u32[]{:S(2)}) collective-permute-start(bf16[4,64,640]{2,1,0:T(8,128)(2,1)} %get-tuple-element.125), channel_id=1, source_target_pairs={{0,16},{1,17},{2,18},{3,19},{4,20},{5,21},{6,22},{7,23},{8,24},{9,... | collective-permute-start | bytes 983048 | tf_op jit(solution)/shard_map/ppermute | solution.py:75
  228.9 15.7 %collective-permute-start.23 = (bf16[4,64,640]{2,1,0:T(8,128)(2,1)}, bf16[4,64,640]{2,1,0:T(8,128)(2,1)}, u32[]{:S(2)}, u32[]{:S(2)}) collective-permute-start(bf16[4,64,640]{2,1,0:T(8,128)(2,1)} %get-tuple-element.123), channel_id=1, source_target_pairs={{0,8},{1,9},{2,10},{3,11},{4,12},{5,13},{6,14},{7,15},{8,16},{9,17... | collective-permute-start | bytes 983048 | tf_op jit(solution)/shard_map/ppermute | solution.py:75
  229.0 17.1 %collective-permute-start.19 = (bf16[4,64,640]{2,1,0:T(8,128)(2,1)S(1)}, bf16[4,64,640]{2,1,0:T(8,128)(2,1)S(1)}, u32[]{:S(2)}, u32[]{:S(2)}) collective-permute-start(bf16[4,64,640]{2,1,0:T(8,128)(2,1)S(1)} %get-tuple-element.122), channel_id=1, source_target_pairs={{0,6},{1,7},{2,0},{3,1},{4,2},{5,3},{6,4},{7,5},{8,14},{9,15},{10,... | collective-permute-start | bytes 983048 | tf_op jit(solution)/shard_map/ppermute | solution.py:75
  229.1 19.0 %collective-permute-start.18 = (bf16[4,64,640]{2,1,0:T(8,128)(2,1)S(1)}, bf16[4,64,640]{2,1,0:T(8,128)(2,1)S(1)}, u32[]{:S(2)}, u32[]{:S(2)}) collective-permute-start(bf16[4,64,640]{2,1,0:T(8,128)(2,1)S(1)} %get-tuple-element.121), channel_id=1, source_target_pairs={{0,4},{1,5},{2,6},{3,7},{4,0},{5,1},{6,2},{7,3},{8,12},{9,13},{10,... | collective-permute-start | bytes 983048 | tf_op jit(solution)/shard_map/ppermute | solution.py:75
  235.6 12.4 %collective-permute-start.17 = (bf16[4,64,640]{2,1,0:T(8,128)(2,1)S(1)}, bf16[4,64,640]{2,1,0:T(8,128)(2,1)S(1)}, u32[]{:S(2)}, u32[]{:S(2)}) collective-permute-start(bf16[4,64,640]{2,1,0:T(8,128)(2,1)S(1)} %get-tuple-element.120), channel_id=1, source_target_pairs={{0,2},{1,3},{2,4},{3,5},{4,6},{5,7},{6,0},{7,1},{8,10},{9,11},{10,... | collective-permute-start | bytes 983048 | tf_op jit(solution)/shard_map/ppermute | solution.py:75
  256.1 10.7 %collective-permute-start.35 = (f32[8,1280]{1,0:T(8,128)S(1)}, f32[8,1280]{1,0:T(8,128)S(1)}, u32[]{:S(2)}, u32[]{:S(2)}) collective-permute-start(f32[8,1280]{1,0:T(8,128)S(1)} %get-tuple-element.141), channel_id=1, source_target_pairs={{0,224},{32,0},{64,32},{96,64},{128,96},{160,128},{192,160},{224,1... | collective-permute-start | bytes 122888 | tf_op jit(solution)/shard_map/ppermute | solution.py:102
  259.5 10.9 %collective-permute-start.34 = (f32[8,1280]{1,0:T(8,128)S(1)}, f32[8,1280]{1,0:T(8,128)S(1)}, u32[]{:S(2)}, u32[]{:S(2)}) collective-permute-start(f32[8,1280]{1,0:T(8,128)S(1)} %get-tuple-element.142), channel_id=1, source_target_pairs={{0,192},{32,224},{64,0},{96,32},{128,64},{160,96},{192,128},{224,1... | collective-permute-start | bytes 122888 | tf_op jit(solution)/shard_map/ppermute | solution.py:102
  261.7 10.4 %collective-permute-start.33 = (f32[8,1280]{1,0:T(8,128)S(1)}, f32[8,1280]{1,0:T(8,128)S(1)}, u32[]{:S(2)}, u32[]{:S(2)}) collective-permute-start(f32[8,1280]{1,0:T(8,128)S(1)} %get-tuple-element.143), channel_id=1, source_target_pairs={{0,160},{32,192},{64,224},{96,0},{128,32},{160,64},{192,96},{224,1... | collective-permute-start | bytes 122888 | tf_op jit(solution)/shard_map/ppermute | solution.py:102
  262.9 9.3 %collective-permute-start.32 = (f32[8,1280]{1,0:T(8,128)S(1)}, f32[8,1280]{1,0:T(8,128)S(1)}, u32[]{:S(2)}, u32[]{:S(2)}) collective-permute-start(f32[8,1280]{1,0:T(8,128)S(1)} %get-tuple-element.144), channel_id=1, source_target_pairs={{0,128},{32,160},{64,192},{96,224},{128,0},{160,32},{192,64},{224,... | collective-permute-start | bytes 122888 | tf_op jit(solution)/shard_map/ppermute | solution.py:102
  275.6 15.0 %collective-permute-start.36 = (f32[8,1280]{1,0:T(8,128)S(1)}, f32[8,1280]{1,0:T(8,128)S(1)}, u32[]{:S(2)}, u32[]{:S(2)}) collective-permute-start(f32[8,1280]{1,0:T(8,128)S(1)} %get-tuple-element.94), channel_id=1, source_target_pairs={{0,32},{32,64},{64,96},{96,128},{128,160},{160,192},{192,224},{224... | collective-permute-start | bytes 122888 | tf_op jit(solution)/shard_map/ppermute | solution.py:106
  281.9 12.4 %collective-permute-start.37 = (f32[8,1280]{1,0:T(8,128)S(1)}, f32[8,1280]{1,0:T(8,128)S(1)}, u32[]{:S(2)}, u32[]{:S(2)}) collective-permute-start(f32[8,1280]{1,0:T(8,128)S(1)} %get-tuple-element.94), channel_id=1, source_target_pairs={{0,64},{32,96},{64,128},{96,160},{128,192},{160,224},{192,0},{224,... | collective-permute-start | bytes 122888 | tf_op jit(solution)/shard_map/ppermute | solution.py:106
  283.4 12.3 %collective-permute-start.38 = (f32[8,1280]{1,0:T(8,128)S(1)}, f32[8,1280]{1,0:T(8,128)S(1)}, u32[]{:S(2)}, u32[]{:S(2)}) collective-permute-start(f32[8,1280]{1,0:T(8,128)S(1)} %get-tuple-element.94), channel_id=1, source_target_pairs={{0,96},{32,128},{64,160},{96,192},{128,224},{160,0},{192,32},{224,... | collective-permute-start | bytes 122888 | tf_op jit(solution)/shard_map/ppermute | solution.py:106
  285.3 10.4 %collective-permute-start.39 = (f32[8,1280]{1,0:T(8,128)S(1)}, f32[8,1280]{1,0:T(8,128)S(1)}, u32[]{:S(2)}, u32[]{:S(2)}) collective-permute-start(f32[8,1280]{1,0:T(8,128)S(1)} %get-tuple-element.94), channel_id=1, source_target_pairs={{0,128},{32,160},{64,192},{96,224},{128,0},{160,32},{192,64},{224,... | collective-permute-start | bytes 122888 | tf_op jit(solution)/shard_map/ppermute | solution.py:106
  (26 other events, 379.1 us)
Sparse Core Ops, SparseCore 0:
  11.1 50.3 all-gather.2
  64.6 63.7 all-gather.4

commit v8 on v6

--- a/solution.py
+++ b/solution.py
@@ -184,7 +184,10 @@
     head_dim = hp_width // head_count
     proj_width = weight_codes.shape[1]
     state_width = (proj_width - hp_width) // 2
-    weights = lax.all_gather(dequantize(weight_codes, scales), "seq", axis=0, tiled=True)
+    local_weights = dequantize(weight_codes, scales)
+    seq_count = lax.axis_size("seq")
+    spread = jnp.broadcast_to(local_weights[None], (seq_count,) + local_weights.shape)
+    weights = lax.all_to_all(spread, "seq", 0, 0, tiled=False).reshape(-1, proj_width)
     projected = jnp.dot(features, weights, preferred_element_type=jnp.float32).astype(jnp.bfloat16)
     block_len = min(128, tok_count)
     block_count = tok_count // block_len

time: 270 us -> 275 us (1.019)
  between operations: 14.8 us -> 1.49 us
  starting transfers between devices: 104 us -> 115 us
  waiting for transfers between devices: 94.6 us -> 104 us
  other arithmetic: 17 us -> 13.6 us
    all_to_all x0 -> x1, waiting for transfers between devices: none -> 60.4 us  [local(): lax.all_to_all(spread, 'seq', 0, 0, tiled=False).reshape(-1, proj_width)]
    all_gather x1 -> x0, waiting for transfers between devices: 50.4 us -> none  [local(): lax.all_gather(dequantize(weight_codes, scales), 'seq', axis=0, tiled=True)]
    all_to_all x0 -> x1, starting transfers between devices: none -> 7.72 us  [local(): lax.all_to_all(spread, 'seq', 0, 0, tiled=False).reshape(-1, proj_width)]
    broadcast_in_dim x0 -> x1, local copies, waits for them, and re-layouts: none -> 2.94 us  [local(): jnp.broadcast_to(local_weights[None], (seq_count,) + local_weights.shape)]
  transfers between devices with their start and end apart: 44 -> 44, of which waited for: 19 -> 18; matrix products, arithmetic and copies ran while one was open for 7% -> 5% of each run, Pallas kernels for 0% -> 0%
where the time goes in v8:
time: 275 us; the launch traced here: 273 us
  starting transfers between devices  115 us (42%)
  waiting for transfers between devices  104 us (38%)
  local copies, waits for them, and re-layouts  21.6 us (8%)
  matrix products  17.2 us (6%)
  other arithmetic  13.6 us (5%)
    all_to_all x1, waiting for transfers between devices, local(): lax.all_to_all(spread, 'seq', 0, 0, tiled=False).reshape(-1, proj_width)  60.4 us
    ppermute x16, starting transfers between devices, shifted(): lax.ppermute(value.astype(jnp.bfloat16), axis, pairs).astype(value.dtype)  50.1 us
    ppermute x13, starting transfers between devices, digit_reduce(): got = lax.ppermute(piece.astype(jnp.bfloat16), axis, pairs)  24.8 us
    ppermute x13, waiting for transfers between devices, digit_reduce(): got = lax.ppermute(piece.astype(jnp.bfloat16), axis, pairs)  22.2 us
    ppermute x7, starting transfers between devices, replicated_sum(): total = total + lax.ppermute(piece, axis, pairs)  17.2 us
    ppermute x16, waiting for transfers between devices, shifted(): lax.ppermute(value.astype(jnp.bfloat16), axis, pairs).astype(value.dtype)  15.4 us
    ppermute x7, starting transfers between devices, replicated_sum(): gathered.append(lax.ppermute(total, axis, pairs))  15.2 us
    convert_element_type x1, local copies, waits for them, and re-layouts, local(): partial_grad = seq_reduce_scatter(lax.dot_general(features, d_proj, (((0,...  7.87 us
  transfers between devices with their start and end apart: 44, of which 18 were waited for; matrix products, arithmetic and copies ran while one was open for 5% of the time, Pallas kernels for 0%

profile of v8, /device:TPU:8, one launch (start us, length us, event | category | flops | bytes accessed | tf_op | source)
XLA Modules:
  0.0 273.1 jit_solution(4614985793865397176)
XLA Ops:
  2.7 2.9 %broadcast_in_dim.95 = bf16[32,64,1280]{2,1,0:T(8,128)(2,1)} broadcast(bf16[64,1280]{1,0:T(8,128)(2,1)S(1)} %fusion.41), dimensions={1,2} | broadcast | bytes 5406720 | tf_op jit(solution)/shard_map/broadcast_in_dim | solution.py:189
  5.7 7.7 %all-to-all-start = ((bf16[32,64,1280]{2,1,0:T(8,128)(2,1)}), bf16[32,64,1280]{2,1,0:T(8,128)(2,1)}, u32[]{:S(2)}, u32[]{:S(2)}) async-start(bf16[32,64,1280]{2,1,0:T(8,128)(2,1)} %broadcast_in_dim.95), calls=%async_computation | async-start | bytes 10485760 | tf_op jit(solution)/shard_map/all_to_all | solution.py:190
  15.4 60.4 %all-to-all-done = bf16[32,64,1280]{2,1,0:T(8,128)(2,1)} async-done(((bf16[32,64,1280]{2,1,0:T(8,128)(2,1)}), bf16[32,64,1280]{2,1,0:T(8,128)(2,1)}, u32[]{:S(2)}, u32[]{:S(2)}) %all-to-all-start) | async-done | bytes 5242912 | tf_op jit(solution)/shard_map/all_to_all | solution.py:190
  75.8 4.1 %fusion.1 = bf16[128,1280]{0,1:T(8,128)(2,1)S(1)} fusion(bf16[2048,1280]{1,0:T(8,128)(2,1)} %bitcast, bf16[1,128,2048]{2,1,0:T(8,128)(2,1)S(1)} %copy-done), kind=kOutput, calls=%fused_computation.7 | convolution fusion | flops 671252480 | bytes 6094848 | tf_op jit(solution)/shard_map/dot_general | solution.py:191
  84.8 4.3 %collective-permute-start.9 = (bf16[16,8448]{1,0:T(8,128)(2,1)S(1)}, bf16[16,8448]{1,0:T(8,128)(2,1)S(1)}, u32[]{:S(2)}, u32[]{:S(2)}) collective-permute-start(bf16[16,8448]{1,0:T(8,128)(2,1)S(1)} %get-tuple-element.155), channel_id=1, source_target_pairs={{0,2},{1,3},{2,4},{3,5},{4,6},{5,7},{6,8},{7,9},{8,10},{9,11},{10,... | collective-permute-start | bytes 811016 | tf_op jit(solution)/shard_map/ppermute | solution.py:15
  91.0 5.7 %collective-permute-start.11 = (bf16[16,8448]{1,0:T(8,128)(2,1)S(1)}, bf16[16,8448]{1,0:T(8,128)(2,1)S(1)}, u32[]{:S(2)}, u32[]{:S(2)}) collective-permute-start(bf16[16,8448]{1,0:T(8,128)(2,1)S(1)} %get-tuple-element.155), channel_id=1, source_target_pairs={{0,4},{1,5},{2,6},{3,7},{4,8},{5,9},{6,10},{7,11},{8,12},{9,13},{1... | collective-permute-start | bytes 811016 | tf_op jit(solution)/shard_map/ppermute | solution.py:15
  96.7 4.6 %collective-permute-start = (bf16[16,8448]{1,0:T(8,128)(2,1)S(1)}, bf16[16,8448]{1,0:T(8,128)(2,1)S(1)}, u32[]{:S(2)}, u32[]{:S(2)}) collective-permute-start(bf16[16,8448]{1,0:T(8,128)(2,1)S(1)} %get-tuple-element.154), channel_id=1, source_target_pairs={{1,0},{2,1},{3,2},{4,3},{5,4},{6,5},{7,6},{8,7},{9,8},{10,9},{11,1... | collective-permute-start | bytes 811016 | tf_op jit(solution)/shard_map/ppermute | solution.py:15
  102.5 2.5 collective-permute-start.1
  107.0 2.9 %collective-permute-start.3 = (bf16[16,8448]{1,0:T(8,128)(2,1)S(1)}, bf16[16,8448]{1,0:T(8,128)(2,1)S(1)}, u32[]{:S(2)}, u32[]{:S(2)}) collective-permute-start(bf16[16,8448]{1,0:T(8,128)(2,1)S(1)} %get-tuple-element.154), channel_id=1, source_target_pairs={{4,0},{5,1},{6,2},{7,3},{8,4},{9,5},{10,6},{11,7},{12,8},{13,9},{1... | collective-permute-start | bytes 811016 | tf_op jit(solution)/shard_map/ppermute | solution.py:15
  111.0 4.1 %collective-permute-start.14 = (bf16[16,8448]{1,0:T(8,128)(2,1)S(1)}, bf16[16,8448]{1,0:T(8,128)(2,1)S(1)}, u32[]{:S(2)}, u32[]{:S(2)}) collective-permute-start(bf16[16,8448]{1,0:T(8,128)(2,1)S(1)} %pad_maximum_fusion.7), channel_id=1, source_target_pairs={{0,4},{1,5},{2,6},{3,7},{4,8},{5,9},{6,10},{7,11},{8,12},{9,13},{1... | collective-permute-start | bytes 811016 | tf_op jit(solution)/shard_map/ppermute | solution.py:15
  115.1 3.2 %collective-permute-start.13 = (bf16[16,8448]{1,0:T(8,128)(2,1)S(1)}, bf16[16,8448]{1,0:T(8,128)(2,1)S(1)}, u32[]{:S(2)}, u32[]{:S(2)}) collective-permute-start(bf16[16,8448]{1,0:T(8,128)(2,1)S(1)} %pad_maximum_fusion.7), channel_id=1, source_target_pairs={{0,8},{1,9},{2,10},{3,11},{4,12},{5,13},{6,14},{7,15},{8,16},{9,17... | collective-permute-start | bytes 811016 | tf_op jit(solution)/shard_map/ppermute | solution.py:15
  118.4 4.7 %collective-permute-start.12 = (bf16[16,8448]{1,0:T(8,128)(2,1)S(1)}, bf16[16,8448]{1,0:T(8,128)(2,1)S(1)}, u32[]{:S(2)}, u32[]{:S(2)}) collective-permute-start(bf16[16,8448]{1,0:T(8,128)(2,1)S(1)} %pad_maximum_fusion.7), channel_id=1, source_target_pairs={{0,12},{1,13},{2,14},{3,15},{4,16},{5,17},{6,18},{7,19},{8,20},{9,... | collective-permute-start | bytes 811016 | tf_op jit(solution)/shard_map/ppermute | solution.py:15
  123.9 4.0 %collective-permute-start.6 = (bf16[16,8448]{1,0:T(8,128)(2,1)S(1)}, bf16[16,8448]{1,0:T(8,128)(2,1)S(1)}, u32[]{:S(2)}, u32[]{:S(2)}) collective-permute-start(bf16[16,8448]{1,0:T(8,128)(2,1)S(1)} %pad_maximum_fusion.5), channel_id=1, source_target_pairs={{4,0},{5,1},{6,2},{7,3},{8,4},{9,5},{10,6},{11,7},{12,8},{13,9},{1... | collective-permute-start | bytes 811016 | tf_op jit(solution)/shard_map/ppermute | solution.py:15
  131.2 5.4 %collective-permute-done.13 = bf16[16,8448]{1,0:T(8,128)(2,1)S(1)} collective-permute-done((bf16[16,8448]{1,0:T(8,128)(2,1)S(1)}, bf16[16,8448]{1,0:T(8,128)(2,1)S(1)}, u32[]{:S(2)}, u32[]{:S(2)}) %collective-permute-start.13) | collective-permute-done | bytes 270368 | tf_op jit(solution)/shard_map/ppermute | solution.py:15
  137.4 3.7 %collective-permute-start.15 = (bf16[16,8448]{1,0:T(8,128)(2,1)S(1)}, bf16[16,8448]{1,0:T(8,128)(2,1)S(1)}, u32[]{:S(2)}, u32[]{:S(2)}) collective-permute-start(bf16[16,8448]{1,0:T(8,128)(2,1)S(1)} %pad_maximum_fusion.8), channel_id=1, source_target_pairs={{0,16},{1,17},{2,18},{3,19},{4,20},{5,21},{6,22},{7,23},{8,24},{9,... | collective-permute-start | bytes 811016 | tf_op jit(solution)/shard_map/ppermute | solution.py:15
  144.8 3.7 %collective-permute-done.15 = bf16[16,8448]{1,0:T(8,128)(2,1)S(1)} collective-permute-done((bf16[16,8448]{1,0:T(8,128)(2,1)S(1)}, bf16[16,8448]{1,0:T(8,128)(2,1)S(1)}, u32[]{:S(2)}, u32[]{:S(2)}) %collective-permute-start.15) | collective-permute-done | bytes 270368 | tf_op jit(solution)/shard_map/ppermute | solution.py:15
  149.2 5.2 %collective-permute-done.7 = bf16[16,8448]{1,0:T(8,128)(2,1)} collective-permute-done((bf16[16,8448]{1,0:T(8,128)(2,1)}, bf16[16,8448]{1,0:T(8,128)(2,1)}, u32[]{:S(2)}, u32[]{:S(2)}) %collective-permute-start.7) | collective-permute-done | bytes 270368 | tf_op jit(solution)/shard_map/ppermute | solution.py:15
  158.7 3.9 %fusion = bf16[2048,1280]{0,1:T(8,128)(2,1)} fusion(bf16[1,128,2048]{2,1,0:T(8,128)(2,1)S(1)} %copy-done, bf16[128,128]{0,1:T(8,128)(2,1)S(1)} %fusion.8, bf16[128,128]{0,1:T(8,128)(2,1)S(1)} %fusion.7, bf16[128,1024]{0,1:T(8,128)(2,1)S(1)} %bitcast.228), kind=kOutput, calls=%fused_computation.2 | convolution fusion | flops 674693120 | bytes 6094848 | tf_op jit(solution)/shard_map/dot_general | solution.py:231
  162.5 7.9 %copy.68 = bf16[2048,1280]{1,0:T(8,128)(2,1)} copy(bf16[2048,1280]{0,1:T(8,128)(2,1)} %fusion) | data formatting | bytes 10485760 | tf_op jit(solution)/shard_map/convert_element_type | solution.py:233
  174.2 4.7 %collective-permute-done.16 = bf16[4,4,64,1280]{3,2,1,0:T(8,128)(2,1)} collective-permute-done((bf16[4,4,64,1280]{3,2,1,0:T(8,128)(2,1)S(1)}, bf16[4,4,64,1280]{3,2,1,0:T(8,128)(2,1)}, u32[]{:S(2)}, u32[]{:S(2)}) %collective-permute-start.16) | collective-permute-done | bytes 2621472 | tf_op jit(solution)/shard_map/ppermute | solution.py:71
  178.9 3.2 %convert_add_fusion = f32[4,4,64,1280]{3,2,1,0:T(8,128)S(1)} fusion(bf16[4,4,64,1280]{3,2,1,0:T(8,128)(2,1)} %collective-permute-done.16, bf16[4,4,2,64,1280]{4,3,2,1,0:T(8,128)(2,1)} %bitcast.226, s32[]{:T(128)S(6)} %select_n.216), kind=kLoop, calls=%fused_computation.3 | loop fusion | flops 3932160 | bytes 10485764 | tf_op jit(solution)/shard_map/add | solution.py:72
  185.0 2.8 %collective-permute-start.25 = (bf16[4,64,640]{2,1,0:T(8,128)(2,1)}, bf16[4,64,640]{2,1,0:T(8,128)(2,1)}, u32[]{:S(2)}, u32[]{:S(2)}) collective-permute-start(bf16[4,64,640]{2,1,0:T(8,128)(2,1)} %get-tuple-element.121), channel_id=1, source_target_pairs={{0,24},{1,25},{2,26},{3,27},{4,28},{5,29},{6,30},{7,31},{8,0},{9,1... | collective-permute-start | bytes 983048 | tf_op jit(solution)/shard_map/ppermute | solution.py:71
  189.4 6.9 %collective-permute-start.19 = (bf16[4,64,640]{2,1,0:T(8,128)(2,1)S(1)}, bf16[4,64,640]{2,1,0:T(8,128)(2,1)S(1)}, u32[]{:S(2)}, u32[]{:S(2)}) collective-permute-start(bf16[4,64,640]{2,1,0:T(8,128)(2,1)S(1)} %get-tuple-element.119), channel_id=1, source_target_pairs={{0,6},{1,7},{2,0},{3,1},{4,2},{5,3},{6,4},{7,5},{8,14},{9,15},{10,... | collective-permute-start | bytes 983048 | tf_op jit(solution)/shard_map/ppermute | solution.py:71
  196.4 6.0 %collective-permute-done.25 = bf16[4,64,640]{2,1,0:T(8,128)(2,1)} collective-permute-done((bf16[4,64,640]{2,1,0:T(8,128)(2,1)}, bf16[4,64,640]{2,1,0:T(8,128)(2,1)}, u32[]{:S(2)}, u32[]{:S(2)}) %collective-permute-start.25) | collective-permute-done | bytes 327712 | tf_op jit(solution)/shard_map/ppermute | solution.py:71
  205.8 8.5 %collective-permute-start.28 = (bf16[64,640]{1,0:T(8,128)(2,1)S(1)}, bf16[64,640]{1,0:T(8,128)(2,1)S(1)}, u32[]{:S(2)}, u32[]{:S(2)}) collective-permute-start(bf16[64,640]{1,0:T(8,128)(2,1)S(1)} %get-tuple-element.127), channel_id=1, source_target_pairs={{0,6},{1,7},{2,0},{3,1},{4,2},{5,3},{6,4},{7,5},{8,14},{9,15},{10,... | collective-permute-start | bytes 245768 | tf_op jit(solution)/shard_map/ppermute | solution.py:71
  215.4 4.4 %collective-permute-done.17 = bf16[4,64,640]{2,1,0:T(8,128)(2,1)S(1)} collective-permute-done((bf16[4,64,640]{2,1,0:T(8,128)(2,1)S(1)}, bf16[4,64,640]{2,1,0:T(8,128)(2,1)S(1)}, u32[]{:S(2)}, u32[]{:S(2)}) %collective-permute-start.17) | collective-permute-done | bytes 327712 | tf_op jit(solution)/shard_map/ppermute | solution.py:71
  227.5 5.9 %collective-permute-start.35 = (f32[8,1280]{1,0:T(8,128)S(1)}, f32[8,1280]{1,0:T(8,128)S(1)}, u32[]{:S(2)}, u32[]{:S(2)}) collective-permute-start(f32[8,1280]{1,0:T(8,128)S(1)} %get-tuple-element.140), channel_id=1, source_target_pairs={{0,224},{32,0},{64,32},{96,64},{128,96},{160,128},{192,160},{224,1... | collective-permute-start | bytes 122888 | tf_op jit(solution)/shard_map/ppermute | solution.py:98
  235.4 5.0 %collective-permute-start.32 = (f32[8,1280]{1,0:T(8,128)S(1)}, f32[8,1280]{1,0:T(8,128)S(1)}, u32[]{:S(2)}, u32[]{:S(2)}) collective-permute-start(f32[8,1280]{1,0:T(8,128)S(1)} %get-tuple-element.143), channel_id=1, source_target_pairs={{0,128},{32,160},{64,192},{96,224},{128,0},{160,32},{192,64},{224,... | collective-permute-start | bytes 122888 | tf_op jit(solution)/shard_map/ppermute | solution.py:98
  249.8 5.3 %convolution_bitcast_fusion = f32[1,128,2048]{2,1,0:T(8,128)} fusion(bf16[2048,1280]{1,0:T(8,128)(2,1)} %bitcast, bf16[128,128]{0,1:T(8,128)(2,1)S(1)} %fusion.8, bf16[128,128]{0,1:T(8,128)(2,1)S(1)} %fusion.7, bf16[128,1024]{0,1:T(8,128)(2,1)S(1)} %bitcast.229), kind=kOutput, calls=%fused_computation.5 | convolution fusion | flops 672071680 | bytes 6619136 | tf_op jit(solution)/shard_map/dot_general | solution.py:224
  258.6 2.6 collective-permute-start.39
  261.2 2.6 collective-permute-start.40
  263.8 3.8 %collective-permute-start.41 = (f32[8,1280]{1,0:T(8,128)S(1)}, f32[8,1280]{1,0:T(8,128)S(1)}, u32[]{:S(2)}, u32[]{:S(2)}) collective-permute-start(f32[8,1280]{1,0:T(8,128)S(1)} %get-tuple-element.76), channel_id=1, source_target_pairs={{0,192},{32,224},{64,0},{96,32},{128,64},{160,96},{192,128},{224,1... | collective-permute-start | bytes 122888 | tf_op jit(solution)/shard_map/ppermute | solution.py:102
  (181 shorter events, 68.9 us)
Async XLA Ops:
  5.7 70.1 %all-to-all-start = ((bf16[32,64,1280]{2,1,0:T(8,128)(2,1)}), bf16[32,64,1280]{2,1,0:T(8,128)(2,1)}, u32[]{:S(2)}, u32[]{:S(2)}) async-start(bf16[32,64,1280]{2,1,0:T(8,128)(2,1)} %broadcast_in_dim.95), calls=%async_computation | async-start | bytes 10485760 | tf_op jit(solution)/shard_map/all_to_all | solution.py:190
  82.8 19.7 %collective-permute-start.8 = (bf16[16,8448]{1,0:T(8,128)(2,1)S(1)}, bf16[16,8448]{1,0:T(8,128)(2,1)S(1)}, u32[]{:S(2)}, u32[]{:S(2)}) collective-permute-start(bf16[16,8448]{1,0:T(8,128)(2,1)S(1)} %get-tuple-element.155), channel_id=1, source_target_pairs={{0,1},{1,2},{2,3},{3,4},{4,5},{5,6},{6,7},{7,8},{8,9},{9,10},{10,1... | collective-permute-start | bytes 811016 | tf_op jit(solution)/shard_map/ppermute | solution.py:15
  84.8 20.3 %collective-permute-start.9 = (bf16[16,8448]{1,0:T(8,128)(2,1)S(1)}, bf16[16,8448]{1,0:T(8,128)(2,1)S(1)}, u32[]{:S(2)}, u32[]{:S(2)}) collective-permute-start(bf16[16,8448]{1,0:T(8,128)(2,1)S(1)} %get-tuple-element.155), channel_id=1, source_target_pairs={{0,2},{1,3},{2,4},{3,5},{4,6},{5,7},{6,8},{7,9},{8,10},{9,11},{10,... | collective-permute-start | bytes 811016 | tf_op jit(solution)/shard_map/ppermute | solution.py:15
  89.1 17.9 %collective-permute-start.10 = (bf16[16,8448]{1,0:T(8,128)(2,1)S(1)}, bf16[16,8448]{1,0:T(8,128)(2,1)S(1)}, u32[]{:S(2)}, u32[]{:S(2)}) collective-permute-start(bf16[16,8448]{1,0:T(8,128)(2,1)S(1)} %get-tuple-element.155), channel_id=1, source_target_pairs={{0,3},{1,4},{2,5},{3,6},{4,7},{5,8},{6,9},{7,10},{8,11},{9,12},{10... | collective-permute-start | bytes 811016 | tf_op jit(solution)/shard_map/ppermute | solution.py:15
  91.0 19.3 %collective-permute-start.11 = (bf16[16,8448]{1,0:T(8,128)(2,1)S(1)}, bf16[16,8448]{1,0:T(8,128)(2,1)S(1)}, u32[]{:S(2)}, u32[]{:S(2)}) collective-permute-start(bf16[16,8448]{1,0:T(8,128)(2,1)S(1)} %get-tuple-element.155), channel_id=1, source_target_pairs={{0,4},{1,5},{2,6},{3,7},{4,8},{5,9},{6,10},{7,11},{8,12},{9,13},{1... | collective-permute-start | bytes 811016 | tf_op jit(solution)/shard_map/ppermute | solution.py:15
  96.7 18.4 %collective-permute-start = (bf16[16,8448]{1,0:T(8,128)(2,1)S(1)}, bf16[16,8448]{1,0:T(8,128)(2,1)S(1)}, u32[]{:S(2)}, u32[]{:S(2)}) collective-permute-start(bf16[16,8448]{1,0:T(8,128)(2,1)S(1)} %get-tuple-element.154), channel_id=1, source_target_pairs={{1,0},{2,1},{3,2},{4,3},{5,4},{6,5},{7,6},{8,7},{9,8},{10,9},{11,1... | collective-permute-start | bytes 811016 | tf_op jit(solution)/shard_map/ppermute | solution.py:15
  102.5 15.9 %collective-permute-start.1 = (bf16[16,8448]{1,0:T(8,128)(2,1)S(1)}, bf16[16,8448]{1,0:T(8,128)(2,1)S(1)}, u32[]{:S(2)}, u32[]{:S(2)}) collective-permute-start(bf16[16,8448]{1,0:T(8,128)(2,1)S(1)} %get-tuple-element.154), channel_id=1, source_target_pairs={{2,0},{3,1},{4,2},{5,3},{6,4},{7,5},{8,6},{9,7},{10,8},{11,9},{12,... | collective-permute-start | bytes 811016 | tf_op jit(solution)/shard_map/ppermute | solution.py:15
  105.0 18.1 %collective-permute-start.2 = (bf16[16,8448]{1,0:T(8,128)(2,1)S(1)}, bf16[16,8448]{1,0:T(8,128)(2,1)S(1)}, u32[]{:S(2)}, u32[]{:S(2)}) collective-permute-start(bf16[16,8448]{1,0:T(8,128)(2,1)S(1)} %get-tuple-element.154), channel_id=1, source_target_pairs={{3,0},{4,1},{5,2},{6,3},{7,4},{8,5},{9,6},{10,7},{11,8},{12,9},{13... | collective-permute-start | bytes 811016 | tf_op jit(solution)/shard_map/ppermute | solution.py:15
  107.0 16.2 %collective-permute-start.3 = (bf16[16,8448]{1,0:T(8,128)(2,1)S(1)}, bf16[16,8448]{1,0:T(8,128)(2,1)S(1)}, u32[]{:S(2)}, u32[]{:S(2)}) collective-permute-start(bf16[16,8448]{1,0:T(8,128)(2,1)S(1)} %get-tuple-element.154), channel_id=1, source_target_pairs={{4,0},{5,1},{6,2},{7,3},{8,4},{9,5},{10,6},{11,7},{12,8},{13,9},{1... | collective-permute-start | bytes 811016 | tf_op jit(solution)/shard_map/ppermute | solution.py:15
  111.0 18.8 %collective-permute-start.14 = (bf16[16,8448]{1,0:T(8,128)(2,1)S(1)}, bf16[16,8448]{1,0:T(8,128)(2,1)S(1)}, u32[]{:S(2)}, u32[]{:S(2)}) collective-permute-start(bf16[16,8448]{1,0:T(8,128)(2,1)S(1)} %pad_maximum_fusion.7), channel_id=1, source_target_pairs={{0,4},{1,5},{2,6},{3,7},{4,8},{5,9},{6,10},{7,11},{8,12},{9,13},{1... | collective-permute-start | bytes 811016 | tf_op jit(solution)/shard_map/ppermute | solution.py:15
  115.1 21.5 %collective-permute-start.13 = (bf16[16,8448]{1,0:T(8,128)(2,1)S(1)}, bf16[16,8448]{1,0:T(8,128)(2,1)S(1)}, u32[]{:S(2)}, u32[]{:S(2)}) collective-permute-start(bf16[16,8448]{1,0:T(8,128)(2,1)S(1)} %pad_maximum_fusion.7), channel_id=1, source_target_pairs={{0,8},{1,9},{2,10},{3,11},{4,12},{5,13},{6,14},{7,15},{8,16},{9,17... | collective-permute-start | bytes 811016 | tf_op jit(solution)/shard_map/ppermute | solution.py:15
  118.4 18.2 %collective-permute-start.12 = (bf16[16,8448]{1,0:T(8,128)(2,1)S(1)}, bf16[16,8448]{1,0:T(8,128)(2,1)S(1)}, u32[]{:S(2)}, u32[]{:S(2)}) collective-permute-start(bf16[16,8448]{1,0:T(8,128)(2,1)S(1)} %pad_maximum_fusion.7), channel_id=1, source_target_pairs={{0,12},{1,13},{2,14},{3,15},{4,16},{5,17},{6,18},{7,19},{8,20},{9,... | collective-permute-start | bytes 811016 | tf_op jit(solution)/shard_map/ppermute | solution.py:15
  123.9 17.2 %collective-permute-start.6 = (bf16[16,8448]{1,0:T(8,128)(2,1)S(1)}, bf16[16,8448]{1,0:T(8,128)(2,1)S(1)}, u32[]{:S(2)}, u32[]{:S(2)}) collective-permute-start(bf16[16,8448]{1,0:T(8,128)(2,1)S(1)} %pad_maximum_fusion.5), channel_id=1, source_target_pairs={{4,0},{5,1},{6,2},{7,3},{8,4},{9,5},{10,6},{11,7},{12,8},{13,9},{1... | collective-permute-start | bytes 811016 | tf_op jit(solution)/shard_map/ppermute | solution.py:15
  127.9 13.3 %collective-permute-start.5 = (bf16[16,8448]{1,0:T(8,128)(2,1)S(1)}, bf16[16,8448]{1,0:T(8,128)(2,1)S(1)}, u32[]{:S(2)}, u32[]{:S(2)}) collective-permute-start(bf16[16,8448]{1,0:T(8,128)(2,1)S(1)} %pad_maximum_fusion.5), channel_id=1, source_target_pairs={{8,0},{9,1},{10,2},{11,3},{12,4},{13,5},{14,6},{15,7},{16,8},{17,9... | collective-permute-start | bytes 811016 | tf_op jit(solution)/shard_map/ppermute | solution.py:15
  129.8 12.1 %collective-permute-start.4 = (bf16[16,8448]{1,0:T(8,128)(2,1)S(1)}, bf16[16,8448]{1,0:T(8,128)(2,1)S(1)}, u32[]{:S(2)}, u32[]{:S(2)}) collective-permute-start(bf16[16,8448]{1,0:T(8,128)(2,1)S(1)} %pad_maximum_fusion.5), channel_id=1, source_target_pairs={{12,0},{13,1},{14,2},{15,3},{16,4},{17,5},{18,6},{19,7},{20,8},{21... | collective-permute-start | bytes 811016 | tf_op jit(solution)/shard_map/ppermute | solution.py:15
  137.4 11.1 %collective-permute-start.15 = (bf16[16,8448]{1,0:T(8,128)(2,1)S(1)}, bf16[16,8448]{1,0:T(8,128)(2,1)S(1)}, u32[]{:S(2)}, u32[]{:S(2)}) collective-permute-start(bf16[16,8448]{1,0:T(8,128)(2,1)S(1)} %pad_maximum_fusion.8), channel_id=1, source_target_pairs={{0,16},{1,17},{2,18},{3,19},{4,20},{5,21},{6,22},{7,23},{8,24},{9,... | collective-permute-start | bytes 811016 | tf_op jit(solution)/shard_map/ppermute | solution.py:15
  143.3 11.1 %collective-permute-start.7 = (bf16[16,8448]{1,0:T(8,128)(2,1)}, bf16[16,8448]{1,0:T(8,128)(2,1)}, u32[]{:S(2)}, u32[]{:S(2)}) collective-permute-start(bf16[16,8448]{1,0:T(8,128)(2,1)} %pad_maximum_fusion.6), channel_id=1, source_target_pairs={{16,0},{17,1},{18,2},{19,3},{20,4},{21,5},{22,6},{23,7},{24,8},{25... | collective-permute-start | bytes 811016 | tf_op jit(solution)/shard_map/ppermute | solution.py:15
  185.0 17.3 %collective-permute-start.25 = (bf16[4,64,640]{2,1,0:T(8,128)(2,1)}, bf16[4,64,640]{2,1,0:T(8,128)(2,1)}, u32[]{:S(2)}, u32[]{:S(2)}) collective-permute-start(bf16[4,64,640]{2,1,0:T(8,128)(2,1)} %get-tuple-element.121), channel_id=1, source_target_pairs={{0,24},{1,25},{2,26},{3,27},{4,28},{5,29},{6,30},{7,31},{8,0},{9,1... | collective-permute-start | bytes 983048 | tf_op jit(solution)/shard_map/ppermute | solution.py:71
  187.8 14.6 %collective-permute-start.24 = (bf16[4,64,640]{2,1,0:T(8,128)(2,1)}, bf16[4,64,640]{2,1,0:T(8,128)(2,1)}, u32[]{:S(2)}, u32[]{:S(2)}) collective-permute-start(bf16[4,64,640]{2,1,0:T(8,128)(2,1)} %get-tuple-element.122), channel_id=1, source_target_pairs={{0,16},{1,17},{2,18},{3,19},{4,20},{5,21},{6,22},{7,23},{8,24},{9,... | collective-permute-start | bytes 983048 | tf_op jit(solution)/shard_map/ppermute | solution.py:71
  187.8 16.4 %collective-permute-start.23 = (bf16[4,64,640]{2,1,0:T(8,128)(2,1)}, bf16[4,64,640]{2,1,0:T(8,128)(2,1)}, u32[]{:S(2)}, u32[]{:S(2)}) collective-permute-start(bf16[4,64,640]{2,1,0:T(8,128)(2,1)} %get-tuple-element.120), channel_id=1, source_target_pairs={{0,8},{1,9},{2,10},{3,11},{4,12},{5,13},{6,14},{7,15},{8,16},{9,17... | collective-permute-start | bytes 983048 | tf_op jit(solution)/shard_map/ppermute | solution.py:71
  189.4 24.9 %collective-permute-start.19 = (bf16[4,64,640]{2,1,0:T(8,128)(2,1)S(1)}, bf16[4,64,640]{2,1,0:T(8,128)(2,1)S(1)}, u32[]{:S(2)}, u32[]{:S(2)}) collective-permute-start(bf16[4,64,640]{2,1,0:T(8,128)(2,1)S(1)} %get-tuple-element.119), channel_id=1, source_target_pairs={{0,6},{1,7},{2,0},{3,1},{4,2},{5,3},{6,4},{7,5},{8,14},{9,15},{10,... | collective-permute-start | bytes 983048 | tf_op jit(solution)/shard_map/ppermute | solution.py:71
  196.4 19.0 %collective-permute-start.18 = (bf16[4,64,640]{2,1,0:T(8,128)(2,1)S(1)}, bf16[4,64,640]{2,1,0:T(8,128)(2,1)S(1)}, u32[]{:S(2)}, u32[]{:S(2)}) collective-permute-start(bf16[4,64,640]{2,1,0:T(8,128)(2,1)S(1)} %get-tuple-element.118), channel_id=1, source_target_pairs={{0,4},{1,5},{2,6},{3,7},{4,0},{5,1},{6,2},{7,3},{8,12},{9,13},{10,... | collective-permute-start | bytes 983048 | tf_op jit(solution)/shard_map/ppermute | solution.py:71
  202.4 17.4 %collective-permute-start.17 = (bf16[4,64,640]{2,1,0:T(8,128)(2,1)S(1)}, bf16[4,64,640]{2,1,0:T(8,128)(2,1)S(1)}, u32[]{:S(2)}, u32[]{:S(2)}) collective-permute-start(bf16[4,64,640]{2,1,0:T(8,128)(2,1)S(1)} %get-tuple-element.117), channel_id=1, source_target_pairs={{0,2},{1,3},{2,4},{3,5},{4,6},{5,7},{6,0},{7,1},{8,10},{9,11},{10,... | collective-permute-start | bytes 983048 | tf_op jit(solution)/shard_map/ppermute | solution.py:71
  205.8 14.4 %collective-permute-start.28 = (bf16[64,640]{1,0:T(8,128)(2,1)S(1)}, bf16[64,640]{1,0:T(8,128)(2,1)S(1)}, u32[]{:S(2)}, u32[]{:S(2)}) collective-permute-start(bf16[64,640]{1,0:T(8,128)(2,1)S(1)} %get-tuple-element.127), channel_id=1, source_target_pairs={{0,6},{1,7},{2,0},{3,1},{4,2},{5,3},{6,4},{7,5},{8,14},{9,15},{10,... | collective-permute-start | bytes 245768 | tf_op jit(solution)/shard_map/ppermute | solution.py:71
  227.5 12.9 %collective-permute-start.35 = (f32[8,1280]{1,0:T(8,128)S(1)}, f32[8,1280]{1,0:T(8,128)S(1)}, u32[]{:S(2)}, u32[]{:S(2)}) collective-permute-start(f32[8,1280]{1,0:T(8,128)S(1)} %get-tuple-element.140), channel_id=1, source_target_pairs={{0,224},{32,0},{64,32},{96,64},{128,96},{160,128},{192,160},{224,1... | collective-permute-start | bytes 122888 | tf_op jit(solution)/shard_map/ppermute | solution.py:98
  233.5 9.4 %collective-permute-start.34 = (f32[8,1280]{1,0:T(8,128)S(1)}, f32[8,1280]{1,0:T(8,128)S(1)}, u32[]{:S(2)}, u32[]{:S(2)}) collective-permute-start(f32[8,1280]{1,0:T(8,128)S(1)} %get-tuple-element.141), channel_id=1, source_target_pairs={{0,192},{32,224},{64,0},{96,32},{128,64},{160,96},{192,128},{224,1... | collective-permute-start | bytes 122888 | tf_op jit(solution)/shard_map/ppermute | solution.py:98
  234.9 10.1 %collective-permute-start.33 = (f32[8,1280]{1,0:T(8,128)S(1)}, f32[8,1280]{1,0:T(8,128)S(1)}, u32[]{:S(2)}, u32[]{:S(2)}) collective-permute-start(f32[8,1280]{1,0:T(8,128)S(1)} %get-tuple-element.142), channel_id=1, source_target_pairs={{0,160},{32,192},{64,224},{96,0},{128,32},{160,64},{192,96},{224,1... | collective-permute-start | bytes 122888 | tf_op jit(solution)/shard_map/ppermute | solution.py:98
  235.4 9.5 %collective-permute-start.32 = (f32[8,1280]{1,0:T(8,128)S(1)}, f32[8,1280]{1,0:T(8,128)S(1)}, u32[]{:S(2)}, u32[]{:S(2)}) collective-permute-start(f32[8,1280]{1,0:T(8,128)S(1)} %get-tuple-element.143), channel_id=1, source_target_pairs={{0,128},{32,160},{64,192},{96,224},{128,0},{160,32},{192,64},{224,... | collective-permute-start | bytes 122888 | tf_op jit(solution)/shard_map/ppermute | solution.py:98
  248.8 15.0 %collective-permute-start.36 = (f32[8,1280]{1,0:T(8,128)S(1)}, f32[8,1280]{1,0:T(8,128)S(1)}, u32[]{:S(2)}, u32[]{:S(2)}) collective-permute-start(f32[8,1280]{1,0:T(8,128)S(1)} %get-tuple-element.76), channel_id=1, source_target_pairs={{0,32},{32,64},{64,96},{96,128},{128,160},{160,192},{192,224},{224... | collective-permute-start | bytes 122888 | tf_op jit(solution)/shard_map/ppermute | solution.py:102
  255.1 12.6 %collective-permute-start.37 = (f32[8,1280]{1,0:T(8,128)S(1)}, f32[8,1280]{1,0:T(8,128)S(1)}, u32[]{:S(2)}, u32[]{:S(2)}) collective-permute-start(f32[8,1280]{1,0:T(8,128)S(1)} %get-tuple-element.76), channel_id=1, source_target_pairs={{0,64},{32,96},{64,128},{96,160},{128,192},{160,224},{192,0},{224,... | collective-permute-start | bytes 122888 | tf_op jit(solution)/shard_map/ppermute | solution.py:102
  256.9 12.4 %collective-permute-start.38 = (f32[8,1280]{1,0:T(8,128)S(1)}, f32[8,1280]{1,0:T(8,128)S(1)}, u32[]{:S(2)}, u32[]{:S(2)}) collective-permute-start(f32[8,1280]{1,0:T(8,128)S(1)} %get-tuple-element.76), channel_id=1, source_target_pairs={{0,96},{32,128},{64,160},{96,192},{128,224},{160,0},{192,32},{224,... | collective-permute-start | bytes 122888 | tf_op jit(solution)/shard_map/ppermute | solution.py:102
  258.6 10.7 %collective-permute-start.39 = (f32[8,1280]{1,0:T(8,128)S(1)}, f32[8,1280]{1,0:T(8,128)S(1)}, u32[]{:S(2)}, u32[]{:S(2)}) collective-permute-start(f32[8,1280]{1,0:T(8,128)S(1)} %get-tuple-element.76), channel_id=1, source_target_pairs={{0,128},{32,160},{64,192},{96,224},{128,0},{160,32},{192,64},{224,... | collective-permute-start | bytes 122888 | tf_op jit(solution)/shard_map/ppermute | solution.py:102
  (20 other events, 378.9 us)

commit v9 on v6

--- a/solution.py
+++ b/solution.py
@@ -4,6 +4,8 @@
 import jax.numpy as jnp
 from jax import lax
 from jax.sharding import PartitionSpec as P
+from jax.experimental import pallas as pl
+from jax.experimental.pallas import tpu as pltpu
 
 
 def shifted(value, axis, step, reverse):
@@ -103,6 +105,33 @@
     stacked = jnp.stack(gathered)
     order = (me - jnp.arange(count)) % count
     return jnp.take(stacked, order, axis=0).reshape(value.shape)
+
+
+def outer_kernel(left_ref, right_ref, out_ref):
+    out_ref[...] = lax.dot_general(
+        left_ref[...], right_ref[...], (((0,), (0,)), ((), ())), preferred_element_type=jnp.float32
+    ).astype(out_ref.dtype)
+
+
+def outer_product(left, right):
+    depth, rows = left.shape
+    cols = right.shape[1]
+    tile = 256
+    return pl.pallas_call(
+        outer_kernel,
+        grid=(rows // tile,),
+        in_specs=[
+            pl.BlockSpec((depth, tile), lambda i: (0, i)),
+            pl.BlockSpec((depth, cols), lambda i: (0, 0)),
+        ],
+        out_specs=pl.BlockSpec((tile, cols), lambda i: (i, 0)),
+        out_shape=jax.ShapeDtypeStruct((rows, cols), jnp.bfloat16),
+        cost_estimate=pl.CostEstimate(
+            flops=2 * depth * rows * cols,
+            bytes_accessed=2 * (depth * rows + depth * cols + rows * cols),
+            transcendentals=0,
+        ),
+    )(left, right)
 
 
 def dequantize(code_rows, scale_rows):
@@ -225,9 +254,7 @@
     group_count = lax.axis_size("dp")
     norm_factor = 1.0 / math.sqrt(group_count * seq_count * tok_count)
     partial_grad = seq_reduce_scatter(
-        lax.dot_general(
-            features, d_proj, (((0,), (0,)), ((), ())), preferred_element_type=jnp.float32
-        ).astype(jnp.bfloat16),
+        outer_product(features, d_proj),
         "seq",
     )
     summed_grad = replicated_sum(partial_grad, "dp")

time: 270 us -> 266 us (0.985)
  local copies, waits for them, and re-layouts: 19.6 us -> 11.9 us
  Pallas kernels: 0 us -> 6.94 us
  starting transfers between devices: 104 us -> 109 us
  matrix products: 17.2 us -> 12.8 us
    convert_element_type x1 -> x0, local copies, waits for them, and re-layouts: 7.87 us -> none  [local(): partial_grad = seq_reduce_scatter(lax.dot_general(features, d_proj, (((0,...]
    pallas_call x0 -> x1, Pallas kernels: none -> 6.94 us  [outer_product(): pl.pallas_call(outer_kernel, grid=(rows // tile,), in_specs=[pl.BlockSpec...]
    ppermute x13, starting transfers between devices: 24.1 us -> 29.4 us  [digit_reduce(): got = lax.ppermute(piece.astype(jnp.bfloat16), axis, pairs)]
    dot_general x1 -> x0, matrix products: 3.88 us -> none  [local(): lax.dot_general(features, d_proj, (((0,), (0,)), ((), ())), preferred_ele...]
  transfers between devices with their start and end apart: 44 -> 44, of which waited for: 19 -> 18; matrix products, arithmetic and copies ran while one was open for 7% -> 7% of each run, Pallas kernels for 0% -> 0%
where the time goes in v9:
time: 266 us; the launch traced here: 264 us
  starting transfers between devices  109 us (41%)
  waiting for transfers between devices  93.2 us (35%)
  between operations  14.8 us (6%)
  other arithmetic  14.7 us (6%)
  matrix products  12.8 us (5%)
  local copies, waits for them, and re-layouts  11.9 us (4%)
  Pallas kernels  6.94 us (3%)
    all_gather x1, waiting for transfers between devices, local(): lax.all_gather(dequantize(weight_codes, scales), 'seq', axis=0, tiled=True)  51.1 us
    ppermute x16, starting transfers between devices, shifted(): lax.ppermute(value.astype(jnp.bfloat16), axis, pairs).astype(value.dtype)  49.8 us
    ppermute x13, starting transfers between devices, digit_reduce(): got = lax.ppermute(piece.astype(jnp.bfloat16), axis, pairs)  29.4 us
    ppermute x13, waiting for transfers between devices, digit_reduce(): got = lax.ppermute(piece.astype(jnp.bfloat16), axis, pairs)  20.4 us
    ppermute x7, starting transfers between devices, replicated_sum(): total = total + lax.ppermute(piece, axis, pairs)  15.8 us
    ppermute x16, waiting for transfers between devices, shifted(): lax.ppermute(value.astype(jnp.bfloat16), axis, pairs).astype(value.dtype)  15.4 us
    ppermute x7, starting transfers between devices, replicated_sum(): gathered.append(lax.ppermute(total, axis, pairs))  14.4 us
    pallas_call x1, Pallas kernels, outer_product(): pl.pallas_call(outer_kernel, grid=(rows // tile,), in_specs=[pl.BlockSpec...  6.94 us
  transfers between devices with their start and end apart: 44, of which 18 were waited for; matrix products, arithmetic and copies ran while one was open for 7% of the time, Pallas kernels for 0%

profile of v9, /device:TPU:8, one launch (start us, length us, event | category | flops | bytes accessed | tf_op | source)
XLA Modules:
  0.0 263.7 jit_solution(15703342001939519150)
XLA Ops:
  15.1 51.1 %all-gather.2.cloned.1.call-done = bf16[2048,1280]{1,0:T(8,128)(2,1)} async-done(((bf16[64,1280]{1,0:T(8,128)(2,1)}), bf16[2048,1280]{1,0:T(8,128)(2,1)}) %all-gather.2.cloned.1.call-update) | async-done | bytes 5242896 | tf_op jit(solution)/shard_map/all_gather | solution.py:216
  66.1 4.2 %fusion = bf16[128,1280]{0,1:T(8,128)(2,1)S(1)} fusion(bf16[2048,1280]{1,0:T(8,128)(2,1)} %all-gather.2.cloned.1.call-done, bf16[1,128,2048]{2,1,0:T(8,128)(2,1)} %param.5), kind=kOutput, calls=%fused_computation.5 | convolution fusion | flops 671252480 | bytes 6094848 | tf_op jit(solution)/shard_map/dot_general | solution.py:217
  76.9 3.7 %collective-permute-start.10 = (bf16[16,8448]{1,0:T(8,128)(2,1)S(1)}, bf16[16,8448]{1,0:T(8,128)(2,1)S(1)}, u32[]{:S(2)}, u32[]{:S(2)}) collective-permute-start(bf16[16,8448]{1,0:T(8,128)(2,1)S(1)} %get-tuple-element.155), channel_id=1, source_target_pairs={{0,3},{1,4},{2,5},{3,6},{4,7},{5,8},{6,9},{7,10},{8,11},{9,12},{10... | collective-permute-start | bytes 811016 | tf_op jit(solution)/shard_map/ppermute | solution.py:17
  80.6 4.7 %collective-permute-start.11 = (bf16[16,8448]{1,0:T(8,128)(2,1)S(1)}, bf16[16,8448]{1,0:T(8,128)(2,1)S(1)}, u32[]{:S(2)}, u32[]{:S(2)}) collective-permute-start(bf16[16,8448]{1,0:T(8,128)(2,1)S(1)} %get-tuple-element.155), channel_id=1, source_target_pairs={{0,4},{1,5},{2,6},{3,7},{4,8},{5,9},{6,10},{7,11},{8,12},{9,13},{1... | collective-permute-start | bytes 811016 | tf_op jit(solution)/shard_map/ppermute | solution.py:17
  85.3 4.3 %collective-permute-start = (bf16[16,8448]{1,0:T(8,128)(2,1)S(1)}, bf16[16,8448]{1,0:T(8,128)(2,1)S(1)}, u32[]{:S(2)}, u32[]{:S(2)}) collective-permute-start(bf16[16,8448]{1,0:T(8,128)(2,1)S(1)} %get-tuple-element.154), channel_id=1, source_target_pairs={{1,0},{2,1},{3,2},{4,3},{5,4},{6,5},{7,6},{8,7},{9,8},{10,9},{11,1... | collective-permute-start | bytes 811016 | tf_op jit(solution)/shard_map/ppermute | solution.py:17
  90.8 2.2 collective-permute-start.1
  95.1 3.0 %collective-permute-start.3 = (bf16[16,8448]{1,0:T(8,128)(2,1)S(1)}, bf16[16,8448]{1,0:T(8,128)(2,1)S(1)}, u32[]{:S(2)}, u32[]{:S(2)}) collective-permute-start(bf16[16,8448]{1,0:T(8,128)(2,1)S(1)} %get-tuple-element.154), channel_id=1, source_target_pairs={{4,0},{5,1},{6,2},{7,3},{8,4},{9,5},{10,6},{11,7},{12,8},{13,9},{1... | collective-permute-start | bytes 811016 | tf_op jit(solution)/shard_map/ppermute | solution.py:17
  100.3 2.8 %collective-permute-start.14 = (bf16[16,8448]{1,0:T(8,128)(2,1)S(1)}, bf16[16,8448]{1,0:T(8,128)(2,1)S(1)}, u32[]{:S(2)}, u32[]{:S(2)}) collective-permute-start(bf16[16,8448]{1,0:T(8,128)(2,1)S(1)} %pad_maximum_fusion.7), channel_id=1, source_target_pairs={{0,4},{1,5},{2,6},{3,7},{4,8},{5,9},{6,10},{7,11},{8,12},{9,13},{1... | collective-permute-start | bytes 811016 | tf_op jit(solution)/shard_map/ppermute | solution.py:17
  103.2 3.9 %collective-permute-start.13 = (bf16[16,8448]{1,0:T(8,128)(2,1)S(1)}, bf16[16,8448]{1,0:T(8,128)(2,1)S(1)}, u32[]{:S(2)}, u32[]{:S(2)}) collective-permute-start(bf16[16,8448]{1,0:T(8,128)(2,1)S(1)} %pad_maximum_fusion.7), channel_id=1, source_target_pairs={{0,8},{1,9},{2,10},{3,11},{4,12},{5,13},{6,14},{7,15},{8,16},{9,17... | collective-permute-start | bytes 811016 | tf_op jit(solution)/shard_map/ppermute | solution.py:17
  107.2 5.6 %collective-permute-start.12 = (bf16[16,8448]{1,0:T(8,128)(2,1)S(1)}, bf16[16,8448]{1,0:T(8,128)(2,1)S(1)}, u32[]{:S(2)}, u32[]{:S(2)}) collective-permute-start(bf16[16,8448]{1,0:T(8,128)(2,1)S(1)} %pad_maximum_fusion.7), channel_id=1, source_target_pairs={{0,12},{1,13},{2,14},{3,15},{4,16},{5,17},{6,18},{7,19},{8,20},{9,... | collective-permute-start | bytes 811016 | tf_op jit(solution)/shard_map/ppermute | solution.py:17
  113.6 4.0 %collective-permute-start.6 = (bf16[16,8448]{1,0:T(8,128)(2,1)S(1)}, bf16[16,8448]{1,0:T(8,128)(2,1)S(1)}, u32[]{:S(2)}, u32[]{:S(2)}) collective-permute-start(bf16[16,8448]{1,0:T(8,128)(2,1)S(1)} %pad_maximum_fusion.5), channel_id=1, source_target_pairs={{4,0},{5,1},{6,2},{7,3},{8,4},{9,5},{10,6},{11,7},{12,8},{13,9},{1... | collective-permute-start | bytes 811016 | tf_op jit(solution)/shard_map/ppermute | solution.py:17
  120.9 4.2 %collective-permute-done.13 = bf16[16,8448]{1,0:T(8,128)(2,1)S(1)} collective-permute-done((bf16[16,8448]{1,0:T(8,128)(2,1)S(1)}, bf16[16,8448]{1,0:T(8,128)(2,1)S(1)}, u32[]{:S(2)}, u32[]{:S(2)}) %collective-permute-start.13) | collective-permute-done | bytes 270368 | tf_op jit(solution)/shard_map/ppermute | solution.py:17
  125.8 4.8 %collective-permute-start.15 = (bf16[16,8448]{1,0:T(8,128)(2,1)S(1)}, bf16[16,8448]{1,0:T(8,128)(2,1)S(1)}, u32[]{:S(2)}, u32[]{:S(2)}) collective-permute-start(bf16[16,8448]{1,0:T(8,128)(2,1)S(1)} %pad_maximum_fusion.8), channel_id=1, source_target_pairs={{0,16},{1,17},{2,18},{3,19},{4,20},{5,21},{6,22},{7,23},{8,24},{9,... | collective-permute-start | bytes 811016 | tf_op jit(solution)/shard_map/ppermute | solution.py:17
  133.6 3.9 %collective-permute-done.15 = bf16[16,8448]{1,0:T(8,128)(2,1)S(1)} collective-permute-done((bf16[16,8448]{1,0:T(8,128)(2,1)S(1)}, bf16[16,8448]{1,0:T(8,128)(2,1)S(1)}, u32[]{:S(2)}, u32[]{:S(2)}) %collective-permute-start.15) | collective-permute-done | bytes 270368 | tf_op jit(solution)/shard_map/ppermute | solution.py:17
  138.2 4.9 %collective-permute-done.7 = bf16[16,8448]{1,0:T(8,128)(2,1)S(1)} collective-permute-done((bf16[16,8448]{1,0:T(8,128)(2,1)S(1)}, bf16[16,8448]{1,0:T(8,128)(2,1)S(1)}, u32[]{:S(2)}, u32[]{:S(2)}) %collective-permute-start.7) | collective-permute-done | bytes 270368 | tf_op jit(solution)/shard_map/ppermute | solution.py:17
  146.7 6.9 %shard_map.68 = bf16[2048,1280]{1,0:T(8,128)(2,1)} custom-call(bf16[128,2048]{1,0:T(8,128)(2,1)} %bitcast.230, bf16[128,1280]{1,0:T(8,128)(2,1)} %pad_maximum_fusion.4.right_ref), custom_call_target="tpu_custom_call" | custom-call | flops 671088640 | bytes 6094848 | tf_op jit(solution)/shard_map/pallas_call | solution.py:120
  157.6 4.7 %collective-permute-done.16 = bf16[4,4,64,1280]{3,2,1,0:T(8,128)(2,1)} collective-permute-done((bf16[4,4,64,1280]{3,2,1,0:T(8,128)(2,1)S(1)}, bf16[4,4,64,1280]{3,2,1,0:T(8,128)(2,1)}, u32[]{:S(2)}, u32[]{:S(2)}) %collective-permute-start.16) | collective-permute-done | bytes 2621472 | tf_op jit(solution)/shard_map/ppermute | solution.py:73
  162.3 3.2 %convert_add_fusion = f32[4,4,64,1280]{3,2,1,0:T(8,128)S(1)} fusion(bf16[4,4,64,1280]{3,2,1,0:T(8,128)(2,1)} %collective-permute-done.16, bf16[4,4,2,64,1280]{4,3,2,1,0:T(8,128)(2,1)} %bitcast.221, s32[]{:T(128)S(6)} %select_n.216), kind=kLoop, calls=%fused_computation.1 | loop fusion | flops 3932160 | bytes 10485764 | tf_op jit(solution)/shard_map/add | solution.py:74
  168.5 2.6 collective-permute-start.25
  172.7 9.3 %collective-permute-start.19 = (bf16[4,64,640]{2,1,0:T(8,128)(2,1)S(1)}, bf16[4,64,640]{2,1,0:T(8,128)(2,1)S(1)}, u32[]{:S(2)}, u32[]{:S(2)}) collective-permute-start(bf16[4,64,640]{2,1,0:T(8,128)(2,1)S(1)} %get-tuple-element.119), channel_id=1, source_target_pairs={{0,6},{1,7},{2,0},{3,1},{4,2},{5,3},{6,4},{7,5},{8,14},{9,15},{10,... | collective-permute-start | bytes 983048 | tf_op jit(solution)/shard_map/ppermute | solution.py:73
  181.9 3.8 %collective-permute-done.25 = bf16[4,64,640]{2,1,0:T(8,128)(2,1)S(1)} collective-permute-done((bf16[4,64,640]{2,1,0:T(8,128)(2,1)}, bf16[4,64,640]{2,1,0:T(8,128)(2,1)S(1)}, u32[]{:S(2)}, u32[]{:S(2)}) %collective-permute-start.25) | collective-permute-done | bytes 327712 | tf_op jit(solution)/shard_map/ppermute | solution.py:73
  189.0 10.9 %collective-permute-start.28 = (bf16[64,640]{1,0:T(8,128)(2,1)S(1)}, bf16[64,640]{1,0:T(8,128)(2,1)S(1)}, u32[]{:S(2)}, u32[]{:S(2)}) collective-permute-start(bf16[64,640]{1,0:T(8,128)(2,1)S(1)} %get-tuple-element.127), channel_id=1, source_target_pairs={{0,6},{1,7},{2,0},{3,1},{4,2},{5,3},{6,4},{7,5},{8,14},{9,15},{10,... | collective-permute-start | bytes 245768 | tf_op jit(solution)/shard_map/ppermute | solution.py:73
  200.9 4.7 %collective-permute-done.17 = bf16[4,64,640]{2,1,0:T(8,128)(2,1)S(1)} collective-permute-done((bf16[4,64,640]{2,1,0:T(8,128)(2,1)S(1)}, bf16[4,64,640]{2,1,0:T(8,128)(2,1)S(1)}, u32[]{:S(2)}, u32[]{:S(2)}) %collective-permute-start.17) | collective-permute-done | bytes 327712 | tf_op jit(solution)/shard_map/ppermute | solution.py:73
  207.9 2.4 collective-permute-done.22
  213.3 3.4 %collective-permute-start.35 = (f32[8,1280]{1,0:T(8,128)S(1)}, f32[8,1280]{1,0:T(8,128)S(1)}, u32[]{:S(2)}, u32[]{:S(2)}) collective-permute-start(f32[8,1280]{1,0:T(8,128)S(1)} %get-tuple-element.140), channel_id=1, source_target_pairs={{0,224},{32,0},{64,32},{96,64},{128,96},{160,128},{192,160},{224,1... | collective-permute-start | bytes 122888 | tf_op jit(solution)/shard_map/ppermute | solution.py:100
  220.1 3.9 %collective-permute-start.32 = (f32[8,1280]{1,0:T(8,128)S(1)}, f32[8,1280]{1,0:T(8,128)S(1)}, u32[]{:S(2)}, u32[]{:S(2)}) collective-permute-start(f32[8,1280]{1,0:T(8,128)S(1)} %get-tuple-element.143), channel_id=1, source_target_pairs={{0,128},{32,160},{64,192},{96,224},{128,0},{160,32},{192,64},{224,... | collective-permute-start | bytes 122888 | tf_op jit(solution)/shard_map/ppermute | solution.py:100
  224.0 3.5 %collective-permute-start.30 = (f32[8,1280]{1,0:T(8,128)S(1)}, f32[8,1280]{1,0:T(8,128)S(1)}, u32[]{:S(2)}, u32[]{:S(2)}) collective-permute-start(f32[8,1280]{1,0:T(8,128)S(1)} %get-tuple-element.145), channel_id=1, source_target_pairs={{0,64},{32,96},{64,128},{96,160},{128,192},{160,224},{192,0},{224,... | collective-permute-start | bytes 122888 | tf_op jit(solution)/shard_map/ppermute | solution.py:100
  233.6 5.3 %convolution_bitcast_fusion = f32[1,128,2048]{2,1,0:T(8,128)} fusion(bf16[2048,1280]{1,0:T(8,128)(2,1)} %all-gather.2.cloned.1.call-done, bf16[128,128]{1,0:T(8,128)(2,1)S(1)} %copy-done.2, bf16[128,128]{1,0:T(8,128)(2,1)S(1)} %copy-done.4, bf16[128,1024]{1,0:T(8,128)(2,1)S(1)} %copy.81), kind=kOutput, calls=%fused_computation.3 | convolution fusion | flops 672071680 | bytes 6619136 | tf_op jit(solution)/shard_map/dot_general | solution.py:250
  242.6 2.6 collective-permute-start.39
  245.2 2.3 collective-permute-start.40
  247.5 3.9 %collective-permute-start.41 = (f32[8,1280]{1,0:T(8,128)S(1)}, f32[8,1280]{1,0:T(8,128)S(1)}, u32[]{:S(2)}, u32[]{:S(2)}) collective-permute-start(f32[8,1280]{1,0:T(8,128)S(1)} %get-tuple-element.76), channel_id=1, source_target_pairs={{0,192},{32,224},{64,0},{96,32},{128,64},{160,96},{192,128},{224,1... | collective-permute-start | bytes 122888 | tf_op jit(solution)/shard_map/ppermute | solution.py:104
  253.1 2.4 collective-permute-done.42
  (176 shorter events, 65.9 us)
Async XLA Ops:
  7.2 59.0 %all-gather.2.cloned.1.call-start = ((), (), s32[]{:S(2)}) async-start(), calls=%async_computation | async-start | bytes 5406720 | tf_op jit(solution)/shard_map/all_gather | solution.py:216
  72.6 18.2 %collective-permute-start.8 = (bf16[16,8448]{1,0:T(8,128)(2,1)S(1)}, bf16[16,8448]{1,0:T(8,128)(2,1)S(1)}, u32[]{:S(2)}, u32[]{:S(2)}) collective-permute-start(bf16[16,8448]{1,0:T(8,128)(2,1)S(1)} %get-tuple-element.155), channel_id=1, source_target_pairs={{0,1},{1,2},{2,3},{3,4},{4,5},{5,6},{6,7},{7,8},{8,9},{9,10},{10,1... | collective-permute-start | bytes 811016 | tf_op jit(solution)/shard_map/ppermute | solution.py:17
  74.8 18.3 %collective-permute-start.9 = (bf16[16,8448]{1,0:T(8,128)(2,1)S(1)}, bf16[16,8448]{1,0:T(8,128)(2,1)S(1)}, u32[]{:S(2)}, u32[]{:S(2)}) collective-permute-start(bf16[16,8448]{1,0:T(8,128)(2,1)S(1)} %get-tuple-element.155), channel_id=1, source_target_pairs={{0,2},{1,3},{2,4},{3,5},{4,6},{5,7},{6,8},{7,9},{8,10},{9,11},{10,... | collective-permute-start | bytes 811016 | tf_op jit(solution)/shard_map/ppermute | solution.py:17
  76.9 18.2 %collective-permute-start.10 = (bf16[16,8448]{1,0:T(8,128)(2,1)S(1)}, bf16[16,8448]{1,0:T(8,128)(2,1)S(1)}, u32[]{:S(2)}, u32[]{:S(2)}) collective-permute-start(bf16[16,8448]{1,0:T(8,128)(2,1)S(1)} %get-tuple-element.155), channel_id=1, source_target_pairs={{0,3},{1,4},{2,5},{3,6},{4,7},{5,8},{6,9},{7,10},{8,11},{9,12},{10... | collective-permute-start | bytes 811016 | tf_op jit(solution)/shard_map/ppermute | solution.py:17
  80.6 19.0 %collective-permute-start.11 = (bf16[16,8448]{1,0:T(8,128)(2,1)S(1)}, bf16[16,8448]{1,0:T(8,128)(2,1)S(1)}, u32[]{:S(2)}, u32[]{:S(2)}) collective-permute-start(bf16[16,8448]{1,0:T(8,128)(2,1)S(1)} %get-tuple-element.155), channel_id=1, source_target_pairs={{0,4},{1,5},{2,6},{3,7},{4,8},{5,9},{6,10},{7,11},{8,12},{9,13},{1... | collective-permute-start | bytes 811016 | tf_op jit(solution)/shard_map/ppermute | solution.py:17
  85.3 17.9 %collective-permute-start = (bf16[16,8448]{1,0:T(8,128)(2,1)S(1)}, bf16[16,8448]{1,0:T(8,128)(2,1)S(1)}, u32[]{:S(2)}, u32[]{:S(2)}) collective-permute-start(bf16[16,8448]{1,0:T(8,128)(2,1)S(1)} %get-tuple-element.154), channel_id=1, source_target_pairs={{1,0},{2,1},{3,2},{4,3},{5,4},{6,5},{7,6},{8,7},{9,8},{10,9},{11,1... | collective-permute-start | bytes 811016 | tf_op jit(solution)/shard_map/ppermute | solution.py:17
  90.8 16.4 %collective-permute-start.1 = (bf16[16,8448]{1,0:T(8,128)(2,1)S(1)}, bf16[16,8448]{1,0:T(8,128)(2,1)S(1)}, u32[]{:S(2)}, u32[]{:S(2)}) collective-permute-start(bf16[16,8448]{1,0:T(8,128)(2,1)S(1)} %get-tuple-element.154), channel_id=1, source_target_pairs={{2,0},{3,1},{4,2},{5,3},{6,4},{7,5},{8,6},{9,7},{10,8},{11,9},{12,... | collective-permute-start | bytes 811016 | tf_op jit(solution)/shard_map/ppermute | solution.py:17
  93.1 19.8 %collective-permute-start.2 = (bf16[16,8448]{1,0:T(8,128)(2,1)S(1)}, bf16[16,8448]{1,0:T(8,128)(2,1)S(1)}, u32[]{:S(2)}, u32[]{:S(2)}) collective-permute-start(bf16[16,8448]{1,0:T(8,128)(2,1)S(1)} %get-tuple-element.154), channel_id=1, source_target_pairs={{3,0},{4,1},{5,2},{6,3},{7,4},{8,5},{9,6},{10,7},{11,8},{12,9},{13... | collective-permute-start | bytes 811016 | tf_op jit(solution)/shard_map/ppermute | solution.py:17
  95.1 17.8 %collective-permute-start.3 = (bf16[16,8448]{1,0:T(8,128)(2,1)S(1)}, bf16[16,8448]{1,0:T(8,128)(2,1)S(1)}, u32[]{:S(2)}, u32[]{:S(2)}) collective-permute-start(bf16[16,8448]{1,0:T(8,128)(2,1)S(1)} %get-tuple-element.154), channel_id=1, source_target_pairs={{4,0},{5,1},{6,2},{7,3},{8,4},{9,5},{10,6},{11,7},{12,8},{13,9},{1... | collective-permute-start | bytes 811016 | tf_op jit(solution)/shard_map/ppermute | solution.py:17
  100.3 19.2 %collective-permute-start.14 = (bf16[16,8448]{1,0:T(8,128)(2,1)S(1)}, bf16[16,8448]{1,0:T(8,128)(2,1)S(1)}, u32[]{:S(2)}, u32[]{:S(2)}) collective-permute-start(bf16[16,8448]{1,0:T(8,128)(2,1)S(1)} %pad_maximum_fusion.7), channel_id=1, source_target_pairs={{0,4},{1,5},{2,6},{3,7},{4,8},{5,9},{6,10},{7,11},{8,12},{9,13},{1... | collective-permute-start | bytes 811016 | tf_op jit(solution)/shard_map/ppermute | solution.py:17
  103.2 21.9 %collective-permute-start.13 = (bf16[16,8448]{1,0:T(8,128)(2,1)S(1)}, bf16[16,8448]{1,0:T(8,128)(2,1)S(1)}, u32[]{:S(2)}, u32[]{:S(2)}) collective-permute-start(bf16[16,8448]{1,0:T(8,128)(2,1)S(1)} %pad_maximum_fusion.7), channel_id=1, source_target_pairs={{0,8},{1,9},{2,10},{3,11},{4,12},{5,13},{6,14},{7,15},{8,16},{9,17... | collective-permute-start | bytes 811016 | tf_op jit(solution)/shard_map/ppermute | solution.py:17
  107.2 17.9 %collective-permute-start.12 = (bf16[16,8448]{1,0:T(8,128)(2,1)S(1)}, bf16[16,8448]{1,0:T(8,128)(2,1)S(1)}, u32[]{:S(2)}, u32[]{:S(2)}) collective-permute-start(bf16[16,8448]{1,0:T(8,128)(2,1)S(1)} %pad_maximum_fusion.7), channel_id=1, source_target_pairs={{0,12},{1,13},{2,14},{3,15},{4,16},{5,17},{6,18},{7,19},{8,20},{9,... | collective-permute-start | bytes 811016 | tf_op jit(solution)/shard_map/ppermute | solution.py:17
  113.6 17.0 %collective-permute-start.6 = (bf16[16,8448]{1,0:T(8,128)(2,1)S(1)}, bf16[16,8448]{1,0:T(8,128)(2,1)S(1)}, u32[]{:S(2)}, u32[]{:S(2)}) collective-permute-start(bf16[16,8448]{1,0:T(8,128)(2,1)S(1)} %pad_maximum_fusion.5), channel_id=1, source_target_pairs={{4,0},{5,1},{6,2},{7,3},{8,4},{9,5},{10,6},{11,7},{12,8},{13,9},{1... | collective-permute-start | bytes 811016 | tf_op jit(solution)/shard_map/ppermute | solution.py:17
  117.6 13.1 %collective-permute-start.5 = (bf16[16,8448]{1,0:T(8,128)(2,1)S(1)}, bf16[16,8448]{1,0:T(8,128)(2,1)S(1)}, u32[]{:S(2)}, u32[]{:S(2)}) collective-permute-start(bf16[16,8448]{1,0:T(8,128)(2,1)S(1)} %pad_maximum_fusion.5), channel_id=1, source_target_pairs={{8,0},{9,1},{10,2},{11,3},{12,4},{13,5},{14,6},{15,7},{16,8},{17,9... | collective-permute-start | bytes 811016 | tf_op jit(solution)/shard_map/ppermute | solution.py:17
  119.5 12.1 %collective-permute-start.4 = (bf16[16,8448]{1,0:T(8,128)(2,1)S(1)}, bf16[16,8448]{1,0:T(8,128)(2,1)S(1)}, u32[]{:S(2)}, u32[]{:S(2)}) collective-permute-start(bf16[16,8448]{1,0:T(8,128)(2,1)S(1)} %pad_maximum_fusion.5), channel_id=1, source_target_pairs={{12,0},{13,1},{14,2},{15,3},{16,4},{17,5},{18,6},{19,7},{20,8},{21... | collective-permute-start | bytes 811016 | tf_op jit(solution)/shard_map/ppermute | solution.py:17
  125.8 11.7 %collective-permute-start.15 = (bf16[16,8448]{1,0:T(8,128)(2,1)S(1)}, bf16[16,8448]{1,0:T(8,128)(2,1)S(1)}, u32[]{:S(2)}, u32[]{:S(2)}) collective-permute-start(bf16[16,8448]{1,0:T(8,128)(2,1)S(1)} %pad_maximum_fusion.8), channel_id=1, source_target_pairs={{0,16},{1,17},{2,18},{3,19},{4,20},{5,21},{6,22},{7,23},{8,24},{9,... | collective-permute-start | bytes 811016 | tf_op jit(solution)/shard_map/ppermute | solution.py:17
  132.3 10.8 %collective-permute-start.7 = (bf16[16,8448]{1,0:T(8,128)(2,1)S(1)}, bf16[16,8448]{1,0:T(8,128)(2,1)S(1)}, u32[]{:S(2)}, u32[]{:S(2)}) collective-permute-start(bf16[16,8448]{1,0:T(8,128)(2,1)S(1)} %pad_maximum_fusion.6), channel_id=1, source_target_pairs={{16,0},{17,1},{18,2},{19,3},{20,4},{21,5},{22,6},{23,7},{24,8},{25... | collective-permute-start | bytes 811016 | tf_op jit(solution)/shard_map/ppermute | solution.py:17
  168.5 17.2 %collective-permute-start.25 = (bf16[4,64,640]{2,1,0:T(8,128)(2,1)}, bf16[4,64,640]{2,1,0:T(8,128)(2,1)S(1)}, u32[]{:S(2)}, u32[]{:S(2)}) collective-permute-start(bf16[4,64,640]{2,1,0:T(8,128)(2,1)} %get-tuple-element.121), channel_id=1, source_target_pairs={{0,24},{1,25},{2,26},{3,27},{4,28},{5,29},{6,30},{7,31},{8,0},{9,1... | collective-permute-start | bytes 983048 | tf_op jit(solution)/shard_map/ppermute | solution.py:73
  171.1 14.6 %collective-permute-start.24 = (bf16[4,64,640]{2,1,0:T(8,128)(2,1)}, bf16[4,64,640]{2,1,0:T(8,128)(2,1)S(1)}, u32[]{:S(2)}, u32[]{:S(2)}) collective-permute-start(bf16[4,64,640]{2,1,0:T(8,128)(2,1)} %get-tuple-element.122), channel_id=1, source_target_pairs={{0,16},{1,17},{2,18},{3,19},{4,20},{5,21},{6,22},{7,23},{8,24},{9,... | collective-permute-start | bytes 983048 | tf_op jit(solution)/shard_map/ppermute | solution.py:73
  171.1 16.6 %collective-permute-start.23 = (bf16[4,64,640]{2,1,0:T(8,128)(2,1)}, bf16[4,64,640]{2,1,0:T(8,128)(2,1)}, u32[]{:S(2)}, u32[]{:S(2)}) collective-permute-start(bf16[4,64,640]{2,1,0:T(8,128)(2,1)} %get-tuple-element.120), channel_id=1, source_target_pairs={{0,8},{1,9},{2,10},{3,11},{4,12},{5,13},{6,14},{7,15},{8,16},{9,17... | collective-permute-start | bytes 983048 | tf_op jit(solution)/shard_map/ppermute | solution.py:73
  172.7 27.3 %collective-permute-start.19 = (bf16[4,64,640]{2,1,0:T(8,128)(2,1)S(1)}, bf16[4,64,640]{2,1,0:T(8,128)(2,1)S(1)}, u32[]{:S(2)}, u32[]{:S(2)}) collective-permute-start(bf16[4,64,640]{2,1,0:T(8,128)(2,1)S(1)} %get-tuple-element.119), channel_id=1, source_target_pairs={{0,6},{1,7},{2,0},{3,1},{4,2},{5,3},{6,4},{7,5},{8,14},{9,15},{10,... | collective-permute-start | bytes 983048 | tf_op jit(solution)/shard_map/ppermute | solution.py:73
  181.9 19.0 %collective-permute-start.18 = (bf16[4,64,640]{2,1,0:T(8,128)(2,1)S(1)}, bf16[4,64,640]{2,1,0:T(8,128)(2,1)S(1)}, u32[]{:S(2)}, u32[]{:S(2)}) collective-permute-start(bf16[4,64,640]{2,1,0:T(8,128)(2,1)S(1)} %get-tuple-element.118), channel_id=1, source_target_pairs={{0,4},{1,5},{2,6},{3,7},{4,0},{5,1},{6,2},{7,3},{8,12},{9,13},{10,... | collective-permute-start | bytes 983048 | tf_op jit(solution)/shard_map/ppermute | solution.py:73
  185.7 19.9 %collective-permute-start.17 = (bf16[4,64,640]{2,1,0:T(8,128)(2,1)S(1)}, bf16[4,64,640]{2,1,0:T(8,128)(2,1)S(1)}, u32[]{:S(2)}, u32[]{:S(2)}) collective-permute-start(bf16[4,64,640]{2,1,0:T(8,128)(2,1)S(1)} %get-tuple-element.117), channel_id=1, source_target_pairs={{0,2},{1,3},{2,4},{3,5},{4,6},{5,7},{6,0},{7,1},{8,10},{9,11},{10,... | collective-permute-start | bytes 983048 | tf_op jit(solution)/shard_map/ppermute | solution.py:73
  189.0 17.8 %collective-permute-start.28 = (bf16[64,640]{1,0:T(8,128)(2,1)S(1)}, bf16[64,640]{1,0:T(8,128)(2,1)S(1)}, u32[]{:S(2)}, u32[]{:S(2)}) collective-permute-start(bf16[64,640]{1,0:T(8,128)(2,1)S(1)} %get-tuple-element.127), channel_id=1, source_target_pairs={{0,6},{1,7},{2,0},{3,1},{4,2},{5,3},{6,4},{7,5},{8,14},{9,15},{10,... | collective-permute-start | bytes 245768 | tf_op jit(solution)/shard_map/ppermute | solution.py:73
  213.3 10.7 %collective-permute-start.35 = (f32[8,1280]{1,0:T(8,128)S(1)}, f32[8,1280]{1,0:T(8,128)S(1)}, u32[]{:S(2)}, u32[]{:S(2)}) collective-permute-start(f32[8,1280]{1,0:T(8,128)S(1)} %get-tuple-element.140), channel_id=1, source_target_pairs={{0,224},{32,0},{64,32},{96,64},{128,96},{160,128},{192,160},{224,1... | collective-permute-start | bytes 122888 | tf_op jit(solution)/shard_map/ppermute | solution.py:100
  216.7 10.9 %collective-permute-start.34 = (f32[8,1280]{1,0:T(8,128)S(1)}, f32[8,1280]{1,0:T(8,128)S(1)}, u32[]{:S(2)}, u32[]{:S(2)}) collective-permute-start(f32[8,1280]{1,0:T(8,128)S(1)} %get-tuple-element.141), channel_id=1, source_target_pairs={{0,192},{32,224},{64,0},{96,32},{128,64},{160,96},{192,128},{224,1... | collective-permute-start | bytes 122888 | tf_op jit(solution)/shard_map/ppermute | solution.py:100
  218.9 10.4 %collective-permute-start.33 = (f32[8,1280]{1,0:T(8,128)S(1)}, f32[8,1280]{1,0:T(8,128)S(1)}, u32[]{:S(2)}, u32[]{:S(2)}) collective-permute-start(f32[8,1280]{1,0:T(8,128)S(1)} %get-tuple-element.142), channel_id=1, source_target_pairs={{0,160},{32,192},{64,224},{96,0},{128,32},{160,64},{192,96},{224,1... | collective-permute-start | bytes 122888 | tf_op jit(solution)/shard_map/ppermute | solution.py:100
  220.1 9.2 %collective-permute-start.32 = (f32[8,1280]{1,0:T(8,128)S(1)}, f32[8,1280]{1,0:T(8,128)S(1)}, u32[]{:S(2)}, u32[]{:S(2)}) collective-permute-start(f32[8,1280]{1,0:T(8,128)S(1)} %get-tuple-element.143), channel_id=1, source_target_pairs={{0,128},{32,160},{64,192},{96,224},{128,0},{160,32},{192,64},{224,... | collective-permute-start | bytes 122888 | tf_op jit(solution)/shard_map/ppermute | solution.py:100
  232.8 14.7 %collective-permute-start.36 = (f32[8,1280]{1,0:T(8,128)S(1)}, f32[8,1280]{1,0:T(8,128)S(1)}, u32[]{:S(2)}, u32[]{:S(2)}) collective-permute-start(f32[8,1280]{1,0:T(8,128)S(1)} %get-tuple-element.76), channel_id=1, source_target_pairs={{0,32},{32,64},{64,96},{96,128},{128,160},{160,192},{192,224},{224... | collective-permute-start | bytes 122888 | tf_op jit(solution)/shard_map/ppermute | solution.py:104
  238.9 12.5 %collective-permute-start.37 = (f32[8,1280]{1,0:T(8,128)S(1)}, f32[8,1280]{1,0:T(8,128)S(1)}, u32[]{:S(2)}, u32[]{:S(2)}) collective-permute-start(f32[8,1280]{1,0:T(8,128)S(1)} %get-tuple-element.76), channel_id=1, source_target_pairs={{0,64},{32,96},{64,128},{96,160},{128,192},{160,224},{192,0},{224,... | collective-permute-start | bytes 122888 | tf_op jit(solution)/shard_map/ppermute | solution.py:104
  240.5 12.0 %collective-permute-start.38 = (f32[8,1280]{1,0:T(8,128)S(1)}, f32[8,1280]{1,0:T(8,128)S(1)}, u32[]{:S(2)}, u32[]{:S(2)}) collective-permute-start(f32[8,1280]{1,0:T(8,128)S(1)} %get-tuple-element.76), channel_id=1, source_target_pairs={{0,96},{32,128},{64,160},{96,192},{128,224},{160,0},{192,32},{224,... | collective-permute-start | bytes 122888 | tf_op jit(solution)/shard_map/ppermute | solution.py:104
  242.6 9.9 %collective-permute-start.39 = (f32[8,1280]{1,0:T(8,128)S(1)}, f32[8,1280]{1,0:T(8,128)S(1)}, u32[]{:S(2)}, u32[]{:S(2)}) collective-permute-start(f32[8,1280]{1,0:T(8,128)S(1)} %get-tuple-element.76), channel_id=1, source_target_pairs={{0,128},{32,160},{64,192},{96,224},{128,0},{160,32},{192,64},{224,... | collective-permute-start | bytes 122888 | tf_op jit(solution)/shard_map/ppermute | solution.py:104
  (17 other events, 185.1 us)
Sparse Core Ops, SparseCore 0:
  11.1 54.9 all-gather.1

commit v10 on v9

--- a/solution.py
+++ b/solution.py
@@ -38,7 +38,7 @@
             decay = decay * later_decay
         return flat, decay
 
-    radix = 4
+    radix = 2
     own = (flat, decay)
     part = chain([send(own, step) for step in range(radix, 0, -1)])
     width = radix
@@ -92,19 +92,29 @@
 def replicated_sum(value, axis):
     count = lax.axis_size(axis)
     me = lax.axis_index(axis)
-    slabs = value.reshape(count, value.shape[0] // count, value.shape[1])
-    total = lax.dynamic_index_in_dim(slabs, me, 0, False)
-    for offset in range(1, count):
-        piece = lax.dynamic_index_in_dim(slabs, (me + offset) % count, 0, False)
-        pairs = [(place, (place + offset) % count) for place in range(count)]
-        total = total + lax.ppermute(piece, axis, pairs)
-    gathered = [total]
-    for offset in range(1, count):
-        pairs = [(place, (place + offset) % count) for place in range(count)]
-        gathered.append(lax.ppermute(total, axis, pairs))
-    stacked = jnp.stack(gathered)
-    order = (me - jnp.arange(count)) % count
-    return jnp.take(stacked, order, axis=0).reshape(value.shape)
+    steps = []
+    step = count // 2
+    while step >= 1:
+        steps.append(step)
+        step //= 2
+    total = value
+    for step in steps:
+        pairs = [(place, place ^ step) for place in range(count)]
+        halves = total.reshape(2, total.shape[0] // 2, total.shape[1])
+        bit = (me // step) % 2
+        keep = lax.dynamic_index_in_dim(halves, bit, 0, False)
+        give = lax.dynamic_index_in_dim(halves, 1 - bit, 0, False)
+        total = keep + lax.ppermute(give, axis, pairs)
+    for step in reversed(steps):
+        pairs = [(place, place ^ step) for place in range(count)]
+        other = lax.ppermute(total, axis, pairs)
+        bit = (me // step) % 2
+        total = jnp.where(
+            bit == 0,
+            jnp.concatenate([total, other], axis=0),
+            jnp.concatenate([other, total], axis=0),
+        )
+    return total
 
 
 def outer_kernel(left_ref, right_ref, out_ref):

time: 266 us -> 267 us (level)
  waiting for transfers between devices: 93.2 us -> 145 us
  starting transfers between devices: 109 us -> 57.5 us
    ppermute x13, starting transfers between devices: 29.4 us -> 7.58 us  [digit_reduce(): got = lax.ppermute(piece.astype(jnp.bfloat16), axis, pairs)]
    ppermute x16 -> x12, waiting for transfers between devices: 15.4 us -> 35.1 us  [shifted(): lax.ppermute(value.astype(jnp.bfloat16), axis, pairs).astype(value.dtype)]
    ppermute x14 -> x6, waiting for transfers between devices: 6.37 us -> 25.8 us  [the longest x3 13.2 us: replicated_sum(): other = lax.ppermute(total, axis, pairs)]
    ppermute x14 -> x6, starting transfers between devices: 30.2 us -> 14.4 us  [the longest x3 8.4 us: replicated_sum(): total = keep + lax.ppermute(give, axis, pairs)]
    ppermute x16 -> x12, starting transfers between devices: 49.8 us -> 35.6 us  [shifted(): lax.ppermute(value.astype(jnp.bfloat16), axis, pairs).astype(value.dtype)]
    ppermute x13, waiting for transfers between devices: 20.4 us -> 33.4 us  [digit_reduce(): got = lax.ppermute(piece.astype(jnp.bfloat16), axis, pairs)]
  transfers between devices with their start and end apart: 44 -> 32, of which waited for: 18 -> 22; matrix products, arithmetic and copies ran while one was open for 7% -> 7% of each run, Pallas kernels for 0% -> 0%
where the time goes in v10:
time: 267 us; the launch traced here: 266 us
  waiting for transfers between devices  145 us (54%)
  starting transfers between devices  57.5 us (22%)
  other arithmetic  17.1 us (6%)
  between operations  14.9 us (6%)
  matrix products  12.8 us (5%)
  local copies, waits for them, and re-layouts  11.7 us (4%)
  Pallas kernels  6.94 us (3%)
    all_gather x1, waiting for transfers between devices, local(): lax.all_gather(dequantize(weight_codes, scales), 'seq', axis=0, tiled=True)  50.6 us
    ppermute x12, starting transfers between devices, shifted(): lax.ppermute(value.astype(jnp.bfloat16), axis, pairs).astype(value.dtype)  35.6 us
    ppermute x12, waiting for transfers between devices, shifted(): lax.ppermute(value.astype(jnp.bfloat16), axis, pairs).astype(value.dtype)  35.1 us
    ppermute x13, waiting for transfers between devices, digit_reduce(): got = lax.ppermute(piece.astype(jnp.bfloat16), axis, pairs)  33.4 us
    ppermute x3, waiting for transfers between devices, replicated_sum(): other = lax.ppermute(total, axis, pairs)  13.2 us
    ppermute x3, waiting for transfers between devices, replicated_sum(): total = keep + lax.ppermute(give, axis, pairs)  12.6 us
    ppermute x3, starting transfers between devices, replicated_sum(): total = keep + lax.ppermute(give, axis, pairs)  8.4 us
    ppermute x13, starting transfers between devices, digit_reduce(): got = lax.ppermute(piece.astype(jnp.bfloat16), axis, pairs)  7.58 us
  transfers between devices with their start and end apart: 32, of which 22 were waited for; matrix products, arithmetic and copies ran while one was open for 7% of the time, Pallas kernels for 0%

profile of v10, /device:TPU:8, one launch (start us, length us, event | category | flops | bytes accessed | tf_op | source)
XLA Modules:
  0.0 265.9 jit_solution(10910439499164888001)
XLA Ops:
  15.6 50.6 %all-gather.2.cloned.1.call-done = bf16[2048,1280]{1,0:T(8,128)(2,1)} async-done(((bf16[64,1280]{1,0:T(8,128)(2,1)}), bf16[2048,1280]{1,0:T(8,128)(2,1)}) %all-gather.2.cloned.1.call-update) | async-done | bytes 5242896 | tf_op jit(solution)/shard_map/all_gather | solution.py:226
  66.1 4.2 %fusion = bf16[128,1280]{0,1:T(8,128)(2,1)S(1)} fusion(bf16[2048,1280]{1,0:T(8,128)(2,1)} %all-gather.2.cloned.1.call-done, bf16[1,128,2048]{2,1,0:T(8,128)(2,1)} %param.5), kind=kOutput, calls=%fused_computation.4 | convolution fusion | flops 671252480 | bytes 6094848 | tf_op jit(solution)/shard_map/dot_general | solution.py:227
  72.6 4.4 %collective-permute-start = (bf16[16,8448]{1,0:T(8,128)(2,1)S(1)}, bf16[16,8448]{1,0:T(8,128)(2,1)S(1)}, u32[]{:S(2)}, u32[]{:S(2)}) collective-permute-start(bf16[16,8448]{1,0:T(8,128)(2,1)S(1)} %get-tuple-element.153), channel_id=1, source_target_pairs={{1,0},{2,1},{3,2},{4,3},{5,4},{6,5},{7,6},{8,7},{9,8},{10,9},{11,1... | collective-permute-start | bytes 811016 | tf_op jit(solution)/shard_map/ppermute | solution.py:17
  77.0 2.1 collective-permute-start.1
  79.2 2.1 collective-permute-start.6
  81.3 3.5 %collective-permute-start.7 = (bf16[16,8448]{1,0:T(8,128)(2,1)S(1)}, bf16[16,8448]{1,0:T(8,128)(2,1)S(1)}, u32[]{:S(2)}, u32[]{:S(2)}) collective-permute-start(bf16[16,8448]{1,0:T(8,128)(2,1)S(1)} %get-tuple-element.154), channel_id=1, source_target_pairs={{0,2},{1,3},{2,4},{3,5},{4,6},{5,7},{6,8},{7,9},{8,10},{9,11},{10,... | collective-permute-start | bytes 811016 | tf_op jit(solution)/shard_map/ppermute | solution.py:17
  87.3 6.5 %collective-permute-start.2 = (bf16[16,8448]{1,0:T(8,128)(2,1)S(1)}, bf16[16,8448]{1,0:T(8,128)(2,1)S(1)}, u32[]{:S(2)}, u32[]{:S(2)}) collective-permute-start(bf16[16,8448]{1,0:T(8,128)(2,1)S(1)} %pad_maximum_fusion.6), channel_id=1, source_target_pairs={{2,0},{3,1},{4,2},{5,3},{6,4},{7,5},{8,6},{9,7},{10,8},{11,9},{12,... | collective-permute-start | bytes 811016 | tf_op jit(solution)/shard_map/ppermute | solution.py:17
  99.2 4.3 %collective-permute-start.3 = (bf16[16,8448]{1,0:T(8,128)(2,1)S(1)}, bf16[16,8448]{1,0:T(8,128)(2,1)S(1)}, u32[]{:S(2)}, u32[]{:S(2)}) collective-permute-start(bf16[16,8448]{1,0:T(8,128)(2,1)S(1)} %pad_maximum_fusion.7), channel_id=1, source_target_pairs={{4,0},{5,1},{6,2},{7,3},{8,4},{9,5},{10,6},{11,7},{12,8},{13,9},{1... | collective-permute-start | bytes 811016 | tf_op jit(solution)/shard_map/ppermute | solution.py:17
  103.5 10.0 %collective-permute-done.8 = bf16[16,8448]{1,0:T(8,128)(2,1)S(1)} collective-permute-done((bf16[16,8448]{1,0:T(8,128)(2,1)S(1)}, bf16[16,8448]{1,0:T(8,128)(2,1)S(1)}, u32[]{:S(2)}, u32[]{:S(2)}) %collective-permute-start.8) | collective-permute-done | bytes 270368 | tf_op jit(solution)/shard_map/ppermute | solution.py:17
  114.0 2.1 collective-permute-start.9
  118.7 7.7 %collective-permute-done.9 = bf16[16,8448]{1,0:T(8,128)(2,1)S(1)} collective-permute-done((bf16[16,8448]{1,0:T(8,128)(2,1)S(1)}, bf16[16,8448]{1,0:T(8,128)(2,1)S(1)}, u32[]{:S(2)}, u32[]{:S(2)}) %collective-permute-start.9) | collective-permute-done | bytes 270368 | tf_op jit(solution)/shard_map/ppermute | solution.py:17
  127.0 2.3 collective-permute-start.10
  130.5 5.4 %collective-permute-done.10 = bf16[16,8448]{1,0:T(8,128)(2,1)S(1)} collective-permute-done((bf16[16,8448]{1,0:T(8,128)(2,1)S(1)}, bf16[16,8448]{1,0:T(8,128)(2,1)S(1)}, u32[]{:S(2)}, u32[]{:S(2)}) %collective-permute-start.10) | collective-permute-done | bytes 270368 | tf_op jit(solution)/shard_map/ppermute | solution.py:17
  136.5 3.2 %collective-permute-start.11 = (bf16[16,8448]{1,0:T(8,128)(2,1)S(1)}, bf16[16,8448]{1,0:T(8,128)(2,1)S(1)}, u32[]{:S(2)}, u32[]{:S(2)}) collective-permute-start(bf16[16,8448]{1,0:T(8,128)(2,1)S(1)} %pad_maximum_fusion.13), channel_id=1, source_target_pairs={{0,16},{1,17},{2,18},{3,19},{4,20},{5,21},{6,22},{7,23},{8,24},{9,... | collective-permute-start | bytes 811016 | tf_op jit(solution)/shard_map/ppermute | solution.py:17
  141.5 2.2 collective-permute-done.11
  144.4 5.7 %collective-permute-done.5 = bf16[16,8448]{1,0:T(8,128)(2,1)} collective-permute-done((bf16[16,8448]{1,0:T(8,128)(2,1)S(1)}, bf16[16,8448]{1,0:T(8,128)(2,1)}, u32[]{:S(2)}, u32[]{:S(2)}) %collective-permute-start.5) | collective-permute-done | bytes 270368 | tf_op jit(solution)/shard_map/ppermute | solution.py:17
  154.8 6.9 %shard_map.68 = bf16[2048,1280]{1,0:T(8,128)(2,1)} custom-call(bf16[128,2048]{1,0:T(8,128)(2,1)} %bitcast.200, bf16[128,1280]{1,0:T(8,128)(2,1)} %pad_maximum_fusion.4.right_ref), custom_call_target="tpu_custom_call" | custom-call | flops 671088640 | bytes 6094848 | tf_op jit(solution)/shard_map/pallas_call | solution.py:130
  164.0 4.9 %collective-permute-done.12 = bf16[4,4,64,1280]{3,2,1,0:T(8,128)(2,1)} collective-permute-done((bf16[4,4,64,1280]{3,2,1,0:T(8,128)(2,1)S(1)}, bf16[4,4,64,1280]{3,2,1,0:T(8,128)(2,1)}, u32[]{:S(2)}, u32[]{:S(2)}) %collective-permute-start.12) | collective-permute-done | bytes 2621472 | tf_op jit(solution)/shard_map/ppermute | solution.py:73
  168.9 3.2 %convert_add_fusion = f32[4,4,64,1280]{3,2,1,0:T(8,128)S(1)} fusion(bf16[4,4,64,1280]{3,2,1,0:T(8,128)(2,1)} %collective-permute-done.12, bf16[4,4,2,64,1280]{4,3,2,1,0:T(8,128)(2,1)} %bitcast.186, s32[]{:T(128)S(6)} %select_n.204), kind=kLoop, calls=%fused_computation | loop fusion | flops 3932160 | bytes 10485764 | tf_op jit(solution)/shard_map/add | solution.py:74
  178.1 14.0 %collective-permute-done.21 = bf16[4,64,640]{2,1,0:T(8,128)(2,1)S(1)} collective-permute-done((bf16[4,64,640]{2,1,0:T(8,128)(2,1)}, bf16[4,64,640]{2,1,0:T(8,128)(2,1)S(1)}, u32[]{:S(2)}, u32[]{:S(2)}) %collective-permute-start.21) | collective-permute-done | bytes 327712 | tf_op jit(solution)/shard_map/ppermute | solution.py:73
  192.1 1.9 collective-permute-done.19
  197.8 7.2 %collective-permute-done.13 = bf16[4,64,640]{2,1,0:T(8,128)(2,1)S(1)} collective-permute-done((bf16[4,64,640]{2,1,0:T(8,128)(2,1)S(1)}, bf16[4,64,640]{2,1,0:T(8,128)(2,1)S(1)}, u32[]{:S(2)}, u32[]{:S(2)}) %collective-permute-start.13) | collective-permute-done | bytes 327712 | tf_op jit(solution)/shard_map/ppermute | solution.py:73
  207.3 2.4 collective-permute-done.18
  212.7 5.8 %collective-permute-start.25 = (f32[32,1280]{1,0:T(8,128)S(1)}, f32[32,1280]{1,0:T(8,128)S(1)}, u32[]{:S(2)}, u32[]{:S(2)}) collective-permute-start(f32[32,1280]{1,0:T(8,128)S(1)} %dynamic-slice_bitcast_fusion.1), channel_id=1, source_target_pairs={{0,128},{32,160},{64,192},{96,224},{128,0},{160,32},{192,64},{224,... | collective-permute-start | bytes 491528 | tf_op jit(solution)/shard_map/ppermute | solution.py:107
  218.5 5.4 %collective-permute-done.25 = f32[32,1280]{1,0:T(8,128)S(1)} collective-permute-done((f32[32,1280]{1,0:T(8,128)S(1)}, f32[32,1280]{1,0:T(8,128)S(1)}, u32[]{:S(2)}, u32[]{:S(2)}) %collective-permute-start.25) | collective-permute-done | bytes 163872 | tf_op jit(solution)/shard_map/ppermute | solution.py:107
  223.9 2.5 collective-permute-start.26
  226.4 3.3 %collective-permute-done.26 = f32[16,1280]{1,0:T(8,128)S(1)} collective-permute-done((f32[16,1280]{1,0:T(8,128)S(1)}, f32[16,1280]{1,0:T(8,128)S(1)}, u32[]{:S(2)}, u32[]{:S(2)}) %collective-permute-start.26) | collective-permute-done | bytes 81952 | tf_op jit(solution)/shard_map/ppermute | solution.py:107
  229.8 4.0 %collective-permute-done.27 = f32[8,1280]{1,0:T(8,128)S(1)} collective-permute-done((f32[8,1280]{1,0:T(8,128)S(1)}, f32[8,1280]{1,0:T(8,128)S(1)}, u32[]{:S(2)}, u32[]{:S(2)}) %collective-permute-start.27) | collective-permute-done | bytes 40992 | tf_op jit(solution)/shard_map/ppermute | solution.py:107
  233.9 4.4 %collective-permute-done.28 = f32[8,1280]{1,0:T(8,128)S(1)} collective-permute-done((f32[8,1280]{1,0:T(8,128)S(1)}, f32[8,1280]{1,0:T(8,128)S(1)}, u32[]{:S(2)}, u32[]{:S(2)}) %collective-permute-start.28) | collective-permute-done | bytes 40992 | tf_op jit(solution)/shard_map/ppermute | solution.py:110
  240.1 7.1 %collective-permute-done.29 = f32[16,1280]{1,0:T(8,128)S(1)} collective-permute-done((f32[16,1280]{1,0:T(8,128)S(1)}, f32[16,1280]{1,0:T(8,128)S(1)}, u32[]{:S(2)}, u32[]{:S(2)}) %collective-permute-start.29) | collective-permute-done | bytes 81952 | tf_op jit(solution)/shard_map/ppermute | solution.py:110
  247.3 4.1 %collective-permute-start.30 = (f32[32,1280]{1,0:T(8,128)S(1)}, f32[32,1280]{1,0:T(8,128)S(1)}, u32[]{:S(2)}, u32[]{:S(2)}) collective-permute-start(f32[32,1280]{1,0:T(8,128)S(1)} %maximum_select_fusion.1), channel_id=1, source_target_pairs={{0,128},{32,160},{64,192},{96,224},{128,0},{160,32},{192,64},{224,... | collective-permute-start | bytes 491528 | tf_op jit(solution)/shard_map/ppermute | solution.py:110
  251.3 5.3 %convolution_bitcast_fusion = f32[1,128,2048]{2,1,0:T(8,128)} fusion(bf16[2048,1280]{1,0:T(8,128)(2,1)} %all-gather.2.cloned.1.call-done, bf16[128,128]{1,0:T(8,128)(2,1)} %copy-done.3, bf16[128,128]{1,0:T(8,128)(2,1)} %copy-done.4, bf16[128,1024]{1,0:T(8,128)(2,1)S(1)} %copy.81), kind=kOutput, calls=%fused_computation.2 | convolution fusion | flops 672071680 | bytes 6619136 | tf_op jit(solution)/shard_map/dot_general | solution.py:260
  (175 shorter events, 52.3 us)
Async XLA Ops:
  7.2 59.0 %all-gather.2.cloned.1.call-start = ((), (), s32[]{:S(2)}) async-start(), calls=%async_computation | async-start | bytes 5406720 | tf_op jit(solution)/shard_map/all_gather | solution.py:226
  72.6 12.2 %collective-permute-start = (bf16[16,8448]{1,0:T(8,128)(2,1)S(1)}, bf16[16,8448]{1,0:T(8,128)(2,1)S(1)}, u32[]{:S(2)}, u32[]{:S(2)}) collective-permute-start(bf16[16,8448]{1,0:T(8,128)(2,1)S(1)} %get-tuple-element.153), channel_id=1, source_target_pairs={{1,0},{2,1},{3,2},{4,3},{5,4},{6,5},{7,6},{8,7},{9,8},{10,9},{11,1... | collective-permute-start | bytes 811016 | tf_op jit(solution)/shard_map/ppermute | solution.py:17
  77.0 9.7 %collective-permute-start.1 = (bf16[16,8448]{1,0:T(8,128)(2,1)S(1)}, bf16[16,8448]{1,0:T(8,128)(2,1)S(1)}, u32[]{:S(2)}, u32[]{:S(2)}) collective-permute-start(bf16[16,8448]{1,0:T(8,128)(2,1)S(1)} %get-tuple-element.153), channel_id=1, source_target_pairs={{2,0},{3,1},{4,2},{5,3},{6,4},{7,5},{8,6},{9,7},{10,8},{11,9},{12,... | collective-permute-start | bytes 811016 | tf_op jit(solution)/shard_map/ppermute | solution.py:17
  79.2 14.7 %collective-permute-start.6 = (bf16[16,8448]{1,0:T(8,128)(2,1)S(1)}, bf16[16,8448]{1,0:T(8,128)(2,1)S(1)}, u32[]{:S(2)}, u32[]{:S(2)}) collective-permute-start(bf16[16,8448]{1,0:T(8,128)(2,1)S(1)} %get-tuple-element.154), channel_id=1, source_target_pairs={{0,1},{1,2},{2,3},{3,4},{4,5},{5,6},{6,7},{7,8},{8,9},{9,10},{10,1... | collective-permute-start | bytes 811016 | tf_op jit(solution)/shard_map/ppermute | solution.py:17
  81.3 13.0 %collective-permute-start.7 = (bf16[16,8448]{1,0:T(8,128)(2,1)S(1)}, bf16[16,8448]{1,0:T(8,128)(2,1)S(1)}, u32[]{:S(2)}, u32[]{:S(2)}) collective-permute-start(bf16[16,8448]{1,0:T(8,128)(2,1)S(1)} %get-tuple-element.154), channel_id=1, source_target_pairs={{0,2},{1,3},{2,4},{3,5},{4,6},{5,7},{6,8},{7,9},{8,10},{9,11},{10,... | collective-permute-start | bytes 811016 | tf_op jit(solution)/shard_map/ppermute | solution.py:17
  87.3 11.3 %collective-permute-start.2 = (bf16[16,8448]{1,0:T(8,128)(2,1)S(1)}, bf16[16,8448]{1,0:T(8,128)(2,1)S(1)}, u32[]{:S(2)}, u32[]{:S(2)}) collective-permute-start(bf16[16,8448]{1,0:T(8,128)(2,1)S(1)} %pad_maximum_fusion.6), channel_id=1, source_target_pairs={{2,0},{3,1},{4,2},{5,3},{6,4},{7,5},{8,6},{9,7},{10,8},{11,9},{12,... | collective-permute-start | bytes 811016 | tf_op jit(solution)/shard_map/ppermute | solution.py:17
  94.9 18.5 %collective-permute-start.8 = (bf16[16,8448]{1,0:T(8,128)(2,1)S(1)}, bf16[16,8448]{1,0:T(8,128)(2,1)S(1)}, u32[]{:S(2)}, u32[]{:S(2)}) collective-permute-start(bf16[16,8448]{1,0:T(8,128)(2,1)S(1)} %pad_maximum_fusion.10), channel_id=1, source_target_pairs={{0,2},{1,3},{2,4},{3,5},{4,6},{5,7},{6,8},{7,9},{8,10},{9,11},{10,... | collective-permute-start | bytes 811016 | tf_op jit(solution)/shard_map/ppermute | solution.py:17
  99.2 16.9 %collective-permute-start.3 = (bf16[16,8448]{1,0:T(8,128)(2,1)S(1)}, bf16[16,8448]{1,0:T(8,128)(2,1)S(1)}, u32[]{:S(2)}, u32[]{:S(2)}) collective-permute-start(bf16[16,8448]{1,0:T(8,128)(2,1)S(1)} %pad_maximum_fusion.7), channel_id=1, source_target_pairs={{4,0},{5,1},{6,2},{7,3},{8,4},{9,5},{10,6},{11,7},{12,8},{13,9},{1... | collective-permute-start | bytes 811016 | tf_op jit(solution)/shard_map/ppermute | solution.py:17
  114.0 12.4 %collective-permute-start.9 = (bf16[16,8448]{1,0:T(8,128)(2,1)S(1)}, bf16[16,8448]{1,0:T(8,128)(2,1)S(1)}, u32[]{:S(2)}, u32[]{:S(2)}) collective-permute-start(bf16[16,8448]{1,0:T(8,128)(2,1)S(1)} %pad_maximum_fusion.11), channel_id=1, source_target_pairs={{0,4},{1,5},{2,6},{3,7},{4,8},{5,9},{6,10},{7,11},{8,12},{9,13},{1... | collective-permute-start | bytes 811016 | tf_op jit(solution)/shard_map/ppermute | solution.py:17
  116.7 13.8 %collective-permute-start.4 = (bf16[16,8448]{1,0:T(8,128)(2,1)S(1)}, bf16[16,8448]{1,0:T(8,128)(2,1)S(1)}, u32[]{:S(2)}, u32[]{:S(2)}) collective-permute-start(bf16[16,8448]{1,0:T(8,128)(2,1)S(1)} %pad_maximum_fusion.8), channel_id=1, source_target_pairs={{8,0},{9,1},{10,2},{11,3},{12,4},{13,5},{14,6},{15,7},{16,8},{17,9... | collective-permute-start | bytes 811016 | tf_op jit(solution)/shard_map/ppermute | solution.py:17
  127.0 8.9 %collective-permute-start.10 = (bf16[16,8448]{1,0:T(8,128)(2,1)S(1)}, bf16[16,8448]{1,0:T(8,128)(2,1)S(1)}, u32[]{:S(2)}, u32[]{:S(2)}) collective-permute-start(bf16[16,8448]{1,0:T(8,128)(2,1)S(1)} %pad_maximum_fusion.12), channel_id=1, source_target_pairs={{0,8},{1,9},{2,10},{3,11},{4,12},{5,13},{6,14},{7,15},{8,16},{9,17... | collective-permute-start | bytes 811016 | tf_op jit(solution)/shard_map/ppermute | solution.py:17
  136.5 7.1 %collective-permute-start.11 = (bf16[16,8448]{1,0:T(8,128)(2,1)S(1)}, bf16[16,8448]{1,0:T(8,128)(2,1)S(1)}, u32[]{:S(2)}, u32[]{:S(2)}) collective-permute-start(bf16[16,8448]{1,0:T(8,128)(2,1)S(1)} %pad_maximum_fusion.13), channel_id=1, source_target_pairs={{0,16},{1,17},{2,18},{3,19},{4,20},{5,21},{6,22},{7,23},{8,24},{9,... | collective-permute-start | bytes 811016 | tf_op jit(solution)/shard_map/ppermute | solution.py:17
  140.2 10.0 %collective-permute-start.5 = (bf16[16,8448]{1,0:T(8,128)(2,1)S(1)}, bf16[16,8448]{1,0:T(8,128)(2,1)}, u32[]{:S(2)}, u32[]{:S(2)}) collective-permute-start(bf16[16,8448]{1,0:T(8,128)(2,1)S(1)} %pad_maximum_fusion.9), channel_id=1, source_target_pairs={{16,0},{17,1},{18,2},{19,3},{20,4},{21,5},{22,6},{23,7},{24,8},{25... | collective-permute-start | bytes 811016 | tf_op jit(solution)/shard_map/ppermute | solution.py:17
  163.6 5.3 %collective-permute-start.12 = (bf16[4,4,64,1280]{3,2,1,0:T(8,128)(2,1)S(1)}, bf16[4,4,64,1280]{3,2,1,0:T(8,128)(2,1)}, u32[]{:S(2)}, u32[]{:S(2)}) collective-permute-start(bf16[4,4,64,1280]{3,2,1,0:T(8,128)(2,1)S(1)} %dynamic-slice_bitcast_fusion), channel_id=1, source_target_pairs={{0,1},{1,0},{2,3},{3,2},{4,5},{5,4},{6,7},{7,6},{8,9},{9,8},{10,11... | collective-permute-start | bytes 7864328 | tf_op jit(solution)/shard_map/ppermute | solution.py:73
  175.1 17.0 %collective-permute-start.21 = (bf16[4,64,640]{2,1,0:T(8,128)(2,1)}, bf16[4,64,640]{2,1,0:T(8,128)(2,1)S(1)}, u32[]{:S(2)}, u32[]{:S(2)}) collective-permute-start(bf16[4,64,640]{2,1,0:T(8,128)(2,1)} %get-tuple-element.135), channel_id=1, source_target_pairs={{0,24},{1,25},{2,26},{3,27},{4,28},{5,29},{6,30},{7,31},{8,0},{9,1... | collective-permute-start | bytes 983048 | tf_op jit(solution)/shard_map/ppermute | solution.py:73
  176.3 15.8 %collective-permute-start.20 = (bf16[4,64,640]{2,1,0:T(8,128)(2,1)}, bf16[4,64,640]{2,1,0:T(8,128)(2,1)S(1)}, u32[]{:S(2)}, u32[]{:S(2)}) collective-permute-start(bf16[4,64,640]{2,1,0:T(8,128)(2,1)} %get-tuple-element.136), channel_id=1, source_target_pairs={{0,16},{1,17},{2,18},{3,19},{4,20},{5,21},{6,22},{7,23},{8,24},{9,... | collective-permute-start | bytes 983048 | tf_op jit(solution)/shard_map/ppermute | solution.py:73
  176.3 17.7 %collective-permute-start.19 = (bf16[4,64,640]{2,1,0:T(8,128)(2,1)}, bf16[4,64,640]{2,1,0:T(8,128)(2,1)}, u32[]{:S(2)}, u32[]{:S(2)}) collective-permute-start(bf16[4,64,640]{2,1,0:T(8,128)(2,1)} %get-tuple-element.134), channel_id=1, source_target_pairs={{0,8},{1,9},{2,10},{3,11},{4,12},{5,13},{6,14},{7,15},{8,16},{9,17... | collective-permute-start | bytes 983048 | tf_op jit(solution)/shard_map/ppermute | solution.py:73
  177.9 18.9 %collective-permute-start.15 = (bf16[4,64,640]{2,1,0:T(8,128)(2,1)S(1)}, bf16[4,64,640]{2,1,0:T(8,128)(2,1)S(1)}, u32[]{:S(2)}, u32[]{:S(2)}) collective-permute-start(bf16[4,64,640]{2,1,0:T(8,128)(2,1)S(1)} %get-tuple-element.133), channel_id=1, source_target_pairs={{0,6},{1,7},{2,0},{3,1},{4,2},{5,3},{6,4},{7,5},{8,14},{9,15},{10,... | collective-permute-start | bytes 983048 | tf_op jit(solution)/shard_map/ppermute | solution.py:73
  178.0 19.8 %collective-permute-start.14 = (bf16[4,64,640]{2,1,0:T(8,128)(2,1)S(1)}, bf16[4,64,640]{2,1,0:T(8,128)(2,1)S(1)}, u32[]{:S(2)}, u32[]{:S(2)}) collective-permute-start(bf16[4,64,640]{2,1,0:T(8,128)(2,1)S(1)} %get-tuple-element.132), channel_id=1, source_target_pairs={{0,4},{1,5},{2,6},{3,7},{4,0},{5,1},{6,2},{7,3},{8,12},{9,13},{10,... | collective-permute-start | bytes 983048 | tf_op jit(solution)/shard_map/ppermute | solution.py:73
  192.1 12.9 %collective-permute-start.13 = (bf16[4,64,640]{2,1,0:T(8,128)(2,1)S(1)}, bf16[4,64,640]{2,1,0:T(8,128)(2,1)S(1)}, u32[]{:S(2)}, u32[]{:S(2)}) collective-permute-start(bf16[4,64,640]{2,1,0:T(8,128)(2,1)S(1)} %get-tuple-element.131), channel_id=1, source_target_pairs={{0,2},{1,3},{2,4},{3,5},{4,6},{5,7},{6,0},{7,1},{8,10},{9,11},{10,... | collective-permute-start | bytes 983048 | tf_op jit(solution)/shard_map/ppermute | solution.py:73
  195.4 10.8 %collective-permute-start.24 = (bf16[64,640]{1,0:T(8,128)(2,1)S(1)}, bf16[64,640]{1,0:T(8,128)(2,1)S(1)}, u32[]{:S(2)}, u32[]{:S(2)}) collective-permute-start(bf16[64,640]{1,0:T(8,128)(2,1)S(1)} %get-tuple-element.141), channel_id=1, source_target_pairs={{0,6},{1,7},{2,0},{3,1},{4,2},{5,3},{6,4},{7,5},{8,14},{9,15},{10,... | collective-permute-start | bytes 245768 | tf_op jit(solution)/shard_map/ppermute | solution.py:73
  196.8 10.5 %collective-permute-start.23 = (bf16[64,640]{1,0:T(8,128)(2,1)S(1)}, bf16[64,640]{1,0:T(8,128)(2,1)S(1)}, u32[]{:S(2)}, u32[]{:S(2)}) collective-permute-start(bf16[64,640]{1,0:T(8,128)(2,1)S(1)} %get-tuple-element.142), channel_id=1, source_target_pairs={{0,4},{1,5},{2,6},{3,7},{4,0},{5,1},{6,2},{7,3},{8,12},{9,13},{10,... | collective-permute-start | bytes 245768 | tf_op jit(solution)/shard_map/ppermute | solution.py:73
  196.8 10.5 %collective-permute-start.22 = (bf16[64,640]{1,0:T(8,128)(2,1)S(1)}, bf16[64,640]{1,0:T(8,128)(2,1)S(1)}, u32[]{:S(2)}, u32[]{:S(2)}) collective-permute-start(bf16[64,640]{1,0:T(8,128)(2,1)S(1)} %get-tuple-element.140), channel_id=1, source_target_pairs={{0,2},{1,3},{2,4},{3,5},{4,6},{5,7},{6,0},{7,1},{8,10},{9,11},{10,... | collective-permute-start | bytes 245768 | tf_op jit(solution)/shard_map/ppermute | solution.py:73
  205.2 4.5 %collective-permute-start.18 = (bf16[64,640]{1,0:T(8,128)(2,1)S(1)}, bf16[64,640]{1,0:T(8,128)(2,1)S(1)}, u32[]{:S(2)}, u32[]{:S(2)}) collective-permute-start(bf16[64,640]{1,0:T(8,128)(2,1)S(1)} %get-tuple-element.138), channel_id=1, source_target_pairs={{0,24},{1,25},{2,26},{3,27},{4,28},{5,29},{6,30},{7,31},{8,0},{9,1... | collective-permute-start | bytes 245768 | tf_op jit(solution)/shard_map/ppermute | solution.py:73
  205.2 6.0 %collective-permute-start.17 = (bf16[64,640]{1,0:T(8,128)(2,1)S(1)}, bf16[64,640]{1,0:T(8,128)(2,1)S(1)}, u32[]{:S(2)}, u32[]{:S(2)}) collective-permute-start(bf16[64,640]{1,0:T(8,128)(2,1)S(1)} %get-tuple-element.139), channel_id=1, source_target_pairs={{0,16},{1,17},{2,18},{3,19},{4,20},{5,21},{6,22},{7,23},{8,24},{9,... | collective-permute-start | bytes 245768 | tf_op jit(solution)/shard_map/ppermute | solution.py:73
  206.2 6.4 %collective-permute-start.16 = (bf16[64,640]{1,0:T(8,128)(2,1)S(1)}, bf16[64,640]{1,0:T(8,128)(2,1)S(1)}, u32[]{:S(2)}, u32[]{:S(2)}) collective-permute-start(bf16[64,640]{1,0:T(8,128)(2,1)S(1)} %get-tuple-element.137), channel_id=1, source_target_pairs={{0,8},{1,9},{2,10},{3,11},{4,12},{5,13},{6,14},{7,15},{8,16},{9,17... | collective-permute-start | bytes 245768 | tf_op jit(solution)/shard_map/ppermute | solution.py:73
  212.7 11.2 %collective-permute-start.25 = (f32[32,1280]{1,0:T(8,128)S(1)}, f32[32,1280]{1,0:T(8,128)S(1)}, u32[]{:S(2)}, u32[]{:S(2)}) collective-permute-start(f32[32,1280]{1,0:T(8,128)S(1)} %dynamic-slice_bitcast_fusion.1), channel_id=1, source_target_pairs={{0,128},{32,160},{64,192},{96,224},{128,0},{160,32},{192,64},{224,... | collective-permute-start | bytes 491528 | tf_op jit(solution)/shard_map/ppermute | solution.py:107
  223.9 5.7 %collective-permute-start.26 = (f32[16,1280]{1,0:T(8,128)S(1)}, f32[16,1280]{1,0:T(8,128)S(1)}, u32[]{:S(2)}, u32[]{:S(2)}) collective-permute-start(f32[16,1280]{1,0:T(8,128)S(1)} %dynamic-slice_bitcast_fusion.2), channel_id=1, source_target_pairs={{0,64},{32,96},{64,0},{96,32},{128,192},{160,224},{192,128},{224,1... | collective-permute-start | bytes 245768 | tf_op jit(solution)/shard_map/ppermute | solution.py:107
  229.7 4.1 %collective-permute-start.27 = (f32[8,1280]{1,0:T(8,128)S(1)}, f32[8,1280]{1,0:T(8,128)S(1)}, u32[]{:S(2)}, u32[]{:S(2)}) collective-permute-start(f32[8,1280]{1,0:T(8,128)S(1)} %dynamic-slice_bitcast_fusion.3), channel_id=1, source_target_pairs={{0,32},{32,0},{64,96},{96,64},{128,160},{160,128},{192,224},{224,1... | collective-permute-start | bytes 122888 | tf_op jit(solution)/shard_map/ppermute | solution.py:107
  233.8 4.5 %collective-permute-start.28 = (f32[8,1280]{1,0:T(8,128)S(1)}, f32[8,1280]{1,0:T(8,128)S(1)}, u32[]{:S(2)}, u32[]{:S(2)}) collective-permute-start(f32[8,1280]{1,0:T(8,128)S(1)} %bitcast_add_fusion.6), channel_id=1, source_target_pairs={{0,32},{32,0},{64,96},{96,64},{128,160},{160,128},{192,224},{224,1... | collective-permute-start | bytes 122888 | tf_op jit(solution)/shard_map/ppermute | solution.py:110
  238.3 8.9 %collective-permute-start.29 = (f32[16,1280]{1,0:T(8,128)S(1)}, f32[16,1280]{1,0:T(8,128)S(1)}, u32[]{:S(2)}, u32[]{:S(2)}) collective-permute-start(f32[16,1280]{1,0:T(8,128)S(1)} %maximum_select_fusion.2), channel_id=1, source_target_pairs={{0,64},{32,96},{64,0},{96,32},{128,192},{160,224},{192,128},{224,1... | collective-permute-start | bytes 245768 | tf_op jit(solution)/shard_map/ppermute | solution.py:110
  247.3 11.1 %collective-permute-start.30 = (f32[32,1280]{1,0:T(8,128)S(1)}, f32[32,1280]{1,0:T(8,128)S(1)}, u32[]{:S(2)}, u32[]{:S(2)}) collective-permute-start(f32[32,1280]{1,0:T(8,128)S(1)} %maximum_select_fusion.1), channel_id=1, source_target_pairs={{0,128},{32,160},{64,192},{96,224},{128,0},{160,32},{192,64},{224,... | collective-permute-start | bytes 491528 | tf_op jit(solution)/shard_map/ppermute | solution.py:110
  (11 other events, 236.2 us)
Sparse Core Ops, SparseCore 0:
  11.1 54.9 all-gather.1

commit v11 on v9

--- a/solution.py
+++ b/solution.py
@@ -38,7 +38,7 @@
             decay = decay * later_decay
         return flat, decay
 
-    radix = 4
+    radix = 2
     own = (flat, decay)
     part = chain([send(own, step) for step in range(radix, 0, -1)])
     width = radix
@@ -108,20 +108,20 @@
 
 
 def outer_kernel(left_ref, right_ref, out_ref):
-    out_ref[...] = lax.dot_general(
-        left_ref[...], right_ref[...], (((0,), (0,)), ((), ())), preferred_element_type=jnp.float32
+    out_ref[...] = jnp.dot(
+        left_ref[...], right_ref[...], preferred_element_type=jnp.float32
     ).astype(out_ref.dtype)
 
 
 def outer_product(left, right):
     depth, rows = left.shape
     cols = right.shape[1]
-    tile = 256
+    tile = 512
     return pl.pallas_call(
         outer_kernel,
         grid=(rows // tile,),
         in_specs=[
-            pl.BlockSpec((depth, tile), lambda i: (0, i)),
+            pl.BlockSpec((tile, depth), lambda i: (i, 0)),
             pl.BlockSpec((depth, cols), lambda i: (0, 0)),
         ],
         out_specs=pl.BlockSpec((tile, cols), lambda i: (i, 0)),
@@ -131,7 +131,7 @@
             bytes_accessed=2 * (depth * rows + depth * cols + rows * cols),
             transcendentals=0,
         ),
-    )(left, right)
+    )(left.T, right)
 
 
 def dequantize(code_rows, scale_rows):

time: 266 us -> 264 us (level)
  starting transfers between devices: 109 us -> 73.2 us
  waiting for transfers between devices: 93.2 us -> 126 us
    ppermute x13, starting transfers between devices: 29.4 us -> 7.59 us  [digit_reduce(): got = lax.ppermute(piece.astype(jnp.bfloat16), axis, pairs)]
    ppermute x16 -> x12, waiting for transfers between devices: 15.4 us -> 35.3 us  [shifted(): lax.ppermute(value.astype(jnp.bfloat16), axis, pairs).astype(value.dtype)]
    ppermute x16 -> x12, starting transfers between devices: 49.8 us -> 35.4 us  [shifted(): lax.ppermute(value.astype(jnp.bfloat16), axis, pairs).astype(value.dtype)]
    ppermute x13, waiting for transfers between devices: 20.4 us -> 33.3 us  [digit_reduce(): got = lax.ppermute(piece.astype(jnp.bfloat16), axis, pairs)]
  transfers between devices with their start and end apart: 44 -> 40, of which waited for: 18 -> 20; matrix products, arithmetic and copies ran while one was open for 7% -> 8% of each run, Pallas kernels for 0% -> 0%
where the time goes in v11:
time: 264 us; the launch traced here: 263 us
  waiting for transfers between devices  126 us (48%)
  starting transfers between devices  73.2 us (28%)
  other arithmetic  17.1 us (6%)
  between operations  14.9 us (6%)
  local copies, waits for them, and re-layouts  14.5 us (5%)
  matrix products  12.8 us (5%)
  Pallas kernels  5.07 us (2%)
    all_gather x1, waiting for transfers between devices, local(): lax.all_gather(dequantize(weight_codes, scales), 'seq', axis=0, tiled=True)  50.6 us
    ppermute x12, starting transfers between devices, shifted(): lax.ppermute(value.astype(jnp.bfloat16), axis, pairs).astype(value.dtype)  35.4 us
    ppermute x12, waiting for transfers between devices, shifted(): lax.ppermute(value.astype(jnp.bfloat16), axis, pairs).astype(value.dtype)  35.3 us
    ppermute x13, waiting for transfers between devices, digit_reduce(): got = lax.ppermute(piece.astype(jnp.bfloat16), axis, pairs)  33.3 us
    ppermute x7, starting transfers between devices, replicated_sum(): total = total + lax.ppermute(piece, axis, pairs)  15.8 us
    ppermute x7, starting transfers between devices, replicated_sum(): gathered.append(lax.ppermute(total, axis, pairs))  14.4 us
    ppermute x13, starting transfers between devices, digit_reduce(): got = lax.ppermute(piece.astype(jnp.bfloat16), axis, pairs)  7.59 us
  transfers between devices with their start and end apart: 40, of which 20 were waited for; matrix products, arithmetic and copies ran while one was open for 8% of the time, Pallas kernels for 0%

profile of v11, /device:TPU:8, one launch (start us, length us, event | category | flops | bytes accessed | tf_op | source)
XLA Modules:
  0.0 263.3 jit_solution(4920523530102364054)
XLA Ops:
  15.6 50.6 %all-gather.2.cloned.1.call-done = bf16[2048,1280]{1,0:T(8,128)(2,1)} async-done(((bf16[64,1280]{1,0:T(8,128)(2,1)}), bf16[2048,1280]{1,0:T(8,128)(2,1)}) %all-gather.2.cloned.1.call-update) | async-done | bytes 5242896 | tf_op jit(solution)/shard_map/all_gather | solution.py:216
  66.1 4.2 %fusion = bf16[128,1280]{0,1:T(8,128)(2,1)S(1)} fusion(bf16[2048,1280]{1,0:T(8,128)(2,1)} %all-gather.2.cloned.1.call-done, bf16[1,128,2048]{2,1,0:T(8,128)(2,1)} %param.5), kind=kOutput, calls=%fused_computation.5 | convolution fusion | flops 671252480 | bytes 6094848 | tf_op jit(solution)/shard_map/dot_general | solution.py:217
  72.6 4.4 %collective-permute-start = (bf16[16,8448]{1,0:T(8,128)(2,1)S(1)}, bf16[16,8448]{1,0:T(8,128)(2,1)S(1)}, u32[]{:S(2)}, u32[]{:S(2)}) collective-permute-start(bf16[16,8448]{1,0:T(8,128)(2,1)S(1)} %get-tuple-element.162), channel_id=1, source_target_pairs={{1,0},{2,1},{3,2},{4,3},{5,4},{6,5},{7,6},{8,7},{9,8},{10,9},{11,1... | collective-permute-start | bytes 811016 | tf_op jit(solution)/shard_map/ppermute | solution.py:17
  77.0 2.1 collective-permute-start.1
  81.2 2.1 collective-permute-start.6
  83.3 3.5 %collective-permute-start.7 = (bf16[16,8448]{1,0:T(8,128)(2,1)S(1)}, bf16[16,8448]{1,0:T(8,128)(2,1)S(1)}, u32[]{:S(2)}, u32[]{:S(2)}) collective-permute-start(bf16[16,8448]{1,0:T(8,128)(2,1)S(1)} %get-tuple-element.163), channel_id=1, source_target_pairs={{0,2},{1,3},{2,4},{3,5},{4,6},{5,7},{6,8},{7,9},{8,10},{9,11},{10,... | collective-permute-start | bytes 811016 | tf_op jit(solution)/shard_map/ppermute | solution.py:17
  87.5 6.3 %collective-permute-start.2 = (bf16[16,8448]{1,0:T(8,128)(2,1)S(1)}, bf16[16,8448]{1,0:T(8,128)(2,1)S(1)}, u32[]{:S(2)}, u32[]{:S(2)}) collective-permute-start(bf16[16,8448]{1,0:T(8,128)(2,1)S(1)} %pad_maximum_fusion.5), channel_id=1, source_target_pairs={{2,0},{3,1},{4,2},{5,3},{6,4},{7,5},{8,6},{9,7},{10,8},{11,9},{12,... | collective-permute-start | bytes 811016 | tf_op jit(solution)/shard_map/ppermute | solution.py:17
  93.9 2.4 collective-permute-done.7
  99.9 4.3 %collective-permute-start.3 = (bf16[16,8448]{1,0:T(8,128)(2,1)S(1)}, bf16[16,8448]{1,0:T(8,128)(2,1)S(1)}, u32[]{:S(2)}, u32[]{:S(2)}) collective-permute-start(bf16[16,8448]{1,0:T(8,128)(2,1)S(1)} %pad_maximum_fusion.6), channel_id=1, source_target_pairs={{4,0},{5,1},{6,2},{7,3},{8,4},{9,5},{10,6},{11,7},{12,8},{13,9},{1... | collective-permute-start | bytes 811016 | tf_op jit(solution)/shard_map/ppermute | solution.py:17
  104.1 11.3 %collective-permute-done.8 = bf16[16,8448]{1,0:T(8,128)(2,1)S(1)} collective-permute-done((bf16[16,8448]{1,0:T(8,128)(2,1)S(1)}, bf16[16,8448]{1,0:T(8,128)(2,1)S(1)}, u32[]{:S(2)}, u32[]{:S(2)}) %collective-permute-start.8) | collective-permute-done | bytes 270368 | tf_op jit(solution)/shard_map/ppermute | solution.py:17
  116.1 2.1 collective-permute-start.9
  120.7 7.7 %collective-permute-done.9 = bf16[16,8448]{1,0:T(8,128)(2,1)S(1)} collective-permute-done((bf16[16,8448]{1,0:T(8,128)(2,1)S(1)}, bf16[16,8448]{1,0:T(8,128)(2,1)S(1)}, u32[]{:S(2)}, u32[]{:S(2)}) %collective-permute-start.9) | collective-permute-done | bytes 270368 | tf_op jit(solution)/shard_map/ppermute | solution.py:17
  129.0 2.3 collective-permute-start.10
  132.6 5.4 %collective-permute-done.10 = bf16[16,8448]{1,0:T(8,128)(2,1)S(1)} collective-permute-done((bf16[16,8448]{1,0:T(8,128)(2,1)S(1)}, bf16[16,8448]{1,0:T(8,128)(2,1)S(1)}, u32[]{:S(2)}, u32[]{:S(2)}) %collective-permute-start.10) | collective-permute-done | bytes 270368 | tf_op jit(solution)/shard_map/ppermute | solution.py:17
  138.6 3.2 %collective-permute-start.11 = (bf16[16,8448]{1,0:T(8,128)(2,1)S(1)}, bf16[16,8448]{1,0:T(8,128)(2,1)S(1)}, u32[]{:S(2)}, u32[]{:S(2)}) collective-permute-start(bf16[16,8448]{1,0:T(8,128)(2,1)S(1)} %pad_maximum_fusion.12), channel_id=1, source_target_pairs={{0,16},{1,17},{2,18},{3,19},{4,20},{5,21},{6,22},{7,23},{8,24},{9,... | collective-permute-start | bytes 811016 | tf_op jit(solution)/shard_map/ppermute | solution.py:17
  143.5 2.2 collective-permute-done.11
  146.4 5.7 %collective-permute-done.5 = bf16[16,8448]{1,0:T(8,128)(2,1)} collective-permute-done((bf16[16,8448]{1,0:T(8,128)(2,1)S(1)}, bf16[16,8448]{1,0:T(8,128)(2,1)}, u32[]{:S(2)}, u32[]{:S(2)}) %collective-permute-start.5) | collective-permute-done | bytes 270368 | tf_op jit(solution)/shard_map/ppermute | solution.py:17
  156.8 5.1 %shard_map.68 = bf16[2048,1280]{1,0:T(8,128)(2,1)} custom-call(bf16[2048,128]{1,0:T(8,128)(2,1)} %bitcast.225, bf16[128,1280]{1,0:T(8,128)(2,1)} %pad_maximum_fusion.4.right_ref), custom_call_target="tpu_custom_call" | custom-call | flops 671088640 | bytes 6094848 | tf_op jit(solution)/shard_map/pallas_call | solution.py:120
  164.2 4.9 %collective-permute-done.12 = bf16[4,4,64,1280]{3,2,1,0:T(8,128)(2,1)} collective-permute-done((bf16[4,4,64,1280]{3,2,1,0:T(8,128)(2,1)S(1)}, bf16[4,4,64,1280]{3,2,1,0:T(8,128)(2,1)}, u32[]{:S(2)}, u32[]{:S(2)}) %collective-permute-start.12) | collective-permute-done | bytes 2621472 | tf_op jit(solution)/shard_map/ppermute | solution.py:73
  169.1 3.2 %convert_add_fusion = f32[4,4,64,1280]{3,2,1,0:T(8,128)S(1)} fusion(bf16[4,4,64,1280]{3,2,1,0:T(8,128)(2,1)} %collective-permute-done.12, bf16[4,4,2,64,1280]{4,3,2,1,0:T(8,128)(2,1)} %bitcast.224, s32[]{:T(128)S(6)} %select_n.216), kind=kLoop, calls=%fused_computation.1 | loop fusion | flops 3932160 | bytes 10485764 | tf_op jit(solution)/shard_map/add | solution.py:74
  178.3 14.0 %collective-permute-done.21 = bf16[4,64,640]{2,1,0:T(8,128)(2,1)S(1)} collective-permute-done((bf16[4,64,640]{2,1,0:T(8,128)(2,1)}, bf16[4,64,640]{2,1,0:T(8,128)(2,1)S(1)}, u32[]{:S(2)}, u32[]{:S(2)}) %collective-permute-start.21) | collective-permute-done | bytes 327712 | tf_op jit(solution)/shard_map/ppermute | solution.py:73
  197.9 7.2 %collective-permute-done.13 = bf16[4,64,640]{2,1,0:T(8,128)(2,1)S(1)} collective-permute-done((bf16[4,64,640]{2,1,0:T(8,128)(2,1)S(1)}, bf16[4,64,640]{2,1,0:T(8,128)(2,1)S(1)}, u32[]{:S(2)}, u32[]{:S(2)}) %collective-permute-start.13) | collective-permute-done | bytes 327712 | tf_op jit(solution)/shard_map/ppermute | solution.py:73
  207.5 2.4 collective-permute-done.18
  212.9 3.4 %collective-permute-start.31 = (f32[8,1280]{1,0:T(8,128)S(1)}, f32[8,1280]{1,0:T(8,128)S(1)}, u32[]{:S(2)}, u32[]{:S(2)}) collective-permute-start(f32[8,1280]{1,0:T(8,128)S(1)} %get-tuple-element.148), channel_id=1, source_target_pairs={{0,224},{32,0},{64,32},{96,64},{128,96},{160,128},{192,160},{224,1... | collective-permute-start | bytes 122888 | tf_op jit(solution)/shard_map/ppermute | solution.py:100
  216.3 2.2 collective-permute-start.30
  219.6 3.9 %collective-permute-start.28 = (f32[8,1280]{1,0:T(8,128)S(1)}, f32[8,1280]{1,0:T(8,128)S(1)}, u32[]{:S(2)}, u32[]{:S(2)}) collective-permute-start(f32[8,1280]{1,0:T(8,128)S(1)} %get-tuple-element.151), channel_id=1, source_target_pairs={{0,128},{32,160},{64,192},{96,224},{128,0},{160,32},{192,64},{224,... | collective-permute-start | bytes 122888 | tf_op jit(solution)/shard_map/ppermute | solution.py:100
  223.6 3.6 %collective-permute-start.26 = (f32[8,1280]{1,0:T(8,128)S(1)}, f32[8,1280]{1,0:T(8,128)S(1)}, u32[]{:S(2)}, u32[]{:S(2)}) collective-permute-start(f32[8,1280]{1,0:T(8,128)S(1)} %get-tuple-element.153), channel_id=1, source_target_pairs={{0,64},{32,96},{64,128},{96,160},{128,192},{160,224},{192,0},{224,... | collective-permute-start | bytes 122888 | tf_op jit(solution)/shard_map/ppermute | solution.py:100
  233.2 5.3 %convolution_bitcast_fusion = f32[1,128,2048]{2,1,0:T(8,128)} fusion(bf16[2048,1280]{1,0:T(8,128)(2,1)} %all-gather.2.cloned.1.call-done, bf16[128,128]{1,0:T(8,128)(2,1)S(1)} %copy-done.4, bf16[128,128]{1,0:T(8,128)(2,1)S(1)} %copy-done.6, bf16[128,1024]{1,0:T(8,128)(2,1)S(1)} %copy.85), kind=kOutput, calls=%fused_computation.3 | convolution fusion | flops 672071680 | bytes 6619136 | tf_op jit(solution)/shard_map/dot_general | solution.py:250
  240.0 2.7 %collective-permute-start.34 = (f32[8,1280]{1,0:T(8,128)S(1)}, f32[8,1280]{1,0:T(8,128)S(1)}, u32[]{:S(2)}, u32[]{:S(2)}) collective-permute-start(f32[8,1280]{1,0:T(8,128)S(1)} %get-tuple-element.95), channel_id=1, source_target_pairs={{0,96},{32,128},{64,160},{96,192},{128,224},{160,0},{192,32},{224,... | collective-permute-start | bytes 122888 | tf_op jit(solution)/shard_map/ppermute | solution.py:104
  244.8 2.5 collective-permute-start.36
  247.3 3.6 %collective-permute-start.37 = (f32[8,1280]{1,0:T(8,128)S(1)}, f32[8,1280]{1,0:T(8,128)S(1)}, u32[]{:S(2)}, u32[]{:S(2)}) collective-permute-start(f32[8,1280]{1,0:T(8,128)S(1)} %get-tuple-element.95), channel_id=1, source_target_pairs={{0,192},{32,224},{64,0},{96,32},{128,64},{160,96},{192,128},{224,1... | collective-permute-start | bytes 122888 | tf_op jit(solution)/shard_map/ppermute | solution.py:104
  252.6 2.4 collective-permute-done.38
  (203 shorter events, 62.1 us)
Async XLA Ops:
  7.2 59.0 %all-gather.2.cloned.1.call-start = ((), (), s32[]{:S(2)}) async-start(), calls=%async_computation | async-start | bytes 5406720 | tf_op jit(solution)/shard_map/all_gather | solution.py:216
  72.6 14.3 %collective-permute-start = (bf16[16,8448]{1,0:T(8,128)(2,1)S(1)}, bf16[16,8448]{1,0:T(8,128)(2,1)S(1)}, u32[]{:S(2)}, u32[]{:S(2)}) collective-permute-start(bf16[16,8448]{1,0:T(8,128)(2,1)S(1)} %get-tuple-element.162), channel_id=1, source_target_pairs={{1,0},{2,1},{3,2},{4,3},{5,4},{6,5},{7,6},{8,7},{9,8},{10,9},{11,1... | collective-permute-start | bytes 811016 | tf_op jit(solution)/shard_map/ppermute | solution.py:17
  77.0 9.9 %collective-permute-start.1 = (bf16[16,8448]{1,0:T(8,128)(2,1)S(1)}, bf16[16,8448]{1,0:T(8,128)(2,1)S(1)}, u32[]{:S(2)}, u32[]{:S(2)}) collective-permute-start(bf16[16,8448]{1,0:T(8,128)(2,1)S(1)} %get-tuple-element.162), channel_id=1, source_target_pairs={{2,0},{3,1},{4,2},{5,3},{6,4},{7,5},{8,6},{9,7},{10,8},{11,9},{12,... | collective-permute-start | bytes 811016 | tf_op jit(solution)/shard_map/ppermute | solution.py:17
  81.2 12.7 %collective-permute-start.6 = (bf16[16,8448]{1,0:T(8,128)(2,1)S(1)}, bf16[16,8448]{1,0:T(8,128)(2,1)S(1)}, u32[]{:S(2)}, u32[]{:S(2)}) collective-permute-start(bf16[16,8448]{1,0:T(8,128)(2,1)S(1)} %get-tuple-element.163), channel_id=1, source_target_pairs={{0,1},{1,2},{2,3},{3,4},{4,5},{5,6},{6,7},{7,8},{8,9},{9,10},{10,1... | collective-permute-start | bytes 811016 | tf_op jit(solution)/shard_map/ppermute | solution.py:17
  83.3 13.0 %collective-permute-start.7 = (bf16[16,8448]{1,0:T(8,128)(2,1)S(1)}, bf16[16,8448]{1,0:T(8,128)(2,1)S(1)}, u32[]{:S(2)}, u32[]{:S(2)}) collective-permute-start(bf16[16,8448]{1,0:T(8,128)(2,1)S(1)} %get-tuple-element.163), channel_id=1, source_target_pairs={{0,2},{1,3},{2,4},{3,5},{4,6},{5,7},{6,8},{7,9},{8,10},{9,11},{10,... | collective-permute-start | bytes 811016 | tf_op jit(solution)/shard_map/ppermute | solution.py:17
  87.5 11.8 %collective-permute-start.2 = (bf16[16,8448]{1,0:T(8,128)(2,1)S(1)}, bf16[16,8448]{1,0:T(8,128)(2,1)S(1)}, u32[]{:S(2)}, u32[]{:S(2)}) collective-permute-start(bf16[16,8448]{1,0:T(8,128)(2,1)S(1)} %pad_maximum_fusion.5), channel_id=1, source_target_pairs={{2,0},{3,1},{4,2},{5,3},{6,4},{7,5},{8,6},{9,7},{10,8},{11,9},{12,... | collective-permute-start | bytes 811016 | tf_op jit(solution)/shard_map/ppermute | solution.py:17
  96.9 18.5 %collective-permute-start.8 = (bf16[16,8448]{1,0:T(8,128)(2,1)S(1)}, bf16[16,8448]{1,0:T(8,128)(2,1)S(1)}, u32[]{:S(2)}, u32[]{:S(2)}) collective-permute-start(bf16[16,8448]{1,0:T(8,128)(2,1)S(1)} %pad_maximum_fusion.9), channel_id=1, source_target_pairs={{0,2},{1,3},{2,4},{3,5},{4,6},{5,7},{6,8},{7,9},{8,10},{9,11},{10,... | collective-permute-start | bytes 811016 | tf_op jit(solution)/shard_map/ppermute | solution.py:17
  99.9 18.2 %collective-permute-start.3 = (bf16[16,8448]{1,0:T(8,128)(2,1)S(1)}, bf16[16,8448]{1,0:T(8,128)(2,1)S(1)}, u32[]{:S(2)}, u32[]{:S(2)}) collective-permute-start(bf16[16,8448]{1,0:T(8,128)(2,1)S(1)} %pad_maximum_fusion.6), channel_id=1, source_target_pairs={{4,0},{5,1},{6,2},{7,3},{8,4},{9,5},{10,6},{11,7},{12,8},{13,9},{1... | collective-permute-start | bytes 811016 | tf_op jit(solution)/shard_map/ppermute | solution.py:17
  116.1 12.4 %collective-permute-start.9 = (bf16[16,8448]{1,0:T(8,128)(2,1)S(1)}, bf16[16,8448]{1,0:T(8,128)(2,1)S(1)}, u32[]{:S(2)}, u32[]{:S(2)}) collective-permute-start(bf16[16,8448]{1,0:T(8,128)(2,1)S(1)} %pad_maximum_fusion.10), channel_id=1, source_target_pairs={{0,4},{1,5},{2,6},{3,7},{4,8},{5,9},{6,10},{7,11},{8,12},{9,13},{1... | collective-permute-start | bytes 811016 | tf_op jit(solution)/shard_map/ppermute | solution.py:17
  118.7 13.8 %collective-permute-start.4 = (bf16[16,8448]{1,0:T(8,128)(2,1)S(1)}, bf16[16,8448]{1,0:T(8,128)(2,1)S(1)}, u32[]{:S(2)}, u32[]{:S(2)}) collective-permute-start(bf16[16,8448]{1,0:T(8,128)(2,1)S(1)} %pad_maximum_fusion.7), channel_id=1, source_target_pairs={{8,0},{9,1},{10,2},{11,3},{12,4},{13,5},{14,6},{15,7},{16,8},{17,9... | collective-permute-start | bytes 811016 | tf_op jit(solution)/shard_map/ppermute | solution.py:17
  129.0 8.9 %collective-permute-start.10 = (bf16[16,8448]{1,0:T(8,128)(2,1)S(1)}, bf16[16,8448]{1,0:T(8,128)(2,1)S(1)}, u32[]{:S(2)}, u32[]{:S(2)}) collective-permute-start(bf16[16,8448]{1,0:T(8,128)(2,1)S(1)} %pad_maximum_fusion.11), channel_id=1, source_target_pairs={{0,8},{1,9},{2,10},{3,11},{4,12},{5,13},{6,14},{7,15},{8,16},{9,17... | collective-permute-start | bytes 811016 | tf_op jit(solution)/shard_map/ppermute | solution.py:17
  142.2 10.0 %collective-permute-start.5 = (bf16[16,8448]{1,0:T(8,128)(2,1)S(1)}, bf16[16,8448]{1,0:T(8,128)(2,1)}, u32[]{:S(2)}, u32[]{:S(2)}) collective-permute-start(bf16[16,8448]{1,0:T(8,128)(2,1)S(1)} %pad_maximum_fusion.8), channel_id=1, source_target_pairs={{16,0},{17,1},{18,2},{19,3},{20,4},{21,5},{22,6},{23,7},{24,8},{25... | collective-permute-start | bytes 811016 | tf_op jit(solution)/shard_map/ppermute | solution.py:17
  175.3 17.0 %collective-permute-start.21 = (bf16[4,64,640]{2,1,0:T(8,128)(2,1)}, bf16[4,64,640]{2,1,0:T(8,128)(2,1)S(1)}, u32[]{:S(2)}, u32[]{:S(2)}) collective-permute-start(bf16[4,64,640]{2,1,0:T(8,128)(2,1)} %get-tuple-element.137), channel_id=1, source_target_pairs={{0,24},{1,25},{2,26},{3,27},{4,28},{5,29},{6,30},{7,31},{8,0},{9,1... | collective-permute-start | bytes 983048 | tf_op jit(solution)/shard_map/ppermute | solution.py:73
  176.5 15.8 %collective-permute-start.20 = (bf16[4,64,640]{2,1,0:T(8,128)(2,1)}, bf16[4,64,640]{2,1,0:T(8,128)(2,1)S(1)}, u32[]{:S(2)}, u32[]{:S(2)}) collective-permute-start(bf16[4,64,640]{2,1,0:T(8,128)(2,1)} %get-tuple-element.138), channel_id=1, source_target_pairs={{0,16},{1,17},{2,18},{3,19},{4,20},{5,21},{6,22},{7,23},{8,24},{9,... | collective-permute-start | bytes 983048 | tf_op jit(solution)/shard_map/ppermute | solution.py:73
  176.5 17.7 %collective-permute-start.19 = (bf16[4,64,640]{2,1,0:T(8,128)(2,1)}, bf16[4,64,640]{2,1,0:T(8,128)(2,1)}, u32[]{:S(2)}, u32[]{:S(2)}) collective-permute-start(bf16[4,64,640]{2,1,0:T(8,128)(2,1)} %get-tuple-element.136), channel_id=1, source_target_pairs={{0,8},{1,9},{2,10},{3,11},{4,12},{5,13},{6,14},{7,15},{8,16},{9,17... | collective-permute-start | bytes 983048 | tf_op jit(solution)/shard_map/ppermute | solution.py:73
  178.1 18.9 %collective-permute-start.15 = (bf16[4,64,640]{2,1,0:T(8,128)(2,1)S(1)}, bf16[4,64,640]{2,1,0:T(8,128)(2,1)S(1)}, u32[]{:S(2)}, u32[]{:S(2)}) collective-permute-start(bf16[4,64,640]{2,1,0:T(8,128)(2,1)S(1)} %get-tuple-element.135), channel_id=1, source_target_pairs={{0,6},{1,7},{2,0},{3,1},{4,2},{5,3},{6,4},{7,5},{8,14},{9,15},{10,... | collective-permute-start | bytes 983048 | tf_op jit(solution)/shard_map/ppermute | solution.py:73
  178.2 19.7 %collective-permute-start.14 = (bf16[4,64,640]{2,1,0:T(8,128)(2,1)S(1)}, bf16[4,64,640]{2,1,0:T(8,128)(2,1)S(1)}, u32[]{:S(2)}, u32[]{:S(2)}) collective-permute-start(bf16[4,64,640]{2,1,0:T(8,128)(2,1)S(1)} %get-tuple-element.134), channel_id=1, source_target_pairs={{0,4},{1,5},{2,6},{3,7},{4,0},{5,1},{6,2},{7,3},{8,12},{9,13},{10,... | collective-permute-start | bytes 983048 | tf_op jit(solution)/shard_map/ppermute | solution.py:73
  192.2 12.9 %collective-permute-start.13 = (bf16[4,64,640]{2,1,0:T(8,128)(2,1)S(1)}, bf16[4,64,640]{2,1,0:T(8,128)(2,1)S(1)}, u32[]{:S(2)}, u32[]{:S(2)}) collective-permute-start(bf16[4,64,640]{2,1,0:T(8,128)(2,1)S(1)} %get-tuple-element.133), channel_id=1, source_target_pairs={{0,2},{1,3},{2,4},{3,5},{4,6},{5,7},{6,0},{7,1},{8,10},{9,11},{10,... | collective-permute-start | bytes 983048 | tf_op jit(solution)/shard_map/ppermute | solution.py:73
  195.6 10.8 %collective-permute-start.24 = (bf16[64,640]{1,0:T(8,128)(2,1)S(1)}, bf16[64,640]{1,0:T(8,128)(2,1)S(1)}, u32[]{:S(2)}, u32[]{:S(2)}) collective-permute-start(bf16[64,640]{1,0:T(8,128)(2,1)S(1)} %get-tuple-element.143), channel_id=1, source_target_pairs={{0,6},{1,7},{2,0},{3,1},{4,2},{5,3},{6,4},{7,5},{8,14},{9,15},{10,... | collective-permute-start | bytes 245768 | tf_op jit(solution)/shard_map/ppermute | solution.py:73
  197.0 10.5 %collective-permute-start.23 = (bf16[64,640]{1,0:T(8,128)(2,1)S(1)}, bf16[64,640]{1,0:T(8,128)(2,1)S(1)}, u32[]{:S(2)}, u32[]{:S(2)}) collective-permute-start(bf16[64,640]{1,0:T(8,128)(2,1)S(1)} %get-tuple-element.144), channel_id=1, source_target_pairs={{0,4},{1,5},{2,6},{3,7},{4,0},{5,1},{6,2},{7,3},{8,12},{9,13},{10,... | collective-permute-start | bytes 245768 | tf_op jit(solution)/shard_map/ppermute | solution.py:73
  197.0 10.5 %collective-permute-start.22 = (bf16[64,640]{1,0:T(8,128)(2,1)S(1)}, bf16[64,640]{1,0:T(8,128)(2,1)S(1)}, u32[]{:S(2)}, u32[]{:S(2)}) collective-permute-start(bf16[64,640]{1,0:T(8,128)(2,1)S(1)} %get-tuple-element.142), channel_id=1, source_target_pairs={{0,2},{1,3},{2,4},{3,5},{4,6},{5,7},{6,0},{7,1},{8,10},{9,11},{10,... | collective-permute-start | bytes 245768 | tf_op jit(solution)/shard_map/ppermute | solution.py:73
  212.9 10.7 %collective-permute-start.31 = (f32[8,1280]{1,0:T(8,128)S(1)}, f32[8,1280]{1,0:T(8,128)S(1)}, u32[]{:S(2)}, u32[]{:S(2)}) collective-permute-start(f32[8,1280]{1,0:T(8,128)S(1)} %get-tuple-element.148), channel_id=1, source_target_pairs={{0,224},{32,0},{64,32},{96,64},{128,96},{160,128},{192,160},{224,1... | collective-permute-start | bytes 122888 | tf_op jit(solution)/shard_map/ppermute | solution.py:100
  216.3 10.9 %collective-permute-start.30 = (f32[8,1280]{1,0:T(8,128)S(1)}, f32[8,1280]{1,0:T(8,128)S(1)}, u32[]{:S(2)}, u32[]{:S(2)}) collective-permute-start(f32[8,1280]{1,0:T(8,128)S(1)} %get-tuple-element.149), channel_id=1, source_target_pairs={{0,192},{32,224},{64,0},{96,32},{128,64},{160,96},{192,128},{224,1... | collective-permute-start | bytes 122888 | tf_op jit(solution)/shard_map/ppermute | solution.py:100
  218.5 10.4 %collective-permute-start.29 = (f32[8,1280]{1,0:T(8,128)S(1)}, f32[8,1280]{1,0:T(8,128)S(1)}, u32[]{:S(2)}, u32[]{:S(2)}) collective-permute-start(f32[8,1280]{1,0:T(8,128)S(1)} %get-tuple-element.150), channel_id=1, source_target_pairs={{0,160},{32,192},{64,224},{96,0},{128,32},{160,64},{192,96},{224,1... | collective-permute-start | bytes 122888 | tf_op jit(solution)/shard_map/ppermute | solution.py:100
  219.6 9.2 %collective-permute-start.28 = (f32[8,1280]{1,0:T(8,128)S(1)}, f32[8,1280]{1,0:T(8,128)S(1)}, u32[]{:S(2)}, u32[]{:S(2)}) collective-permute-start(f32[8,1280]{1,0:T(8,128)S(1)} %get-tuple-element.151), channel_id=1, source_target_pairs={{0,128},{32,160},{64,192},{96,224},{128,0},{160,32},{192,64},{224,... | collective-permute-start | bytes 122888 | tf_op jit(solution)/shard_map/ppermute | solution.py:100
  223.6 7.2 %collective-permute-start.27 = (f32[8,1280]{1,0:T(8,128)S(1)}, f32[8,1280]{1,0:T(8,128)S(1)}, u32[]{:S(2)}, u32[]{:S(2)}) collective-permute-start(f32[8,1280]{1,0:T(8,128)S(1)} %get-tuple-element.152), channel_id=1, source_target_pairs={{0,96},{32,128},{64,160},{96,192},{128,224},{160,0},{192,32},{224,... | collective-permute-start | bytes 122888 | tf_op jit(solution)/shard_map/ppermute | solution.py:100
  223.6 8.0 %collective-permute-start.26 = (f32[8,1280]{1,0:T(8,128)S(1)}, f32[8,1280]{1,0:T(8,128)S(1)}, u32[]{:S(2)}, u32[]{:S(2)}) collective-permute-start(f32[8,1280]{1,0:T(8,128)S(1)} %get-tuple-element.153), channel_id=1, source_target_pairs={{0,64},{32,96},{64,128},{96,160},{128,192},{160,224},{192,0},{224,... | collective-permute-start | bytes 122888 | tf_op jit(solution)/shard_map/ppermute | solution.py:100
  232.4 14.9 %collective-permute-start.32 = (f32[8,1280]{1,0:T(8,128)S(1)}, f32[8,1280]{1,0:T(8,128)S(1)}, u32[]{:S(2)}, u32[]{:S(2)}) collective-permute-start(f32[8,1280]{1,0:T(8,128)S(1)} %get-tuple-element.95), channel_id=1, source_target_pairs={{0,32},{32,64},{64,96},{96,128},{128,160},{160,192},{192,224},{224... | collective-permute-start | bytes 122888 | tf_op jit(solution)/shard_map/ppermute | solution.py:104
  238.4 12.5 %collective-permute-start.33 = (f32[8,1280]{1,0:T(8,128)S(1)}, f32[8,1280]{1,0:T(8,128)S(1)}, u32[]{:S(2)}, u32[]{:S(2)}) collective-permute-start(f32[8,1280]{1,0:T(8,128)S(1)} %get-tuple-element.95), channel_id=1, source_target_pairs={{0,64},{32,96},{64,128},{96,160},{128,192},{160,224},{192,0},{224,... | collective-permute-start | bytes 122888 | tf_op jit(solution)/shard_map/ppermute | solution.py:104
  240.0 12.0 %collective-permute-start.34 = (f32[8,1280]{1,0:T(8,128)S(1)}, f32[8,1280]{1,0:T(8,128)S(1)}, u32[]{:S(2)}, u32[]{:S(2)}) collective-permute-start(f32[8,1280]{1,0:T(8,128)S(1)} %get-tuple-element.95), channel_id=1, source_target_pairs={{0,96},{32,128},{64,160},{96,192},{128,224},{160,0},{192,32},{224,... | collective-permute-start | bytes 122888 | tf_op jit(solution)/shard_map/ppermute | solution.py:104
  242.8 9.3 %collective-permute-start.35 = (f32[8,1280]{1,0:T(8,128)S(1)}, f32[8,1280]{1,0:T(8,128)S(1)}, u32[]{:S(2)}, u32[]{:S(2)}) collective-permute-start(f32[8,1280]{1,0:T(8,128)S(1)} %get-tuple-element.95), channel_id=1, source_target_pairs={{0,128},{32,160},{64,192},{96,224},{128,0},{160,32},{192,64},{224,... | collective-permute-start | bytes 122888 | tf_op jit(solution)/shard_map/ppermute | solution.py:104
  244.8 7.3 %collective-permute-start.36 = (f32[8,1280]{1,0:T(8,128)S(1)}, f32[8,1280]{1,0:T(8,128)S(1)}, u32[]{:S(2)}, u32[]{:S(2)}) collective-permute-start(f32[8,1280]{1,0:T(8,128)S(1)} %get-tuple-element.95), channel_id=1, source_target_pairs={{0,160},{32,192},{64,224},{96,0},{128,32},{160,64},{192,96},{224,1... | collective-permute-start | bytes 122888 | tf_op jit(solution)/shard_map/ppermute | solution.py:104
  (21 other events, 355.1 us)
Sparse Core Ops, SparseCore 0:
  11.1 54.9 all-gather.1

commit v12 on v11

--- a/solution.py
+++ b/solution.py
@@ -81,12 +81,8 @@
     block = rows // count
     value = partial.reshape(count // 8, 4, 2, block, cols)
     value = digit_reduce(value, axis, 2, 1, 2)
-    half = cols // 2
-    first = digit_reduce(value[..., :half], axis, 1, 2, 4)
-    first = digit_reduce(first, axis, 0, 8, count // 8)
-    second = digit_reduce(value[..., half:], axis, 0, 8, count // 8)
-    second = digit_reduce(second, axis, 0, 2, 4)
-    return jnp.concatenate([first, second], axis=1)
+    value = digit_reduce(value, axis, 1, 2, 4)
+    return digit_reduce(value, axis, 0, 8, count // 8)
 
 
 def replicated_sum(value, axis):
@@ -116,7 +112,7 @@
 def outer_product(left, right):
     depth, rows = left.shape
     cols = right.shape[1]
-    tile = 512
+    tile = 1024
     return pl.pallas_call(
         outer_kernel,
         grid=(rows // tile,),

time: 264 us -> 272 us (1.030)
  waiting for transfers between devices: 126 us -> 136 us
    ppermute x13 -> x7, waiting for transfers between devices: 33.3 us -> 43.9 us  [digit_reduce(): got = lax.ppermute(piece.astype(jnp.bfloat16), axis, pairs)]
    ppermute x13 -> x7, starting transfers between devices: 7.59 us -> 5.17 us  [digit_reduce(): got = lax.ppermute(piece.astype(jnp.bfloat16), axis, pairs)]
    unnamed x32 -> x28, local copies, waits for them, and re-layouts: 4.76 us -> 5.59 us
  transfers between devices with their start and end apart: 40 -> 34, of which waited for: 20 -> 19; matrix products, arithmetic and copies ran while one was open for 8% -> 7% of each run, Pallas kernels for 0% -> 0%
where the time goes in v12:
time: 272 us; the launch traced here: 271 us
  waiting for transfers between devices  136 us (50%)
  starting transfers between devices  71 us (26%)
  other arithmetic  17.2 us (6%)
  local copies, waits for them, and re-layouts  14.9 us (5%)
  between operations  14.9 us (5%)
  matrix products  12.8 us (5%)
  Pallas kernels  4.28 us (2%)
    all_gather x1, waiting for transfers between devices, local(): lax.all_gather(dequantize(weight_codes, scales), 'seq', axis=0, tiled=True)  50.6 us
    ppermute x7, waiting for transfers between devices, digit_reduce(): got = lax.ppermute(piece.astype(jnp.bfloat16), axis, pairs)  43.9 us
    ppermute x12, starting transfers between devices, shifted(): lax.ppermute(value.astype(jnp.bfloat16), axis, pairs).astype(value.dtype)  35.4 us
    ppermute x12, waiting for transfers between devices, shifted(): lax.ppermute(value.astype(jnp.bfloat16), axis, pairs).astype(value.dtype)  35.3 us
    ppermute x7, starting transfers between devices, replicated_sum(): total = total + lax.ppermute(piece, axis, pairs)  15.8 us
    ppermute x7, starting transfers between devices, replicated_sum(): gathered.append(lax.ppermute(total, axis, pairs))  14.6 us
    unnamed x28, local copies, waits for them, and re-layouts  5.59 us
  transfers between devices with their start and end apart: 34, of which 19 were waited for; matrix products, arithmetic and copies ran while one was open for 7% of the time, Pallas kernels for 0%

profile of v12, /device:TPU:8, one launch (start us, length us, event | category | flops | bytes accessed | tf_op | source)
XLA Modules:
  0.0 271.3 jit_solution(14566261489575231983)
XLA Ops:
  15.6 50.6 %all-gather.2.cloned.1.call-done = bf16[2048,1280]{1,0:T(8,128)(2,1)} async-done(((bf16[64,1280]{1,0:T(8,128)(2,1)}), bf16[2048,1280]{1,0:T(8,128)(2,1)}) %all-gather.2.cloned.1.call-update) | async-done | bytes 5242896 | tf_op jit(solution)/shard_map/all_gather | solution.py:212
  66.1 4.2 %fusion = bf16[128,1280]{0,1:T(8,128)(2,1)S(1)} fusion(bf16[2048,1280]{1,0:T(8,128)(2,1)} %all-gather.2.cloned.1.call-done, bf16[1,128,2048]{2,1,0:T(8,128)(2,1)} %param.5), kind=kOutput, calls=%fused_computation.5 | convolution fusion | flops 671252480 | bytes 6094848 | tf_op jit(solution)/shard_map/dot_general | solution.py:213
  72.6 4.4 %collective-permute-start = (bf16[16,8448]{1,0:T(8,128)(2,1)S(1)}, bf16[16,8448]{1,0:T(8,128)(2,1)S(1)}, u32[]{:S(2)}, u32[]{:S(2)}) collective-permute-start(bf16[16,8448]{1,0:T(8,128)(2,1)S(1)} %get-tuple-element.154), channel_id=1, source_target_pairs={{1,0},{2,1},{3,2},{4,3},{5,4},{6,5},{7,6},{8,7},{9,8},{10,9},{11,1... | collective-permute-start | bytes 811016 | tf_op jit(solution)/shard_map/ppermute | solution.py:17
  77.0 2.1 collective-permute-start.1
  81.2 2.1 collective-permute-start.6
  83.3 3.5 %collective-permute-start.7 = (bf16[16,8448]{1,0:T(8,128)(2,1)S(1)}, bf16[16,8448]{1,0:T(8,128)(2,1)S(1)}, u32[]{:S(2)}, u32[]{:S(2)}) collective-permute-start(bf16[16,8448]{1,0:T(8,128)(2,1)S(1)} %get-tuple-element.155), channel_id=1, source_target_pairs={{0,2},{1,3},{2,4},{3,5},{4,6},{5,7},{6,8},{7,9},{8,10},{9,11},{10,... | collective-permute-start | bytes 811016 | tf_op jit(solution)/shard_map/ppermute | solution.py:17
  87.5 6.3 %collective-permute-start.2 = (bf16[16,8448]{1,0:T(8,128)(2,1)S(1)}, bf16[16,8448]{1,0:T(8,128)(2,1)S(1)}, u32[]{:S(2)}, u32[]{:S(2)}) collective-permute-start(bf16[16,8448]{1,0:T(8,128)(2,1)S(1)} %pad_maximum_fusion.5), channel_id=1, source_target_pairs={{2,0},{3,1},{4,2},{5,3},{6,4},{7,5},{8,6},{9,7},{10,8},{11,9},{12,... | collective-permute-start | bytes 811016 | tf_op jit(solution)/shard_map/ppermute | solution.py:17
  93.9 2.4 collective-permute-done.7
  99.9 4.3 %collective-permute-start.3 = (bf16[16,8448]{1,0:T(8,128)(2,1)S(1)}, bf16[16,8448]{1,0:T(8,128)(2,1)S(1)}, u32[]{:S(2)}, u32[]{:S(2)}) collective-permute-start(bf16[16,8448]{1,0:T(8,128)(2,1)S(1)} %pad_maximum_fusion.6), channel_id=1, source_target_pairs={{4,0},{5,1},{6,2},{7,3},{8,4},{9,5},{10,6},{11,7},{12,8},{13,9},{1... | collective-permute-start | bytes 811016 | tf_op jit(solution)/shard_map/ppermute | solution.py:17
  104.1 11.3 %collective-permute-done.8 = bf16[16,8448]{1,0:T(8,128)(2,1)S(1)} collective-permute-done((bf16[16,8448]{1,0:T(8,128)(2,1)S(1)}, bf16[16,8448]{1,0:T(8,128)(2,1)S(1)}, u32[]{:S(2)}, u32[]{:S(2)}) %collective-permute-start.8) | collective-permute-done | bytes 270368 | tf_op jit(solution)/shard_map/ppermute | solution.py:17
  120.7 7.7 %collective-permute-done.9 = bf16[16,8448]{1,0:T(8,128)(2,1)S(1)} collective-permute-done((bf16[16,8448]{1,0:T(8,128)(2,1)S(1)}, bf16[16,8448]{1,0:T(8,128)(2,1)S(1)}, u32[]{:S(2)}, u32[]{:S(2)}) %collective-permute-start.9) | collective-permute-done | bytes 270368 | tf_op jit(solution)/shard_map/ppermute | solution.py:17
  129.0 2.3 collective-permute-start.10
  132.6 5.4 %collective-permute-done.10 = bf16[16,8448]{1,0:T(8,128)(2,1)S(1)} collective-permute-done((bf16[16,8448]{1,0:T(8,128)(2,1)S(1)}, bf16[16,8448]{1,0:T(8,128)(2,1)S(1)}, u32[]{:S(2)}, u32[]{:S(2)}) %collective-permute-start.10) | collective-permute-done | bytes 270368 | tf_op jit(solution)/shard_map/ppermute | solution.py:17
  138.6 3.2 %collective-permute-start.11 = (bf16[16,8448]{1,0:T(8,128)(2,1)S(1)}, bf16[16,8448]{1,0:T(8,128)(2,1)S(1)}, u32[]{:S(2)}, u32[]{:S(2)}) collective-permute-start(bf16[16,8448]{1,0:T(8,128)(2,1)S(1)} %pad_maximum_fusion.12), channel_id=1, source_target_pairs={{0,16},{1,17},{2,18},{3,19},{4,20},{5,21},{6,22},{7,23},{8,24},{9,... | collective-permute-start | bytes 811016 | tf_op jit(solution)/shard_map/ppermute | solution.py:17
  143.5 2.2 collective-permute-done.11
  146.4 5.7 %collective-permute-done.5 = bf16[16,8448]{1,0:T(8,128)(2,1)} collective-permute-done((bf16[16,8448]{1,0:T(8,128)(2,1)S(1)}, bf16[16,8448]{1,0:T(8,128)(2,1)}, u32[]{:S(2)}, u32[]{:S(2)}) %collective-permute-start.5) | collective-permute-done | bytes 270368 | tf_op jit(solution)/shard_map/ppermute | solution.py:17
  156.8 4.3 %shard_map.68 = bf16[2048,1280]{1,0:T(8,128)(2,1)} custom-call(bf16[2048,128]{1,0:T(8,128)(2,1)} %bitcast.197, bf16[128,1280]{1,0:T(8,128)(2,1)} %pad_maximum_fusion.4.right_ref), custom_call_target="tpu_custom_call" | custom-call | flops 671088640 | bytes 6094848 | tf_op jit(solution)/shard_map/pallas_call | solution.py:116
  163.4 4.9 %collective-permute-done.12 = bf16[4,4,64,1280]{3,2,1,0:T(8,128)(2,1)} collective-permute-done((bf16[4,4,64,1280]{3,2,1,0:T(8,128)(2,1)S(1)}, bf16[4,4,64,1280]{3,2,1,0:T(8,128)(2,1)}, u32[]{:S(2)}, u32[]{:S(2)}) %collective-permute-start.12) | collective-permute-done | bytes 2621472 | tf_op jit(solution)/shard_map/ppermute | solution.py:73
  168.3 3.2 %convert_add_fusion = f32[4,4,64,1280]{3,2,1,0:T(8,128)S(1)} fusion(bf16[4,4,64,1280]{3,2,1,0:T(8,128)(2,1)} %collective-permute-done.12, bf16[4,4,2,64,1280]{4,3,2,1,0:T(8,128)(2,1)} %bitcast.196, s32[]{:T(128)S(6)} %select_n.189), kind=kLoop, calls=%fused_computation.1 | loop fusion | flops 3932160 | bytes 10485764 | tf_op jit(solution)/shard_map/add | solution.py:74
  171.5 2.3 copy-done
  177.0 15.8 %collective-permute-done.15 = bf16[4,64,1280]{2,1,0:T(8,128)(2,1)S(1)} collective-permute-done((bf16[4,64,1280]{2,1,0:T(8,128)(2,1)}, bf16[4,64,1280]{2,1,0:T(8,128)(2,1)S(1)}, u32[]{:S(2)}, u32[]{:S(2)}) %collective-permute-start.15) | collective-permute-done | bytes 655392 | tf_op jit(solution)/shard_map/ppermute | solution.py:73
  194.1 13.2 %collective-permute-done.13 = bf16[4,64,1280]{2,1,0:T(8,128)(2,1)S(1)} collective-permute-done((bf16[4,64,1280]{2,1,0:T(8,128)(2,1)S(1)}, bf16[4,64,1280]{2,1,0:T(8,128)(2,1)S(1)}, u32[]{:S(2)}, u32[]{:S(2)}) %collective-permute-start.13) | collective-permute-done | bytes 655392 | tf_op jit(solution)/shard_map/ppermute | solution.py:73
  211.8 6.8 %collective-permute-done.18 = bf16[64,1280]{1,0:T(8,128)(2,1)S(1)} collective-permute-done((bf16[64,1280]{1,0:T(8,128)(2,1)S(1)}, bf16[64,1280]{1,0:T(8,128)(2,1)S(1)}, u32[]{:S(2)}, u32[]{:S(2)}) %collective-permute-start.18) | collective-permute-done | bytes 163872 | tf_op jit(solution)/shard_map/ppermute | solution.py:73
  220.6 3.4 %collective-permute-start.25 = (f32[8,1280]{1,0:T(8,128)S(1)}, f32[8,1280]{1,0:T(8,128)S(1)}, u32[]{:S(2)}, u32[]{:S(2)}) collective-permute-start(f32[8,1280]{1,0:T(8,128)S(1)} %get-tuple-element.140), channel_id=1, source_target_pairs={{0,224},{32,0},{64,32},{96,64},{128,96},{160,128},{192,160},{224,1... | collective-permute-start | bytes 122888 | tf_op jit(solution)/shard_map/ppermute | solution.py:96
  224.0 2.2 collective-permute-start.24
  227.3 3.9 %collective-permute-start.22 = (f32[8,1280]{1,0:T(8,128)S(1)}, f32[8,1280]{1,0:T(8,128)S(1)}, u32[]{:S(2)}, u32[]{:S(2)}) collective-permute-start(f32[8,1280]{1,0:T(8,128)S(1)} %get-tuple-element.143), channel_id=1, source_target_pairs={{0,128},{32,160},{64,192},{96,224},{128,0},{160,32},{192,64},{224,... | collective-permute-start | bytes 122888 | tf_op jit(solution)/shard_map/ppermute | solution.py:96
  231.3 3.6 %collective-permute-start.20 = (f32[8,1280]{1,0:T(8,128)S(1)}, f32[8,1280]{1,0:T(8,128)S(1)}, u32[]{:S(2)}, u32[]{:S(2)}) collective-permute-start(f32[8,1280]{1,0:T(8,128)S(1)} %get-tuple-element.145), channel_id=1, source_target_pairs={{0,64},{32,96},{64,128},{96,160},{128,192},{160,224},{192,0},{224,... | collective-permute-start | bytes 122888 | tf_op jit(solution)/shard_map/ppermute | solution.py:96
  241.0 5.3 %convolution_bitcast_fusion = f32[1,128,2048]{2,1,0:T(8,128)} fusion(bf16[2048,1280]{1,0:T(8,128)(2,1)} %all-gather.2.cloned.1.call-done, bf16[128,128]{1,0:T(8,128)(2,1)} %copy-done.3, bf16[128,128]{1,0:T(8,128)(2,1)} %copy-done.4, bf16[128,1024]{1,0:T(8,128)(2,1)S(1)} %copy.88), kind=kOutput, calls=%fused_computation.3 | convolution fusion | flops 672071680 | bytes 6619136 | tf_op jit(solution)/shard_map/dot_general | solution.py:246
  249.8 3.0 %collective-permute-start.29 = (f32[8,1280]{1,0:T(8,128)S(1)}, f32[8,1280]{1,0:T(8,128)S(1)}, u32[]{:S(2)}, u32[]{:S(2)}) collective-permute-start(f32[8,1280]{1,0:T(8,128)S(1)} %get-tuple-element.95), channel_id=1, source_target_pairs={{0,128},{32,160},{64,192},{96,224},{128,0},{160,32},{192,64},{224,... | collective-permute-start | bytes 122888 | tf_op jit(solution)/shard_map/ppermute | solution.py:100
  252.8 2.2 collective-permute-start.30
  255.0 3.9 %collective-permute-start.31 = (f32[8,1280]{1,0:T(8,128)S(1)}, f32[8,1280]{1,0:T(8,128)S(1)}, u32[]{:S(2)}, u32[]{:S(2)}) collective-permute-start(f32[8,1280]{1,0:T(8,128)S(1)} %get-tuple-element.95), channel_id=1, source_target_pairs={{0,192},{32,224},{64,0},{96,32},{128,64},{160,96},{192,128},{224,1... | collective-permute-start | bytes 122888 | tf_op jit(solution)/shard_map/ppermute | solution.py:100
  260.8 2.3 collective-permute-done.32
  (181 shorter events, 58.3 us)
Async XLA Ops:
  7.2 59.0 %all-gather.2.cloned.1.call-start = ((), (), s32[]{:S(2)}) async-start(), calls=%async_computation | async-start | bytes 5406720 | tf_op jit(solution)/shard_map/all_gather | solution.py:212
  72.6 14.3 %collective-permute-start = (bf16[16,8448]{1,0:T(8,128)(2,1)S(1)}, bf16[16,8448]{1,0:T(8,128)(2,1)S(1)}, u32[]{:S(2)}, u32[]{:S(2)}) collective-permute-start(bf16[16,8448]{1,0:T(8,128)(2,1)S(1)} %get-tuple-element.154), channel_id=1, source_target_pairs={{1,0},{2,1},{3,2},{4,3},{5,4},{6,5},{7,6},{8,7},{9,8},{10,9},{11,1... | collective-permute-start | bytes 811016 | tf_op jit(solution)/shard_map/ppermute | solution.py:17
  77.0 9.9 %collective-permute-start.1 = (bf16[16,8448]{1,0:T(8,128)(2,1)S(1)}, bf16[16,8448]{1,0:T(8,128)(2,1)S(1)}, u32[]{:S(2)}, u32[]{:S(2)}) collective-permute-start(bf16[16,8448]{1,0:T(8,128)(2,1)S(1)} %get-tuple-element.154), channel_id=1, source_target_pairs={{2,0},{3,1},{4,2},{5,3},{6,4},{7,5},{8,6},{9,7},{10,8},{11,9},{12,... | collective-permute-start | bytes 811016 | tf_op jit(solution)/shard_map/ppermute | solution.py:17
  81.2 12.7 %collective-permute-start.6 = (bf16[16,8448]{1,0:T(8,128)(2,1)S(1)}, bf16[16,8448]{1,0:T(8,128)(2,1)S(1)}, u32[]{:S(2)}, u32[]{:S(2)}) collective-permute-start(bf16[16,8448]{1,0:T(8,128)(2,1)S(1)} %get-tuple-element.155), channel_id=1, source_target_pairs={{0,1},{1,2},{2,3},{3,4},{4,5},{5,6},{6,7},{7,8},{8,9},{9,10},{10,1... | collective-permute-start | bytes 811016 | tf_op jit(solution)/shard_map/ppermute | solution.py:17
  83.3 13.0 %collective-permute-start.7 = (bf16[16,8448]{1,0:T(8,128)(2,1)S(1)}, bf16[16,8448]{1,0:T(8,128)(2,1)S(1)}, u32[]{:S(2)}, u32[]{:S(2)}) collective-permute-start(bf16[16,8448]{1,0:T(8,128)(2,1)S(1)} %get-tuple-element.155), channel_id=1, source_target_pairs={{0,2},{1,3},{2,4},{3,5},{4,6},{5,7},{6,8},{7,9},{8,10},{9,11},{10,... | collective-permute-start | bytes 811016 | tf_op jit(solution)/shard_map/ppermute | solution.py:17
  87.5 11.8 %collective-permute-start.2 = (bf16[16,8448]{1,0:T(8,128)(2,1)S(1)}, bf16[16,8448]{1,0:T(8,128)(2,1)S(1)}, u32[]{:S(2)}, u32[]{:S(2)}) collective-permute-start(bf16[16,8448]{1,0:T(8,128)(2,1)S(1)} %pad_maximum_fusion.5), channel_id=1, source_target_pairs={{2,0},{3,1},{4,2},{5,3},{6,4},{7,5},{8,6},{9,7},{10,8},{11,9},{12,... | collective-permute-start | bytes 811016 | tf_op jit(solution)/shard_map/ppermute | solution.py:17
  96.9 18.5 %collective-permute-start.8 = (bf16[16,8448]{1,0:T(8,128)(2,1)S(1)}, bf16[16,8448]{1,0:T(8,128)(2,1)S(1)}, u32[]{:S(2)}, u32[]{:S(2)}) collective-permute-start(bf16[16,8448]{1,0:T(8,128)(2,1)S(1)} %pad_maximum_fusion.9), channel_id=1, source_target_pairs={{0,2},{1,3},{2,4},{3,5},{4,6},{5,7},{6,8},{7,9},{8,10},{9,11},{10,... | collective-permute-start | bytes 811016 | tf_op jit(solution)/shard_map/ppermute | solution.py:17
  99.9 18.2 %collective-permute-start.3 = (bf16[16,8448]{1,0:T(8,128)(2,1)S(1)}, bf16[16,8448]{1,0:T(8,128)(2,1)S(1)}, u32[]{:S(2)}, u32[]{:S(2)}) collective-permute-start(bf16[16,8448]{1,0:T(8,128)(2,1)S(1)} %pad_maximum_fusion.6), channel_id=1, source_target_pairs={{4,0},{5,1},{6,2},{7,3},{8,4},{9,5},{10,6},{11,7},{12,8},{13,9},{1... | collective-permute-start | bytes 811016 | tf_op jit(solution)/shard_map/ppermute | solution.py:17
  116.1 12.4 %collective-permute-start.9 = (bf16[16,8448]{1,0:T(8,128)(2,1)S(1)}, bf16[16,8448]{1,0:T(8,128)(2,1)S(1)}, u32[]{:S(2)}, u32[]{:S(2)}) collective-permute-start(bf16[16,8448]{1,0:T(8,128)(2,1)S(1)} %pad_maximum_fusion.10), channel_id=1, source_target_pairs={{0,4},{1,5},{2,6},{3,7},{4,8},{5,9},{6,10},{7,11},{8,12},{9,13},{1... | collective-permute-start | bytes 811016 | tf_op jit(solution)/shard_map/ppermute | solution.py:17
  118.7 13.8 %collective-permute-start.4 = (bf16[16,8448]{1,0:T(8,128)(2,1)S(1)}, bf16[16,8448]{1,0:T(8,128)(2,1)S(1)}, u32[]{:S(2)}, u32[]{:S(2)}) collective-permute-start(bf16[16,8448]{1,0:T(8,128)(2,1)S(1)} %pad_maximum_fusion.7), channel_id=1, source_target_pairs={{8,0},{9,1},{10,2},{11,3},{12,4},{13,5},{14,6},{15,7},{16,8},{17,9... | collective-permute-start | bytes 811016 | tf_op jit(solution)/shard_map/ppermute | solution.py:17
  129.0 8.9 %collective-permute-start.10 = (bf16[16,8448]{1,0:T(8,128)(2,1)S(1)}, bf16[16,8448]{1,0:T(8,128)(2,1)S(1)}, u32[]{:S(2)}, u32[]{:S(2)}) collective-permute-start(bf16[16,8448]{1,0:T(8,128)(2,1)S(1)} %pad_maximum_fusion.11), channel_id=1, source_target_pairs={{0,8},{1,9},{2,10},{3,11},{4,12},{5,13},{6,14},{7,15},{8,16},{9,17... | collective-permute-start | bytes 811016 | tf_op jit(solution)/shard_map/ppermute | solution.py:17
  138.6 7.1 %collective-permute-start.11 = (bf16[16,8448]{1,0:T(8,128)(2,1)S(1)}, bf16[16,8448]{1,0:T(8,128)(2,1)S(1)}, u32[]{:S(2)}, u32[]{:S(2)}) collective-permute-start(bf16[16,8448]{1,0:T(8,128)(2,1)S(1)} %pad_maximum_fusion.12), channel_id=1, source_target_pairs={{0,16},{1,17},{2,18},{3,19},{4,20},{5,21},{6,22},{7,23},{8,24},{9,... | collective-permute-start | bytes 811016 | tf_op jit(solution)/shard_map/ppermute | solution.py:17
  142.2 10.0 %collective-permute-start.5 = (bf16[16,8448]{1,0:T(8,128)(2,1)S(1)}, bf16[16,8448]{1,0:T(8,128)(2,1)}, u32[]{:S(2)}, u32[]{:S(2)}) collective-permute-start(bf16[16,8448]{1,0:T(8,128)(2,1)S(1)} %pad_maximum_fusion.8), channel_id=1, source_target_pairs={{16,0},{17,1},{18,2},{19,3},{20,4},{21,5},{22,6},{23,7},{24,8},{25... | collective-permute-start | bytes 811016 | tf_op jit(solution)/shard_map/ppermute | solution.py:17
  163.0 5.3 %collective-permute-start.12 = (bf16[4,4,64,1280]{3,2,1,0:T(8,128)(2,1)S(1)}, bf16[4,4,64,1280]{3,2,1,0:T(8,128)(2,1)}, u32[]{:S(2)}, u32[]{:S(2)}) collective-permute-start(bf16[4,4,64,1280]{3,2,1,0:T(8,128)(2,1)S(1)} %dynamic-slice_bitcast_fusion), channel_id=1, source_target_pairs={{0,1},{1,0},{2,3},{3,2},{4,5},{5,4},{6,7},{7,6},{8,9},{9,8},{10,11... | collective-permute-start | bytes 7864328 | tf_op jit(solution)/shard_map/ppermute | solution.py:73
  174.9 17.8 %collective-permute-start.15 = (bf16[4,64,1280]{2,1,0:T(8,128)(2,1)}, bf16[4,64,1280]{2,1,0:T(8,128)(2,1)S(1)}, u32[]{:S(2)}, u32[]{:S(2)}) collective-permute-start(bf16[4,64,1280]{2,1,0:T(8,128)(2,1)} %get-tuple-element.132), channel_id=1, source_target_pairs={{0,6},{1,7},{2,0},{3,1},{4,2},{5,3},{6,4},{7,5},{8,14},{9,15},{10,... | collective-permute-start | bytes 1966088 | tf_op jit(solution)/shard_map/ppermute | solution.py:73
  174.9 19.1 %collective-permute-start.14 = (bf16[4,64,1280]{2,1,0:T(8,128)(2,1)S(1)}, bf16[4,64,1280]{2,1,0:T(8,128)(2,1)S(1)}, u32[]{:S(2)}, u32[]{:S(2)}) collective-permute-start(bf16[4,64,1280]{2,1,0:T(8,128)(2,1)S(1)} %get-tuple-element.133), channel_id=1, source_target_pairs={{0,4},{1,5},{2,6},{3,7},{4,0},{5,1},{6,2},{7,3},{8,12},{9,13},{10,... | collective-permute-start | bytes 1966088 | tf_op jit(solution)/shard_map/ppermute | solution.py:73
  174.9 32.3 %collective-permute-start.13 = (bf16[4,64,1280]{2,1,0:T(8,128)(2,1)S(1)}, bf16[4,64,1280]{2,1,0:T(8,128)(2,1)S(1)}, u32[]{:S(2)}, u32[]{:S(2)}) collective-permute-start(bf16[4,64,1280]{2,1,0:T(8,128)(2,1)S(1)} %get-tuple-element.131), channel_id=1, source_target_pairs={{0,2},{1,3},{2,4},{3,5},{4,6},{5,7},{6,0},{7,1},{8,10},{9,11},{10,... | collective-permute-start | bytes 1966088 | tf_op jit(solution)/shard_map/ppermute | solution.py:73
  208.9 9.7 %collective-permute-start.18 = (bf16[64,1280]{1,0:T(8,128)(2,1)S(1)}, bf16[64,1280]{1,0:T(8,128)(2,1)S(1)}, u32[]{:S(2)}, u32[]{:S(2)}) collective-permute-start(bf16[64,1280]{1,0:T(8,128)(2,1)S(1)} %get-tuple-element.135), channel_id=1, source_target_pairs={{0,24},{1,25},{2,26},{3,27},{4,28},{5,29},{6,30},{7,31},{8,0},{9,1... | collective-permute-start | bytes 491528 | tf_op jit(solution)/shard_map/ppermute | solution.py:73
  210.2 8.4 %collective-permute-start.17 = (bf16[64,1280]{1,0:T(8,128)(2,1)S(1)}, bf16[64,1280]{1,0:T(8,128)(2,1)S(1)}, u32[]{:S(2)}, u32[]{:S(2)}) collective-permute-start(bf16[64,1280]{1,0:T(8,128)(2,1)S(1)} %get-tuple-element.136), channel_id=1, source_target_pairs={{0,16},{1,17},{2,18},{3,19},{4,20},{5,21},{6,22},{7,23},{8,24},{9,... | collective-permute-start | bytes 491528 | tf_op jit(solution)/shard_map/ppermute | solution.py:73
  210.2 10.2 %collective-permute-start.16 = (bf16[64,1280]{1,0:T(8,128)(2,1)S(1)}, bf16[64,1280]{1,0:T(8,128)(2,1)S(1)}, u32[]{:S(2)}, u32[]{:S(2)}) collective-permute-start(bf16[64,1280]{1,0:T(8,128)(2,1)S(1)} %get-tuple-element.134), channel_id=1, source_target_pairs={{0,8},{1,9},{2,10},{3,11},{4,12},{5,13},{6,14},{7,15},{8,16},{9,17... | collective-permute-start | bytes 491528 | tf_op jit(solution)/shard_map/ppermute | solution.py:73
  220.6 10.7 %collective-permute-start.25 = (f32[8,1280]{1,0:T(8,128)S(1)}, f32[8,1280]{1,0:T(8,128)S(1)}, u32[]{:S(2)}, u32[]{:S(2)}) collective-permute-start(f32[8,1280]{1,0:T(8,128)S(1)} %get-tuple-element.140), channel_id=1, source_target_pairs={{0,224},{32,0},{64,32},{96,64},{128,96},{160,128},{192,160},{224,1... | collective-permute-start | bytes 122888 | tf_op jit(solution)/shard_map/ppermute | solution.py:96
  224.0 10.9 %collective-permute-start.24 = (f32[8,1280]{1,0:T(8,128)S(1)}, f32[8,1280]{1,0:T(8,128)S(1)}, u32[]{:S(2)}, u32[]{:S(2)}) collective-permute-start(f32[8,1280]{1,0:T(8,128)S(1)} %get-tuple-element.141), channel_id=1, source_target_pairs={{0,192},{32,224},{64,0},{96,32},{128,64},{160,96},{192,128},{224,1... | collective-permute-start | bytes 122888 | tf_op jit(solution)/shard_map/ppermute | solution.py:96
  226.2 10.4 %collective-permute-start.23 = (f32[8,1280]{1,0:T(8,128)S(1)}, f32[8,1280]{1,0:T(8,128)S(1)}, u32[]{:S(2)}, u32[]{:S(2)}) collective-permute-start(f32[8,1280]{1,0:T(8,128)S(1)} %get-tuple-element.142), channel_id=1, source_target_pairs={{0,160},{32,192},{64,224},{96,0},{128,32},{160,64},{192,96},{224,1... | collective-permute-start | bytes 122888 | tf_op jit(solution)/shard_map/ppermute | solution.py:96
  227.3 9.2 %collective-permute-start.22 = (f32[8,1280]{1,0:T(8,128)S(1)}, f32[8,1280]{1,0:T(8,128)S(1)}, u32[]{:S(2)}, u32[]{:S(2)}) collective-permute-start(f32[8,1280]{1,0:T(8,128)S(1)} %get-tuple-element.143), channel_id=1, source_target_pairs={{0,128},{32,160},{64,192},{96,224},{128,0},{160,32},{192,64},{224,... | collective-permute-start | bytes 122888 | tf_op jit(solution)/shard_map/ppermute | solution.py:96
  231.3 7.4 %collective-permute-start.21 = (f32[8,1280]{1,0:T(8,128)S(1)}, f32[8,1280]{1,0:T(8,128)S(1)}, u32[]{:S(2)}, u32[]{:S(2)}) collective-permute-start(f32[8,1280]{1,0:T(8,128)S(1)} %get-tuple-element.144), channel_id=1, source_target_pairs={{0,96},{32,128},{64,160},{96,192},{128,224},{160,0},{192,32},{224,... | collective-permute-start | bytes 122888 | tf_op jit(solution)/shard_map/ppermute | solution.py:96
  231.3 8.3 %collective-permute-start.20 = (f32[8,1280]{1,0:T(8,128)S(1)}, f32[8,1280]{1,0:T(8,128)S(1)}, u32[]{:S(2)}, u32[]{:S(2)}) collective-permute-start(f32[8,1280]{1,0:T(8,128)S(1)} %get-tuple-element.145), channel_id=1, source_target_pairs={{0,64},{32,96},{64,128},{96,160},{128,192},{160,224},{192,0},{224,... | collective-permute-start | bytes 122888 | tf_op jit(solution)/shard_map/ppermute | solution.py:96
  240.1 15.0 %collective-permute-start.26 = (f32[8,1280]{1,0:T(8,128)S(1)}, f32[8,1280]{1,0:T(8,128)S(1)}, u32[]{:S(2)}, u32[]{:S(2)}) collective-permute-start(f32[8,1280]{1,0:T(8,128)S(1)} %get-tuple-element.95), channel_id=1, source_target_pairs={{0,32},{32,64},{64,96},{96,128},{128,160},{160,192},{192,224},{224... | collective-permute-start | bytes 122888 | tf_op jit(solution)/shard_map/ppermute | solution.py:100
  246.2 12.7 %collective-permute-start.27 = (f32[8,1280]{1,0:T(8,128)S(1)}, f32[8,1280]{1,0:T(8,128)S(1)}, u32[]{:S(2)}, u32[]{:S(2)}) collective-permute-start(f32[8,1280]{1,0:T(8,128)S(1)} %get-tuple-element.95), channel_id=1, source_target_pairs={{0,64},{32,96},{64,128},{96,160},{128,192},{160,224},{192,0},{224,... | collective-permute-start | bytes 122888 | tf_op jit(solution)/shard_map/ppermute | solution.py:100
  248.0 12.1 %collective-permute-start.28 = (f32[8,1280]{1,0:T(8,128)S(1)}, f32[8,1280]{1,0:T(8,128)S(1)}, u32[]{:S(2)}, u32[]{:S(2)}) collective-permute-start(f32[8,1280]{1,0:T(8,128)S(1)} %get-tuple-element.95), channel_id=1, source_target_pairs={{0,96},{32,128},{64,160},{96,192},{128,224},{160,0},{192,32},{224,... | collective-permute-start | bytes 122888 | tf_op jit(solution)/shard_map/ppermute | solution.py:100
  249.8 10.2 %collective-permute-start.29 = (f32[8,1280]{1,0:T(8,128)S(1)}, f32[8,1280]{1,0:T(8,128)S(1)}, u32[]{:S(2)}, u32[]{:S(2)}) collective-permute-start(f32[8,1280]{1,0:T(8,128)S(1)} %get-tuple-element.95), channel_id=1, source_target_pairs={{0,128},{32,160},{64,192},{96,224},{128,0},{160,32},{192,64},{224,... | collective-permute-start | bytes 122888 | tf_op jit(solution)/shard_map/ppermute | solution.py:100
  252.8 7.2 %collective-permute-start.30 = (f32[8,1280]{1,0:T(8,128)S(1)}, f32[8,1280]{1,0:T(8,128)S(1)}, u32[]{:S(2)}, u32[]{:S(2)}) collective-permute-start(f32[8,1280]{1,0:T(8,128)S(1)} %get-tuple-element.95), channel_id=1, source_target_pairs={{0,160},{32,192},{64,224},{96,0},{128,32},{160,64},{192,96},{224,1... | collective-permute-start | bytes 122888 | tf_op jit(solution)/shard_map/ppermute | solution.py:100
  255.0 5.7 %collective-permute-start.31 = (f32[8,1280]{1,0:T(8,128)S(1)}, f32[8,1280]{1,0:T(8,128)S(1)}, u32[]{:S(2)}, u32[]{:S(2)}) collective-permute-start(f32[8,1280]{1,0:T(8,128)S(1)} %get-tuple-element.95), channel_id=1, source_target_pairs={{0,192},{32,224},{64,0},{96,32},{128,64},{160,96},{192,128},{224,1... | collective-permute-start | bytes 122888 | tf_op jit(solution)/shard_map/ppermute | solution.py:100
  (13 other events, 244.4 us)
Sparse Core Ops, SparseCore 0:
  11.1 54.9 all-gather.1

commit v13 on v11

--- a/solution.py
+++ b/solution.py
@@ -116,7 +116,7 @@
 def outer_product(left, right):
     depth, rows = left.shape
     cols = right.shape[1]
-    tile = 512
+    tile = 2048
     return pl.pallas_call(
         outer_kernel,
         grid=(rows // tile,),

time: 264 us -> 264 us (level)
  no operation moved by 1% of the time
where the time goes in v13:
time: 264 us; the launch traced here: 263 us
  waiting for transfers between devices  125 us (47%)
  starting transfers between devices  73.2 us (28%)
  other arithmetic  17.1 us (6%)
  between operations  14.9 us (6%)
  local copies, waits for them, and re-layouts  14.5 us (5%)
  matrix products  12.8 us (5%)
  Pallas kernels  4.99 us (2%)
    all_gather x1, waiting for transfers between devices, local(): lax.all_gather(dequantize(weight_codes, scales), 'seq', axis=0, tiled=True)  50.6 us
    ppermute x12, starting transfers between devices, shifted(): lax.ppermute(value.astype(jnp.bfloat16), axis, pairs).astype(value.dtype)  35.6 us
    ppermute x12, waiting for transfers between devices, shifted(): lax.ppermute(value.astype(jnp.bfloat16), axis, pairs).astype(value.dtype)  35.1 us
    ppermute x13, waiting for transfers between devices, digit_reduce(): got = lax.ppermute(piece.astype(jnp.bfloat16), axis, pairs)  33.3 us
    ppermute x7, starting transfers between devices, replicated_sum(): total = total + lax.ppermute(piece, axis, pairs)  15.8 us
    ppermute x7, starting transfers between devices, replicated_sum(): gathered.append(lax.ppermute(total, axis, pairs))  14.4 us
    ppermute x13, starting transfers between devices, digit_reduce(): got = lax.ppermute(piece.astype(jnp.bfloat16), axis, pairs)  7.4 us
  transfers between devices with their start and end apart: 40, of which 20 were waited for; matrix products, arithmetic and copies ran while one was open for 8% of the time, Pallas kernels for 0%

profile of v13, /device:TPU:8, one launch (start us, length us, event | category | flops | bytes accessed | tf_op | source)
XLA Modules:
  0.0 263.0 jit_solution(12866612485180472346)
XLA Ops:
  15.6 50.6 %all-gather.2.cloned.1.call-done = bf16[2048,1280]{1,0:T(8,128)(2,1)} async-done(((bf16[64,1280]{1,0:T(8,128)(2,1)}), bf16[2048,1280]{1,0:T(8,128)(2,1)}) %all-gather.2.cloned.1.call-update) | async-done | bytes 5242896 | tf_op jit(solution)/shard_map/all_gather | solution.py:216
  66.1 4.2 %fusion = bf16[128,1280]{0,1:T(8,128)(2,1)S(1)} fusion(bf16[2048,1280]{1,0:T(8,128)(2,1)} %all-gather.2.cloned.1.call-done, bf16[1,128,2048]{2,1,0:T(8,128)(2,1)} %param.5), kind=kOutput, calls=%fused_computation.5 | convolution fusion | flops 671252480 | bytes 6094848 | tf_op jit(solution)/shard_map/dot_general | solution.py:217
  72.6 4.4 %collective-permute-start = (bf16[16,8448]{1,0:T(8,128)(2,1)S(1)}, bf16[16,8448]{1,0:T(8,128)(2,1)S(1)}, u32[]{:S(2)}, u32[]{:S(2)}) collective-permute-start(bf16[16,8448]{1,0:T(8,128)(2,1)S(1)} %get-tuple-element.162), channel_id=1, source_target_pairs={{1,0},{2,1},{3,2},{4,3},{5,4},{6,5},{7,6},{8,7},{9,8},{10,9},{11,1... | collective-permute-start | bytes 811016 | tf_op jit(solution)/shard_map/ppermute | solution.py:17
  77.0 2.1 collective-permute-start.1
  81.2 2.1 collective-permute-start.6
  83.3 3.5 %collective-permute-start.7 = (bf16[16,8448]{1,0:T(8,128)(2,1)S(1)}, bf16[16,8448]{1,0:T(8,128)(2,1)S(1)}, u32[]{:S(2)}, u32[]{:S(2)}) collective-permute-start(bf16[16,8448]{1,0:T(8,128)(2,1)S(1)} %get-tuple-element.163), channel_id=1, source_target_pairs={{0,2},{1,3},{2,4},{3,5},{4,6},{5,7},{6,8},{7,9},{8,10},{9,11},{10,... | collective-permute-start | bytes 811016 | tf_op jit(solution)/shard_map/ppermute | solution.py:17
  87.5 6.3 %collective-permute-start.2 = (bf16[16,8448]{1,0:T(8,128)(2,1)S(1)}, bf16[16,8448]{1,0:T(8,128)(2,1)S(1)}, u32[]{:S(2)}, u32[]{:S(2)}) collective-permute-start(bf16[16,8448]{1,0:T(8,128)(2,1)S(1)} %pad_maximum_fusion.5), channel_id=1, source_target_pairs={{2,0},{3,1},{4,2},{5,3},{6,4},{7,5},{8,6},{9,7},{10,8},{11,9},{12,... | collective-permute-start | bytes 811016 | tf_op jit(solution)/shard_map/ppermute | solution.py:17
  93.9 2.4 collective-permute-done.7
  99.9 4.3 %collective-permute-start.3 = (bf16[16,8448]{1,0:T(8,128)(2,1)S(1)}, bf16[16,8448]{1,0:T(8,128)(2,1)S(1)}, u32[]{:S(2)}, u32[]{:S(2)}) collective-permute-start(bf16[16,8448]{1,0:T(8,128)(2,1)S(1)} %pad_maximum_fusion.6), channel_id=1, source_target_pairs={{4,0},{5,1},{6,2},{7,3},{8,4},{9,5},{10,6},{11,7},{12,8},{13,9},{1... | collective-permute-start | bytes 811016 | tf_op jit(solution)/shard_map/ppermute | solution.py:17
  104.1 11.3 %collective-permute-done.8 = bf16[16,8448]{1,0:T(8,128)(2,1)S(1)} collective-permute-done((bf16[16,8448]{1,0:T(8,128)(2,1)S(1)}, bf16[16,8448]{1,0:T(8,128)(2,1)S(1)}, u32[]{:S(2)}, u32[]{:S(2)}) %collective-permute-start.8) | collective-permute-done | bytes 270368 | tf_op jit(solution)/shard_map/ppermute | solution.py:17
  116.1 2.1 collective-permute-start.9
  120.7 7.7 %collective-permute-done.9 = bf16[16,8448]{1,0:T(8,128)(2,1)S(1)} collective-permute-done((bf16[16,8448]{1,0:T(8,128)(2,1)S(1)}, bf16[16,8448]{1,0:T(8,128)(2,1)S(1)}, u32[]{:S(2)}, u32[]{:S(2)}) %collective-permute-start.9) | collective-permute-done | bytes 270368 | tf_op jit(solution)/shard_map/ppermute | solution.py:17
  129.0 2.3 collective-permute-start.10
  132.6 5.4 %collective-permute-done.10 = bf16[16,8448]{1,0:T(8,128)(2,1)S(1)} collective-permute-done((bf16[16,8448]{1,0:T(8,128)(2,1)S(1)}, bf16[16,8448]{1,0:T(8,128)(2,1)S(1)}, u32[]{:S(2)}, u32[]{:S(2)}) %collective-permute-start.10) | collective-permute-done | bytes 270368 | tf_op jit(solution)/shard_map/ppermute | solution.py:17
  138.6 3.2 %collective-permute-start.11 = (bf16[16,8448]{1,0:T(8,128)(2,1)S(1)}, bf16[16,8448]{1,0:T(8,128)(2,1)S(1)}, u32[]{:S(2)}, u32[]{:S(2)}) collective-permute-start(bf16[16,8448]{1,0:T(8,128)(2,1)S(1)} %pad_maximum_fusion.12), channel_id=1, source_target_pairs={{0,16},{1,17},{2,18},{3,19},{4,20},{5,21},{6,22},{7,23},{8,24},{9,... | collective-permute-start | bytes 811016 | tf_op jit(solution)/shard_map/ppermute | solution.py:17
  143.6 2.1 collective-permute-done.11
  146.4 5.7 %collective-permute-done.5 = bf16[16,8448]{1,0:T(8,128)(2,1)} collective-permute-done((bf16[16,8448]{1,0:T(8,128)(2,1)S(1)}, bf16[16,8448]{1,0:T(8,128)(2,1)}, u32[]{:S(2)}, u32[]{:S(2)}) %collective-permute-start.5) | collective-permute-done | bytes 270368 | tf_op jit(solution)/shard_map/ppermute | solution.py:17
  156.8 5.0 %shard_map.68 = bf16[2048,1280]{1,0:T(8,128)(2,1)} custom-call(bf16[2048,128]{1,0:T(8,128)(2,1)} %bitcast.225, bf16[128,1280]{1,0:T(8,128)(2,1)} %pad_maximum_fusion.4.right_ref), custom_call_target="tpu_custom_call" | custom-call | flops 671088640 | bytes 6094848 | tf_op jit(solution)/shard_map/pallas_call | solution.py:120
  163.9 4.9 %collective-permute-done.12 = bf16[4,4,64,1280]{3,2,1,0:T(8,128)(2,1)} collective-permute-done((bf16[4,4,64,1280]{3,2,1,0:T(8,128)(2,1)S(1)}, bf16[4,4,64,1280]{3,2,1,0:T(8,128)(2,1)}, u32[]{:S(2)}, u32[]{:S(2)}) %collective-permute-start.12) | collective-permute-done | bytes 2621472 | tf_op jit(solution)/shard_map/ppermute | solution.py:73
  168.8 3.2 %convert_add_fusion = f32[4,4,64,1280]{3,2,1,0:T(8,128)S(1)} fusion(bf16[4,4,64,1280]{3,2,1,0:T(8,128)(2,1)} %collective-permute-done.12, bf16[4,4,2,64,1280]{4,3,2,1,0:T(8,128)(2,1)} %bitcast.224, s32[]{:T(128)S(6)} %select_n.216), kind=kLoop, calls=%fused_computation.1 | loop fusion | flops 3932160 | bytes 10485764 | tf_op jit(solution)/shard_map/add | solution.py:74
  178.0 14.0 %collective-permute-done.21 = bf16[4,64,640]{2,1,0:T(8,128)(2,1)S(1)} collective-permute-done((bf16[4,64,640]{2,1,0:T(8,128)(2,1)}, bf16[4,64,640]{2,1,0:T(8,128)(2,1)S(1)}, u32[]{:S(2)}, u32[]{:S(2)}) %collective-permute-start.21) | collective-permute-done | bytes 327712 | tf_op jit(solution)/shard_map/ppermute | solution.py:73
  197.7 7.2 %collective-permute-done.13 = bf16[4,64,640]{2,1,0:T(8,128)(2,1)S(1)} collective-permute-done((bf16[4,64,640]{2,1,0:T(8,128)(2,1)S(1)}, bf16[4,64,640]{2,1,0:T(8,128)(2,1)S(1)}, u32[]{:S(2)}, u32[]{:S(2)}) %collective-permute-start.13) | collective-permute-done | bytes 327712 | tf_op jit(solution)/shard_map/ppermute | solution.py:73
  207.2 2.4 collective-permute-done.18
  212.6 3.4 %collective-permute-start.31 = (f32[8,1280]{1,0:T(8,128)S(1)}, f32[8,1280]{1,0:T(8,128)S(1)}, u32[]{:S(2)}, u32[]{:S(2)}) collective-permute-start(f32[8,1280]{1,0:T(8,128)S(1)} %get-tuple-element.148), channel_id=1, source_target_pairs={{0,224},{32,0},{64,32},{96,64},{128,96},{160,128},{192,160},{224,1... | collective-permute-start | bytes 122888 | tf_op jit(solution)/shard_map/ppermute | solution.py:100
  216.0 2.2 collective-permute-start.30
  219.4 3.9 %collective-permute-start.28 = (f32[8,1280]{1,0:T(8,128)S(1)}, f32[8,1280]{1,0:T(8,128)S(1)}, u32[]{:S(2)}, u32[]{:S(2)}) collective-permute-start(f32[8,1280]{1,0:T(8,128)S(1)} %get-tuple-element.151), channel_id=1, source_target_pairs={{0,128},{32,160},{64,192},{96,224},{128,0},{160,32},{192,64},{224,... | collective-permute-start | bytes 122888 | tf_op jit(solution)/shard_map/ppermute | solution.py:100
  223.3 3.6 %collective-permute-start.26 = (f32[8,1280]{1,0:T(8,128)S(1)}, f32[8,1280]{1,0:T(8,128)S(1)}, u32[]{:S(2)}, u32[]{:S(2)}) collective-permute-start(f32[8,1280]{1,0:T(8,128)S(1)} %get-tuple-element.153), channel_id=1, source_target_pairs={{0,64},{32,96},{64,128},{96,160},{128,192},{160,224},{192,0},{224,... | collective-permute-start | bytes 122888 | tf_op jit(solution)/shard_map/ppermute | solution.py:100
  232.9 5.3 %convolution_bitcast_fusion = f32[1,128,2048]{2,1,0:T(8,128)} fusion(bf16[2048,1280]{1,0:T(8,128)(2,1)} %all-gather.2.cloned.1.call-done, bf16[128,128]{1,0:T(8,128)(2,1)S(1)} %copy-done.4, bf16[128,128]{1,0:T(8,128)(2,1)S(1)} %copy-done.6, bf16[128,1024]{1,0:T(8,128)(2,1)S(1)} %copy.85), kind=kOutput, calls=%fused_computation.3 | convolution fusion | flops 672071680 | bytes 6619136 | tf_op jit(solution)/shard_map/dot_general | solution.py:250
  239.8 2.8 %collective-permute-start.34 = (f32[8,1280]{1,0:T(8,128)S(1)}, f32[8,1280]{1,0:T(8,128)S(1)}, u32[]{:S(2)}, u32[]{:S(2)}) collective-permute-start(f32[8,1280]{1,0:T(8,128)S(1)} %get-tuple-element.95), channel_id=1, source_target_pairs={{0,96},{32,128},{64,160},{96,192},{128,224},{160,0},{192,32},{224,... | collective-permute-start | bytes 122888 | tf_op jit(solution)/shard_map/ppermute | solution.py:104
  244.5 2.5 collective-permute-start.36
  247.0 3.6 %collective-permute-start.37 = (f32[8,1280]{1,0:T(8,128)S(1)}, f32[8,1280]{1,0:T(8,128)S(1)}, u32[]{:S(2)}, u32[]{:S(2)}) collective-permute-start(f32[8,1280]{1,0:T(8,128)S(1)} %get-tuple-element.95), channel_id=1, source_target_pairs={{0,192},{32,224},{64,0},{96,32},{128,64},{160,96},{192,128},{224,1... | collective-permute-start | bytes 122888 | tf_op jit(solution)/shard_map/ppermute | solution.py:104
  252.3 2.4 collective-permute-done.38
  (203 shorter events, 62.1 us)
Async XLA Ops:
  7.2 59.0 %all-gather.2.cloned.1.call-start = ((), (), s32[]{:S(2)}) async-start(), calls=%async_computation | async-start | bytes 5406720 | tf_op jit(solution)/shard_map/all_gather | solution.py:216
  72.6 14.3 %collective-permute-start = (bf16[16,8448]{1,0:T(8,128)(2,1)S(1)}, bf16[16,8448]{1,0:T(8,128)(2,1)S(1)}, u32[]{:S(2)}, u32[]{:S(2)}) collective-permute-start(bf16[16,8448]{1,0:T(8,128)(2,1)S(1)} %get-tuple-element.162), channel_id=1, source_target_pairs={{1,0},{2,1},{3,2},{4,3},{5,4},{6,5},{7,6},{8,7},{9,8},{10,9},{11,1... | collective-permute-start | bytes 811016 | tf_op jit(solution)/shard_map/ppermute | solution.py:17
  77.0 9.9 %collective-permute-start.1 = (bf16[16,8448]{1,0:T(8,128)(2,1)S(1)}, bf16[16,8448]{1,0:T(8,128)(2,1)S(1)}, u32[]{:S(2)}, u32[]{:S(2)}) collective-permute-start(bf16[16,8448]{1,0:T(8,128)(2,1)S(1)} %get-tuple-element.162), channel_id=1, source_target_pairs={{2,0},{3,1},{4,2},{5,3},{6,4},{7,5},{8,6},{9,7},{10,8},{11,9},{12,... | collective-permute-start | bytes 811016 | tf_op jit(solution)/shard_map/ppermute | solution.py:17
  81.2 12.7 %collective-permute-start.6 = (bf16[16,8448]{1,0:T(8,128)(2,1)S(1)}, bf16[16,8448]{1,0:T(8,128)(2,1)S(1)}, u32[]{:S(2)}, u32[]{:S(2)}) collective-permute-start(bf16[16,8448]{1,0:T(8,128)(2,1)S(1)} %get-tuple-element.163), channel_id=1, source_target_pairs={{0,1},{1,2},{2,3},{3,4},{4,5},{5,6},{6,7},{7,8},{8,9},{9,10},{10,1... | collective-permute-start | bytes 811016 | tf_op jit(solution)/shard_map/ppermute | solution.py:17
  83.3 13.0 %collective-permute-start.7 = (bf16[16,8448]{1,0:T(8,128)(2,1)S(1)}, bf16[16,8448]{1,0:T(8,128)(2,1)S(1)}, u32[]{:S(2)}, u32[]{:S(2)}) collective-permute-start(bf16[16,8448]{1,0:T(8,128)(2,1)S(1)} %get-tuple-element.163), channel_id=1, source_target_pairs={{0,2},{1,3},{2,4},{3,5},{4,6},{5,7},{6,8},{7,9},{8,10},{9,11},{10,... | collective-permute-start | bytes 811016 | tf_op jit(solution)/shard_map/ppermute | solution.py:17
  87.5 11.8 %collective-permute-start.2 = (bf16[16,8448]{1,0:T(8,128)(2,1)S(1)}, bf16[16,8448]{1,0:T(8,128)(2,1)S(1)}, u32[]{:S(2)}, u32[]{:S(2)}) collective-permute-start(bf16[16,8448]{1,0:T(8,128)(2,1)S(1)} %pad_maximum_fusion.5), channel_id=1, source_target_pairs={{2,0},{3,1},{4,2},{5,3},{6,4},{7,5},{8,6},{9,7},{10,8},{11,9},{12,... | collective-permute-start | bytes 811016 | tf_op jit(solution)/shard_map/ppermute | solution.py:17
  96.9 18.5 %collective-permute-start.8 = (bf16[16,8448]{1,0:T(8,128)(2,1)S(1)}, bf16[16,8448]{1,0:T(8,128)(2,1)S(1)}, u32[]{:S(2)}, u32[]{:S(2)}) collective-permute-start(bf16[16,8448]{1,0:T(8,128)(2,1)S(1)} %pad_maximum_fusion.9), channel_id=1, source_target_pairs={{0,2},{1,3},{2,4},{3,5},{4,6},{5,7},{6,8},{7,9},{8,10},{9,11},{10,... | collective-permute-start | bytes 811016 | tf_op jit(solution)/shard_map/ppermute | solution.py:17
  99.9 18.2 %collective-permute-start.3 = (bf16[16,8448]{1,0:T(8,128)(2,1)S(1)}, bf16[16,8448]{1,0:T(8,128)(2,1)S(1)}, u32[]{:S(2)}, u32[]{:S(2)}) collective-permute-start(bf16[16,8448]{1,0:T(8,128)(2,1)S(1)} %pad_maximum_fusion.6), channel_id=1, source_target_pairs={{4,0},{5,1},{6,2},{7,3},{8,4},{9,5},{10,6},{11,7},{12,8},{13,9},{1... | collective-permute-start | bytes 811016 | tf_op jit(solution)/shard_map/ppermute | solution.py:17
  116.1 12.4 %collective-permute-start.9 = (bf16[16,8448]{1,0:T(8,128)(2,1)S(1)}, bf16[16,8448]{1,0:T(8,128)(2,1)S(1)}, u32[]{:S(2)}, u32[]{:S(2)}) collective-permute-start(bf16[16,8448]{1,0:T(8,128)(2,1)S(1)} %pad_maximum_fusion.10), channel_id=1, source_target_pairs={{0,4},{1,5},{2,6},{3,7},{4,8},{5,9},{6,10},{7,11},{8,12},{9,13},{1... | collective-permute-start | bytes 811016 | tf_op jit(solution)/shard_map/ppermute | solution.py:17
  118.7 13.8 %collective-permute-start.4 = (bf16[16,8448]{1,0:T(8,128)(2,1)S(1)}, bf16[16,8448]{1,0:T(8,128)(2,1)S(1)}, u32[]{:S(2)}, u32[]{:S(2)}) collective-permute-start(bf16[16,8448]{1,0:T(8,128)(2,1)S(1)} %pad_maximum_fusion.7), channel_id=1, source_target_pairs={{8,0},{9,1},{10,2},{11,3},{12,4},{13,5},{14,6},{15,7},{16,8},{17,9... | collective-permute-start | bytes 811016 | tf_op jit(solution)/shard_map/ppermute | solution.py:17
  129.0 8.9 %collective-permute-start.10 = (bf16[16,8448]{1,0:T(8,128)(2,1)S(1)}, bf16[16,8448]{1,0:T(8,128)(2,1)S(1)}, u32[]{:S(2)}, u32[]{:S(2)}) collective-permute-start(bf16[16,8448]{1,0:T(8,128)(2,1)S(1)} %pad_maximum_fusion.11), channel_id=1, source_target_pairs={{0,8},{1,9},{2,10},{3,11},{4,12},{5,13},{6,14},{7,15},{8,16},{9,17... | collective-permute-start | bytes 811016 | tf_op jit(solution)/shard_map/ppermute | solution.py:17
  142.2 10.0 %collective-permute-start.5 = (bf16[16,8448]{1,0:T(8,128)(2,1)S(1)}, bf16[16,8448]{1,0:T(8,128)(2,1)}, u32[]{:S(2)}, u32[]{:S(2)}) collective-permute-start(bf16[16,8448]{1,0:T(8,128)(2,1)S(1)} %pad_maximum_fusion.8), channel_id=1, source_target_pairs={{16,0},{17,1},{18,2},{19,3},{20,4},{21,5},{22,6},{23,7},{24,8},{25... | collective-permute-start | bytes 811016 | tf_op jit(solution)/shard_map/ppermute | solution.py:17
  175.0 17.0 %collective-permute-start.21 = (bf16[4,64,640]{2,1,0:T(8,128)(2,1)}, bf16[4,64,640]{2,1,0:T(8,128)(2,1)S(1)}, u32[]{:S(2)}, u32[]{:S(2)}) collective-permute-start(bf16[4,64,640]{2,1,0:T(8,128)(2,1)} %get-tuple-element.137), channel_id=1, source_target_pairs={{0,24},{1,25},{2,26},{3,27},{4,28},{5,29},{6,30},{7,31},{8,0},{9,1... | collective-permute-start | bytes 983048 | tf_op jit(solution)/shard_map/ppermute | solution.py:73
  176.2 15.8 %collective-permute-start.20 = (bf16[4,64,640]{2,1,0:T(8,128)(2,1)}, bf16[4,64,640]{2,1,0:T(8,128)(2,1)S(1)}, u32[]{:S(2)}, u32[]{:S(2)}) collective-permute-start(bf16[4,64,640]{2,1,0:T(8,128)(2,1)} %get-tuple-element.138), channel_id=1, source_target_pairs={{0,16},{1,17},{2,18},{3,19},{4,20},{5,21},{6,22},{7,23},{8,24},{9,... | collective-permute-start | bytes 983048 | tf_op jit(solution)/shard_map/ppermute | solution.py:73
  176.2 17.7 %collective-permute-start.19 = (bf16[4,64,640]{2,1,0:T(8,128)(2,1)}, bf16[4,64,640]{2,1,0:T(8,128)(2,1)}, u32[]{:S(2)}, u32[]{:S(2)}) collective-permute-start(bf16[4,64,640]{2,1,0:T(8,128)(2,1)} %get-tuple-element.136), channel_id=1, source_target_pairs={{0,8},{1,9},{2,10},{3,11},{4,12},{5,13},{6,14},{7,15},{8,16},{9,17... | collective-permute-start | bytes 983048 | tf_op jit(solution)/shard_map/ppermute | solution.py:73
  177.8 18.9 %collective-permute-start.15 = (bf16[4,64,640]{2,1,0:T(8,128)(2,1)S(1)}, bf16[4,64,640]{2,1,0:T(8,128)(2,1)S(1)}, u32[]{:S(2)}, u32[]{:S(2)}) collective-permute-start(bf16[4,64,640]{2,1,0:T(8,128)(2,1)S(1)} %get-tuple-element.135), channel_id=1, source_target_pairs={{0,6},{1,7},{2,0},{3,1},{4,2},{5,3},{6,4},{7,5},{8,14},{9,15},{10,... | collective-permute-start | bytes 983048 | tf_op jit(solution)/shard_map/ppermute | solution.py:73
  177.9 19.7 %collective-permute-start.14 = (bf16[4,64,640]{2,1,0:T(8,128)(2,1)S(1)}, bf16[4,64,640]{2,1,0:T(8,128)(2,1)S(1)}, u32[]{:S(2)}, u32[]{:S(2)}) collective-permute-start(bf16[4,64,640]{2,1,0:T(8,128)(2,1)S(1)} %get-tuple-element.134), channel_id=1, source_target_pairs={{0,4},{1,5},{2,6},{3,7},{4,0},{5,1},{6,2},{7,3},{8,12},{9,13},{10,... | collective-permute-start | bytes 983048 | tf_op jit(solution)/shard_map/ppermute | solution.py:73
  192.0 12.9 %collective-permute-start.13 = (bf16[4,64,640]{2,1,0:T(8,128)(2,1)S(1)}, bf16[4,64,640]{2,1,0:T(8,128)(2,1)S(1)}, u32[]{:S(2)}, u32[]{:S(2)}) collective-permute-start(bf16[4,64,640]{2,1,0:T(8,128)(2,1)S(1)} %get-tuple-element.133), channel_id=1, source_target_pairs={{0,2},{1,3},{2,4},{3,5},{4,6},{5,7},{6,0},{7,1},{8,10},{9,11},{10,... | collective-permute-start | bytes 983048 | tf_op jit(solution)/shard_map/ppermute | solution.py:73
  195.3 10.8 %collective-permute-start.24 = (bf16[64,640]{1,0:T(8,128)(2,1)S(1)}, bf16[64,640]{1,0:T(8,128)(2,1)S(1)}, u32[]{:S(2)}, u32[]{:S(2)}) collective-permute-start(bf16[64,640]{1,0:T(8,128)(2,1)S(1)} %get-tuple-element.143), channel_id=1, source_target_pairs={{0,6},{1,7},{2,0},{3,1},{4,2},{5,3},{6,4},{7,5},{8,14},{9,15},{10,... | collective-permute-start | bytes 245768 | tf_op jit(solution)/shard_map/ppermute | solution.py:73
  196.7 10.5 %collective-permute-start.23 = (bf16[64,640]{1,0:T(8,128)(2,1)S(1)}, bf16[64,640]{1,0:T(8,128)(2,1)S(1)}, u32[]{:S(2)}, u32[]{:S(2)}) collective-permute-start(bf16[64,640]{1,0:T(8,128)(2,1)S(1)} %get-tuple-element.144), channel_id=1, source_target_pairs={{0,4},{1,5},{2,6},{3,7},{4,0},{5,1},{6,2},{7,3},{8,12},{9,13},{10,... | collective-permute-start | bytes 245768 | tf_op jit(solution)/shard_map/ppermute | solution.py:73
  196.7 10.5 %collective-permute-start.22 = (bf16[64,640]{1,0:T(8,128)(2,1)S(1)}, bf16[64,640]{1,0:T(8,128)(2,1)S(1)}, u32[]{:S(2)}, u32[]{:S(2)}) collective-permute-start(bf16[64,640]{1,0:T(8,128)(2,1)S(1)} %get-tuple-element.142), channel_id=1, source_target_pairs={{0,2},{1,3},{2,4},{3,5},{4,6},{5,7},{6,0},{7,1},{8,10},{9,11},{10,... | collective-permute-start | bytes 245768 | tf_op jit(solution)/shard_map/ppermute | solution.py:73
  212.6 10.7 %collective-permute-start.31 = (f32[8,1280]{1,0:T(8,128)S(1)}, f32[8,1280]{1,0:T(8,128)S(1)}, u32[]{:S(2)}, u32[]{:S(2)}) collective-permute-start(f32[8,1280]{1,0:T(8,128)S(1)} %get-tuple-element.148), channel_id=1, source_target_pairs={{0,224},{32,0},{64,32},{96,64},{128,96},{160,128},{192,160},{224,1... | collective-permute-start | bytes 122888 | tf_op jit(solution)/shard_map/ppermute | solution.py:100
  216.0 10.9 %collective-permute-start.30 = (f32[8,1280]{1,0:T(8,128)S(1)}, f32[8,1280]{1,0:T(8,128)S(1)}, u32[]{:S(2)}, u32[]{:S(2)}) collective-permute-start(f32[8,1280]{1,0:T(8,128)S(1)} %get-tuple-element.149), channel_id=1, source_target_pairs={{0,192},{32,224},{64,0},{96,32},{128,64},{160,96},{192,128},{224,1... | collective-permute-start | bytes 122888 | tf_op jit(solution)/shard_map/ppermute | solution.py:100
  218.2 10.4 %collective-permute-start.29 = (f32[8,1280]{1,0:T(8,128)S(1)}, f32[8,1280]{1,0:T(8,128)S(1)}, u32[]{:S(2)}, u32[]{:S(2)}) collective-permute-start(f32[8,1280]{1,0:T(8,128)S(1)} %get-tuple-element.150), channel_id=1, source_target_pairs={{0,160},{32,192},{64,224},{96,0},{128,32},{160,64},{192,96},{224,1... | collective-permute-start | bytes 122888 | tf_op jit(solution)/shard_map/ppermute | solution.py:100
  219.4 9.2 %collective-permute-start.28 = (f32[8,1280]{1,0:T(8,128)S(1)}, f32[8,1280]{1,0:T(8,128)S(1)}, u32[]{:S(2)}, u32[]{:S(2)}) collective-permute-start(f32[8,1280]{1,0:T(8,128)S(1)} %get-tuple-element.151), channel_id=1, source_target_pairs={{0,128},{32,160},{64,192},{96,224},{128,0},{160,32},{192,64},{224,... | collective-permute-start | bytes 122888 | tf_op jit(solution)/shard_map/ppermute | solution.py:100
  223.3 7.2 %collective-permute-start.27 = (f32[8,1280]{1,0:T(8,128)S(1)}, f32[8,1280]{1,0:T(8,128)S(1)}, u32[]{:S(2)}, u32[]{:S(2)}) collective-permute-start(f32[8,1280]{1,0:T(8,128)S(1)} %get-tuple-element.152), channel_id=1, source_target_pairs={{0,96},{32,128},{64,160},{96,192},{128,224},{160,0},{192,32},{224,... | collective-permute-start | bytes 122888 | tf_op jit(solution)/shard_map/ppermute | solution.py:100
  223.3 8.0 %collective-permute-start.26 = (f32[8,1280]{1,0:T(8,128)S(1)}, f32[8,1280]{1,0:T(8,128)S(1)}, u32[]{:S(2)}, u32[]{:S(2)}) collective-permute-start(f32[8,1280]{1,0:T(8,128)S(1)} %get-tuple-element.153), channel_id=1, source_target_pairs={{0,64},{32,96},{64,128},{96,160},{128,192},{160,224},{192,0},{224,... | collective-permute-start | bytes 122888 | tf_op jit(solution)/shard_map/ppermute | solution.py:100
  232.1 14.9 %collective-permute-start.32 = (f32[8,1280]{1,0:T(8,128)S(1)}, f32[8,1280]{1,0:T(8,128)S(1)}, u32[]{:S(2)}, u32[]{:S(2)}) collective-permute-start(f32[8,1280]{1,0:T(8,128)S(1)} %get-tuple-element.95), channel_id=1, source_target_pairs={{0,32},{32,64},{64,96},{96,128},{128,160},{160,192},{192,224},{224... | collective-permute-start | bytes 122888 | tf_op jit(solution)/shard_map/ppermute | solution.py:104
  238.2 12.5 %collective-permute-start.33 = (f32[8,1280]{1,0:T(8,128)S(1)}, f32[8,1280]{1,0:T(8,128)S(1)}, u32[]{:S(2)}, u32[]{:S(2)}) collective-permute-start(f32[8,1280]{1,0:T(8,128)S(1)} %get-tuple-element.95), channel_id=1, source_target_pairs={{0,64},{32,96},{64,128},{96,160},{128,192},{160,224},{192,0},{224,... | collective-permute-start | bytes 122888 | tf_op jit(solution)/shard_map/ppermute | solution.py:104
  239.8 12.1 %collective-permute-start.34 = (f32[8,1280]{1,0:T(8,128)S(1)}, f32[8,1280]{1,0:T(8,128)S(1)}, u32[]{:S(2)}, u32[]{:S(2)}) collective-permute-start(f32[8,1280]{1,0:T(8,128)S(1)} %get-tuple-element.95), channel_id=1, source_target_pairs={{0,96},{32,128},{64,160},{96,192},{128,224},{160,0},{192,32},{224,... | collective-permute-start | bytes 122888 | tf_op jit(solution)/shard_map/ppermute | solution.py:104
  242.5 9.3 %collective-permute-start.35 = (f32[8,1280]{1,0:T(8,128)S(1)}, f32[8,1280]{1,0:T(8,128)S(1)}, u32[]{:S(2)}, u32[]{:S(2)}) collective-permute-start(f32[8,1280]{1,0:T(8,128)S(1)} %get-tuple-element.95), channel_id=1, source_target_pairs={{0,128},{32,160},{64,192},{96,224},{128,0},{160,32},{192,64},{224,... | collective-permute-start | bytes 122888 | tf_op jit(solution)/shard_map/ppermute | solution.py:104
  244.5 7.3 %collective-permute-start.36 = (f32[8,1280]{1,0:T(8,128)S(1)}, f32[8,1280]{1,0:T(8,128)S(1)}, u32[]{:S(2)}, u32[]{:S(2)}) collective-permute-start(f32[8,1280]{1,0:T(8,128)S(1)} %get-tuple-element.95), channel_id=1, source_target_pairs={{0,160},{32,192},{64,224},{96,0},{128,32},{160,64},{192,96},{224,1... | collective-permute-start | bytes 122888 | tf_op jit(solution)/shard_map/ppermute | solution.py:104
  (21 other events, 354.7 us)
Sparse Core Ops, SparseCore 0:
  11.1 54.9 all-gather.1

commit v14 on v13

--- a/solution.py
+++ b/solution.py
@@ -64,8 +64,9 @@
     count = lax.axis_size(axis)
     digit = (lax.axis_index(axis) // stride) % radix
     total = lax.dynamic_index_in_dim(value, digit, where, False).astype(jnp.float32)
+    low = value.astype(jnp.bfloat16)
     for offset in range(1, radix):
-        piece = lax.dynamic_index_in_dim(value, (digit + offset) % radix, where, False)
+        piece = lax.dynamic_index_in_dim(low, (digit + offset) % radix, where, False)
         pairs = [
             (place, place + (((place // stride) % radix + offset) % radix - (place // stride) % radix) * stride)
             for place in range(count)

time: 264 us -> 260 us (0.985)
  local copies, waits for them, and re-layouts: 14.5 us -> 11.7 us
  transfers between devices with their start and end apart: 40 -> 40, of which waited for: 20 -> 21; matrix products, arithmetic and copies ran while one was open for 8% -> 7% of each run, Pallas kernels for 0% -> 0%
where the time goes in v14:
time: 260 us; the launch traced here: 259 us
  waiting for transfers between devices  125 us (48%)
  starting transfers between devices  73.2 us (28%)
  other arithmetic  16 us (6%)
  between operations  15.1 us (6%)
  matrix products  12.7 us (5%)
  local copies, waits for them, and re-layouts  11.7 us (4%)
  Pallas kernels  4.98 us (2%)
    all_gather x1, waiting for transfers between devices, local(): lax.all_gather(dequantize(weight_codes, scales), 'seq', axis=0, tiled=True)  50.5 us
    ppermute x12, starting transfers between devices, shifted(): lax.ppermute(value.astype(jnp.bfloat16), axis, pairs).astype(value.dtype)  35.3 us
    ppermute x12, waiting for transfers between devices, shifted(): lax.ppermute(value.astype(jnp.bfloat16), axis, pairs).astype(value.dtype)  35.1 us
    ppermute x13, waiting for transfers between devices, digit_reduce(): got = lax.ppermute(piece.astype(jnp.bfloat16), axis, pairs)  33.2 us
    ppermute x7, starting transfers between devices, replicated_sum(): total = total + lax.ppermute(piece, axis, pairs)  15.8 us
    ppermute x7, starting transfers between devices, replicated_sum(): gathered.append(lax.ppermute(total, axis, pairs))  14.3 us
    ppermute x13, starting transfers between devices, digit_reduce(): got = lax.ppermute(piece.astype(jnp.bfloat16), axis, pairs)  7.71 us
    dot_general x1, matrix products, local(): lax.dot_general(d_proj, weights, (((1,), (1,)), ((), ())), preferred_elem...  5.27 us
  transfers between devices with their start and end apart: 40, of which 21 were waited for; matrix products, arithmetic and copies ran while one was open for 7% of the time, Pallas kernels for 0%

profile of v14, /device:TPU:8, one launch (start us, length us, event | category | flops | bytes accessed | tf_op | source)
XLA Modules:
  0.0 258.9 jit_solution(3584377117706956910)
XLA Ops:
  15.6 50.5 %all-gather.2.cloned.1.call-done = bf16[2048,1280]{1,0:T(8,128)(2,1)} async-done(((bf16[64,1280]{1,0:T(8,128)(2,1)}), bf16[2048,1280]{1,0:T(8,128)(2,1)}) %all-gather.2.cloned.1.call-update) | async-done | bytes 5242896 | tf_op jit(solution)/shard_map/all_gather | solution.py:217
  66.2 4.1 %fusion = bf16[128,1280]{0,1:T(8,128)(2,1)S(1)} fusion(bf16[2048,1280]{1,0:T(8,128)(2,1)} %all-gather.2.cloned.1.call-done, bf16[1,128,2048]{2,1,0:T(8,128)(2,1)S(1)} %copy-done.2), kind=kOutput, calls=%fused_computation.5 | convolution fusion | flops 671252480 | bytes 6094848 | tf_op jit(solution)/shard_map/dot_general | solution.py:218
  72.5 4.4 %collective-permute-start = (bf16[16,8448]{1,0:T(8,128)(2,1)S(1)}, bf16[16,8448]{1,0:T(8,128)(2,1)S(1)}, u32[]{:S(2)}, u32[]{:S(2)}) collective-permute-start(bf16[16,8448]{1,0:T(8,128)(2,1)S(1)} %get-tuple-element.168), channel_id=1, source_target_pairs={{1,0},{2,1},{3,2},{4,3},{5,4},{6,5},{7,6},{8,7},{9,8},{10,9},{11,1... | collective-permute-start | bytes 811016 | tf_op jit(solution)/shard_map/ppermute | solution.py:17
  76.9 2.1 collective-permute-start.1
  80.1 2.1 collective-permute-start.6
  82.2 3.6 %collective-permute-start.7 = (bf16[16,8448]{1,0:T(8,128)(2,1)S(1)}, bf16[16,8448]{1,0:T(8,128)(2,1)S(1)}, u32[]{:S(2)}, u32[]{:S(2)}) collective-permute-start(bf16[16,8448]{1,0:T(8,128)(2,1)S(1)} %get-tuple-element.169), channel_id=1, source_target_pairs={{0,2},{1,3},{2,4},{3,5},{4,6},{5,7},{6,8},{7,9},{8,10},{9,11},{10,... | collective-permute-start | bytes 811016 | tf_op jit(solution)/shard_map/ppermute | solution.py:17
  87.3 6.5 %collective-permute-start.2 = (bf16[16,8448]{1,0:T(8,128)(2,1)S(1)}, bf16[16,8448]{1,0:T(8,128)(2,1)S(1)}, u32[]{:S(2)}, u32[]{:S(2)}) collective-permute-start(bf16[16,8448]{1,0:T(8,128)(2,1)S(1)} %pad_maximum_fusion.5), channel_id=1, source_target_pairs={{2,0},{3,1},{4,2},{5,3},{6,4},{7,5},{8,6},{9,7},{10,8},{11,9},{12,... | collective-permute-start | bytes 811016 | tf_op jit(solution)/shard_map/ppermute | solution.py:17
  95.8 1.9 collective-permute-start.8
  99.1 4.1 %collective-permute-start.3 = (bf16[16,8448]{1,0:T(8,128)(2,1)S(1)}, bf16[16,8448]{1,0:T(8,128)(2,1)S(1)}, u32[]{:S(2)}, u32[]{:S(2)}) collective-permute-start(bf16[16,8448]{1,0:T(8,128)(2,1)S(1)} %pad_maximum_fusion.6), channel_id=1, source_target_pairs={{4,0},{5,1},{6,2},{7,3},{8,4},{9,5},{10,6},{11,7},{12,8},{13,9},{1... | collective-permute-start | bytes 811016 | tf_op jit(solution)/shard_map/ppermute | solution.py:17
  103.3 11.1 %collective-permute-done.8 = bf16[16,8448]{1,0:T(8,128)(2,1)S(1)} collective-permute-done((bf16[16,8448]{1,0:T(8,128)(2,1)S(1)}, bf16[16,8448]{1,0:T(8,128)(2,1)S(1)}, u32[]{:S(2)}, u32[]{:S(2)}) %collective-permute-start.8) | collective-permute-done | bytes 270368 | tf_op jit(solution)/shard_map/ppermute | solution.py:17
  119.4 7.7 %collective-permute-done.9 = bf16[16,8448]{1,0:T(8,128)(2,1)S(1)} collective-permute-done((bf16[16,8448]{1,0:T(8,128)(2,1)S(1)}, bf16[16,8448]{1,0:T(8,128)(2,1)S(1)}, u32[]{:S(2)}, u32[]{:S(2)}) %collective-permute-start.9) | collective-permute-done | bytes 270368 | tf_op jit(solution)/shard_map/ppermute | solution.py:17
  127.8 2.3 collective-permute-start.10
  131.3 5.4 %collective-permute-done.10 = bf16[16,8448]{1,0:T(8,128)(2,1)S(1)} collective-permute-done((bf16[16,8448]{1,0:T(8,128)(2,1)S(1)}, bf16[16,8448]{1,0:T(8,128)(2,1)S(1)}, u32[]{:S(2)}, u32[]{:S(2)}) %collective-permute-start.10) | collective-permute-done | bytes 270368 | tf_op jit(solution)/shard_map/ppermute | solution.py:17
  137.3 3.0 %collective-permute-start.11 = (bf16[16,8448]{1,0:T(8,128)(2,1)S(1)}, bf16[16,8448]{1,0:T(8,128)(2,1)S(1)}, u32[]{:S(2)}, u32[]{:S(2)}) collective-permute-start(bf16[16,8448]{1,0:T(8,128)(2,1)S(1)} %pad_maximum_fusion.12), channel_id=1, source_target_pairs={{0,16},{1,17},{2,18},{3,19},{4,20},{5,21},{6,22},{7,23},{8,24},{9,... | collective-permute-start | bytes 811016 | tf_op jit(solution)/shard_map/ppermute | solution.py:17
  142.2 2.1 collective-permute-done.11
  145.0 5.7 %collective-permute-done.5 = bf16[16,8448]{1,0:T(8,128)(2,1)} collective-permute-done((bf16[16,8448]{1,0:T(8,128)(2,1)S(1)}, bf16[16,8448]{1,0:T(8,128)(2,1)}, u32[]{:S(2)}, u32[]{:S(2)}) %collective-permute-start.5) | collective-permute-done | bytes 270368 | tf_op jit(solution)/shard_map/ppermute | solution.py:17
  155.4 5.0 %shard_map.68 = bf16[2048,1280]{1,0:T(8,128)(2,1)} custom-call(bf16[2048,128]{1,0:T(8,128)(2,1)} %bitcast.213, bf16[128,1280]{1,0:T(8,128)(2,1)} %pad_maximum_fusion.4.right_ref), custom_call_target="tpu_custom_call" | custom-call | flops 671088640 | bytes 6094848 | tf_op jit(solution)/shard_map/pallas_call | solution.py:121
  162.7 4.7 %collective-permute-done.12 = bf16[4,4,64,1280]{3,2,1,0:T(8,128)(2,1)} collective-permute-done((bf16[4,4,64,1280]{3,2,1,0:T(8,128)(2,1)S(1)}, bf16[4,4,64,1280]{3,2,1,0:T(8,128)(2,1)}, u32[]{:S(2)}, u32[]{:S(2)}) %collective-permute-start.12) | collective-permute-done | bytes 2621472 | tf_op jit(solution)/shard_map/ppermute | solution.py:74
  167.4 3.2 %convert_add_fusion = f32[4,4,64,1280]{3,2,1,0:T(8,128)S(1)} fusion(bf16[4,4,64,1280]{3,2,1,0:T(8,128)(2,1)} %collective-permute-done.12, bf16[4,4,2,64,1280]{4,3,2,1,0:T(8,128)(2,1)} %bitcast.212, s32[]{:T(128)S(6)} %select_n.219), kind=kLoop, calls=%fused_computation.1 | loop fusion | flops 3932160 | bytes 10485764 | tf_op jit(solution)/shard_map/add | solution.py:75
  175.0 13.0 %collective-permute-done.21 = bf16[4,64,640]{2,1,0:T(8,128)(2,1)S(1)} collective-permute-done((bf16[4,64,640]{2,1,0:T(8,128)(2,1)S(1)}, bf16[4,64,640]{2,1,0:T(8,128)(2,1)S(1)}, u32[]{:S(2)}, u32[]{:S(2)}) %collective-permute-start.21) | collective-permute-done | bytes 327712 | tf_op jit(solution)/shard_map/ppermute | solution.py:74
  192.5 8.3 %collective-permute-done.13 = bf16[4,64,640]{2,1,0:T(8,128)(2,1)S(1)} collective-permute-done((bf16[4,64,640]{2,1,0:T(8,128)(2,1)S(1)}, bf16[4,64,640]{2,1,0:T(8,128)(2,1)S(1)}, u32[]{:S(2)}, u32[]{:S(2)}) %collective-permute-start.13) | collective-permute-done | bytes 327712 | tf_op jit(solution)/shard_map/ppermute | solution.py:74
  203.2 2.4 collective-permute-done.18
  208.6 3.4 %collective-permute-start.31 = (f32[8,1280]{1,0:T(8,128)S(1)}, f32[8,1280]{1,0:T(8,128)S(1)}, u32[]{:S(2)}, u32[]{:S(2)}) collective-permute-start(f32[8,1280]{1,0:T(8,128)S(1)} %get-tuple-element.148), channel_id=1, source_target_pairs={{0,224},{32,0},{64,32},{96,64},{128,96},{160,128},{192,160},{224,1... | collective-permute-start | bytes 122888 | tf_op jit(solution)/shard_map/ppermute | solution.py:101
  212.0 2.2 collective-permute-start.30
  215.4 3.9 %collective-permute-start.28 = (f32[8,1280]{1,0:T(8,128)S(1)}, f32[8,1280]{1,0:T(8,128)S(1)}, u32[]{:S(2)}, u32[]{:S(2)}) collective-permute-start(f32[8,1280]{1,0:T(8,128)S(1)} %get-tuple-element.151), channel_id=1, source_target_pairs={{0,128},{32,160},{64,192},{96,224},{128,0},{160,32},{192,64},{224,... | collective-permute-start | bytes 122888 | tf_op jit(solution)/shard_map/ppermute | solution.py:101
  219.3 3.5 %collective-permute-start.26 = (f32[8,1280]{1,0:T(8,128)S(1)}, f32[8,1280]{1,0:T(8,128)S(1)}, u32[]{:S(2)}, u32[]{:S(2)}) collective-permute-start(f32[8,1280]{1,0:T(8,128)S(1)} %get-tuple-element.153), channel_id=1, source_target_pairs={{0,64},{32,96},{64,128},{96,160},{128,192},{160,224},{192,0},{224,... | collective-permute-start | bytes 122888 | tf_op jit(solution)/shard_map/ppermute | solution.py:101
  224.6 1.9 collective-permute-done.27
  229.0 5.3 %convolution_bitcast_fusion = f32[1,128,2048]{2,1,0:T(8,128)} fusion(bf16[2048,1280]{1,0:T(8,128)(2,1)} %all-gather.2.cloned.1.call-done, bf16[128,128]{1,0:T(8,128)(2,1)S(1)} %fusion.7, bf16[128,128]{1,0:T(8,128)(2,1)S(1)} %fusion.6, bf16[128,1024]{1,0:T(8,128)(2,1)S(1)} %copy.82), kind=kOutput, calls=%fused_computation.3 | convolution fusion | flops 672071680 | bytes 6619136 | tf_op jit(solution)/shard_map/dot_general | solution.py:251
  237.6 2.9 %collective-permute-start.35 = (f32[8,1280]{1,0:T(8,128)S(1)}, f32[8,1280]{1,0:T(8,128)S(1)}, u32[]{:S(2)}, u32[]{:S(2)}) collective-permute-start(f32[8,1280]{1,0:T(8,128)S(1)} %get-tuple-element.95), channel_id=1, source_target_pairs={{0,128},{32,160},{64,192},{96,224},{128,0},{160,32},{192,64},{224,... | collective-permute-start | bytes 122888 | tf_op jit(solution)/shard_map/ppermute | solution.py:105
  240.5 2.4 collective-permute-start.36
  242.9 3.7 %collective-permute-start.37 = (f32[8,1280]{1,0:T(8,128)S(1)}, f32[8,1280]{1,0:T(8,128)S(1)}, u32[]{:S(2)}, u32[]{:S(2)}) collective-permute-start(f32[8,1280]{1,0:T(8,128)S(1)} %get-tuple-element.95), channel_id=1, source_target_pairs={{0,192},{32,224},{64,0},{96,32},{128,64},{160,96},{192,128},{224,1... | collective-permute-start | bytes 122888 | tf_op jit(solution)/shard_map/ppermute | solution.py:105
  248.3 2.3 collective-permute-done.38
  (198 shorter events, 59.0 us)
Async XLA Ops:
  7.2 59.0 %all-gather.2.cloned.1.call-start = ((), (), s32[]{:S(2)}) async-start(), calls=%async_computation | async-start | bytes 5406720 | tf_op jit(solution)/shard_map/all_gather | solution.py:217
  72.5 13.2 %collective-permute-start = (bf16[16,8448]{1,0:T(8,128)(2,1)S(1)}, bf16[16,8448]{1,0:T(8,128)(2,1)S(1)}, u32[]{:S(2)}, u32[]{:S(2)}) collective-permute-start(bf16[16,8448]{1,0:T(8,128)(2,1)S(1)} %get-tuple-element.168), channel_id=1, source_target_pairs={{1,0},{2,1},{3,2},{4,3},{5,4},{6,5},{7,6},{8,7},{9,8},{10,9},{11,1... | collective-permute-start | bytes 811016 | tf_op jit(solution)/shard_map/ppermute | solution.py:17
  76.9 9.7 %collective-permute-start.1 = (bf16[16,8448]{1,0:T(8,128)(2,1)S(1)}, bf16[16,8448]{1,0:T(8,128)(2,1)S(1)}, u32[]{:S(2)}, u32[]{:S(2)}) collective-permute-start(bf16[16,8448]{1,0:T(8,128)(2,1)S(1)} %get-tuple-element.168), channel_id=1, source_target_pairs={{2,0},{3,1},{4,2},{5,3},{6,4},{7,5},{8,6},{9,7},{10,8},{11,9},{12,... | collective-permute-start | bytes 811016 | tf_op jit(solution)/shard_map/ppermute | solution.py:17
  80.1 13.7 %collective-permute-start.6 = (bf16[16,8448]{1,0:T(8,128)(2,1)S(1)}, bf16[16,8448]{1,0:T(8,128)(2,1)S(1)}, u32[]{:S(2)}, u32[]{:S(2)}) collective-permute-start(bf16[16,8448]{1,0:T(8,128)(2,1)S(1)} %get-tuple-element.169), channel_id=1, source_target_pairs={{0,1},{1,2},{2,3},{3,4},{4,5},{5,6},{6,7},{7,8},{8,9},{9,10},{10,1... | collective-permute-start | bytes 811016 | tf_op jit(solution)/shard_map/ppermute | solution.py:17
  82.2 13.0 %collective-permute-start.7 = (bf16[16,8448]{1,0:T(8,128)(2,1)S(1)}, bf16[16,8448]{1,0:T(8,128)(2,1)S(1)}, u32[]{:S(2)}, u32[]{:S(2)}) collective-permute-start(bf16[16,8448]{1,0:T(8,128)(2,1)S(1)} %get-tuple-element.169), channel_id=1, source_target_pairs={{0,2},{1,3},{2,4},{3,5},{4,6},{5,7},{6,8},{7,9},{8,10},{9,11},{10,... | collective-permute-start | bytes 811016 | tf_op jit(solution)/shard_map/ppermute | solution.py:17
  87.3 11.3 %collective-permute-start.2 = (bf16[16,8448]{1,0:T(8,128)(2,1)S(1)}, bf16[16,8448]{1,0:T(8,128)(2,1)S(1)}, u32[]{:S(2)}, u32[]{:S(2)}) collective-permute-start(bf16[16,8448]{1,0:T(8,128)(2,1)S(1)} %pad_maximum_fusion.5), channel_id=1, source_target_pairs={{2,0},{3,1},{4,2},{5,3},{6,4},{7,5},{8,6},{9,7},{10,8},{11,9},{12,... | collective-permute-start | bytes 811016 | tf_op jit(solution)/shard_map/ppermute | solution.py:17
  95.8 18.5 %collective-permute-start.8 = (bf16[16,8448]{1,0:T(8,128)(2,1)S(1)}, bf16[16,8448]{1,0:T(8,128)(2,1)S(1)}, u32[]{:S(2)}, u32[]{:S(2)}) collective-permute-start(bf16[16,8448]{1,0:T(8,128)(2,1)S(1)} %pad_maximum_fusion.9), channel_id=1, source_target_pairs={{0,2},{1,3},{2,4},{3,5},{4,6},{5,7},{6,8},{7,9},{8,10},{9,11},{10,... | collective-permute-start | bytes 811016 | tf_op jit(solution)/shard_map/ppermute | solution.py:17
  99.1 17.7 %collective-permute-start.3 = (bf16[16,8448]{1,0:T(8,128)(2,1)S(1)}, bf16[16,8448]{1,0:T(8,128)(2,1)S(1)}, u32[]{:S(2)}, u32[]{:S(2)}) collective-permute-start(bf16[16,8448]{1,0:T(8,128)(2,1)S(1)} %pad_maximum_fusion.6), channel_id=1, source_target_pairs={{4,0},{5,1},{6,2},{7,3},{8,4},{9,5},{10,6},{11,7},{12,8},{13,9},{1... | collective-permute-start | bytes 811016 | tf_op jit(solution)/shard_map/ppermute | solution.py:17
  114.9 12.2 %collective-permute-start.9 = (bf16[16,8448]{1,0:T(8,128)(2,1)S(1)}, bf16[16,8448]{1,0:T(8,128)(2,1)S(1)}, u32[]{:S(2)}, u32[]{:S(2)}) collective-permute-start(bf16[16,8448]{1,0:T(8,128)(2,1)S(1)} %pad_maximum_fusion.10), channel_id=1, source_target_pairs={{0,4},{1,5},{2,6},{3,7},{4,8},{5,9},{6,10},{7,11},{8,12},{9,13},{1... | collective-permute-start | bytes 811016 | tf_op jit(solution)/shard_map/ppermute | solution.py:17
  117.5 13.8 %collective-permute-start.4 = (bf16[16,8448]{1,0:T(8,128)(2,1)S(1)}, bf16[16,8448]{1,0:T(8,128)(2,1)S(1)}, u32[]{:S(2)}, u32[]{:S(2)}) collective-permute-start(bf16[16,8448]{1,0:T(8,128)(2,1)S(1)} %pad_maximum_fusion.7), channel_id=1, source_target_pairs={{8,0},{9,1},{10,2},{11,3},{12,4},{13,5},{14,6},{15,7},{16,8},{17,9... | collective-permute-start | bytes 811016 | tf_op jit(solution)/shard_map/ppermute | solution.py:17
  127.8 8.9 %collective-permute-start.10 = (bf16[16,8448]{1,0:T(8,128)(2,1)S(1)}, bf16[16,8448]{1,0:T(8,128)(2,1)S(1)}, u32[]{:S(2)}, u32[]{:S(2)}) collective-permute-start(bf16[16,8448]{1,0:T(8,128)(2,1)S(1)} %pad_maximum_fusion.11), channel_id=1, source_target_pairs={{0,8},{1,9},{2,10},{3,11},{4,12},{5,13},{6,14},{7,15},{8,16},{9,17... | collective-permute-start | bytes 811016 | tf_op jit(solution)/shard_map/ppermute | solution.py:17
  140.7 10.0 %collective-permute-start.5 = (bf16[16,8448]{1,0:T(8,128)(2,1)S(1)}, bf16[16,8448]{1,0:T(8,128)(2,1)}, u32[]{:S(2)}, u32[]{:S(2)}) collective-permute-start(bf16[16,8448]{1,0:T(8,128)(2,1)S(1)} %pad_maximum_fusion.8), channel_id=1, source_target_pairs={{16,0},{17,1},{18,2},{19,3},{20,4},{21,5},{22,6},{23,7},{24,8},{25... | collective-permute-start | bytes 811016 | tf_op jit(solution)/shard_map/ppermute | solution.py:17
  171.2 16.9 %collective-permute-start.21 = (bf16[4,64,640]{2,1,0:T(8,128)(2,1)S(1)}, bf16[4,64,640]{2,1,0:T(8,128)(2,1)S(1)}, u32[]{:S(2)}, u32[]{:S(2)}) collective-permute-start(bf16[4,64,640]{2,1,0:T(8,128)(2,1)S(1)} %get-tuple-element.143), channel_id=1, source_target_pairs={{0,24},{1,25},{2,26},{3,27},{4,28},{5,29},{6,30},{7,31},{8,0},{9,1... | collective-permute-start | bytes 983048 | tf_op jit(solution)/shard_map/ppermute | solution.py:74
  172.5 15.5 %collective-permute-start.20 = (bf16[4,64,640]{2,1,0:T(8,128)(2,1)S(1)}, bf16[4,64,640]{2,1,0:T(8,128)(2,1)S(1)}, u32[]{:S(2)}, u32[]{:S(2)}) collective-permute-start(bf16[4,64,640]{2,1,0:T(8,128)(2,1)S(1)} %get-tuple-element.144), channel_id=1, source_target_pairs={{0,16},{1,17},{2,18},{3,19},{4,20},{5,21},{6,22},{7,23},{8,24},{9,... | collective-permute-start | bytes 983048 | tf_op jit(solution)/shard_map/ppermute | solution.py:74
  172.5 17.4 %collective-permute-start.19 = (bf16[4,64,640]{2,1,0:T(8,128)(2,1)S(1)}, bf16[4,64,640]{2,1,0:T(8,128)(2,1)S(1)}, u32[]{:S(2)}, u32[]{:S(2)}) collective-permute-start(bf16[4,64,640]{2,1,0:T(8,128)(2,1)S(1)} %get-tuple-element.142), channel_id=1, source_target_pairs={{0,8},{1,9},{2,10},{3,11},{4,12},{5,13},{6,14},{7,15},{8,16},{9,17... | collective-permute-start | bytes 983048 | tf_op jit(solution)/shard_map/ppermute | solution.py:74
  174.2 17.4 %collective-permute-start.15 = (bf16[4,64,640]{2,1,0:T(8,128)(2,1)S(1)}, bf16[4,64,640]{2,1,0:T(8,128)(2,1)S(1)}, u32[]{:S(2)}, u32[]{:S(2)}) collective-permute-start(bf16[4,64,640]{2,1,0:T(8,128)(2,1)S(1)} %get-tuple-element.140), channel_id=1, source_target_pairs={{0,6},{1,7},{2,0},{3,1},{4,2},{5,3},{6,4},{7,5},{8,14},{9,15},{10,... | collective-permute-start | bytes 983048 | tf_op jit(solution)/shard_map/ppermute | solution.py:74
  174.3 18.3 %collective-permute-start.14 = (bf16[4,64,640]{2,1,0:T(8,128)(2,1)S(1)}, bf16[4,64,640]{2,1,0:T(8,128)(2,1)S(1)}, u32[]{:S(2)}, u32[]{:S(2)}) collective-permute-start(bf16[4,64,640]{2,1,0:T(8,128)(2,1)S(1)} %get-tuple-element.141), channel_id=1, source_target_pairs={{0,4},{1,5},{2,6},{3,7},{4,0},{5,1},{6,2},{7,3},{8,12},{9,13},{10,... | collective-permute-start | bytes 983048 | tf_op jit(solution)/shard_map/ppermute | solution.py:74
  188.0 12.8 %collective-permute-start.13 = (bf16[4,64,640]{2,1,0:T(8,128)(2,1)S(1)}, bf16[4,64,640]{2,1,0:T(8,128)(2,1)S(1)}, u32[]{:S(2)}, u32[]{:S(2)}) collective-permute-start(bf16[4,64,640]{2,1,0:T(8,128)(2,1)S(1)} %get-tuple-element.139), channel_id=1, source_target_pairs={{0,2},{1,3},{2,4},{3,5},{4,6},{5,7},{6,0},{7,1},{8,10},{9,11},{10,... | collective-permute-start | bytes 983048 | tf_op jit(solution)/shard_map/ppermute | solution.py:74
  190.1 12.0 %collective-permute-start.24 = (bf16[64,640]{1,0:T(8,128)(2,1)S(1)}, bf16[64,640]{1,0:T(8,128)(2,1)S(1)}, u32[]{:S(2)}, u32[]{:S(2)}) collective-permute-start(bf16[64,640]{1,0:T(8,128)(2,1)S(1)} %get-tuple-element.158), channel_id=1, source_target_pairs={{0,6},{1,7},{2,0},{3,1},{4,2},{5,3},{6,4},{7,5},{8,14},{9,15},{10,... | collective-permute-start | bytes 245768 | tf_op jit(solution)/shard_map/ppermute | solution.py:74
  191.5 11.6 %collective-permute-start.23 = (bf16[64,640]{1,0:T(8,128)(2,1)S(1)}, bf16[64,640]{1,0:T(8,128)(2,1)S(1)}, u32[]{:S(2)}, u32[]{:S(2)}) collective-permute-start(bf16[64,640]{1,0:T(8,128)(2,1)S(1)} %get-tuple-element.159), channel_id=1, source_target_pairs={{0,4},{1,5},{2,6},{3,7},{4,0},{5,1},{6,2},{7,3},{8,12},{9,13},{10,... | collective-permute-start | bytes 245768 | tf_op jit(solution)/shard_map/ppermute | solution.py:74
  191.6 11.6 %collective-permute-start.22 = (bf16[64,640]{1,0:T(8,128)(2,1)S(1)}, bf16[64,640]{1,0:T(8,128)(2,1)S(1)}, u32[]{:S(2)}, u32[]{:S(2)}) collective-permute-start(bf16[64,640]{1,0:T(8,128)(2,1)S(1)} %get-tuple-element.157), channel_id=1, source_target_pairs={{0,2},{1,3},{2,4},{3,5},{4,6},{5,7},{6,0},{7,1},{8,10},{9,11},{10,... | collective-permute-start | bytes 245768 | tf_op jit(solution)/shard_map/ppermute | solution.py:74
  208.6 10.7 %collective-permute-start.31 = (f32[8,1280]{1,0:T(8,128)S(1)}, f32[8,1280]{1,0:T(8,128)S(1)}, u32[]{:S(2)}, u32[]{:S(2)}) collective-permute-start(f32[8,1280]{1,0:T(8,128)S(1)} %get-tuple-element.148), channel_id=1, source_target_pairs={{0,224},{32,0},{64,32},{96,64},{128,96},{160,128},{192,160},{224,1... | collective-permute-start | bytes 122888 | tf_op jit(solution)/shard_map/ppermute | solution.py:101
  212.0 10.9 %collective-permute-start.30 = (f32[8,1280]{1,0:T(8,128)S(1)}, f32[8,1280]{1,0:T(8,128)S(1)}, u32[]{:S(2)}, u32[]{:S(2)}) collective-permute-start(f32[8,1280]{1,0:T(8,128)S(1)} %get-tuple-element.149), channel_id=1, source_target_pairs={{0,192},{32,224},{64,0},{96,32},{128,64},{160,96},{192,128},{224,1... | collective-permute-start | bytes 122888 | tf_op jit(solution)/shard_map/ppermute | solution.py:101
  214.2 10.4 %collective-permute-start.29 = (f32[8,1280]{1,0:T(8,128)S(1)}, f32[8,1280]{1,0:T(8,128)S(1)}, u32[]{:S(2)}, u32[]{:S(2)}) collective-permute-start(f32[8,1280]{1,0:T(8,128)S(1)} %get-tuple-element.150), channel_id=1, source_target_pairs={{0,160},{32,192},{64,224},{96,0},{128,32},{160,64},{192,96},{224,1... | collective-permute-start | bytes 122888 | tf_op jit(solution)/shard_map/ppermute | solution.py:101
  215.4 9.2 %collective-permute-start.28 = (f32[8,1280]{1,0:T(8,128)S(1)}, f32[8,1280]{1,0:T(8,128)S(1)}, u32[]{:S(2)}, u32[]{:S(2)}) collective-permute-start(f32[8,1280]{1,0:T(8,128)S(1)} %get-tuple-element.151), channel_id=1, source_target_pairs={{0,128},{32,160},{64,192},{96,224},{128,0},{160,32},{192,64},{224,... | collective-permute-start | bytes 122888 | tf_op jit(solution)/shard_map/ppermute | solution.py:101
  219.3 7.3 %collective-permute-start.27 = (f32[8,1280]{1,0:T(8,128)S(1)}, f32[8,1280]{1,0:T(8,128)S(1)}, u32[]{:S(2)}, u32[]{:S(2)}) collective-permute-start(f32[8,1280]{1,0:T(8,128)S(1)} %get-tuple-element.152), channel_id=1, source_target_pairs={{0,96},{32,128},{64,160},{96,192},{128,224},{160,0},{192,32},{224,... | collective-permute-start | bytes 122888 | tf_op jit(solution)/shard_map/ppermute | solution.py:101
  219.3 8.4 %collective-permute-start.26 = (f32[8,1280]{1,0:T(8,128)S(1)}, f32[8,1280]{1,0:T(8,128)S(1)}, u32[]{:S(2)}, u32[]{:S(2)}) collective-permute-start(f32[8,1280]{1,0:T(8,128)S(1)} %get-tuple-element.153), channel_id=1, source_target_pairs={{0,64},{32,96},{64,128},{96,160},{128,192},{160,224},{192,0},{224,... | collective-permute-start | bytes 122888 | tf_op jit(solution)/shard_map/ppermute | solution.py:101
  228.1 14.8 %collective-permute-start.32 = (f32[8,1280]{1,0:T(8,128)S(1)}, f32[8,1280]{1,0:T(8,128)S(1)}, u32[]{:S(2)}, u32[]{:S(2)}) collective-permute-start(f32[8,1280]{1,0:T(8,128)S(1)} %get-tuple-element.95), channel_id=1, source_target_pairs={{0,32},{32,64},{64,96},{96,128},{128,160},{160,192},{192,224},{224... | collective-permute-start | bytes 122888 | tf_op jit(solution)/shard_map/ppermute | solution.py:105
  234.3 12.3 %collective-permute-start.33 = (f32[8,1280]{1,0:T(8,128)S(1)}, f32[8,1280]{1,0:T(8,128)S(1)}, u32[]{:S(2)}, u32[]{:S(2)}) collective-permute-start(f32[8,1280]{1,0:T(8,128)S(1)} %get-tuple-element.95), channel_id=1, source_target_pairs={{0,64},{32,96},{64,128},{96,160},{128,192},{160,224},{192,0},{224,... | collective-permute-start | bytes 122888 | tf_op jit(solution)/shard_map/ppermute | solution.py:105
  235.7 12.0 %collective-permute-start.34 = (f32[8,1280]{1,0:T(8,128)S(1)}, f32[8,1280]{1,0:T(8,128)S(1)}, u32[]{:S(2)}, u32[]{:S(2)}) collective-permute-start(f32[8,1280]{1,0:T(8,128)S(1)} %get-tuple-element.95), channel_id=1, source_target_pairs={{0,96},{32,128},{64,160},{96,192},{128,224},{160,0},{192,32},{224,... | collective-permute-start | bytes 122888 | tf_op jit(solution)/shard_map/ppermute | solution.py:105
  237.6 10.2 %collective-permute-start.35 = (f32[8,1280]{1,0:T(8,128)S(1)}, f32[8,1280]{1,0:T(8,128)S(1)}, u32[]{:S(2)}, u32[]{:S(2)}) collective-permute-start(f32[8,1280]{1,0:T(8,128)S(1)} %get-tuple-element.95), channel_id=1, source_target_pairs={{0,128},{32,160},{64,192},{96,224},{128,0},{160,32},{192,64},{224,... | collective-permute-start | bytes 122888 | tf_op jit(solution)/shard_map/ppermute | solution.py:105
  240.5 7.3 %collective-permute-start.36 = (f32[8,1280]{1,0:T(8,128)S(1)}, f32[8,1280]{1,0:T(8,128)S(1)}, u32[]{:S(2)}, u32[]{:S(2)}) collective-permute-start(f32[8,1280]{1,0:T(8,128)S(1)} %get-tuple-element.95), channel_id=1, source_target_pairs={{0,160},{32,192},{64,224},{96,0},{128,32},{160,64},{192,96},{224,1... | collective-permute-start | bytes 122888 | tf_op jit(solution)/shard_map/ppermute | solution.py:105
  (18 other events, 253.4 us)
Sparse Core Ops, SparseCore 0:
  11.1 54.9 all-gather.1

commit v15 on v14

--- a/solution.py
+++ b/solution.py
@@ -65,7 +65,7 @@
     digit = (lax.axis_index(axis) // stride) % radix
     total = lax.dynamic_index_in_dim(value, digit, where, False).astype(jnp.float32)
     low = value.astype(jnp.bfloat16)
-    for offset in range(1, radix):
+    for offset in sorted(range(1, radix), key=lambda o: -min(o, radix - o)):
         piece = lax.dynamic_index_in_dim(low, (digit + offset) % radix, where, False)
         pairs = [
             (place, place + (((place // stride) % radix + offset) % radix - (place // stride) % radix) * stride)

time: 260 us -> 260 us (level)
  starting transfers between devices: 73.2 us -> 79 us
  waiting for transfers between devices: 125 us -> 120 us
    ppermute x13, starting transfers between devices: 7.71 us -> 13.4 us  [digit_reduce(): got = lax.ppermute(piece.astype(jnp.bfloat16), axis, pairs)]
    ppermute x13, waiting for transfers between devices: 33.2 us -> 27.5 us  [digit_reduce(): got = lax.ppermute(piece.astype(jnp.bfloat16), axis, pairs)]
  transfers between devices with their start and end apart: 40 -> 40, of which waited for: 21 -> 19; matrix products, arithmetic and copies ran while one was open for 7% -> 7% of each run, Pallas kernels for 0% -> 0%
where the time goes in v15:
time: 260 us; the launch traced here: 259 us
  waiting for transfers between devices  120 us (46%)
  starting transfers between devices  79 us (30%)
  other arithmetic  16 us (6%)
  between operations  15.1 us (6%)
  matrix products  12.7 us (5%)
  local copies, waits for them, and re-layouts  11.7 us (4%)
  Pallas kernels  4.98 us (2%)
    all_gather x1, waiting for transfers between devices, local(): lax.all_gather(dequantize(weight_codes, scales), 'seq', axis=0, tiled=True)  50.5 us
    ppermute x12, starting transfers between devices, shifted(): lax.ppermute(value.astype(jnp.bfloat16), axis, pairs).astype(value.dtype)  35.3 us
    ppermute x12, waiting for transfers between devices, shifted(): lax.ppermute(value.astype(jnp.bfloat16), axis, pairs).astype(value.dtype)  35.1 us
    ppermute x13, waiting for transfers between devices, digit_reduce(): got = lax.ppermute(piece.astype(jnp.bfloat16), axis, pairs)  27.5 us
    ppermute x7, starting transfers between devices, replicated_sum(): total = total + lax.ppermute(piece, axis, pairs)  15.8 us
    ppermute x7, starting transfers between devices, replicated_sum(): gathered.append(lax.ppermute(total, axis, pairs))  14.4 us
    ppermute x13, starting transfers between devices, digit_reduce(): got = lax.ppermute(piece.astype(jnp.bfloat16), axis, pairs)  13.4 us
    dot_general x1, matrix products, local(): lax.dot_general(d_proj, weights, (((1,), (1,)), ((), ())), preferred_elem...  5.27 us
  transfers between devices with their start and end apart: 40, of which 19 were waited for; matrix products, arithmetic and copies ran while one was open for 7% of the time, Pallas kernels for 0%

profile of v15, /device:TPU:8, one launch (start us, length us, event | category | flops | bytes accessed | tf_op | source)
XLA Modules:
  0.0 259.0 jit_solution(9647544229241249567)
XLA Ops:
  15.6 50.5 %all-gather.2.cloned.1.call-done = bf16[2048,1280]{1,0:T(8,128)(2,1)} async-done(((bf16[64,1280]{1,0:T(8,128)(2,1)}), bf16[2048,1280]{1,0:T(8,128)(2,1)}) %all-gather.2.cloned.1.call-update) | async-done | bytes 5242896 | tf_op jit(solution)/shard_map/all_gather | solution.py:217
  66.2 4.1 %fusion = bf16[128,1280]{0,1:T(8,128)(2,1)S(1)} fusion(bf16[2048,1280]{1,0:T(8,128)(2,1)} %all-gather.2.cloned.1.call-done, bf16[1,128,2048]{2,1,0:T(8,128)(2,1)S(1)} %copy-done.2), kind=kOutput, calls=%fused_computation.5 | convolution fusion | flops 671252480 | bytes 6094848 | tf_op jit(solution)/shard_map/dot_general | solution.py:218
  72.5 4.4 %collective-permute-start = (bf16[16,8448]{1,0:T(8,128)(2,1)S(1)}, bf16[16,8448]{1,0:T(8,128)(2,1)S(1)}, u32[]{:S(2)}, u32[]{:S(2)}) collective-permute-start(bf16[16,8448]{1,0:T(8,128)(2,1)S(1)} %get-tuple-element.168), channel_id=1, source_target_pairs={{1,0},{2,1},{3,2},{4,3},{5,4},{6,5},{7,6},{8,7},{9,8},{10,9},{11,1... | collective-permute-start | bytes 811016 | tf_op jit(solution)/shard_map/ppermute | solution.py:17
  76.9 2.1 collective-permute-start.1
  80.1 2.1 collective-permute-start.6
  82.2 3.6 %collective-permute-start.7 = (bf16[16,8448]{1,0:T(8,128)(2,1)S(1)}, bf16[16,8448]{1,0:T(8,128)(2,1)S(1)}, u32[]{:S(2)}, u32[]{:S(2)}) collective-permute-start(bf16[16,8448]{1,0:T(8,128)(2,1)S(1)} %get-tuple-element.169), channel_id=1, source_target_pairs={{0,2},{1,3},{2,4},{3,5},{4,6},{5,7},{6,8},{7,9},{8,10},{9,11},{10,... | collective-permute-start | bytes 811016 | tf_op jit(solution)/shard_map/ppermute | solution.py:17
  87.3 6.5 %collective-permute-start.2 = (bf16[16,8448]{1,0:T(8,128)(2,1)S(1)}, bf16[16,8448]{1,0:T(8,128)(2,1)S(1)}, u32[]{:S(2)}, u32[]{:S(2)}) collective-permute-start(bf16[16,8448]{1,0:T(8,128)(2,1)S(1)} %pad_maximum_fusion.5), channel_id=1, source_target_pairs={{2,0},{3,1},{4,2},{5,3},{6,4},{7,5},{8,6},{9,7},{10,8},{11,9},{12,... | collective-permute-start | bytes 811016 | tf_op jit(solution)/shard_map/ppermute | solution.py:17
  99.1 4.1 %collective-permute-start.3 = (bf16[16,8448]{1,0:T(8,128)(2,1)S(1)}, bf16[16,8448]{1,0:T(8,128)(2,1)S(1)}, u32[]{:S(2)}, u32[]{:S(2)}) collective-permute-start(bf16[16,8448]{1,0:T(8,128)(2,1)S(1)} %pad_maximum_fusion.6), channel_id=1, source_target_pairs={{4,0},{5,1},{6,2},{7,3},{8,4},{9,5},{10,6},{11,7},{12,8},{13,9},{1... | collective-permute-start | bytes 811016 | tf_op jit(solution)/shard_map/ppermute | solution.py:17
  103.3 11.1 %collective-permute-done.8 = bf16[16,8448]{1,0:T(8,128)(2,1)S(1)} collective-permute-done((bf16[16,8448]{1,0:T(8,128)(2,1)S(1)}, bf16[16,8448]{1,0:T(8,128)(2,1)S(1)}, u32[]{:S(2)}, u32[]{:S(2)}) %collective-permute-start.8) | collective-permute-done | bytes 270368 | tf_op jit(solution)/shard_map/ppermute | solution.py:17
  119.4 7.7 %collective-permute-done.9 = bf16[16,8448]{1,0:T(8,128)(2,1)S(1)} collective-permute-done((bf16[16,8448]{1,0:T(8,128)(2,1)S(1)}, bf16[16,8448]{1,0:T(8,128)(2,1)S(1)}, u32[]{:S(2)}, u32[]{:S(2)}) %collective-permute-start.9) | collective-permute-done | bytes 270368 | tf_op jit(solution)/shard_map/ppermute | solution.py:17
  127.8 2.3 collective-permute-start.10
  131.3 5.4 %collective-permute-done.10 = bf16[16,8448]{1,0:T(8,128)(2,1)S(1)} collective-permute-done((bf16[16,8448]{1,0:T(8,128)(2,1)S(1)}, bf16[16,8448]{1,0:T(8,128)(2,1)S(1)}, u32[]{:S(2)}, u32[]{:S(2)}) %collective-permute-start.10) | collective-permute-done | bytes 270368 | tf_op jit(solution)/shard_map/ppermute | solution.py:17
  137.3 3.0 %collective-permute-start.11 = (bf16[16,8448]{1,0:T(8,128)(2,1)S(1)}, bf16[16,8448]{1,0:T(8,128)(2,1)S(1)}, u32[]{:S(2)}, u32[]{:S(2)}) collective-permute-start(bf16[16,8448]{1,0:T(8,128)(2,1)S(1)} %pad_maximum_fusion.12), channel_id=1, source_target_pairs={{0,16},{1,17},{2,18},{3,19},{4,20},{5,21},{6,22},{7,23},{8,24},{9,... | collective-permute-start | bytes 811016 | tf_op jit(solution)/shard_map/ppermute | solution.py:17
  145.0 5.7 %collective-permute-done.5 = bf16[16,8448]{1,0:T(8,128)(2,1)} collective-permute-done((bf16[16,8448]{1,0:T(8,128)(2,1)S(1)}, bf16[16,8448]{1,0:T(8,128)(2,1)}, u32[]{:S(2)}, u32[]{:S(2)}) %collective-permute-start.5) | collective-permute-done | bytes 270368 | tf_op jit(solution)/shard_map/ppermute | solution.py:17
  155.4 5.0 %shard_map.68 = bf16[2048,1280]{1,0:T(8,128)(2,1)} custom-call(bf16[2048,128]{1,0:T(8,128)(2,1)} %bitcast.213, bf16[128,1280]{1,0:T(8,128)(2,1)} %pad_maximum_fusion.4.right_ref), custom_call_target="tpu_custom_call" | custom-call | flops 671088640 | bytes 6094848 | tf_op jit(solution)/shard_map/pallas_call | solution.py:121
  162.7 4.7 %collective-permute-done.12 = bf16[4,4,64,1280]{3,2,1,0:T(8,128)(2,1)} collective-permute-done((bf16[4,4,64,1280]{3,2,1,0:T(8,128)(2,1)S(1)}, bf16[4,4,64,1280]{3,2,1,0:T(8,128)(2,1)}, u32[]{:S(2)}, u32[]{:S(2)}) %collective-permute-start.12) | collective-permute-done | bytes 2621472 | tf_op jit(solution)/shard_map/ppermute | solution.py:74
  167.4 3.2 %convert_add_fusion = f32[4,4,64,1280]{3,2,1,0:T(8,128)S(1)} fusion(bf16[4,4,64,1280]{3,2,1,0:T(8,128)(2,1)} %collective-permute-done.12, bf16[4,4,2,64,1280]{4,3,2,1,0:T(8,128)(2,1)} %bitcast.212, s32[]{:T(128)S(6)} %select_n.219), kind=kLoop, calls=%fused_computation.1 | loop fusion | flops 3932160 | bytes 10485764 | tf_op jit(solution)/shard_map/add | solution.py:75
  177.5 10.5 %collective-permute-done.21 = bf16[4,64,640]{2,1,0:T(8,128)(2,1)S(1)} collective-permute-done((bf16[4,64,640]{2,1,0:T(8,128)(2,1)S(1)}, bf16[4,64,640]{2,1,0:T(8,128)(2,1)S(1)}, u32[]{:S(2)}, u32[]{:S(2)}) %collective-permute-start.21) | collective-permute-done | bytes 327712 | tf_op jit(solution)/shard_map/ppermute | solution.py:74
  190.4 3.5 %collective-permute-start.22 = (bf16[64,640]{1,0:T(8,128)(2,1)S(1)}, bf16[64,640]{1,0:T(8,128)(2,1)S(1)}, u32[]{:S(2)}, u32[]{:S(2)}) collective-permute-start(bf16[64,640]{1,0:T(8,128)(2,1)S(1)} %get-tuple-element.157), channel_id=1, source_target_pairs={{0,4},{1,5},{2,6},{3,7},{4,0},{5,1},{6,2},{7,3},{8,12},{9,13},{10,... | collective-permute-start | bytes 245768 | tf_op jit(solution)/shard_map/ppermute | solution.py:74
  193.9 6.4 %collective-permute-done.13 = bf16[4,64,640]{2,1,0:T(8,128)(2,1)S(1)} collective-permute-done((bf16[4,64,640]{2,1,0:T(8,128)(2,1)S(1)}, bf16[4,64,640]{2,1,0:T(8,128)(2,1)S(1)}, u32[]{:S(2)}, u32[]{:S(2)}) %collective-permute-start.13) | collective-permute-done | bytes 327712 | tf_op jit(solution)/shard_map/ppermute | solution.py:74
  202.6 2.4 collective-permute-done.18
  205.1 3.4 %collective-permute-done.16 = bf16[64,640]{1,0:T(8,128)(2,1)S(1)} collective-permute-done((bf16[64,640]{1,0:T(8,128)(2,1)S(1)}, bf16[64,640]{1,0:T(8,128)(2,1)S(1)}, u32[]{:S(2)}, u32[]{:S(2)}) %collective-permute-start.16) | collective-permute-done | bytes 81952 | tf_op jit(solution)/shard_map/ppermute | solution.py:74
  208.6 3.4 %collective-permute-start.31 = (f32[8,1280]{1,0:T(8,128)S(1)}, f32[8,1280]{1,0:T(8,128)S(1)}, u32[]{:S(2)}, u32[]{:S(2)}) collective-permute-start(f32[8,1280]{1,0:T(8,128)S(1)} %get-tuple-element.148), channel_id=1, source_target_pairs={{0,224},{32,0},{64,32},{96,64},{128,96},{160,128},{192,160},{224,1... | collective-permute-start | bytes 122888 | tf_op jit(solution)/shard_map/ppermute | solution.py:101
  212.0 2.2 collective-permute-start.30
  215.4 3.9 %collective-permute-start.28 = (f32[8,1280]{1,0:T(8,128)S(1)}, f32[8,1280]{1,0:T(8,128)S(1)}, u32[]{:S(2)}, u32[]{:S(2)}) collective-permute-start(f32[8,1280]{1,0:T(8,128)S(1)} %get-tuple-element.151), channel_id=1, source_target_pairs={{0,128},{32,160},{64,192},{96,224},{128,0},{160,32},{192,64},{224,... | collective-permute-start | bytes 122888 | tf_op jit(solution)/shard_map/ppermute | solution.py:101
  219.4 3.5 %collective-permute-start.26 = (f32[8,1280]{1,0:T(8,128)S(1)}, f32[8,1280]{1,0:T(8,128)S(1)}, u32[]{:S(2)}, u32[]{:S(2)}) collective-permute-start(f32[8,1280]{1,0:T(8,128)S(1)} %get-tuple-element.153), channel_id=1, source_target_pairs={{0,64},{32,96},{64,128},{96,160},{128,192},{160,224},{192,0},{224,... | collective-permute-start | bytes 122888 | tf_op jit(solution)/shard_map/ppermute | solution.py:101
  228.9 5.3 %convolution_bitcast_fusion = f32[1,128,2048]{2,1,0:T(8,128)} fusion(bf16[2048,1280]{1,0:T(8,128)(2,1)} %all-gather.2.cloned.1.call-done, bf16[128,128]{1,0:T(8,128)(2,1)S(1)} %fusion.7, bf16[128,128]{1,0:T(8,128)(2,1)S(1)} %fusion.6, bf16[128,1024]{1,0:T(8,128)(2,1)S(1)} %copy.82), kind=kOutput, calls=%fused_computation.3 | convolution fusion | flops 672071680 | bytes 6619136 | tf_op jit(solution)/shard_map/dot_general | solution.py:251
  235.8 2.2 collective-permute-start.34
  238.0 2.6 collective-permute-start.35
  240.6 2.3 collective-permute-start.36
  242.8 3.9 %collective-permute-start.37 = (f32[8,1280]{1,0:T(8,128)S(1)}, f32[8,1280]{1,0:T(8,128)S(1)}, u32[]{:S(2)}, u32[]{:S(2)}) collective-permute-start(f32[8,1280]{1,0:T(8,128)S(1)} %get-tuple-element.95), channel_id=1, source_target_pairs={{0,192},{32,224},{64,0},{96,32},{128,64},{160,96},{192,128},{224,1... | collective-permute-start | bytes 122888 | tf_op jit(solution)/shard_map/ppermute | solution.py:105
  248.4 2.4 collective-permute-done.38
  (198 shorter events, 60.4 us)
Async XLA Ops:
  7.2 59.0 %all-gather.2.cloned.1.call-start = ((), (), s32[]{:S(2)}) async-start(), calls=%async_computation | async-start | bytes 5406720 | tf_op jit(solution)/shard_map/all_gather | solution.py:217
  72.5 13.2 %collective-permute-start = (bf16[16,8448]{1,0:T(8,128)(2,1)S(1)}, bf16[16,8448]{1,0:T(8,128)(2,1)S(1)}, u32[]{:S(2)}, u32[]{:S(2)}) collective-permute-start(bf16[16,8448]{1,0:T(8,128)(2,1)S(1)} %get-tuple-element.168), channel_id=1, source_target_pairs={{1,0},{2,1},{3,2},{4,3},{5,4},{6,5},{7,6},{8,7},{9,8},{10,9},{11,1... | collective-permute-start | bytes 811016 | tf_op jit(solution)/shard_map/ppermute | solution.py:17
  76.9 9.7 %collective-permute-start.1 = (bf16[16,8448]{1,0:T(8,128)(2,1)S(1)}, bf16[16,8448]{1,0:T(8,128)(2,1)S(1)}, u32[]{:S(2)}, u32[]{:S(2)}) collective-permute-start(bf16[16,8448]{1,0:T(8,128)(2,1)S(1)} %get-tuple-element.168), channel_id=1, source_target_pairs={{2,0},{3,1},{4,2},{5,3},{6,4},{7,5},{8,6},{9,7},{10,8},{11,9},{12,... | collective-permute-start | bytes 811016 | tf_op jit(solution)/shard_map/ppermute | solution.py:17
  80.1 13.7 %collective-permute-start.6 = (bf16[16,8448]{1,0:T(8,128)(2,1)S(1)}, bf16[16,8448]{1,0:T(8,128)(2,1)S(1)}, u32[]{:S(2)}, u32[]{:S(2)}) collective-permute-start(bf16[16,8448]{1,0:T(8,128)(2,1)S(1)} %get-tuple-element.169), channel_id=1, source_target_pairs={{0,1},{1,2},{2,3},{3,4},{4,5},{5,6},{6,7},{7,8},{8,9},{9,10},{10,1... | collective-permute-start | bytes 811016 | tf_op jit(solution)/shard_map/ppermute | solution.py:17
  82.2 13.0 %collective-permute-start.7 = (bf16[16,8448]{1,0:T(8,128)(2,1)S(1)}, bf16[16,8448]{1,0:T(8,128)(2,1)S(1)}, u32[]{:S(2)}, u32[]{:S(2)}) collective-permute-start(bf16[16,8448]{1,0:T(8,128)(2,1)S(1)} %get-tuple-element.169), channel_id=1, source_target_pairs={{0,2},{1,3},{2,4},{3,5},{4,6},{5,7},{6,8},{7,9},{8,10},{9,11},{10,... | collective-permute-start | bytes 811016 | tf_op jit(solution)/shard_map/ppermute | solution.py:17
  87.3 11.3 %collective-permute-start.2 = (bf16[16,8448]{1,0:T(8,128)(2,1)S(1)}, bf16[16,8448]{1,0:T(8,128)(2,1)S(1)}, u32[]{:S(2)}, u32[]{:S(2)}) collective-permute-start(bf16[16,8448]{1,0:T(8,128)(2,1)S(1)} %pad_maximum_fusion.5), channel_id=1, source_target_pairs={{2,0},{3,1},{4,2},{5,3},{6,4},{7,5},{8,6},{9,7},{10,8},{11,9},{12,... | collective-permute-start | bytes 811016 | tf_op jit(solution)/shard_map/ppermute | solution.py:17
  95.8 18.5 %collective-permute-start.8 = (bf16[16,8448]{1,0:T(8,128)(2,1)S(1)}, bf16[16,8448]{1,0:T(8,128)(2,1)S(1)}, u32[]{:S(2)}, u32[]{:S(2)}) collective-permute-start(bf16[16,8448]{1,0:T(8,128)(2,1)S(1)} %pad_maximum_fusion.9), channel_id=1, source_target_pairs={{0,2},{1,3},{2,4},{3,5},{4,6},{5,7},{6,8},{7,9},{8,10},{9,11},{10,... | collective-permute-start | bytes 811016 | tf_op jit(solution)/shard_map/ppermute | solution.py:17
  99.1 17.7 %collective-permute-start.3 = (bf16[16,8448]{1,0:T(8,128)(2,1)S(1)}, bf16[16,8448]{1,0:T(8,128)(2,1)S(1)}, u32[]{:S(2)}, u32[]{:S(2)}) collective-permute-start(bf16[16,8448]{1,0:T(8,128)(2,1)S(1)} %pad_maximum_fusion.6), channel_id=1, source_target_pairs={{4,0},{5,1},{6,2},{7,3},{8,4},{9,5},{10,6},{11,7},{12,8},{13,9},{1... | collective-permute-start | bytes 811016 | tf_op jit(solution)/shard_map/ppermute | solution.py:17
  114.9 12.2 %collective-permute-start.9 = (bf16[16,8448]{1,0:T(8,128)(2,1)S(1)}, bf16[16,8448]{1,0:T(8,128)(2,1)S(1)}, u32[]{:S(2)}, u32[]{:S(2)}) collective-permute-start(bf16[16,8448]{1,0:T(8,128)(2,1)S(1)} %pad_maximum_fusion.10), channel_id=1, source_target_pairs={{0,4},{1,5},{2,6},{3,7},{4,8},{5,9},{6,10},{7,11},{8,12},{9,13},{1... | collective-permute-start | bytes 811016 | tf_op jit(solution)/shard_map/ppermute | solution.py:17
  117.5 13.8 %collective-permute-start.4 = (bf16[16,8448]{1,0:T(8,128)(2,1)S(1)}, bf16[16,8448]{1,0:T(8,128)(2,1)S(1)}, u32[]{:S(2)}, u32[]{:S(2)}) collective-permute-start(bf16[16,8448]{1,0:T(8,128)(2,1)S(1)} %pad_maximum_fusion.7), channel_id=1, source_target_pairs={{8,0},{9,1},{10,2},{11,3},{12,4},{13,5},{14,6},{15,7},{16,8},{17,9... | collective-permute-start | bytes 811016 | tf_op jit(solution)/shard_map/ppermute | solution.py:17
  127.8 8.9 %collective-permute-start.10 = (bf16[16,8448]{1,0:T(8,128)(2,1)S(1)}, bf16[16,8448]{1,0:T(8,128)(2,1)S(1)}, u32[]{:S(2)}, u32[]{:S(2)}) collective-permute-start(bf16[16,8448]{1,0:T(8,128)(2,1)S(1)} %pad_maximum_fusion.11), channel_id=1, source_target_pairs={{0,8},{1,9},{2,10},{3,11},{4,12},{5,13},{6,14},{7,15},{8,16},{9,17... | collective-permute-start | bytes 811016 | tf_op jit(solution)/shard_map/ppermute | solution.py:17
  140.7 10.0 %collective-permute-start.5 = (bf16[16,8448]{1,0:T(8,128)(2,1)S(1)}, bf16[16,8448]{1,0:T(8,128)(2,1)}, u32[]{:S(2)}, u32[]{:S(2)}) collective-permute-start(bf16[16,8448]{1,0:T(8,128)(2,1)S(1)} %pad_maximum_fusion.8), channel_id=1, source_target_pairs={{16,0},{17,1},{18,2},{19,3},{20,4},{21,5},{22,6},{23,7},{24,8},{25... | collective-permute-start | bytes 811016 | tf_op jit(solution)/shard_map/ppermute | solution.py:17
  171.2 16.9 %collective-permute-start.21 = (bf16[4,64,640]{2,1,0:T(8,128)(2,1)S(1)}, bf16[4,64,640]{2,1,0:T(8,128)(2,1)S(1)}, u32[]{:S(2)}, u32[]{:S(2)}) collective-permute-start(bf16[4,64,640]{2,1,0:T(8,128)(2,1)S(1)} %get-tuple-element.143), channel_id=1, source_target_pairs={{0,24},{1,25},{2,26},{3,27},{4,28},{5,29},{6,30},{7,31},{8,0},{9,1... | collective-permute-start | bytes 983048 | tf_op jit(solution)/shard_map/ppermute | solution.py:74
  172.5 15.5 %collective-permute-start.20 = (bf16[4,64,640]{2,1,0:T(8,128)(2,1)S(1)}, bf16[4,64,640]{2,1,0:T(8,128)(2,1)S(1)}, u32[]{:S(2)}, u32[]{:S(2)}) collective-permute-start(bf16[4,64,640]{2,1,0:T(8,128)(2,1)S(1)} %get-tuple-element.144), channel_id=1, source_target_pairs={{0,8},{1,9},{2,10},{3,11},{4,12},{5,13},{6,14},{7,15},{8,16},{9,17... | collective-permute-start | bytes 983048 | tf_op jit(solution)/shard_map/ppermute | solution.py:74
  173.3 14.8 %collective-permute-start.19 = (bf16[4,64,640]{2,1,0:T(8,128)(2,1)S(1)}, bf16[4,64,640]{2,1,0:T(8,128)(2,1)S(1)}, u32[]{:S(2)}, u32[]{:S(2)}) collective-permute-start(bf16[4,64,640]{2,1,0:T(8,128)(2,1)S(1)} %get-tuple-element.142), channel_id=1, source_target_pairs={{0,16},{1,17},{2,18},{3,19},{4,20},{5,21},{6,22},{7,23},{8,24},{9,... | collective-permute-start | bytes 983048 | tf_op jit(solution)/shard_map/ppermute | solution.py:74
  174.8 15.6 %collective-permute-start.15 = (bf16[4,64,640]{2,1,0:T(8,128)(2,1)S(1)}, bf16[4,64,640]{2,1,0:T(8,128)(2,1)S(1)}, u32[]{:S(2)}, u32[]{:S(2)}) collective-permute-start(bf16[4,64,640]{2,1,0:T(8,128)(2,1)S(1)} %get-tuple-element.140), channel_id=1, source_target_pairs={{0,6},{1,7},{2,0},{3,1},{4,2},{5,3},{6,4},{7,5},{8,14},{9,15},{10,... | collective-permute-start | bytes 983048 | tf_op jit(solution)/shard_map/ppermute | solution.py:74
  174.9 19.0 %collective-permute-start.14 = (bf16[4,64,640]{2,1,0:T(8,128)(2,1)S(1)}, bf16[4,64,640]{2,1,0:T(8,128)(2,1)S(1)}, u32[]{:S(2)}, u32[]{:S(2)}) collective-permute-start(bf16[4,64,640]{2,1,0:T(8,128)(2,1)S(1)} %get-tuple-element.141), channel_id=1, source_target_pairs={{0,2},{1,3},{2,4},{3,5},{4,6},{5,7},{6,0},{7,1},{8,10},{9,11},{10,... | collective-permute-start | bytes 983048 | tf_op jit(solution)/shard_map/ppermute | solution.py:74
  188.0 12.2 %collective-permute-start.13 = (bf16[4,64,640]{2,1,0:T(8,128)(2,1)S(1)}, bf16[4,64,640]{2,1,0:T(8,128)(2,1)S(1)}, u32[]{:S(2)}, u32[]{:S(2)}) collective-permute-start(bf16[4,64,640]{2,1,0:T(8,128)(2,1)S(1)} %get-tuple-element.139), channel_id=1, source_target_pairs={{0,4},{1,5},{2,6},{3,7},{4,0},{5,1},{6,2},{7,3},{8,12},{9,13},{10,... | collective-permute-start | bytes 983048 | tf_op jit(solution)/shard_map/ppermute | solution.py:74
  188.2 14.3 %collective-permute-start.24 = (bf16[64,640]{1,0:T(8,128)(2,1)S(1)}, bf16[64,640]{1,0:T(8,128)(2,1)S(1)}, u32[]{:S(2)}, u32[]{:S(2)}) collective-permute-start(bf16[64,640]{1,0:T(8,128)(2,1)S(1)} %get-tuple-element.158), channel_id=1, source_target_pairs={{0,6},{1,7},{2,0},{3,1},{4,2},{5,3},{6,4},{7,5},{8,14},{9,15},{10,... | collective-permute-start | bytes 245768 | tf_op jit(solution)/shard_map/ppermute | solution.py:74
  188.3 14.2 %collective-permute-start.23 = (bf16[64,640]{1,0:T(8,128)(2,1)S(1)}, bf16[64,640]{1,0:T(8,128)(2,1)S(1)}, u32[]{:S(2)}, u32[]{:S(2)}) collective-permute-start(bf16[64,640]{1,0:T(8,128)(2,1)S(1)} %get-tuple-element.159), channel_id=1, source_target_pairs={{0,2},{1,3},{2,4},{3,5},{4,6},{5,7},{6,0},{7,1},{8,10},{9,11},{10,... | collective-permute-start | bytes 245768 | tf_op jit(solution)/shard_map/ppermute | solution.py:74
  190.4 12.2 %collective-permute-start.22 = (bf16[64,640]{1,0:T(8,128)(2,1)S(1)}, bf16[64,640]{1,0:T(8,128)(2,1)S(1)}, u32[]{:S(2)}, u32[]{:S(2)}) collective-permute-start(bf16[64,640]{1,0:T(8,128)(2,1)S(1)} %get-tuple-element.157), channel_id=1, source_target_pairs={{0,4},{1,5},{2,6},{3,7},{4,0},{5,1},{6,2},{7,3},{8,12},{9,13},{10,... | collective-permute-start | bytes 245768 | tf_op jit(solution)/shard_map/ppermute | solution.py:74
  208.6 10.7 %collective-permute-start.31 = (f32[8,1280]{1,0:T(8,128)S(1)}, f32[8,1280]{1,0:T(8,128)S(1)}, u32[]{:S(2)}, u32[]{:S(2)}) collective-permute-start(f32[8,1280]{1,0:T(8,128)S(1)} %get-tuple-element.148), channel_id=1, source_target_pairs={{0,224},{32,0},{64,32},{96,64},{128,96},{160,128},{192,160},{224,1... | collective-permute-start | bytes 122888 | tf_op jit(solution)/shard_map/ppermute | solution.py:101
  212.0 10.9 %collective-permute-start.30 = (f32[8,1280]{1,0:T(8,128)S(1)}, f32[8,1280]{1,0:T(8,128)S(1)}, u32[]{:S(2)}, u32[]{:S(2)}) collective-permute-start(f32[8,1280]{1,0:T(8,128)S(1)} %get-tuple-element.149), channel_id=1, source_target_pairs={{0,192},{32,224},{64,0},{96,32},{128,64},{160,96},{192,128},{224,1... | collective-permute-start | bytes 122888 | tf_op jit(solution)/shard_map/ppermute | solution.py:101
  214.2 10.4 %collective-permute-start.29 = (f32[8,1280]{1,0:T(8,128)S(1)}, f32[8,1280]{1,0:T(8,128)S(1)}, u32[]{:S(2)}, u32[]{:S(2)}) collective-permute-start(f32[8,1280]{1,0:T(8,128)S(1)} %get-tuple-element.150), channel_id=1, source_target_pairs={{0,160},{32,192},{64,224},{96,0},{128,32},{160,64},{192,96},{224,1... | collective-permute-start | bytes 122888 | tf_op jit(solution)/shard_map/ppermute | solution.py:101
  215.4 9.2 %collective-permute-start.28 = (f32[8,1280]{1,0:T(8,128)S(1)}, f32[8,1280]{1,0:T(8,128)S(1)}, u32[]{:S(2)}, u32[]{:S(2)}) collective-permute-start(f32[8,1280]{1,0:T(8,128)S(1)} %get-tuple-element.151), channel_id=1, source_target_pairs={{0,128},{32,160},{64,192},{96,224},{128,0},{160,32},{192,64},{224,... | collective-permute-start | bytes 122888 | tf_op jit(solution)/shard_map/ppermute | solution.py:101
  219.3 7.2 %collective-permute-start.27 = (f32[8,1280]{1,0:T(8,128)S(1)}, f32[8,1280]{1,0:T(8,128)S(1)}, u32[]{:S(2)}, u32[]{:S(2)}) collective-permute-start(f32[8,1280]{1,0:T(8,128)S(1)} %get-tuple-element.152), channel_id=1, source_target_pairs={{0,96},{32,128},{64,160},{96,192},{128,224},{160,0},{192,32},{224,... | collective-permute-start | bytes 122888 | tf_op jit(solution)/shard_map/ppermute | solution.py:101
  219.4 8.0 %collective-permute-start.26 = (f32[8,1280]{1,0:T(8,128)S(1)}, f32[8,1280]{1,0:T(8,128)S(1)}, u32[]{:S(2)}, u32[]{:S(2)}) collective-permute-start(f32[8,1280]{1,0:T(8,128)S(1)} %get-tuple-element.153), channel_id=1, source_target_pairs={{0,64},{32,96},{64,128},{96,160},{128,192},{160,224},{192,0},{224,... | collective-permute-start | bytes 122888 | tf_op jit(solution)/shard_map/ppermute | solution.py:101
  228.1 14.7 %collective-permute-start.32 = (f32[8,1280]{1,0:T(8,128)S(1)}, f32[8,1280]{1,0:T(8,128)S(1)}, u32[]{:S(2)}, u32[]{:S(2)}) collective-permute-start(f32[8,1280]{1,0:T(8,128)S(1)} %get-tuple-element.95), channel_id=1, source_target_pairs={{0,32},{32,64},{64,96},{96,128},{128,160},{160,192},{192,224},{224... | collective-permute-start | bytes 122888 | tf_op jit(solution)/shard_map/ppermute | solution.py:105
  234.2 12.5 %collective-permute-start.33 = (f32[8,1280]{1,0:T(8,128)S(1)}, f32[8,1280]{1,0:T(8,128)S(1)}, u32[]{:S(2)}, u32[]{:S(2)}) collective-permute-start(f32[8,1280]{1,0:T(8,128)S(1)} %get-tuple-element.95), channel_id=1, source_target_pairs={{0,64},{32,96},{64,128},{96,160},{128,192},{160,224},{192,0},{224,... | collective-permute-start | bytes 122888 | tf_op jit(solution)/shard_map/ppermute | solution.py:105
  235.8 12.0 %collective-permute-start.34 = (f32[8,1280]{1,0:T(8,128)S(1)}, f32[8,1280]{1,0:T(8,128)S(1)}, u32[]{:S(2)}, u32[]{:S(2)}) collective-permute-start(f32[8,1280]{1,0:T(8,128)S(1)} %get-tuple-element.95), channel_id=1, source_target_pairs={{0,96},{32,128},{64,160},{96,192},{128,224},{160,0},{192,32},{224,... | collective-permute-start | bytes 122888 | tf_op jit(solution)/shard_map/ppermute | solution.py:105
  238.0 9.9 %collective-permute-start.35 = (f32[8,1280]{1,0:T(8,128)S(1)}, f32[8,1280]{1,0:T(8,128)S(1)}, u32[]{:S(2)}, u32[]{:S(2)}) collective-permute-start(f32[8,1280]{1,0:T(8,128)S(1)} %get-tuple-element.95), channel_id=1, source_target_pairs={{0,128},{32,160},{64,192},{96,224},{128,0},{160,32},{192,64},{224,... | collective-permute-start | bytes 122888 | tf_op jit(solution)/shard_map/ppermute | solution.py:105
  240.6 7.3 %collective-permute-start.36 = (f32[8,1280]{1,0:T(8,128)S(1)}, f32[8,1280]{1,0:T(8,128)S(1)}, u32[]{:S(2)}, u32[]{:S(2)}) collective-permute-start(f32[8,1280]{1,0:T(8,128)S(1)} %get-tuple-element.95), channel_id=1, source_target_pairs={{0,160},{32,192},{64,224},{96,0},{128,32},{160,64},{192,96},{224,1... | collective-permute-start | bytes 122888 | tf_op jit(solution)/shard_map/ppermute | solution.py:105
  (18 other events, 251.6 us)
Sparse Core Ops, SparseCore 0:
  11.1 54.9 all-gather.1
